TPU v7x, 128 devices: a whole 4x4x4 slice. The times are simulated.
128 devices in a mesh: pair: 8 (over z, core), tile: 16 (over y, x).
Axes of the slice: x: 4, y: 4, z: 4, core: 2. Of those that a mesh axis runs over, the one named last changes fastest.
Arguments:
- phase: float32 [2000, 16, 1024], P('pair', 'tile'), may hold values from -12 to 12
- incidence: int32 [2000, 2], P('pair'), may hold values from 0 to 399, as said below
- pair_weight: float32 [2000], P('pair'), may hold values from 0.3 to 3
Outputs:
- solution_field: float32 [400, 16, 1024], P(None, 'tile', 'pair')
- residual: float32 [400, 16, 1024], P(None, 'tile', 'pair')
Inputs may be any that keep to these rules, and one draw needn't show every extreme that they name: `incidence`: each row holds a reference date and a strictly later secondary date, at most 7 dates after the reference date; every pair of consecutive dates (t, t + 1) is some row.
All inputs are finite; a program needn't handle non-finite values.
Results may differ from a plain program's by a relative error of at most 0.00028.
Values sent between devices are 32-bit elements; how exact they have to be, the bound alone decides.
No kernel may reach another device: no remote copies, remote signals or barrier semaphores. Data moves between devices by JAX's collectives and lax.ppermute only.
A program may use at most 64 MiB of HBM per device.

v0:
```python
import jax
import jax.numpy as jnp
from jax import lax
from jax.sharding import PartitionSpec as P

DATES = 400
ITERS = 3


temporal_weight = 2.0
spatial_weight = 0.5
ridge_weight = 0.05


def padded_2(cells, sides, width):
    for axis, dim in sides:
        count = lax.axis_size(axis)
        ends = count - 1
        head = lax.slice_in_dim(cells, 0, width, axis=dim)
        tail = lax.slice_in_dim(cells, cells.shape[dim] - width, cells.shape[dim], axis=dim)
        cells = jnp.concatenate(
            [
                lax.ppermute(tail, axis, [(i, (i + 1) % count) for i in range(ends)]),
                cells,
                lax.ppermute(head, axis, [((i + 1) % count, i) for i in range(ends)]),
            ],
            axis=dim,
        )
    return cells


def design(incidence):
    dates = jnp.arange(DATES, dtype=jnp.int32)
    later = (dates[None, :] == incidence[:, 1:2]).astype(jnp.float32)
    earlier = (dates[None, :] == incidence[:, 0:1]).astype(jnp.float32)
    return later - earlier


def adjoint(network, weighted):
    return jnp.einsum("kt,krc->trc", network, weighted, precision=lax.Precision.HIGHEST)


def normal_local(network, weights, field):
    forward = jnp.einsum("kt,trc->krc", network, field, precision=lax.Precision.HIGHEST)
    return adjoint(network, weights[:, None, None] * forward)


def reduce_terms(terms):
    return lax.psum_scatter(terms, "pair", scatter_dimension=2, tiled=True)


def regularize(field):
    second = field[:-2] - 2.0 * field[1:-1] + field[2:]
    temporal = (
        jnp.pad(second, ((2, 0), (0, 0), (0, 0)))
        - 2.0 * jnp.pad(second, ((1, 1), (0, 0), (0, 0)))
        + jnp.pad(second, ((0, 2), (0, 0), (0, 0)))
    )
    padded = padded_2(field, (("pair", 2), ("tile", 1)), 1)
    spatial = (
        4.0 * field
        - padded[:, 2:, 1:-1]
        - padded[:, :-2, 1:-1]
        - padded[:, 1:-1, 2:]
        - padded[:, 1:-1, :-2]
    )
    return temporal_weight * temporal + spatial_weight * spatial + ridge_weight * field


def squares(residual):
    return lax.psum(jnp.sum(residual * residual), ("pair", "tile"))


def body(phase, incidence, pair_weight):
    network = design(incidence)
    right_side = reduce_terms(adjoint(network, pair_weight[:, None, None] * phase))
    solution_field = jnp.zeros_like(right_side)
    residual = right_side
    direction = right_side
    norm_now = squares(residual)
    for iteration in range(ITERS):
        image = reduce_terms(
            normal_local(
                network, pair_weight, lax.all_gather(direction, "pair", axis=2, tiled=True)
            )
        ) + regularize(direction)
        alpha = norm_now / lax.psum(jnp.sum(direction * image), ("pair", "tile"))
        solution_field = solution_field + alpha * direction
        residual = residual - alpha * image
        norm_next = squares(residual)
        direction = residual + norm_next / norm_now * direction
        norm_now = norm_next
    return (solution_field, residual)


def solution(mesh):
    return jax.shard_map(
        body,
        mesh=mesh,
        in_specs=(P("pair", "tile", None), P("pair", None), P("pair")),
        out_specs=(P(None, "tile", "pair"), P(None, "tile", "pair")),
        check_vma=False,
    )
```

profile of v0, /device:TPU:1, one launch (start us, length us, event | category | flops | bytes accessed | tf_op | source)
XLA Modules:
  0.0 583.9 jit_solution(5298408395924067616)
XLA Ops:
  7.2 0.8 fusion.58
  8.0 2.0 broadcast_multiply_fusion
  10.0 2.9 convolution_bitcast_fusion.3
  12.9 33.4 %reduce-scatter.5.cloned.1.call-done = f32[400,1,128]{2,0,1:T(8,128)} async-done(((f32[400,1,1024]{2,0,1:T(8,128)}), f32[400,1,128]{2,0,1:T(8,128)}) %reduce-scatter.5.cloned.1.call-update) | async-done | bytes 204816 | tf_op jit(solution)/shard_map/reduce_scatter | solution.py:49
  46.4 29.4 %all-gather.4.cloned.1.call-done = f32[400,1,1024]{2,0,1:T(8,128)} async-done(((f32[400,1,128]{2,0,1:T(8,128)}), f32[400,1,1024]{2,0,1:T(8,128)}) %all-gather.4.cloned.1.call-update) | async-done | bytes 1638416 | tf_op jit(solution)/shard_map/all_gather | solution.py:84
  75.7 3.4 fusion.6
  79.1 2.8 convolution_bitcast_fusion.2
  82.1 2.6 collective-permute-start
  84.8 1.9 collective-permute-start.1
  86.7 0.8 collective-permute-done
  87.4 4.4 collective-permute-done.1
  92.1 3.1 collective-permute-start.3
  95.2 1.3 collective-permute-start.2
  96.6 4.6 collective-permute-done.3
  101.2 4.1 collective-permute-done.2
  105.3 7.2 %reduce-scatter.7.cloned.1.call-done = f32[400,1,128]{2,0,1:T(8,128)} async-done(((f32[400,1,1024]{2,0,1:T(8,128)}), f32[400,1,128]{2,0,1:T(8,128)}) %reduce-scatter.7.cloned.1.call-update) | async-done | bytes 204816 | tf_op jit(solution)/shard_map/reduce_scatter | solution.py:49
  112.5 1.9 multiply_reduce_fusion.4
  114.4 67.8 %all-reduce.9 = (f32[]{:T(128)}, f32[]{:T(128)}) all-reduce(f32[]{:T(128)} %get-tuple-element.5, f32[]{:T(128)} %get-tuple-element.4), channel_id=1, replica_groups=mesh['pair'=8,'tile'=16] {'pair','tile'}, use_global_device_ids=true, to_apply=%region_2.0 | all-reduce | flops 2 | bytes 16 | tf_op jit(solution)/shard_map/psum | solution.py:71
  184.2 62.5 %psum.44 = f32[]{:T(128)} all-reduce(f32[]{:T(128)} %multiply_reduce_fusion.3), channel_id=1, replica_groups=mesh['pair'=8,'tile'=16] {'pair','tile'}, use_global_device_ids=true, to_apply=%region_7.8 | all-reduce | flops 1 | bytes 8 | tf_op jit(solution)/shard_map/psum | solution.py:71
  249.1 23.0 %all-gather.6.cloned.1.call-done = f32[400,1,1024]{2,0,1:T(8,128)} async-done(((f32[400,1,128]{2,0,1:T(8,128)}), f32[400,1,1024]{2,0,1:T(8,128)}) %all-gather.6.cloned.1.call-update) | async-done | bytes 1638416 | tf_op jit(solution)/shard_map/all_gather | solution.py:84
  272.1 3.4 fusion.9
  275.5 2.8 convolution_bitcast_fusion.1
  278.5 2.6 collective-permute-start.4
  281.1 1.9 collective-permute-start.5
  283.1 0.8 collective-permute-done.4
  283.8 4.4 collective-permute-done.5
  288.4 3.1 collective-permute-start.7
  291.6 1.3 collective-permute-start.6
  292.9 4.6 collective-permute-done.7
  297.6 4.1 collective-permute-done.6
  301.7 7.2 %reduce-scatter.9.cloned.1.call-done = f32[400,1,128]{2,0,1:T(8,128)} async-done(((f32[400,1,1024]{2,0,1:T(8,128)}), f32[400,1,128]{2,0,1:T(8,128)}) %reduce-scatter.9.cloned.1.call-update) | async-done | bytes 204816 | tf_op jit(solution)/shard_map/reduce_scatter | solution.py:49
  308.9 1.9 multiply_reduce_fusion.2
  310.8 67.8 %psum.45 = f32[]{:T(128)} all-reduce(f32[]{:T(128)} %get-tuple-element.12), channel_id=1, replica_groups=mesh['pair'=8,'tile'=16] {'pair','tile'}, use_global_device_ids=true, to_apply=%region_10.11 | all-reduce | flops 1 | bytes 8 | tf_op jit(solution)/shard_map/psum | solution.py:87
  380.6 62.5 %psum.46 = f32[]{:T(128)} all-reduce(f32[]{:T(128)} %get-tuple-element.10), channel_id=1, replica_groups=mesh['pair'=8,'tile'=16] {'pair','tile'}, use_global_device_ids=true, to_apply=%region_12.13 | all-reduce | flops 1 | bytes 8 | tf_op jit(solution)/shard_map/psum | solution.py:71
  445.3 23.2 %all-gather.8.cloned.1.call-done = f32[400,1,1024]{2,0,1:T(8,128)} async-done(((f32[400,1,128]{2,0,1:T(8,128)}), f32[400,1,1024]{2,0,1:T(8,128)}) %all-gather.8.cloned.1.call-update) | async-done | bytes 1638416 | tf_op jit(solution)/shard_map/all_gather | solution.py:84
  468.5 3.4 fusion.12
  471.9 2.8 convolution_bitcast_fusion
  474.8 2.6 collective-permute-start.8
  477.5 1.9 collective-permute-start.9
  480.1 4.4 collective-permute-done.9
  484.8 3.1 collective-permute-start.11
  487.9 1.3 collective-permute-start.10
  489.3 4.6 collective-permute-done.11
  493.9 4.1 collective-permute-done.10
  498.0 7.3 %reduce-scatter.11.cloned.1.call-done = f32[400,1,128]{2,0,1:T(8,128)} async-done(((f32[400,1,1024]{2,0,1:T(8,128)}), f32[400,1,128]{2,0,1:T(8,128)}) %reduce-scatter.11.cloned.1.call-update) | async-done | bytes 204816 | tf_op jit(solution)/shard_map/reduce_scatter | solution.py:49
  505.3 1.9 multiply_reduce_fusion
  507.2 67.7 %psum.47 = f32[]{:T(128)} all-reduce(f32[]{:T(128)} %get-tuple-element.8), channel_id=1, replica_groups=mesh['pair'=8,'tile'=16] {'pair','tile'}, use_global_device_ids=true, to_apply=%region_15.16 | all-reduce | flops 1 | bytes 8 | tf_op jit(solution)/shard_map/psum | solution.py:87
  576.3 0.8 multiply_subtract_fusion
  (36 shorter events, 5.3 us)
Async XLA Ops:
  7.2 39.1 %reduce-scatter.5.cloned.1.call-start = ((), (), s32[]{:S(2)}) async-start(), calls=%async_computation.4 | async-start | bytes 1843200 | tf_op jit(solution)/shard_map/reduce_scatter | solution.py:49
  10.0 65.7 %copy-start.3 = (f32[250]{0:T(256)S(1)}, f32[250]{0:T(256)}, u32[]{:S(2)}) copy-start(f32[250]{0:T(256)} %param.5) | copy-start | bytes 3004
  12.9 62.8 %all-gather.4.cloned.1.call-start = ((), (), s32[]{:S(2)}) async-start(), calls=%async_computation.5 | async-start | bytes 1843200 | tf_op jit(solution)/shard_map/all_gather | solution.py:84
  46.3 66.2 %reduce-scatter.7.cloned.1.call-start = ((), (), s32[]{:S(2)}) async-start(), calls=%async_computation.6 | async-start | bytes 1843200 | tf_op jit(solution)/shard_map/reduce_scatter | solution.py:49
  79.1 2.9 copy-start
  82.0 190.1 %all-gather.6.cloned.1.call-start = ((), (), s32[]{:S(2)}) async-start(), calls=%async_computation.7 | async-start | bytes 1843200 | tf_op jit(solution)/shard_map/all_gather | solution.py:84
  82.1 5.3 collective-permute-start
  84.8 7.1 %collective-permute-start.1 = (f32[400,1,1]{2,0,1:T(8,128)S(1)}, f32[400,1,1]{2,0,1:T(8,128)S(1)}, u32[]{:S(2)}, u32[]{:S(2)}) collective-permute-start(f32[400,1,1]{2,0,1:T(8,128)S(1)} %get-tuple-element.19), channel_id=1, source_target_pairs={{16,0},{32,16},{48,32},{64,48},{80,64},{96,80},{112,96},{17,1},{33... | collective-permute-start | bytes 4808 | tf_op jit(solution)/shard_map/ppermute | solution.py:25
  92.1 9.1 %collective-permute-start.3 = (f32[400,1,130]{2,0,1:T(8,128)S(1)}, f32[400,1,130]{2,0,1:T(8,128)S(1)}, u32[]{:S(2)}, u32[]{:S(2)}) collective-permute-start(f32[400,1,130]{2,0,1:T(8,128)S(1)} %pad_maximum_fusion), channel_id=1, source_target_pairs={{0,1},{1,2},{2,3},{3,4},{4,5},{5,6},{6,7},{7,8},{8,9},{9,10},{10,1... | collective-permute-start | bytes 624008 | tf_op jit(solution)/shard_map/ppermute | solution.py:23
  95.2 10.1 %collective-permute-start.2 = (f32[400,1,130]{2,0,1:T(8,128)S(1)}, f32[400,1,130]{2,0,1:T(8,128)S(1)}, u32[]{:S(2)}, u32[]{:S(2)}) collective-permute-start(f32[400,1,130]{2,0,1:T(8,128)S(1)} %pad_maximum_fusion), channel_id=1, source_target_pairs={{1,0},{2,1},{3,2},{4,3},{5,4},{6,5},{7,6},{8,7},{9,8},{10,9},{11,1... | collective-permute-start | bytes 624008 | tf_op jit(solution)/shard_map/ppermute | solution.py:25
  248.8 60.1 %reduce-scatter.9.cloned.1.call-start = ((), (), s32[]{:S(2)}) async-start(), calls=%async_computation.8 | async-start | bytes 1843200 | tf_op jit(solution)/shard_map/reduce_scatter | solution.py:49
  275.5 2.9 copy-start.1
  278.3 190.1 %all-gather.8.cloned.1.call-start = ((), (), s32[]{:S(2)}) async-start(), calls=%async_computation.9 | async-start | bytes 1843200 | tf_op jit(solution)/shard_map/all_gather | solution.py:84
  278.5 5.3 collective-permute-start.4
  281.1 7.1 %collective-permute-start.5 = (f32[400,1,1]{2,0,1:T(8,128)S(1)}, f32[400,1,1]{2,0,1:T(8,128)S(1)}, u32[]{:S(2)}, u32[]{:S(2)}) collective-permute-start(f32[400,1,1]{2,0,1:T(8,128)S(1)} %get-tuple-element.17), channel_id=1, source_target_pairs={{16,0},{32,16},{48,32},{64,48},{80,64},{96,80},{112,96},{17,1},{33... | collective-permute-start | bytes 4808 | tf_op jit(solution)/shard_map/ppermute | solution.py:25
  288.4 9.1 %collective-permute-start.7 = (f32[400,1,130]{2,0,1:T(8,128)S(1)}, f32[400,1,130]{2,0,1:T(8,128)S(1)}, u32[]{:S(2)}, u32[]{:S(2)}) collective-permute-start(f32[400,1,130]{2,0,1:T(8,128)S(1)} %pad_maximum_fusion.1), channel_id=1, source_target_pairs={{0,1},{1,2},{2,3},{3,4},{4,5},{5,6},{6,7},{7,8},{8,9},{9,10},{10,1... | collective-permute-start | bytes 624008 | tf_op jit(solution)/shard_map/ppermute | solution.py:23
  291.6 10.1 %collective-permute-start.6 = (f32[400,1,130]{2,0,1:T(8,128)S(1)}, f32[400,1,130]{2,0,1:T(8,128)S(1)}, u32[]{:S(2)}, u32[]{:S(2)}) collective-permute-start(f32[400,1,130]{2,0,1:T(8,128)S(1)} %pad_maximum_fusion.1), channel_id=1, source_target_pairs={{1,0},{2,1},{3,2},{4,3},{5,4},{6,5},{7,6},{8,7},{9,8},{10,9},{11,1... | collective-permute-start | bytes 624008 | tf_op jit(solution)/shard_map/ppermute | solution.py:25
  445.2 60.1 %reduce-scatter.11.cloned.1.call-start = ((), (), s32[]{:S(2)}) async-start(), calls=%async_computation.10 | async-start | bytes 1843200 | tf_op jit(solution)/shard_map/reduce_scatter | solution.py:49
  471.9 2.8 copy-start.2
  474.8 5.3 collective-permute-start.8
  477.5 7.1 %collective-permute-start.9 = (f32[400,1,1]{2,0,1:T(8,128)S(1)}, f32[400,1,1]{2,0,1:T(8,128)S(1)}, u32[]{:S(2)}, u32[]{:S(2)}) collective-permute-start(f32[400,1,1]{2,0,1:T(8,128)S(1)} %get-tuple-element.15), channel_id=1, source_target_pairs={{16,0},{32,16},{48,32},{64,48},{80,64},{96,80},{112,96},{17,1},{33... | collective-permute-start | bytes 4808 | tf_op jit(solution)/shard_map/ppermute | solution.py:25
  484.8 9.1 %collective-permute-start.11 = (f32[400,1,130]{2,0,1:T(8,128)S(1)}, f32[400,1,130]{2,0,1:T(8,128)S(1)}, u32[]{:S(2)}, u32[]{:S(2)}) collective-permute-start(f32[400,1,130]{2,0,1:T(8,128)S(1)} %pad_maximum_fusion.2), channel_id=1, source_target_pairs={{0,1},{1,2},{2,3},{3,4},{4,5},{5,6},{6,7},{7,8},{8,9},{9,10},{10,1... | collective-permute-start | bytes 624008 | tf_op jit(solution)/shard_map/ppermute | solution.py:23
  487.9 10.1 %collective-permute-start.10 = (f32[400,1,130]{2,0,1:T(8,128)S(1)}, f32[400,1,130]{2,0,1:T(8,128)S(1)}, u32[]{:S(2)}, u32[]{:S(2)}) collective-permute-start(f32[400,1,130]{2,0,1:T(8,128)S(1)} %pad_maximum_fusion.2), channel_id=1, source_target_pairs={{1,0},{2,1},{3,2},{4,3},{5,4},{6,5},{7,6},{8,7},{9,8},{10,9},{11,1... | collective-permute-start | bytes 624008 | tf_op jit(solution)/shard_map/ppermute | solution.py:25
Sparse Core Ops, SparseCore 0:
  13.0 33.2 reduce-scatter.4
  48.0 27.7 all-gather.3
  82.1 30.4 reduce-scatter.6
  249.0 23.0 all-gather.5
  278.5 30.4 reduce-scatter.8
  445.3 23.0 all-gather.7
  474.8 30.4 reduce-scatter.10
where the time goes:
time: 585 us; the launch traced here: 584 us
  blocking collectives  328 us (56%)
  waiting for transfers between devices  172 us (29%)
  starting transfers between devices  27.3 us (5%)
  matrix products  21.5 us (4%)
  between operations  21.2 us (4%)
  other arithmetic  12 us (2%)
    psum x3, blocking collectives, squares(): return lax.psum(jnp.sum(residual * residual), ('pair', 'tile'))  193 us
    psum x2, blocking collectives, body(): alpha = norm_now / lax.psum(jnp.sum(direction * image), ('pair', 'tile'))  136 us
    all_gather x3, waiting for transfers between devices, body(): lax.all_gather(direction, 'pair', axis=2, tiled=True)  75.6 us
    reduce_scatter x4, waiting for transfers between devices, reduce_terms(): return lax.psum_scatter(terms, 'pair', scatter_dimension=2, tiled=True)  55.1 us
    ppermute x6, waiting for transfers between devices, padded_2(): lax.ppermute(head, axis, [((i + 1) % count, i) for i in range(ends)])  25.6 us
    ppermute x6, starting transfers between devices, padded_2(): lax.ppermute(tail, axis, [(i, (i + 1) % count) for i in range(ends)])  17.2 us
    ppermute x6, waiting for transfers between devices, padded_2(): lax.ppermute(tail, axis, [(i, (i + 1) % count) for i in range(ends)])  16.1 us
  transfers between devices with their start and end apart: 19, of which 19 were waited for; matrix products, arithmetic and copies ran while one was open for 0% of the time, Pallas kernels for 0%

commit v1 on v0

v1 whole, which is shorter than its diff:
```python
import numpy as np
import jax
import jax.numpy as jnp
from jax import lax
from jax.sharding import PartitionSpec as P

DATES = 400
ITERS = 3
SPAN = 8

temporal_weight = 2.0
spatial_weight = 0.5
ridge_weight = 0.05

HIGHEST = lax.Precision.HIGHEST


def temporal_matrix():
    second = np.zeros((DATES - 2, DATES), np.float64)
    rows = np.arange(DATES - 2)
    second[rows, rows] = 1.0
    second[rows, rows + 1] = -2.0
    second[rows, rows + 2] = 1.0
    return (second.T @ second).astype(np.float32)


def from_prev(cells, axis):
    count = lax.axis_size(axis)
    return lax.ppermute(cells, axis, [(i, i + 1) for i in range(count - 1)])


def from_next(cells, axis):
    count = lax.axis_size(axis)
    return lax.ppermute(cells, axis, [(i + 1, i) for i in range(count - 1)])


def exchange(cells):
    return (
        from_prev(cells, "tile"),
        from_next(cells, "tile"),
        from_prev(cells[:, -1:], "pair"),
        from_next(cells[:, :1], "pair"),
    )


def neighbours(cells, halo):
    above, below, left, right = halo
    west = jnp.concatenate([left, cells[:, :-1]], axis=1)
    east = jnp.concatenate([cells[:, 1:], right], axis=1)
    return above + below + west + east


def apply_operator(matrix, cells, halo):
    return jnp.dot(matrix, cells, precision=HIGHEST) - spatial_weight * neighbours(cells, halo)


def total(parts):
    count = lax.axis_size("pair") * lax.axis_size("tile")
    sent = jnp.broadcast_to(parts[None, :], (count, parts.shape[0]))
    got = lax.all_to_all(sent, ("pair", "tile"), 0, 0, tiled=True)
    return jnp.sum(got, axis=0)


def normal_matrix(weights):
    dates = jnp.arange(DATES, dtype=jnp.int32)
    offset = dates[None, :] - dates[:, None]
    upper = jnp.zeros((DATES, DATES), jnp.float32)
    for d in range(1, SPAN):
        upper = upper + jnp.where(offset == d, -weights[:, d : d + 1], 0.0)
    coupling = upper + upper.T
    degree = -jnp.sum(coupling, axis=1)
    diagonal = degree + (4.0 * spatial_weight + ridge_weight)
    return coupling + jnp.where(offset == 0, diagonal[:, None], 0.0) + temporal_weight * temporal_matrix()


def body(phase, incidence, pair_weight):
    groups = lax.axis_size("pair")
    cols = phase.shape[2] // groups
    dates = jnp.arange(DATES, dtype=jnp.int32)
    earlier = incidence[:, 0:1]
    later = incidence[:, 1:2]
    network = (dates[None, :] == later).astype(jnp.float32) - (dates[None, :] == earlier).astype(jnp.float32)
    weighted = (pair_weight[:, None] * phase[:, 0, :]).reshape(-1, groups, cols)
    part = jnp.einsum("kt,kjc->jtc", network, weighted, precision=HIGHEST)
    span_hot = (jnp.arange(SPAN, dtype=jnp.int32)[None, :] == (later - earlier)).astype(jnp.float32)
    start_hot = (dates[None, :] == earlier).astype(jnp.float32)
    span_weights = jnp.einsum("kt,kd->td", start_hot, span_hot * pair_weight[:, None], precision=HIGHEST)
    stacked = jnp.concatenate([part, jnp.broadcast_to(span_weights, (groups, DATES, SPAN))], axis=2)
    reduced = lax.psum_scatter(stacked, "pair", scatter_dimension=0, tiled=True)[0]
    residual = reduced[:, :cols]
    matrix = normal_matrix(reduced[:, cols:])

    residual_halo = exchange(residual)
    solution_field = jnp.zeros_like(residual)
    for iteration in range(ITERS):
        image_of_residual = apply_operator(matrix, residual, residual_halo)
        if iteration == 0:
            parts = jnp.stack([jnp.sum(residual * residual), jnp.sum(residual * image_of_residual)])
        else:
            parts = jnp.stack(
                [
                    jnp.sum(residual * residual),
                    jnp.sum(residual * image_of_residual),
                    jnp.sum(residual * image),
                    jnp.sum(direction * image_of_residual),
                    jnp.sum(direction * image),
                ]
            )
        if iteration < ITERS - 1:
            image_halo = exchange(image_of_residual)
        sums = total(parts)
        norm_now = sums[0]
        if iteration == 0:
            alpha = norm_now / sums[1]
            direction = residual
            image = image_of_residual
            if iteration < ITERS - 1:
                halo_image = image_halo
        else:
            beta = norm_now / norm_prev
            curvature = sums[1] + beta * (sums[2] + sums[3]) + beta * beta * sums[4]
            alpha = norm_now / curvature
            direction = residual + beta * direction
            image = image_of_residual + beta * image
            if iteration < ITERS - 1:
                halo_image = tuple(a + beta * b for a, b in zip(image_halo, halo_image))
        solution_field = solution_field + alpha * direction
        residual = residual - alpha * image
        if iteration < ITERS - 1:
            residual_halo = tuple(a - alpha * b for a, b in zip(residual_halo, halo_image))
        norm_prev = norm_now
    return (solution_field[:, None, :], residual[:, None, :])


def solution(mesh):
    return jax.shard_map(
        body,
        mesh=mesh,
        in_specs=(P("pair", "tile", None), P("pair", None), P("pair")),
        out_specs=(P(None, "tile", "pair"), P(None, "tile", "pair")),
        check_vma=False,
    )
```

time: 585 us -> 171 us (0.29)
  blocking collectives: 328 us -> 19.7 us
  waiting for transfers between devices: 172 us -> 34.9 us
  starting transfers between devices: 27.3 us -> 56.3 us
  local copies, waits for them, and re-layouts: 1.12 us -> 14.6 us
  matrix products: 21.5 us -> 13.4 us
  other arithmetic: 12 us -> 6.05 us
    psum x5 -> x0, blocking collectives: 328 us -> none  [the longest x3 193 us: squares(): return lax.psum(jnp.sum(residual * residual), ('pair', 'tile'))]
    all_gather x3 -> x0, waiting for transfers between devices: 75.6 us -> none  [body(): lax.all_gather(direction, 'pair', axis=2, tiled=True)]
    ppermute x12, waiting for transfers between devices: 41.7 us -> 0.58 us  [the longest x6 0.57 us: from_prev(): return lax.ppermute(cells, axis, [(i, i + 1) for i in range(count - 1)])]
    all_to_all x0 -> x2, starting transfers between devices: none -> 20.8 us  [total(): got = lax.all_to_all(sent, ('pair', 'tile'), 0, 0, tiled=True)]
    reduce_scatter x4 -> x1, waiting for transfers between devices: 55.1 us -> 34.3 us  [body(): lax.psum_scatter(stacked, 'pair', scatter_dimension=0, tiled=True)[0]]
    all_to_all x0 -> x1, blocking collectives: none -> 19.7 us  [total(): got = lax.all_to_all(sent, ('pair', 'tile'), 0, 0, tiled=True)]
    ppermute x12, starting transfers between devices: 26.8 us -> 35.4 us  [the longest x6 19.1 us: from_prev(): return lax.ppermute(cells, axis, [(i, i + 1) for i in range(count - 1)])]
    dot_general x7 -> x5, matrix products: 21.5 us -> 13.4 us  [the longest x3 7.45 us: apply_operator(): jnp.dot(matrix, cells, precision=HIGHEST)]
  transfers between devices with their start and end apart: 19 -> 15, of which waited for: 19 -> 2; matrix products, arithmetic and copies ran while one was open for 0% -> 2% of each run, Pallas kernels for 0% -> 0%
where the time goes in v1:
time: 171 us; the launch traced here: 170 us
  starting transfers between devices  56.3 us (33%)
  waiting for transfers between devices  34.9 us (20%)
  between operations  24.7 us (14%)
  blocking collectives  19.7 us (12%)
  local copies, waits for them, and re-layouts  14.6 us (9%)
  matrix products  13.4 us (8%)
  other arithmetic  6.05 us (4%)
    reduce_scatter x1, waiting for transfers between devices, body(): lax.psum_scatter(stacked, 'pair', scatter_dimension=0, tiled=True)[0]  34.3 us
    all_to_all x2, starting transfers between devices, total(): got = lax.all_to_all(sent, ('pair', 'tile'), 0, 0, tiled=True)  20.8 us
    all_to_all x1, blocking collectives, total(): got = lax.all_to_all(sent, ('pair', 'tile'), 0, 0, tiled=True)  19.7 us
    ppermute x6, starting transfers between devices, from_prev(): return lax.ppermute(cells, axis, [(i, i + 1) for i in range(count - 1)])  19.1 us
    ppermute x6, starting transfers between devices, from_next(): return lax.ppermute(cells, axis, [(i + 1, i) for i in range(count - 1)])  16.2 us
    dot_general x3, matrix products, apply_operator(): jnp.dot(matrix, cells, precision=HIGHEST)  7.45 us
    another operation x2, local copies, waits for them, and re-layouts, body(): jnp.stack([jnp.sum(residual * residual), jnp.sum(residual * image_of_resi...  6.53 us
    dot_general x1, matrix products, body(): part = jnp.einsum('kt,kjc->jtc', network, weighted, precision=HIGHEST)  4.9 us
  transfers between devices with their start and end apart: 15, of which 2 were waited for; matrix products, arithmetic and copies ran while one was open for 2% of the time, Pallas kernels for 0%

profile of v1, /device:TPU:1, one launch (start us, length us, event | category | flops | bytes accessed | tf_op | source)
XLA Modules:
  0.0 169.6 jit_solution(16012787759464022431)
XLA Ops:
  7.2 0.0 reduce-scatter.2.cloned.1.call-start
  7.2 0.8 fusion.46
  8.0 1.0 fusion.20
  9.0 4.9 %convolution_bitcast_fusion = f32[8,400,128]{1,2,0:T(8,128)S(1)} fusion(f32[250,8,128]{2,1,0:T(8,128)} %bitcast.52, f32[250]{0:T(256)} %param.6, s32[250]{0:T(256)S(1)} %bitcast.83, s32[250]{0:T(256)S(1)} %bitcast.81), kind=kOutput, calls=%fused_computation.1 | convolution fusion | flops 1229555968 | bytes 2665400 | tf_op jit(solution)/shard_map/kt,kjc->jtc/dot_general | solution.py:84
  13.9 1.6 pad_maximum_fusion
  15.6 0.0 reduce-scatter.2.cloned.1.call-update
  15.6 34.3 %reduce-scatter.2.cloned.1.call-done = f32[1,400,136]{1,2,0:T(8,128)} async-done(((f32[8,400,136]{1,2,0:T(8,128)}), f32[1,400,136]{1,2,0:T(8,128)}) %reduce-scatter.2.cloned.1.call-update) | async-done | bytes 217616 | tf_op jit(solution)/shard_map/reduce_scatter | solution.py:89
  49.9 1.0 slice_negate_fusion.6
  50.9 1.0 slice.148
  51.9 1.3 collective-permute-start.1
  53.2 4.0 %collective-permute-start = (f32[400,128]{0,1:T(8,128)S(1)}, f32[400,128]{0,1:T(8,128)S(1)}, u32[]{:S(2)}, u32[]{:S(2)}) collective-permute-start(f32[400,128]{0,1:T(8,128)S(1)} %slice.148), channel_id=1, source_target_pairs={{0,1},{1,2},{2,3},{3,4},{4,5},{5,6},{6,7},{7,8},{8,9},{9,10},{10,1... | collective-permute-start | bytes 614408 | tf_op jit(solution)/shard_map/ppermute | solution.py:29
  57.2 1.1 fusion.41
  58.3 6.3 %collective-permute-start.3 = (f32[400,1]{0,1:T(1,128)S(1)}, f32[400,1]{0,1:T(1,128)S(1)}, u32[]{:S(2)}, u32[]{:S(2)}) collective-permute-start(f32[400,1]{0,1:T(1,128)S(1)} %get-tuple-element.28), channel_id=1, source_target_pairs={{16,0},{32,16},{48,32},{64,48},{80,64},{96,80},{112,96},{17,1},{33... | collective-permute-start | bytes 4808 | tf_op jit(solution)/shard_map/ppermute | solution.py:34
  64.6 1.9 %collective-permute-start.2 = (f32[400,1]{0,1:T(1,128)S(1)}, f32[400,1]{0,1:T(1,128)S(1)}, u32[]{:S(2)}, u32[]{:S(2)}) collective-permute-start(f32[400,1]{0,1:T(1,128)S(1)} %get-tuple-element.29), channel_id=1, source_target_pairs={{0,16},{16,32},{32,48},{48,64},{64,80},{80,96},{96,112},{1,17},{17... | collective-permute-start | bytes 4808 | tf_op jit(solution)/shard_map/ppermute | solution.py:29
  66.5 0.6 fusion.17
  67.0 0.0 collective-permute-done.3
  67.1 0.6 collective-permute-done.2
  67.6 3.1 %multiply_reduce_fusion.10 = (f32[]{:T(128)}, f32[]{:T(128)}, f32[400,128]{0,1:T(8,128)S(1)}) fusion(f32[400,136]{0,1:T(8,128)} %bitcast.47, f32[400,1]{0,1:T(1,128)S(1)} %collective-permute-done.3, f32[400,127]{0,1:T(8,128)S(1)} %get-tuple-element.36, f32[400,127]{0,1:T(8,128)S(1)} %get-tuple-element.37, f32[400,1]{0,1:T(1,128)S(1)} %collective-permute-done.2, ...), kind=kOutput, calls=%fused_computation.61 | convolution fusion | flops 253843200 | bytes 2631688 | tf_op jit(solution)/shard_map/dot_general | solution.py:54
  70.7 1.4 pad_maximum_fusion.1
  72.1 0.7 broadcast_in_dim.142
  72.7 9.8 %all-to-all-start = ((f32[128,1,2]{2,1,0:T(1,128)}), f32[128,1,2]{2,1,0:T(1,128)S(1)}, u32[]{:S(2)}, u32[]{:S(2)}) async-start(f32[128,1,2]{2,1,0:T(1,128)} %broadcast_in_dim.142), calls=%async_computation.1 | async-start | bytes 131072 | tf_op jit(solution)/shard_map/all_to_all | solution.py:60
  82.6 1.3 collective-permute-start.5
  83.9 4.0 %collective-permute-start.4 = (f32[400,128]{0,1:T(8,128)S(1)}, f32[400,128]{0,1:T(8,128)S(1)}, u32[]{:S(2)}, u32[]{:S(2)}) collective-permute-start(f32[400,128]{0,1:T(8,128)S(1)} %get-tuple-element.63), channel_id=1, source_target_pairs={{0,1},{1,2},{2,3},{3,4},{4,5},{5,6},{6,7},{7,8},{8,9},{9,10},{10,1... | collective-permute-start | bytes 614408 | tf_op jit(solution)/shard_map/ppermute | solution.py:29
  87.9 3.5 %collective-permute-start.7 = (f32[400,1]{0,1:T(1,128)S(1)}, f32[400,1]{0,1:T(1,128)S(1)}, u32[]{:S(2)}, u32[]{:S(2)}) collective-permute-start(f32[400,1]{0,1:T(1,128)S(1)} %get-tuple-element.46), channel_id=1, source_target_pairs={{16,0},{32,16},{48,32},{64,48},{80,64},{96,80},{112,96},{17,1},{33... | collective-permute-start | bytes 4808 | tf_op jit(solution)/shard_map/ppermute | solution.py:34
  91.5 2.6 %collective-permute-start.6 = (f32[400,1]{0,1:T(1,128)S(1)}, f32[400,1]{0,1:T(1,128)S(1)}, u32[]{:S(2)}, u32[]{:S(2)}) collective-permute-start(f32[400,1]{0,1:T(1,128)S(1)} %get-tuple-element.47), channel_id=1, source_target_pairs={{0,16},{16,32},{32,48},{48,64},{64,80},{80,96},{96,112},{1,17},{17... | collective-permute-start | bytes 4808 | tf_op jit(solution)/shard_map/ppermute | solution.py:29
  94.1 0.2 reduce_sum.142
  94.2 0.6 fusion.49
  96.2 2.1 %multiply_reduce_fusion.5 = (f32[]{:T(128)}, f32[]{:T(128)}, f32[]{:T(128)}, f32[]{:T(128)}, f32[400,128]{0,1:T(8,128)S(1)}) fusion(f32[400,136]{0,1:T(8,128)S(1)} %bitcast.49, f32[400,128]{0,1:T(8,128)S(1)} %multiply_subtract_fusion.3, f32[400,128]{0,1:T(8,128)S(1)} %get-tuple-element.63, f32[400,1]{0,1:T(1,128)S(1)} %multiply_subtract_fusion.6, ...), kind=kOutput, calls=%fused_computation.53 | convolution fusion | flops 254252800 | bytes 3680276 | tf_op jit(solution)/shard_map/dot_general | solution.py:54
  98.4 3.3 %stack.50 = f32[5]{0:T(128)S(1)} concatenate(f32[1]{0:T(128)} %bitcast.18, f32[1]{0:T(128)} %bitcast.19, f32[1]{0:T(128)} %bitcast.20, f32[1]{0:T(128)} %bitcast.21, f32[1]{0:T(128)} %bitcast.15), dimensions={0} | concatenate | bytes 40 | tf_op jit(solution)/shard_map/stack | solution.py:100
  101.7 0.7 broadcast_in_dim.143
  102.4 11.0 %all-to-all-start.1 = ((f32[128,1,5]{2,1,0:T(1,128)}), f32[128,1,5]{2,1,0:T(1,128)S(1)}, u32[]{:S(2)}, u32[]{:S(2)}) async-start(f32[128,1,5]{2,1,0:T(1,128)} %broadcast_in_dim.143), calls=%async_computation.2 | async-start | bytes 131072 | tf_op jit(solution)/shard_map/all_to_all | solution.py:60
  113.4 3.3 %collective-permute-start.8 = (f32[400,128]{0,1:T(8,128)S(1)}, f32[400,128]{0,1:T(8,128)S(1)}, u32[]{:S(2)}, u32[]{:S(2)}) collective-permute-start(f32[400,128]{0,1:T(8,128)S(1)} %get-tuple-element.64), channel_id=1, source_target_pairs={{0,1},{1,2},{2,3},{3,4},{4,5},{5,6},{6,7},{7,8},{8,9},{9,10},{10,1... | collective-permute-start | bytes 614408 | tf_op jit(solution)/shard_map/ppermute | solution.py:29
  116.7 1.3 collective-permute-start.9
  118.0 2.5 %collective-permute-start.11 = (f32[400,1]{0,1:T(1,128)S(1)}, f32[400,1]{0,1:T(1,128)S(1)}, u32[]{:S(2)}, u32[]{:S(2)}) collective-permute-start(f32[400,1]{0,1:T(1,128)S(1)} %get-tuple-element.42), channel_id=1, source_target_pairs={{16,0},{32,16},{48,32},{64,48},{80,64},{96,80},{112,96},{17,1},{33... | collective-permute-start | bytes 4808 | tf_op jit(solution)/shard_map/ppermute | solution.py:34
  120.6 3.3 %collective-permute-start.10 = (f32[400,1]{0,1:T(1,128)S(1)}, f32[400,1]{0,1:T(1,128)S(1)}, u32[]{:S(2)}, u32[]{:S(2)}) collective-permute-start(f32[400,1]{0,1:T(1,128)S(1)} %get-tuple-element.43), channel_id=1, source_target_pairs={{0,16},{16,32},{32,48},{48,64},{64,80},{80,96},{96,112},{1,17},{17... | collective-permute-start | bytes 4808 | tf_op jit(solution)/shard_map/ppermute | solution.py:29
  123.9 0.2 reduce_sum.147
  124.0 0.7 fusion.48
  129.3 0.0 copy-start.2
  129.3 0.1 multiply_subtract_fusion
  129.5 0.9 copy-done.2
  130.4 2.2 %multiply_reduce_fusion = (f32[]{:T(128)}, f32[]{:T(128)}, f32[]{:T(128)}, f32[]{:T(128)}, f32[]{:T(128)}, /*index=5*/f32[400,128]{0,1:T(8,128)S(1)}) fusion(f32[400,128]{0,1:T(8,128)S(1)} %get-tuple-element.26, f32[400,128]{0,1:T(8,128)S(1)} %multiply_subtract_fusion.3, f32[]{:T(128)S(6)} %div.16, f32[400,136]{0,1:T(8,128)S(1)} %bitcast.50, ...), kind=kOutput, calls=%fused_computation.45 | convolution fusion | flops 254867200 | bytes 4466720 | tf_op jit(solution)/shard_map/dot_general | solution.py:54
  132.7 3.2 %stack.56 = f32[5]{0:T(128)S(1)} concatenate(f32[1]{0:T(128)} %bitcast.26, f32[1]{0:T(128)} %bitcast.27, f32[1]{0:T(128)} %bitcast.28, f32[1]{0:T(128)} %bitcast.29, f32[1]{0:T(128)} %bitcast.30), dimensions={0} | concatenate | bytes 40 | tf_op jit(solution)/shard_map/stack | solution.py:100
  135.9 19.7 %all_to_all.18 = f32[128,1,5]{2,1,0:T(1,128)S(1)} all-to-all(f32[128,1,5]{2,1,0:T(1,128)S(1)} %broadcast_in_dim.144), channel_id=1, replica_groups=mesh['pair'=8,'tile'=16] {'pair','tile'}, dimensions={0} | all-to-all | bytes 5120 | tf_op jit(solution)/shard_map/all_to_all | solution.py:60
  155.6 0.2 reduce_sum.153
  155.8 0.7 fusion.47
  160.9 0.2 subtract_bitcast_fusion
  161.1 0.8 copy.41
  161.9 0.8 copy.40
  (28 shorter events, 0.3 us)
Async XLA Ops:
  7.2 42.8 %reduce-scatter.2.cloned.1.call-start = ((), (), s32[]{:S(2)}) async-start(), calls=%async_computation.4 | async-start | bytes 2506752 | tf_op jit(solution)/shard_map/reduce_scatter | solution.py:89
  15.6 52.1 %copy-start.1 = (f32[400,400]{1,0:T(8,128)S(1)}, f32[400,400]{1,0:T(8,128)}, u32[]{:S(2)}) copy-start(f32[400,400]{1,0:T(8,128)} %constant.25.clone) | copy-start | bytes 1920004
  51.9 15.7 %collective-permute-start.1 = (f32[400,128]{0,1:T(8,128)S(1)}, f32[400,128]{0,1:T(8,128)S(1)}, u32[]{:S(2)}, u32[]{:S(2)}) collective-permute-start(f32[400,128]{0,1:T(8,128)S(1)} %slice.148), channel_id=1, source_target_pairs={{1,0},{2,1},{3,2},{4,3},{5,4},{6,5},{7,6},{8,7},{9,8},{10,9},{11,1... | collective-permute-start | bytes 614408 | tf_op jit(solution)/shard_map/ppermute | solution.py:34
  53.2 14.4 %collective-permute-start = (f32[400,128]{0,1:T(8,128)S(1)}, f32[400,128]{0,1:T(8,128)S(1)}, u32[]{:S(2)}, u32[]{:S(2)}) collective-permute-start(f32[400,128]{0,1:T(8,128)S(1)} %slice.148), channel_id=1, source_target_pairs={{0,1},{1,2},{2,3},{3,4},{4,5},{5,6},{6,7},{7,8},{8,9},{9,10},{10,1... | collective-permute-start | bytes 614408 | tf_op jit(solution)/shard_map/ppermute | solution.py:29
  58.3 8.8 %collective-permute-start.3 = (f32[400,1]{0,1:T(1,128)S(1)}, f32[400,1]{0,1:T(1,128)S(1)}, u32[]{:S(2)}, u32[]{:S(2)}) collective-permute-start(f32[400,1]{0,1:T(1,128)S(1)} %get-tuple-element.28), channel_id=1, source_target_pairs={{16,0},{32,16},{48,32},{64,48},{80,64},{96,80},{112,96},{17,1},{33... | collective-permute-start | bytes 4808 | tf_op jit(solution)/shard_map/ppermute | solution.py:34
  64.6 3.1 %collective-permute-start.2 = (f32[400,1]{0,1:T(1,128)S(1)}, f32[400,1]{0,1:T(1,128)S(1)}, u32[]{:S(2)}, u32[]{:S(2)}) collective-permute-start(f32[400,1]{0,1:T(1,128)S(1)} %get-tuple-element.29), channel_id=1, source_target_pairs={{0,16},{16,32},{32,48},{48,64},{64,80},{80,96},{96,112},{1,17},{17... | collective-permute-start | bytes 4808 | tf_op jit(solution)/shard_map/ppermute | solution.py:29
  67.6 28.4 %copy-start = (f32[1,400,136]{1,2,0:T(8,128)S(1)}, f32[1,400,136]{1,2,0:T(8,128)}, u32[]{:S(2)}) copy-start(f32[1,400,136]{1,2,0:T(8,128)} %reduce-scatter.2.cloned.1.call-done) | copy-start | bytes 652804
  72.7 21.3 %all-to-all-start = ((f32[128,1,2]{2,1,0:T(1,128)}), f32[128,1,2]{2,1,0:T(1,128)S(1)}, u32[]{:S(2)}, u32[]{:S(2)}) async-start(f32[128,1,2]{2,1,0:T(1,128)} %broadcast_in_dim.142), calls=%async_computation.1 | async-start | bytes 131072 | tf_op jit(solution)/shard_map/all_to_all | solution.py:60
  82.6 13.6 %collective-permute-start.5 = (f32[400,128]{0,1:T(8,128)S(1)}, f32[400,128]{0,1:T(8,128)S(1)}, u32[]{:S(2)}, u32[]{:S(2)}) collective-permute-start(f32[400,128]{0,1:T(8,128)S(1)} %get-tuple-element.63), channel_id=1, source_target_pairs={{1,0},{2,1},{3,2},{4,3},{5,4},{6,5},{7,6},{8,7},{9,8},{10,9},{11,1... | collective-permute-start | bytes 614408 | tf_op jit(solution)/shard_map/ppermute | solution.py:34
  83.9 12.3 %collective-permute-start.4 = (f32[400,128]{0,1:T(8,128)S(1)}, f32[400,128]{0,1:T(8,128)S(1)}, u32[]{:S(2)}, u32[]{:S(2)}) collective-permute-start(f32[400,128]{0,1:T(8,128)S(1)} %get-tuple-element.63), channel_id=1, source_target_pairs={{0,1},{1,2},{2,3},{3,4},{4,5},{5,6},{6,7},{7,8},{8,9},{9,10},{10,1... | collective-permute-start | bytes 614408 | tf_op jit(solution)/shard_map/ppermute | solution.py:29
  87.9 8.3 %collective-permute-start.7 = (f32[400,1]{0,1:T(1,128)S(1)}, f32[400,1]{0,1:T(1,128)S(1)}, u32[]{:S(2)}, u32[]{:S(2)}) collective-permute-start(f32[400,1]{0,1:T(1,128)S(1)} %get-tuple-element.46), channel_id=1, source_target_pairs={{16,0},{32,16},{48,32},{64,48},{80,64},{96,80},{112,96},{17,1},{33... | collective-permute-start | bytes 4808 | tf_op jit(solution)/shard_map/ppermute | solution.py:34
  91.5 4.7 %collective-permute-start.6 = (f32[400,1]{0,1:T(1,128)S(1)}, f32[400,1]{0,1:T(1,128)S(1)}, u32[]{:S(2)}, u32[]{:S(2)}) collective-permute-start(f32[400,1]{0,1:T(1,128)S(1)} %get-tuple-element.47), channel_id=1, source_target_pairs={{0,16},{16,32},{32,48},{48,64},{64,80},{80,96},{96,112},{1,17},{17... | collective-permute-start | bytes 4808 | tf_op jit(solution)/shard_map/ppermute | solution.py:29
  102.4 21.5 %all-to-all-start.1 = ((f32[128,1,5]{2,1,0:T(1,128)}), f32[128,1,5]{2,1,0:T(1,128)S(1)}, u32[]{:S(2)}, u32[]{:S(2)}) async-start(f32[128,1,5]{2,1,0:T(1,128)} %broadcast_in_dim.143), calls=%async_computation.2 | async-start | bytes 131072 | tf_op jit(solution)/shard_map/all_to_all | solution.py:60
  113.4 16.1 %collective-permute-start.8 = (f32[400,128]{0,1:T(8,128)S(1)}, f32[400,128]{0,1:T(8,128)S(1)}, u32[]{:S(2)}, u32[]{:S(2)}) collective-permute-start(f32[400,128]{0,1:T(8,128)S(1)} %get-tuple-element.64), channel_id=1, source_target_pairs={{0,1},{1,2},{2,3},{3,4},{4,5},{5,6},{6,7},{7,8},{8,9},{9,10},{10,1... | collective-permute-start | bytes 614408 | tf_op jit(solution)/shard_map/ppermute | solution.py:29
  116.7 12.8 %collective-permute-start.9 = (f32[400,128]{0,1:T(8,128)S(1)}, f32[400,128]{0,1:T(8,128)S(1)}, u32[]{:S(2)}, u32[]{:S(2)}) collective-permute-start(f32[400,128]{0,1:T(8,128)S(1)} %get-tuple-element.64), channel_id=1, source_target_pairs={{1,0},{2,1},{3,2},{4,3},{5,4},{6,5},{7,6},{8,7},{9,8},{10,9},{11,1... | collective-permute-start | bytes 614408 | tf_op jit(solution)/shard_map/ppermute | solution.py:34
  118.0 11.4 %collective-permute-start.11 = (f32[400,1]{0,1:T(1,128)S(1)}, f32[400,1]{0,1:T(1,128)S(1)}, u32[]{:S(2)}, u32[]{:S(2)}) collective-permute-start(f32[400,1]{0,1:T(1,128)S(1)} %get-tuple-element.42), channel_id=1, source_target_pairs={{16,0},{32,16},{48,32},{64,48},{80,64},{96,80},{112,96},{17,1},{33... | collective-permute-start | bytes 4808 | tf_op jit(solution)/shard_map/ppermute | solution.py:34
  120.6 8.9 %collective-permute-start.10 = (f32[400,1]{0,1:T(1,128)S(1)}, f32[400,1]{0,1:T(1,128)S(1)}, u32[]{:S(2)}, u32[]{:S(2)}) collective-permute-start(f32[400,1]{0,1:T(1,128)S(1)} %get-tuple-element.43), channel_id=1, source_target_pairs={{0,16},{16,32},{32,48},{48,64},{64,80},{80,96},{96,112},{1,17},{17... | collective-permute-start | bytes 4808 | tf_op jit(solution)/shard_map/ppermute | solution.py:29
  129.3 1.1 copy-start.2
Sparse Core Ops, SparseCore 0:
  15.7 34.1 reduce-scatter.1

commit v2 on v1

--- a/solution.py
+++ b/solution.py
@@ -76,21 +76,32 @@
 def body(phase, incidence, pair_weight):
     groups = lax.axis_size("pair")
     cols = phase.shape[2] // groups
-    dates = jnp.arange(DATES, dtype=jnp.int32)
-    earlier = incidence[:, 0:1]
-    later = incidence[:, 1:2]
+    padded = jnp.pad(phase[:, 0, :], ((0, 0), (1, 1)))
+    windows = jnp.stack([padded[:, j * cols : j * cols + cols + 2] for j in range(groups)])
+    meta = jnp.stack(
+        [incidence[:, 0].astype(jnp.float32), incidence[:, 1].astype(jnp.float32), pair_weight], axis=1
+    )
+    meta = jnp.pad(meta, ((0, 0), (0, 3)))
+    chunks = jnp.concatenate([windows, jnp.broadcast_to(meta, (groups,) + meta.shape)], axis=2)
+    got = lax.all_to_all(chunks, "pair", 0, 0, tiled=True).reshape(-1, chunks.shape[2])
+    values = got[:, : cols + 2]
+    earlier = got[:, cols + 2 : cols + 3]
+    later = got[:, cols + 3 : cols + 4]
+    weight = got[:, cols + 4 : cols + 5]
+    dates = jnp.arange(DATES, dtype=jnp.float32)
     network = (dates[None, :] == later).astype(jnp.float32) - (dates[None, :] == earlier).astype(jnp.float32)
-    weighted = (pair_weight[:, None] * phase[:, 0, :]).reshape(-1, groups, cols)
-    part = jnp.einsum("kt,kjc->jtc", network, weighted, precision=HIGHEST)
-    span_hot = (jnp.arange(SPAN, dtype=jnp.int32)[None, :] == (later - earlier)).astype(jnp.float32)
+    right_wide = jnp.einsum("kt,kc->tc", network, weight * values, precision=HIGHEST)
+    span_hot = (jnp.arange(SPAN, dtype=jnp.float32)[None, :] == (later - earlier)).astype(jnp.float32)
     start_hot = (dates[None, :] == earlier).astype(jnp.float32)
-    span_weights = jnp.einsum("kt,kd->td", start_hot, span_hot * pair_weight[:, None], precision=HIGHEST)
-    stacked = jnp.concatenate([part, jnp.broadcast_to(span_weights, (groups, DATES, SPAN))], axis=2)
-    reduced = lax.psum_scatter(stacked, "pair", scatter_dimension=0, tiled=True)[0]
-    residual = reduced[:, :cols]
-    matrix = normal_matrix(reduced[:, cols:])
-
-    residual_halo = exchange(residual)
+    span_weights = jnp.einsum("kt,kd->td", start_hot, span_hot * weight, precision=HIGHEST)
+    matrix = normal_matrix(span_weights)
+    residual = right_wide[:, 1:-1]
+    residual_halo = (
+        from_prev(residual, "tile"),
+        from_next(residual, "tile"),
+        right_wide[:, :1],
+        right_wide[:, -1:],
+    )
     solution_field = jnp.zeros_like(residual)
     for iteration in range(ITERS):
         image_of_residual = apply_operator(matrix, residual, residual_halo)

time: 171 us -> 139 us (0.81)
  waiting for transfers between devices: 34.9 us -> 2.11 us
  blocking collectives: 19.7 us -> 42.4 us
  between operations: 24.7 us -> 11.3 us
  starting transfers between devices: 56.3 us -> 50.1 us
  other arithmetic: 6.05 us -> 3.58 us
  local copies, waits for them, and re-layouts: 14.6 us -> 16.4 us
    reduce_scatter x1 -> x0, waiting for transfers between devices: 34.3 us -> none  [body(): lax.psum_scatter(stacked, 'pair', scatter_dimension=0, tiled=True)[0]]
    all_to_all x0 -> x1, blocking collectives: none -> 22.7 us  [body(): lax.all_to_all(chunks, 'pair', 0, 0, tiled=True)]
    ppermute x6 -> x5, starting transfers between devices: 16.2 us -> 10.1 us  [from_next(): return lax.ppermute(cells, axis, [(i + 1, i) for i in range(count - 1)])]
    unnamed x8 -> x16, local copies, waits for them, and re-layouts: 2.58 us -> 5.59 us
    ppermute x6 -> x5, starting transfers between devices: 19.1 us -> 17 us  [from_prev(): return lax.ppermute(cells, axis, [(i, i + 1) for i in range(count - 1)])]
    all_to_all x2, starting transfers between devices: 20.8 us -> 22.9 us  [total(): got = lax.all_to_all(sent, ('pair', 'tile'), 0, 0, tiled=True)]
  transfers between devices with their start and end apart: 15 -> 12, of which waited for: 2 -> 2; matrix products, arithmetic and copies ran while one was open for 2% -> 3% of each run, Pallas kernels for 0% -> 0%
where the time goes in v2:
time: 139 us; the launch traced here: 138 us
  starting transfers between devices  50.1 us (36%)
  blocking collectives  42.4 us (31%)
  local copies, waits for them, and re-layouts  16.4 us (12%)
  matrix products  12.6 us (9%)
  between operations  11.3 us (8%)
  other arithmetic  3.58 us (3%)
  waiting for transfers between devices  2.11 us (2%)
    all_to_all x2, starting transfers between devices, total(): got = lax.all_to_all(sent, ('pair', 'tile'), 0, 0, tiled=True)  22.9 us
    all_to_all x1, blocking collectives, body(): lax.all_to_all(chunks, 'pair', 0, 0, tiled=True)  22.7 us
    all_to_all x1, blocking collectives, total(): got = lax.all_to_all(sent, ('pair', 'tile'), 0, 0, tiled=True)  19.7 us
    ppermute x5, starting transfers between devices, from_prev(): return lax.ppermute(cells, axis, [(i, i + 1) for i in range(count - 1)])  17 us
    ppermute x5, starting transfers between devices, from_next(): return lax.ppermute(cells, axis, [(i + 1, i) for i in range(count - 1)])  10.1 us
    dot_general x3, matrix products, apply_operator(): jnp.dot(matrix, cells, precision=HIGHEST)  7.46 us
    another operation x2, local copies, waits for them, and re-layouts, body(): jnp.stack([jnp.sum(residual * residual), jnp.sum(residual * image_of_resi...  6.53 us
    unnamed x16, local copies, waits for them, and re-layouts  5.59 us
  transfers between devices with their start and end apart: 12, of which 2 were waited for; matrix products, arithmetic and copies ran while one was open for 3% of the time, Pallas kernels for 0%

profile of v2, /device:TPU:1, one launch (start us, length us, event | category | flops | bytes accessed | tf_op | source)
XLA Modules:
  0.0 138.5 jit_solution(15328882329483446690)
XLA Ops:
  0.6 0.8 slice_convert_fusion.1
  1.4 2.4 %copy.43 = f32[250,1,1024]{0,2,1:T(8,128)S(1)} copy(f32[250,1,1024]{2,1,0:T(1,128)} %param.4) | data formatting | bytes 2048000 | tf_op args[0]
  3.8 0.0 copy-start
  3.9 0.6 copy-done
  4.5 0.1 pad_maximum_fusion
  4.6 22.7 %all_to_all.23 = f32[8,250,136]{1,2,0:T(8,128)S(1)} all-to-all(f32[8,250,136]{1,2,0:T(8,128)S(1)} %pad_maximum_fusion), channel_id=1, replica_groups=mesh['pair'=8,'tile'=16] {'pair'}, dimensions={0} | all-to-all | bytes 2176000 | tf_op jit(solution)/shard_map/all_to_all | solution.py:86
  27.3 0.4 copy.44
  27.7 0.5 reshape.31
  28.2 3.3 %fusion = f32[400,130]{0,1:T(8,128)S(1)} fusion(f32[2000]{0:T(1024)S(1)} %bitcast.113, f32[2000]{0:T(1024)S(1)} %bitcast.115, f32[2000,136]{0,1:T(8,128)S(1)} %reshape.31, f32[2000]{0:T(1024)S(1)} %bitcast.111), kind=kOutput, calls=%fused_computation | convolution fusion | flops 1252259968 | bytes 1320000 | tf_op jit(solution)/shard_map/kt,kc->tc/dot_general | solution.py:93
  31.5 0.0 copy-start.1
  31.5 1.4 %collective-permute-start.1 = (f32[400,128]{0,1:T(8,128)S(1)}, f32[400,128]{0,1:T(8,128)S(1)}, u32[]{:S(2)}, u32[]{:S(2)}) collective-permute-start(f32[400,128]{0,1:T(8,128)S(1)} %slice.198), channel_id=1, source_target_pairs={{1,0},{2,1},{3,2},{4,3},{5,4},{6,5},{7,6},{8,7},{9,8},{10,9},{11,1... | collective-permute-start | bytes 614408 | tf_op jit(solution)/shard_map/ppermute | solution.py:34
  33.0 4.0 %collective-permute-start = (f32[400,128]{0,1:T(8,128)S(1)}, f32[400,128]{0,1:T(8,128)S(1)}, u32[]{:S(2)}, u32[]{:S(2)}) collective-permute-start(f32[400,128]{0,1:T(8,128)S(1)} %slice.198), channel_id=1, source_target_pairs={{0,1},{1,2},{2,3},{3,4},{4,5},{5,6},{6,7},{7,8},{8,9},{9,10},{10,1... | collective-permute-start | bytes 614408 | tf_op jit(solution)/shard_map/ppermute | solution.py:29
  37.0 1.9 %fusion.3 = f32[400,8]{0,1:T(8,128)S(1)} fusion(f32[2000]{0:T(1024)S(1)} %bitcast.114, f32[2000]{0:T(1024)S(1)} %bitcast.112, f32[2000]{0:T(1024)S(1)} %bitcast.110), kind=kOutput, calls=%fused_computation.4 | convolution fusion | flops 77632000 | bytes 36800 | tf_op jit(solution)/shard_map/kt,kd->td/dot_general | solution.py:96
  38.9 0.6 fusion.28
  39.4 1.2 collective-permute-done.1
  40.7 0.9 collective-permute-done
  41.5 2.0 %multiply_reduce_fusion.10 = (f32[]{:T(128)}, f32[]{:T(128)}, f32[400,128]{0,1:T(8,128)S(1)}) fusion(f32[400,130]{0,1:T(8,128)S(1)} %fusion, f32[400,128]{0,1:T(8,128)S(1)} %collective-permute-done, f32[400,128]{0,1:T(8,128)S(1)} %collective-permute-done.1, f32[400,400]{1,0:T(8,128)S(1)} %copy-done.1, f32[400]{0:T(512)S(1)} %negate_add_fusion, ...), kind=kOutput, calls=%fused_computation.70 | convolution fusion | flops 253740800 | bytes 2627592 | tf_op jit(solution)/shard_map/dot_general | solution.py:54
  43.5 1.4 pad_maximum_fusion.1
  44.9 0.7 broadcast_in_dim.140
  45.5 11.9 %all-to-all-start.1 = ((f32[128,1,2]{2,1,0:T(1,128)}), f32[128,1,2]{2,1,0:T(1,128)S(1)}, u32[]{:S(2)}, u32[]{:S(2)}) async-start(f32[128,1,2]{2,1,0:T(1,128)} %broadcast_in_dim.140), calls=%async_computation.1 | async-start | bytes 131072 | tf_op jit(solution)/shard_map/all_to_all | solution.py:60
  57.5 1.3 collective-permute-start.3
  58.8 4.0 %collective-permute-start.2 = (f32[400,128]{0,1:T(8,128)S(1)}, f32[400,128]{0,1:T(8,128)S(1)}, u32[]{:S(2)}, u32[]{:S(2)}) collective-permute-start(f32[400,128]{0,1:T(8,128)S(1)} %get-tuple-element.64), channel_id=1, source_target_pairs={{0,1},{1,2},{2,3},{3,4},{4,5},{5,6},{6,7},{7,8},{8,9},{9,10},{10,1... | collective-permute-start | bytes 614408 | tf_op jit(solution)/shard_map/ppermute | solution.py:29
  62.8 3.5 %collective-permute-start.5 = (f32[400,1]{0,1:T(1,128)S(1)}, f32[400,1]{0,1:T(1,128)S(1)}, u32[]{:S(2)}, u32[]{:S(2)}) collective-permute-start(f32[400,1]{0,1:T(1,128)S(1)} %get-tuple-element.41), channel_id=1, source_target_pairs={{16,0},{32,16},{48,32},{64,48},{80,64},{96,80},{112,96},{17,1},{33... | collective-permute-start | bytes 4808 | tf_op jit(solution)/shard_map/ppermute | solution.py:34
  66.3 2.6 %collective-permute-start.4 = (f32[400,1]{0,1:T(1,128)S(1)}, f32[400,1]{0,1:T(1,128)S(1)}, u32[]{:S(2)}, u32[]{:S(2)}) collective-permute-start(f32[400,1]{0,1:T(1,128)S(1)} %get-tuple-element.42), channel_id=1, source_target_pairs={{0,16},{16,32},{32,48},{48,64},{64,80},{80,96},{96,112},{1,17},{17... | collective-permute-start | bytes 4808 | tf_op jit(solution)/shard_map/ppermute | solution.py:29
  69.0 0.2 reduce_sum.142
  69.1 0.6 fusion.56
  71.1 0.0 collective-permute-done.4
  71.1 3.3 %multiply_reduce_fusion.5 = (f32[]{:T(128)}, f32[]{:T(128)}, f32[]{:T(128)}, f32[]{:T(128)}, f32[400,128]{0,1:T(8,128)S(1)}) fusion(f32[400,130]{0,1:T(8,128)S(1)} %fusion, f32[400,128]{0,1:T(8,128)S(1)} %multiply_subtract_fusion.3, f32[400,128]{0,1:T(8,128)S(1)} %get-tuple-element.64, f32[400,1]{0,1:T(1,128)S(1)} %get-tuple-element.31, ...), kind=kOutput, calls=%fused_computation.62 | convolution fusion | flops 254252800 | bytes 3501076 | tf_op jit(solution)/shard_map/dot_general | solution.py:54
  74.4 3.3 %stack.96 = f32[5]{0:T(128)S(1)} concatenate(f32[1]{0:T(128)} %bitcast.25, f32[1]{0:T(128)} %bitcast.26, f32[1]{0:T(128)} %bitcast.27, f32[1]{0:T(128)} %bitcast.28, f32[1]{0:T(128)} %bitcast.22), dimensions={0} | concatenate | bytes 40 | tf_op jit(solution)/shard_map/stack | solution.py:111
  77.7 0.7 broadcast_in_dim.141
  78.4 11.0 %all-to-all-start.2 = ((f32[128,1,5]{2,1,0:T(1,128)}), f32[128,1,5]{2,1,0:T(1,128)S(1)}, u32[]{:S(2)}, u32[]{:S(2)}) async-start(f32[128,1,5]{2,1,0:T(1,128)} %broadcast_in_dim.141), calls=%async_computation.2 | async-start | bytes 131072 | tf_op jit(solution)/shard_map/all_to_all | solution.py:60
  89.4 3.3 %collective-permute-start.6 = (f32[400,128]{0,1:T(8,128)S(1)}, f32[400,128]{0,1:T(8,128)S(1)}, u32[]{:S(2)}, u32[]{:S(2)}) collective-permute-start(f32[400,128]{0,1:T(8,128)S(1)} %get-tuple-element.65), channel_id=1, source_target_pairs={{0,1},{1,2},{2,3},{3,4},{4,5},{5,6},{6,7},{7,8},{8,9},{9,10},{10,1... | collective-permute-start | bytes 614408 | tf_op jit(solution)/shard_map/ppermute | solution.py:29
  92.7 1.3 collective-permute-start.7
  94.0 2.5 %collective-permute-start.9 = (f32[400,1]{0,1:T(1,128)S(1)}, f32[400,1]{0,1:T(1,128)S(1)}, u32[]{:S(2)}, u32[]{:S(2)}) collective-permute-start(f32[400,1]{0,1:T(1,128)S(1)} %get-tuple-element.37), channel_id=1, source_target_pairs={{16,0},{32,16},{48,32},{64,48},{80,64},{96,80},{112,96},{17,1},{33... | collective-permute-start | bytes 4808 | tf_op jit(solution)/shard_map/ppermute | solution.py:34
  96.6 3.1 %collective-permute-start.8 = (f32[400,1]{0,1:T(1,128)S(1)}, f32[400,1]{0,1:T(1,128)S(1)}, u32[]{:S(2)}, u32[]{:S(2)}) collective-permute-start(f32[400,1]{0,1:T(1,128)S(1)} %get-tuple-element.38), channel_id=1, source_target_pairs={{0,16},{16,32},{32,48},{48,64},{64,80},{80,96},{96,112},{1,17},{17... | collective-permute-start | bytes 4808 | tf_op jit(solution)/shard_map/ppermute | solution.py:29
  99.7 0.2 reduce_sum.147
  99.9 0.7 fusion.55
  105.1 0.0 copy-start.2
  105.1 0.1 multiply_subtract_fusion
  105.3 0.9 copy-done.2
  106.3 2.2 %multiply_reduce_fusion = (f32[]{:T(128)}, f32[]{:T(128)}, f32[]{:T(128)}, f32[]{:T(128)}, f32[]{:T(128)}, /*index=5*/f32[400,128]{0,1:T(8,128)S(1)}) fusion(f32[400,128]{0,1:T(8,128)S(1)} %get-tuple-element.26, f32[400,128]{0,1:T(8,128)S(1)} %multiply_subtract_fusion.3, f32[]{:T(128)S(6)} %div.16, f32[400,130]{0,1:T(8,128)S(1)} %fusion, ...), kind=kOutput, calls=%fused_computation.54 | convolution fusion | flops 254867200 | bytes 4466720 | tf_op jit(solution)/shard_map/dot_general | solution.py:54
  108.5 3.2 %stack.102 = f32[5]{0:T(128)S(1)} concatenate(f32[1]{0:T(128)} %bitcast.33, f32[1]{0:T(128)} %bitcast.34, f32[1]{0:T(128)} %bitcast.35, f32[1]{0:T(128)} %bitcast.36, f32[1]{0:T(128)} %bitcast.37), dimensions={0} | concatenate | bytes 40 | tf_op jit(solution)/shard_map/stack | solution.py:111
  111.7 19.7 %all_to_all.24 = f32[128,1,5]{2,1,0:T(1,128)S(1)} all-to-all(f32[128,1,5]{2,1,0:T(1,128)S(1)} %broadcast_in_dim.142), channel_id=1, replica_groups=mesh['pair'=8,'tile'=16] {'pair','tile'}, dimensions={0} | all-to-all | bytes 5120 | tf_op jit(solution)/shard_map/all_to_all | solution.py:60
  131.4 0.2 reduce_sum.153
  131.6 0.7 fusion.54
  136.7 0.2 subtract_bitcast_fusion
  136.9 0.8 copy.52
  137.7 0.8 copy.51
  (33 shorter events, 0.4 us)
Async XLA Ops:
  3.8 0.7 copy-start
  31.5 10.0 %copy-start.1 = (f32[400,400]{1,0:T(8,128)S(1)}, f32[400,400]{1,0:T(8,128)}, u32[]{:S(2)}) copy-start(f32[400,400]{1,0:T(8,128)} %constant.27.clone) | copy-start | bytes 1920004
  31.5 9.1 %collective-permute-start.1 = (f32[400,128]{0,1:T(8,128)S(1)}, f32[400,128]{0,1:T(8,128)S(1)}, u32[]{:S(2)}, u32[]{:S(2)}) collective-permute-start(f32[400,128]{0,1:T(8,128)S(1)} %slice.198), channel_id=1, source_target_pairs={{1,0},{2,1},{3,2},{4,3},{5,4},{6,5},{7,6},{8,7},{9,8},{10,9},{11,1... | collective-permute-start | bytes 614408 | tf_op jit(solution)/shard_map/ppermute | solution.py:34
  33.0 8.5 %collective-permute-start = (f32[400,128]{0,1:T(8,128)S(1)}, f32[400,128]{0,1:T(8,128)S(1)}, u32[]{:S(2)}, u32[]{:S(2)}) collective-permute-start(f32[400,128]{0,1:T(8,128)S(1)} %slice.198), channel_id=1, source_target_pairs={{0,1},{1,2},{2,3},{3,4},{4,5},{5,6},{6,7},{7,8},{8,9},{9,10},{10,1... | collective-permute-start | bytes 614408 | tf_op jit(solution)/shard_map/ppermute | solution.py:29
  45.5 23.4 %all-to-all-start.1 = ((f32[128,1,2]{2,1,0:T(1,128)}), f32[128,1,2]{2,1,0:T(1,128)S(1)}, u32[]{:S(2)}, u32[]{:S(2)}) async-start(f32[128,1,2]{2,1,0:T(1,128)} %broadcast_in_dim.140), calls=%async_computation.1 | async-start | bytes 131072 | tf_op jit(solution)/shard_map/all_to_all | solution.py:60
  57.5 13.6 %collective-permute-start.3 = (f32[400,128]{0,1:T(8,128)S(1)}, f32[400,128]{0,1:T(8,128)S(1)}, u32[]{:S(2)}, u32[]{:S(2)}) collective-permute-start(f32[400,128]{0,1:T(8,128)S(1)} %get-tuple-element.64), channel_id=1, source_target_pairs={{1,0},{2,1},{3,2},{4,3},{5,4},{6,5},{7,6},{8,7},{9,8},{10,9},{11,1... | collective-permute-start | bytes 614408 | tf_op jit(solution)/shard_map/ppermute | solution.py:34
  58.8 12.3 %collective-permute-start.2 = (f32[400,128]{0,1:T(8,128)S(1)}, f32[400,128]{0,1:T(8,128)S(1)}, u32[]{:S(2)}, u32[]{:S(2)}) collective-permute-start(f32[400,128]{0,1:T(8,128)S(1)} %get-tuple-element.64), channel_id=1, source_target_pairs={{0,1},{1,2},{2,3},{3,4},{4,5},{5,6},{6,7},{7,8},{8,9},{9,10},{10,1... | collective-permute-start | bytes 614408 | tf_op jit(solution)/shard_map/ppermute | solution.py:29
  62.8 8.3 %collective-permute-start.5 = (f32[400,1]{0,1:T(1,128)S(1)}, f32[400,1]{0,1:T(1,128)S(1)}, u32[]{:S(2)}, u32[]{:S(2)}) collective-permute-start(f32[400,1]{0,1:T(1,128)S(1)} %get-tuple-element.41), channel_id=1, source_target_pairs={{16,0},{32,16},{48,32},{64,48},{80,64},{96,80},{112,96},{17,1},{33... | collective-permute-start | bytes 4808 | tf_op jit(solution)/shard_map/ppermute | solution.py:34
  66.3 4.7 %collective-permute-start.4 = (f32[400,1]{0,1:T(1,128)S(1)}, f32[400,1]{0,1:T(1,128)S(1)}, u32[]{:S(2)}, u32[]{:S(2)}) collective-permute-start(f32[400,1]{0,1:T(1,128)S(1)} %get-tuple-element.42), channel_id=1, source_target_pairs={{0,16},{16,32},{32,48},{48,64},{64,80},{80,96},{96,112},{1,17},{17... | collective-permute-start | bytes 4808 | tf_op jit(solution)/shard_map/ppermute | solution.py:29
  78.4 21.3 %all-to-all-start.2 = ((f32[128,1,5]{2,1,0:T(1,128)}), f32[128,1,5]{2,1,0:T(1,128)S(1)}, u32[]{:S(2)}, u32[]{:S(2)}) async-start(f32[128,1,5]{2,1,0:T(1,128)} %broadcast_in_dim.141), calls=%async_computation.2 | async-start | bytes 131072 | tf_op jit(solution)/shard_map/all_to_all | solution.py:60
  89.4 15.9 %collective-permute-start.6 = (f32[400,128]{0,1:T(8,128)S(1)}, f32[400,128]{0,1:T(8,128)S(1)}, u32[]{:S(2)}, u32[]{:S(2)}) collective-permute-start(f32[400,128]{0,1:T(8,128)S(1)} %get-tuple-element.65), channel_id=1, source_target_pairs={{0,1},{1,2},{2,3},{3,4},{4,5},{5,6},{6,7},{7,8},{8,9},{9,10},{10,1... | collective-permute-start | bytes 614408 | tf_op jit(solution)/shard_map/ppermute | solution.py:29
  92.7 12.6 %collective-permute-start.7 = (f32[400,128]{0,1:T(8,128)S(1)}, f32[400,128]{0,1:T(8,128)S(1)}, u32[]{:S(2)}, u32[]{:S(2)}) collective-permute-start(f32[400,128]{0,1:T(8,128)S(1)} %get-tuple-element.65), channel_id=1, source_target_pairs={{1,0},{2,1},{3,2},{4,3},{5,4},{6,5},{7,6},{8,7},{9,8},{10,9},{11,1... | collective-permute-start | bytes 614408 | tf_op jit(solution)/shard_map/ppermute | solution.py:34
  94.0 11.2 %collective-permute-start.9 = (f32[400,1]{0,1:T(1,128)S(1)}, f32[400,1]{0,1:T(1,128)S(1)}, u32[]{:S(2)}, u32[]{:S(2)}) collective-permute-start(f32[400,1]{0,1:T(1,128)S(1)} %get-tuple-element.37), channel_id=1, source_target_pairs={{16,0},{32,16},{48,32},{64,48},{80,64},{96,80},{112,96},{17,1},{33... | collective-permute-start | bytes 4808 | tf_op jit(solution)/shard_map/ppermute | solution.py:34
  96.6 8.7 %collective-permute-start.8 = (f32[400,1]{0,1:T(1,128)S(1)}, f32[400,1]{0,1:T(1,128)S(1)}, u32[]{:S(2)}, u32[]{:S(2)}) collective-permute-start(f32[400,1]{0,1:T(1,128)S(1)} %get-tuple-element.38), channel_id=1, source_target_pairs={{0,16},{16,32},{32,48},{48,64},{64,80},{80,96},{96,112},{1,17},{17... | collective-permute-start | bytes 4808 | tf_op jit(solution)/shard_map/ppermute | solution.py:29
  105.1 1.1 copy-start.2

commit v3 on v2

--- a/solution.py
+++ b/solution.py
@@ -106,30 +106,29 @@
     for iteration in range(ITERS):
         image_of_residual = apply_operator(matrix, residual, residual_halo)
         if iteration == 0:
-            parts = jnp.stack([jnp.sum(residual * residual), jnp.sum(residual * image_of_residual)])
+            products = [residual * residual, residual * image_of_residual]
         else:
-            parts = jnp.stack(
-                [
-                    jnp.sum(residual * residual),
-                    jnp.sum(residual * image_of_residual),
-                    jnp.sum(residual * image),
-                    jnp.sum(direction * image_of_residual),
-                    jnp.sum(direction * image),
-                ]
-            )
+            products = [
+                residual * residual,
+                residual * image_of_residual,
+                residual * image,
+                direction * image_of_residual,
+                direction * image,
+            ]
+        parts = jnp.sum(jnp.stack(products), axis=(1, 2))
         if iteration < ITERS - 1:
             image_halo = exchange(image_of_residual)
-        sums = total(parts)
-        norm_now = sums[0]
+        sums = total(parts)[:, None]
+        norm_now = sums[0:1]
         if iteration == 0:
-            alpha = norm_now / sums[1]
+            alpha = norm_now / sums[1:2]
             direction = residual
             image = image_of_residual
             if iteration < ITERS - 1:
                 halo_image = image_halo
         else:
             beta = norm_now / norm_prev
-            curvature = sums[1] + beta * (sums[2] + sums[3]) + beta * beta * sums[4]
+            curvature = sums[1:2] + beta * (sums[2:3] + sums[3:4]) + beta * beta * sums[4:5]
             alpha = norm_now / curvature
             direction = residual + beta * direction
             image = image_of_residual + beta * image

time: 139 us -> 134 us (0.964)
  local copies, waits for them, and re-layouts: 16.4 us -> 9.9 us
  starting transfers between devices: 50.1 us -> 51.9 us
    another operation x2 -> x1, local copies, waits for them, and re-layouts: 6.53 us -> 0.02 us  [body(): parts = jnp.sum(jnp.stack(products), axis=(1, 2))]
    ppermute x5, starting transfers between devices: 17 us -> 18.6 us  [from_prev(): return lax.ppermute(cells, axis, [(i, i + 1) for i in range(count - 1)])]
where the time goes in v3:
time: 134 us; the launch traced here: 133 us
  starting transfers between devices  51.9 us (39%)
  blocking collectives  42.4 us (32%)
  matrix products  11.8 us (9%)
  between operations  11.6 us (9%)
  local copies, waits for them, and re-layouts  9.9 us (7%)
  other arithmetic  3.13 us (2%)
  waiting for transfers between devices  2.11 us (2%)
    all_to_all x1, blocking collectives, body(): lax.all_to_all(chunks, 'pair', 0, 0, tiled=True)  22.7 us
    all_to_all x2, starting transfers between devices, total(): got = lax.all_to_all(sent, ('pair', 'tile'), 0, 0, tiled=True)  22.2 us
    all_to_all x1, blocking collectives, total(): got = lax.all_to_all(sent, ('pair', 'tile'), 0, 0, tiled=True)  19.7 us
    ppermute x5, starting transfers between devices, from_prev(): return lax.ppermute(cells, axis, [(i, i + 1) for i in range(count - 1)])  18.6 us
    ppermute x5, starting transfers between devices, from_next(): return lax.ppermute(cells, axis, [(i + 1, i) for i in range(count - 1)])  11.1 us
    dot_general x3, matrix products, apply_operator(): jnp.dot(matrix, cells, precision=HIGHEST)  6.61 us
    unnamed x16, local copies, waits for them, and re-layouts  5.55 us
    dot_general x1, matrix products, body(): jnp.einsum('kt,kc->tc', network, weight * values, precision=HIGHEST)  3.28 us
  transfers between devices with their start and end apart: 12, of which 2 were waited for; matrix products, arithmetic and copies ran while one was open for 3% of the time, Pallas kernels for 0%

profile of v3, /device:TPU:1, one launch (start us, length us, event | category | flops | bytes accessed | tf_op | source)
XLA Modules:
  0.0 132.8 jit_solution(3528277327701620623)
XLA Ops:
  0.6 0.8 slice_convert_fusion.1
  1.4 2.4 %copy.43 = f32[250,1,1024]{0,2,1:T(8,128)S(1)} copy(f32[250,1,1024]{2,1,0:T(1,128)} %param.4) | data formatting | bytes 2048000 | tf_op args[0]
  3.9 0.6 copy-done
  4.5 0.1 pad_maximum_fusion
  4.6 22.7 %all_to_all.23 = f32[8,250,136]{1,2,0:T(8,128)S(1)} all-to-all(f32[8,250,136]{1,2,0:T(8,128)S(1)} %pad_maximum_fusion), channel_id=1, replica_groups=mesh['pair'=8,'tile'=16] {'pair'}, dimensions={0} | all-to-all | bytes 2176000 | tf_op jit(solution)/shard_map/all_to_all | solution.py:86
  27.3 0.4 copy.44
  27.7 0.5 reshape.49
  28.2 3.3 %fusion = f32[400,130]{0,1:T(8,128)S(1)} fusion(f32[2000]{0:T(1024)S(1)} %bitcast.129, f32[2000]{0:T(1024)S(1)} %bitcast.131, f32[2000,136]{0,1:T(8,128)S(1)} %reshape.49, f32[2000]{0:T(1024)S(1)} %bitcast.127), kind=kOutput, calls=%fused_computation | convolution fusion | flops 1252259968 | bytes 1320000 | tf_op jit(solution)/shard_map/kt,kc->tc/dot_general | solution.py:93
  31.5 1.4 %collective-permute-start.1 = (f32[400,128]{0,1:T(8,128)S(1)}, f32[400,128]{0,1:T(8,128)S(1)}, u32[]{:S(2)}, u32[]{:S(2)}) collective-permute-start(f32[400,128]{0,1:T(8,128)S(1)} %slice.234), channel_id=1, source_target_pairs={{1,0},{2,1},{3,2},{4,3},{5,4},{6,5},{7,6},{8,7},{9,8},{10,9},{11,1... | collective-permute-start | bytes 614408 | tf_op jit(solution)/shard_map/ppermute | solution.py:34
  33.0 4.0 %collective-permute-start = (f32[400,128]{0,1:T(8,128)S(1)}, f32[400,128]{0,1:T(8,128)S(1)}, u32[]{:S(2)}, u32[]{:S(2)}) collective-permute-start(f32[400,128]{0,1:T(8,128)S(1)} %slice.234), channel_id=1, source_target_pairs={{0,1},{1,2},{2,3},{3,4},{4,5},{5,6},{6,7},{7,8},{8,9},{9,10},{10,1... | collective-permute-start | bytes 614408 | tf_op jit(solution)/shard_map/ppermute | solution.py:29
  37.0 1.9 %fusion.3 = f32[400,8]{0,1:T(8,128)S(1)} fusion(f32[2000]{0:T(1024)S(1)} %bitcast.130, f32[2000]{0:T(1024)S(1)} %bitcast.128, f32[2000]{0:T(1024)S(1)} %bitcast.126), kind=kOutput, calls=%fused_computation.4 | convolution fusion | flops 77632000 | bytes 36800 | tf_op jit(solution)/shard_map/kt,kd->td/dot_general | solution.py:96
  38.9 0.6 fusion.28
  39.4 1.2 collective-permute-done.1
  40.7 0.9 collective-permute-done
  41.5 1.4 %fusion.30 = f32[400,128]{0,1:T(8,128)S(1)} fusion(f32[400,130]{0,1:T(8,128)S(1)} %fusion, f32[400,128]{0,1:T(8,128)S(1)} %collective-permute-done, f32[400,128]{0,1:T(8,128)S(1)} %collective-permute-done.1, f32[400,400]{1,0:T(8,128)S(1)} %copy-done.1, f32[400]{0:T(512)S(1)} %negate_add_fusion, f32[400]{0:T(512)S(1)} %bitcast.103, f32[400]{0:T(512)S(1)} %bitcast.107, ...), kind=kOutput, calls=%fused_computation.44 | convolution fusion | flops 253536000 | bytes 2365440 | tf_op jit(solution)/shard_map/dot_general | solution.py:54
  42.9 0.2 maximum_reduce_fusion
  43.1 0.7 broadcast_in_dim.143
  43.8 11.9 %all-to-all-start.1 = ((f32[128,1,2]{2,1,0:T(1,128)}), f32[128,1,2]{2,1,0:T(1,128)S(1)}, u32[]{:S(2)}, u32[]{:S(2)}) async-start(f32[128,1,2]{2,1,0:T(1,128)} %broadcast_in_dim.143), calls=%async_computation.1 | async-start | bytes 131072 | tf_op jit(solution)/shard_map/all_to_all | solution.py:60
  55.7 1.3 collective-permute-start.3
  57.0 4.7 %collective-permute-start.2 = (f32[400,128]{0,1:T(8,128)S(1)}, f32[400,128]{0,1:T(8,128)}, u32[]{:S(2)}, u32[]{:S(2)}) collective-permute-start(f32[400,128]{0,1:T(8,128)S(1)} %fusion.30), channel_id=1, source_target_pairs={{0,1},{1,2},{2,3},{3,4},{4,5},{5,6},{6,7},{7,8},{8,9},{9,10},{10,1... | collective-permute-start | bytes 614408 | tf_op jit(solution)/shard_map/ppermute | solution.py:29
  61.7 3.5 %collective-permute-start.5 = (f32[400,1]{0,1:T(1,128)S(1)}, f32[400,1]{0,1:T(1,128)S(1)}, u32[]{:S(2)}, u32[]{:S(2)}) collective-permute-start(f32[400,1]{0,1:T(1,128)S(1)} %get-tuple-element.35), channel_id=1, source_target_pairs={{16,0},{32,16},{48,32},{64,48},{80,64},{96,80},{112,96},{17,1},{33... | collective-permute-start | bytes 4808 | tf_op jit(solution)/shard_map/ppermute | solution.py:34
  65.2 2.6 %collective-permute-start.4 = (f32[400,1]{0,1:T(1,128)S(1)}, f32[400,1]{0,1:T(1,128)S(1)}, u32[]{:S(2)}, u32[]{:S(2)}) collective-permute-start(f32[400,1]{0,1:T(1,128)S(1)} %get-tuple-element.36), channel_id=1, source_target_pairs={{0,16},{16,32},{32,48},{48,64},{64,80},{80,96},{96,112},{1,17},{17... | collective-permute-start | bytes 4808 | tf_op jit(solution)/shard_map/ppermute | solution.py:29
  67.9 0.2 reduce_sum.65
  68.0 0.6 fusion.56
  70.0 0.1 bitcast_dynamic-update-slice_fusion.8
  70.1 2.6 %bitcast_dynamic-update-slice_fusion.7 = (f32[5,400,128]{1,2,0:T(8,128)S(1)}, f32[400,128]{0,1:T(8,128)S(1)}) fusion(f32[5,400,128]{1,2,0:T(8,128)S(1)} %get-tuple-element.17, f32[400,128]{0,1:T(8,128)S(1)} %get-tuple-element.18, f32[400,1]{0,1:T(1,128)S(1)} %get-tuple-element.23, f32[400,127]{0,1:T(8,128)S(1)} %get-tuple-element.33, ...), kind=kOutput, calls=%fused_computation.60 | convolution fusion | flops 253894400 | bytes 3181572 | tf_op jit(solution)/shard_map/dot_general | solution.py:54
  72.9 0.2 reduce_sum.66
  73.1 0.7 broadcast_in_dim.144
  73.8 10.3 %all-to-all-start.2 = ((f32[128,1,5]{2,1,0:T(1,128)}), f32[128,1,5]{2,1,0:T(1,128)S(1)}, u32[]{:S(2)}, u32[]{:S(2)}) async-start(f32[128,1,5]{2,1,0:T(1,128)} %broadcast_in_dim.144), calls=%async_computation.2 | async-start | bytes 131072 | tf_op jit(solution)/shard_map/all_to_all | solution.py:60
  84.1 1.3 collective-permute-start.7
  85.4 4.7 %collective-permute-start.6 = (f32[400,128]{0,1:T(8,128)S(1)}, f32[400,128]{0,1:T(8,128)}, u32[]{:S(2)}, u32[]{:S(2)}) collective-permute-start(f32[400,128]{0,1:T(8,128)S(1)} %get-tuple-element.59), channel_id=1, source_target_pairs={{0,1},{1,2},{2,3},{3,4},{4,5},{5,6},{6,7},{7,8},{8,9},{9,10},{10,1... | collective-permute-start | bytes 614408 | tf_op jit(solution)/shard_map/ppermute | solution.py:29
  90.1 3.5 %collective-permute-start.9 = (f32[400,1]{0,1:T(1,128)S(1)}, f32[400,1]{0,1:T(1,128)S(1)}, u32[]{:S(2)}, u32[]{:S(2)}) collective-permute-start(f32[400,1]{0,1:T(1,128)S(1)} %get-tuple-element.31), channel_id=1, source_target_pairs={{16,0},{32,16},{48,32},{64,48},{80,64},{96,80},{112,96},{17,1},{33... | collective-permute-start | bytes 4808 | tf_op jit(solution)/shard_map/ppermute | solution.py:34
  93.6 2.6 %collective-permute-start.8 = (f32[400,1]{0,1:T(1,128)S(1)}, f32[400,1]{0,1:T(1,128)S(1)}, u32[]{:S(2)}, u32[]{:S(2)}) collective-permute-start(f32[400,1]{0,1:T(1,128)S(1)} %get-tuple-element.32), channel_id=1, source_target_pairs={{0,16},{16,32},{32,48},{48,64},{64,80},{80,96},{96,112},{1,17},{17... | collective-permute-start | bytes 4808 | tf_op jit(solution)/shard_map/ppermute | solution.py:29
  96.3 0.2 reduce_sum.67
  96.4 0.7 fusion.55
  101.8 0.0 copy-start.2
  101.8 0.1 bitcast_dynamic-update-slice_fusion.4
  102.0 0.9 copy-done.2
  102.9 2.6 %bitcast_dynamic-update-slice_fusion.3 = (f32[5,400,128]{1,2,0:T(8,128)S(1)}, f32[400,128]{0,1:T(8,128)S(1)}) fusion(f32[5,400,128]{1,2,0:T(8,128)S(1)} %get-tuple-element.14, f32[400,128]{0,1:T(8,128)S(1)} %get-tuple-element.15, f32[400,1]{0,1:T(1,128)S(1)} %multiply_subtract_fusion.4, f32[400,127]{0,1:T(8,128)S(1)} %get-tuple-element.29, ...), kind=kOutput, calls=%fused_computation.56 | convolution fusion | flops 254304000 | bytes 3770380 | tf_op jit(solution)/shard_map/dot_general | solution.py:54
  105.6 0.1 bitcast_dynamic-update-slice_fusion.1
  105.6 0.1 bitcast_dynamic-update-slice_fusion
  105.7 0.2 reduce_sum.68
  106.0 19.7 %all_to_all.24 = f32[128,1,5]{2,1,0:T(1,128)S(1)} all-to-all(f32[128,1,5]{2,1,0:T(1,128)S(1)} %broadcast_in_dim.145), channel_id=1, replica_groups=mesh['pair'=8,'tile'=16] {'pair','tile'}, dimensions={0} | all-to-all | bytes 5120 | tf_op jit(solution)/shard_map/all_to_all | solution.py:60
  125.7 0.2 reduce_sum.69
  125.8 0.7 fusion.54
  131.0 0.2 subtract_bitcast_fusion
  131.1 0.8 copy.52
  132.0 0.8 copy.51
  (40 shorter events, 0.6 us)
Async XLA Ops:
  3.8 0.7 copy-start
  31.5 10.0 %copy-start.1 = (f32[400,400]{1,0:T(8,128)S(1)}, f32[400,400]{1,0:T(8,128)}, u32[]{:S(2)}) copy-start(f32[400,400]{1,0:T(8,128)} %constant.27.clone) | copy-start | bytes 1920004
  31.5 9.1 %collective-permute-start.1 = (f32[400,128]{0,1:T(8,128)S(1)}, f32[400,128]{0,1:T(8,128)S(1)}, u32[]{:S(2)}, u32[]{:S(2)}) collective-permute-start(f32[400,128]{0,1:T(8,128)S(1)} %slice.234), channel_id=1, source_target_pairs={{1,0},{2,1},{3,2},{4,3},{5,4},{6,5},{7,6},{8,7},{9,8},{10,9},{11,1... | collective-permute-start | bytes 614408 | tf_op jit(solution)/shard_map/ppermute | solution.py:34
  33.0 8.5 %collective-permute-start = (f32[400,128]{0,1:T(8,128)S(1)}, f32[400,128]{0,1:T(8,128)S(1)}, u32[]{:S(2)}, u32[]{:S(2)}) collective-permute-start(f32[400,128]{0,1:T(8,128)S(1)} %slice.234), channel_id=1, source_target_pairs={{0,1},{1,2},{2,3},{3,4},{4,5},{5,6},{6,7},{7,8},{8,9},{9,10},{10,1... | collective-permute-start | bytes 614408 | tf_op jit(solution)/shard_map/ppermute | solution.py:29
  43.8 24.1 %all-to-all-start.1 = ((f32[128,1,2]{2,1,0:T(1,128)}), f32[128,1,2]{2,1,0:T(1,128)S(1)}, u32[]{:S(2)}, u32[]{:S(2)}) async-start(f32[128,1,2]{2,1,0:T(1,128)} %broadcast_in_dim.143), calls=%async_computation.1 | async-start | bytes 131072 | tf_op jit(solution)/shard_map/all_to_all | solution.py:60
  55.7 14.4 %collective-permute-start.3 = (f32[400,128]{0,1:T(8,128)S(1)}, f32[400,128]{0,1:T(8,128)}, u32[]{:S(2)}, u32[]{:S(2)}) collective-permute-start(f32[400,128]{0,1:T(8,128)S(1)} %fusion.30), channel_id=1, source_target_pairs={{1,0},{2,1},{3,2},{4,3},{5,4},{6,5},{7,6},{8,7},{9,8},{10,9},{11,1... | collective-permute-start | bytes 614408 | tf_op jit(solution)/shard_map/ppermute | solution.py:34
  57.0 13.1 %collective-permute-start.2 = (f32[400,128]{0,1:T(8,128)S(1)}, f32[400,128]{0,1:T(8,128)}, u32[]{:S(2)}, u32[]{:S(2)}) collective-permute-start(f32[400,128]{0,1:T(8,128)S(1)} %fusion.30), channel_id=1, source_target_pairs={{0,1},{1,2},{2,3},{3,4},{4,5},{5,6},{6,7},{7,8},{8,9},{9,10},{10,1... | collective-permute-start | bytes 614408 | tf_op jit(solution)/shard_map/ppermute | solution.py:29
  61.7 8.4 %collective-permute-start.5 = (f32[400,1]{0,1:T(1,128)S(1)}, f32[400,1]{0,1:T(1,128)S(1)}, u32[]{:S(2)}, u32[]{:S(2)}) collective-permute-start(f32[400,1]{0,1:T(1,128)S(1)} %get-tuple-element.35), channel_id=1, source_target_pairs={{16,0},{32,16},{48,32},{64,48},{80,64},{96,80},{112,96},{17,1},{33... | collective-permute-start | bytes 4808 | tf_op jit(solution)/shard_map/ppermute | solution.py:34
  65.2 4.8 %collective-permute-start.4 = (f32[400,1]{0,1:T(1,128)S(1)}, f32[400,1]{0,1:T(1,128)S(1)}, u32[]{:S(2)}, u32[]{:S(2)}) collective-permute-start(f32[400,1]{0,1:T(1,128)S(1)} %get-tuple-element.36), channel_id=1, source_target_pairs={{0,16},{16,32},{32,48},{48,64},{64,80},{80,96},{96,112},{1,17},{17... | collective-permute-start | bytes 4808 | tf_op jit(solution)/shard_map/ppermute | solution.py:29
  73.8 22.5 %all-to-all-start.2 = ((f32[128,1,5]{2,1,0:T(1,128)}), f32[128,1,5]{2,1,0:T(1,128)S(1)}, u32[]{:S(2)}, u32[]{:S(2)}) async-start(f32[128,1,5]{2,1,0:T(1,128)} %broadcast_in_dim.144), calls=%async_computation.2 | async-start | bytes 131072 | tf_op jit(solution)/shard_map/all_to_all | solution.py:60
  84.1 17.9 %collective-permute-start.7 = (f32[400,128]{0,1:T(8,128)S(1)}, f32[400,128]{0,1:T(8,128)}, u32[]{:S(2)}, u32[]{:S(2)}) collective-permute-start(f32[400,128]{0,1:T(8,128)S(1)} %get-tuple-element.59), channel_id=1, source_target_pairs={{1,0},{2,1},{3,2},{4,3},{5,4},{6,5},{7,6},{8,7},{9,8},{10,9},{11,1... | collective-permute-start | bytes 614408 | tf_op jit(solution)/shard_map/ppermute | solution.py:34
  85.4 16.6 %collective-permute-start.6 = (f32[400,128]{0,1:T(8,128)S(1)}, f32[400,128]{0,1:T(8,128)}, u32[]{:S(2)}, u32[]{:S(2)}) collective-permute-start(f32[400,128]{0,1:T(8,128)S(1)} %get-tuple-element.59), channel_id=1, source_target_pairs={{0,1},{1,2},{2,3},{3,4},{4,5},{5,6},{6,7},{7,8},{8,9},{9,10},{10,1... | collective-permute-start | bytes 614408 | tf_op jit(solution)/shard_map/ppermute | solution.py:29
  90.1 11.8 %collective-permute-start.9 = (f32[400,1]{0,1:T(1,128)S(1)}, f32[400,1]{0,1:T(1,128)S(1)}, u32[]{:S(2)}, u32[]{:S(2)}) collective-permute-start(f32[400,1]{0,1:T(1,128)S(1)} %get-tuple-element.31), channel_id=1, source_target_pairs={{16,0},{32,16},{48,32},{64,48},{80,64},{96,80},{112,96},{17,1},{33... | collective-permute-start | bytes 4808 | tf_op jit(solution)/shard_map/ppermute | solution.py:34
  93.6 8.3 %collective-permute-start.8 = (f32[400,1]{0,1:T(1,128)S(1)}, f32[400,1]{0,1:T(1,128)S(1)}, u32[]{:S(2)}, u32[]{:S(2)}) collective-permute-start(f32[400,1]{0,1:T(1,128)S(1)} %get-tuple-element.32), channel_id=1, source_target_pairs={{0,16},{16,32},{32,48},{48,64},{64,80},{80,96},{96,112},{1,17},{17... | collective-permute-start | bytes 4808 | tf_op jit(solution)/shard_map/ppermute | solution.py:29
  101.8 1.1 copy-start.2

commit v4 on v3

--- a/solution.py
+++ b/solution.py
@@ -3,6 +3,8 @@
 import jax.numpy as jnp
 from jax import lax
 from jax.sharding import PartitionSpec as P
+from jax.experimental import pallas as pl
+from jax.experimental.pallas import tpu as pltpu
 
 DATES = 400
 ITERS = 3
@@ -71,6 +73,119 @@
     degree = -jnp.sum(coupling, axis=1)
     diagonal = degree + (4.0 * spatial_weight + ridge_weight)
     return coupling + jnp.where(offset == 0, diagonal[:, None], 0.0) + temporal_weight * temporal_matrix()
+
+
+def lane_value(vector, j):
+    lanes = lax.broadcasted_iota(jnp.int32, vector.shape, 1)
+    return jnp.sum(jnp.where(lanes == j, vector, 0.0), axis=1, keepdims=True)
+
+
+def shifted(cells, left, right):
+    width = cells.shape[1]
+    lanes = lax.broadcasted_iota(jnp.int32, cells.shape, 1)
+    probe = pltpu.roll(lanes, 1, 1)
+    forward = probe == jnp.where(lanes == 0, width - 1, lanes - 1)
+    one = pltpu.roll(cells, 1, 1)
+    back = pltpu.roll(cells, width - 1, 1)
+    west = jnp.where(lanes == 0, left, jnp.where(forward, one, back))
+    east = jnp.where(lanes == width - 1, right, jnp.where(forward, back, one))
+    return west, east
+
+
+def operate(matrix, cells, above, below, left, right):
+    west, east = shifted(cells, left, right)
+    return jnp.dot(matrix, cells, precision=HIGHEST, preferred_element_type=jnp.float32) - spatial_weight * (
+        above + below + west + east
+    )
+
+
+def send_buffer(send_ref, values):
+    lanes = lax.broadcasted_iota(jnp.int32, (1, send_ref.shape[1]), 1)
+    row = jnp.zeros((1, send_ref.shape[1]), jnp.float32)
+    for j, value in enumerate(values):
+        row = row + jnp.where(lanes == j, jnp.sum(value, keepdims=True), 0.0)
+    send_ref[...] = jnp.broadcast_to(row, send_ref.shape)
+
+
+def first_kernel(k_ref, r_ref, ru_ref, rd_ref, rl_ref, rr_ref, w_ref, send_ref):
+    r = r_ref[...]
+    w = operate(k_ref[...], r, ru_ref[...], rd_ref[...], rl_ref[...], rr_ref[...])
+    w_ref[...] = w
+    send_buffer(send_ref, [r * r, r * w])
+
+
+def second_kernel(got_ref, k_ref, r_ref, ru_ref, rd_ref, rl_ref, rr_ref, w_ref, wu_ref, wd_ref, wl_ref, wr_ref,
+                  r_out, x_out, w_out, send_ref, scal_ref):
+    sums = jnp.sum(got_ref[...], axis=0, keepdims=True)
+    norm = lane_value(sums, 0)
+    alpha = norm / lane_value(sums, 1)
+    p = r_ref[...]
+    q = w_ref[...]
+    x_out[...] = alpha * p
+    r = p - alpha * q
+    r_out[...] = r
+    halo = [h[...] - alpha * g[...] for h, g in zip((ru_ref, rd_ref, rl_ref, rr_ref), (wu_ref, wd_ref, wl_ref, wr_ref))]
+    w = operate(k_ref[...], r, *halo)
+    w_out[...] = w
+    send_buffer(send_ref, [r * r, r * w, r * q, p * w, p * q])
+    lanes = lax.broadcasted_iota(jnp.int32, scal_ref.shape, 1)
+    scal_ref[...] = jnp.where(lanes == 0, norm, jnp.where(lanes == 1, alpha, 0.0))
+
+
+def step_scalars(got_ref, scal_ref):
+    sums = jnp.sum(got_ref[...], axis=0, keepdims=True)
+    previous = scal_ref[...]
+    norm = lane_value(sums, 0)
+    beta = norm / lane_value(previous, 0)
+    curvature = lane_value(sums, 1) + beta * (lane_value(sums, 2) + lane_value(sums, 3)) + beta * beta * lane_value(sums, 4)
+    return norm, beta, norm / curvature
+
+
+def third_kernel(got_ref, scal_ref, k_ref, r_ref, p_ref, q_ref, x_ref, w_ref,
+                 ru_ref, rd_ref, rl_ref, rr_ref, qu_ref, qd_ref, ql_ref, qr_ref, wu_ref, wd_ref, wl_ref, wr_ref,
+                 r_out, p_out, q_out, x_out, w_out, send_ref, scal_out):
+    norm, beta, alpha = step_scalars(got_ref, scal_ref)
+    alpha_first = lane_value(scal_ref[...], 1)
+    p = r_ref[...] + beta * p_ref[...]
+    q = w_ref[...] + beta * q_ref[...]
+    p_out[...] = p
+    q_out[...] = q
+    x_out[...] = x_ref[...] + alpha * p
+    r = r_ref[...] - alpha * q
+    r_out[...] = r
+    halo = []
+    for h, k, g in zip((ru_ref, rd_ref, rl_ref, rr_ref), (qu_ref, qd_ref, ql_ref, qr_ref), (wu_ref, wd_ref, wl_ref, wr_ref)):
+        halo.append((h[...] - alpha_first * k[...]) - alpha * (g[...] + beta * k[...]))
+    w = operate(k_ref[...], r, *halo)
+    w_out[...] = w
+    send_buffer(send_ref, [r * r, r * w, r * q, p * w, p * q])
+    lanes = lax.broadcasted_iota(jnp.int32, scal_out.shape, 1)
+    scal_out[...] = jnp.where(lanes == 0, norm, jnp.where(lanes == 1, alpha, 0.0))
+
+
+def last_kernel(got_ref, scal_ref, r_ref, p_ref, q_ref, x_ref, w_ref, x_out, r_out):
+    norm, beta, alpha = step_scalars(got_ref, scal_ref)
+    p = r_ref[...] + beta * p_ref[...]
+    q = w_ref[...] + beta * q_ref[...]
+    x_out[...] = x_ref[...] + alpha * p
+    r_out[...] = r_ref[...] - alpha * q
+
+
+def call(kernel, shapes, *args):
+    return pl.pallas_call(kernel, out_shape=[jax.ShapeDtypeStruct(s, jnp.float32) for s in shapes])(*args)
+
+
+def reduce_all(send):
+    return lax.all_to_all(send, ("pair", "tile"), 0, 0, tiled=True)
+
+
+def exchange_rows_cols(cells):
+    return (
+        from_prev(cells, "tile"),
+        from_next(cells, "tile"),
+        from_prev(cells[:, -1:], "pair"),
+        from_next(cells[:, :1], "pair"),
+    )
 
 
 def body(phase, incidence, pair_weight):
@@ -102,43 +217,25 @@
         right_wide[:, :1],
         right_wide[:, -1:],
     )
-    solution_field = jnp.zeros_like(residual)
-    for iteration in range(ITERS):
-        image_of_residual = apply_operator(matrix, residual, residual_halo)
-        if iteration == 0:
-            products = [residual * residual, residual * image_of_residual]
-        else:
-            products = [
-                residual * residual,
-                residual * image_of_residual,
-                residual * image,
-                direction * image_of_residual,
-                direction * image,
-            ]
-        parts = jnp.sum(jnp.stack(products), axis=(1, 2))
-        if iteration < ITERS - 1:
-            image_halo = exchange(image_of_residual)
-        sums = total(parts)[:, None]
-        norm_now = sums[0:1]
-        if iteration == 0:
-            alpha = norm_now / sums[1:2]
-            direction = residual
-            image = image_of_residual
-            if iteration < ITERS - 1:
-                halo_image = image_halo
-        else:
-            beta = norm_now / norm_prev
-            curvature = sums[1:2] + beta * (sums[2:3] + sums[3:4]) + beta * beta * sums[4:5]
-            alpha = norm_now / curvature
-            direction = residual + beta * direction
-            image = image_of_residual + beta * image
-            if iteration < ITERS - 1:
-                halo_image = tuple(a + beta * b for a, b in zip(image_halo, halo_image))
-        solution_field = solution_field + alpha * direction
-        residual = residual - alpha * image
-        if iteration < ITERS - 1:
-            residual_halo = tuple(a - alpha * b for a, b in zip(residual_halo, halo_image))
-        norm_prev = norm_now
+    count = lax.axis_size("pair") * lax.axis_size("tile")
+    field = residual.shape
+    lanes = 128
+    send_shape = (count, lanes)
+    w0, send = call(first_kernel, [field, send_shape], matrix, residual, *residual_halo)
+    w0_halo = exchange_rows_cols(w0)
+    got = reduce_all(send)
+    r1, x1, w1, send, scal = call(
+        second_kernel, [field, field, field, send_shape, (1, lanes)], got, matrix, residual, *residual_halo, w0, *w0_halo
+    )
+    w1_halo = exchange_rows_cols(w1)
+    got = reduce_all(send)
+    r2, p1, q1, x2, w2, send, scal = call(
+        third_kernel,
+        [field, field, field, field, field, send_shape, (1, lanes)],
+        got, scal, matrix, r1, residual, w0, x1, w1, *residual_halo, *w0_halo, *w1_halo,
+    )
+    got = reduce_all(send)
+    solution_field, residual = call(last_kernel, [field, field], got, scal, r2, p1, q1, x2, w2)
     return (solution_field[:, None, :], residual[:, None, :])
 
 

time: 134 us -> 139 us (1.037)
  Pallas kernels: 0 us -> 13 us
  between operations: 11.6 us -> 0.97 us
  waiting for transfers between devices: 2.11 us -> 5.65 us
  matrix products: 11.8 us -> 9.14 us
  starting transfers between devices: 51.9 us -> 53.4 us
    pallas_call x0 -> x4, Pallas kernels: none -> 13 us  [call(): pl.pallas_call(kernel, out_shape=[jax.ShapeDtypeStruct(s, jnp.float32) fo...]
    dot_general x3 -> x0, matrix products: 6.61 us -> none  [apply_operator(): jnp.dot(matrix, cells, precision=HIGHEST)]
    dot_general x1, matrix products: 3.28 us -> 7.28 us  [body(): jnp.einsum('kt,kc->tc', network, weight * values, precision=HIGHEST)]
    all_to_all x2, starting transfers between devices: 22.2 us -> 26 us  [reduce_all(): return lax.all_to_all(send, ('pair', 'tile'), 0, 0, tiled=True)]
    ppermute x5, waiting for transfers between devices: 1.24 us -> 4.03 us  [from_next(): return lax.ppermute(cells, axis, [(i + 1, i) for i in range(count - 1)])]
    add x0 -> x1, other arithmetic: none -> 2.22 us  [normal_matrix(): coupling + jnp.where(offset == 0, diagonal[:, None], 0.0)]
    slice x7 -> x3, local copies, waits for them, and re-layouts: 2.05 us -> 3.09 us  [the longest x2 2.28 us: exchange_rows_cols(): cells[:, :1]]
    unnamed x16 -> x38, local copies, waits for them, and re-layouts: 5.55 us -> 5.32 us
  transfers between devices with their start and end apart: 12 -> 12, of which waited for: 2 -> 6; matrix products, arithmetic and copies ran while one was open for 3% -> 6% of each run, Pallas kernels for 0% -> 0%
where the time goes in v4:
time: 139 us
  starting transfers between devices  53.4 us (38%)
  blocking collectives  43.5 us (31%)
  Pallas kernels  13 us (9%)
  local copies, waits for them, and re-layouts  9.41 us (7%)
  matrix products  9.14 us (7%)
  waiting for transfers between devices  5.65 us (4%)
  other arithmetic  3.68 us (3%)
    all_to_all x2, starting transfers between devices, reduce_all(): return lax.all_to_all(send, ('pair', 'tile'), 0, 0, tiled=True)  26 us
    all_to_all x1, blocking collectives, body(): lax.all_to_all(chunks, 'pair', 0, 0, tiled=True)  22.7 us
    all_to_all x1, blocking collectives, reduce_all(): return lax.all_to_all(send, ('pair', 'tile'), 0, 0, tiled=True)  20.8 us
    ppermute x5, starting transfers between devices, from_prev(): return lax.ppermute(cells, axis, [(i, i + 1) for i in range(count - 1)])  17.4 us
    pallas_call x4, Pallas kernels, call(): pl.pallas_call(kernel, out_shape=[jax.ShapeDtypeStruct(s, jnp.float32) fo...  13 us
    ppermute x5, starting transfers between devices, from_next(): return lax.ppermute(cells, axis, [(i + 1, i) for i in range(count - 1)])  9.94 us
    dot_general x1, matrix products, body(): jnp.einsum('kt,kc->tc', network, weight * values, precision=HIGHEST)  7.28 us
    unnamed x38, local copies, waits for them, and re-layouts  5.32 us
  transfers between devices with their start and end apart: 12, of which 6 were waited for; matrix products, arithmetic and copies ran while one was open for 6% of the time, Pallas kernels for 0%

profile of v4, /device:TPU:1, one launch (start us, length us, event | category | flops | bytes accessed | tf_op | source)
XLA Modules:
  0.0 138.6 jit_solution(2370763304662268460)
XLA Ops:
  0.6 0.8 slice_convert_fusion.1
  1.4 2.4 %copy.19 = f32[250,1,1024]{0,2,1:T(8,128)S(1)} copy(f32[250,1,1024]{2,1,0:T(1,128)} %param.4) | data formatting | bytes 2048000 | tf_op args[0]
  3.9 0.6 copy-done.14
  4.5 0.1 pad_maximum_fusion
  4.6 22.7 %all_to_all.38 = f32[8,250,136]{1,2,0:T(8,128)S(1)} all-to-all(f32[8,250,136]{1,2,0:T(8,128)S(1)} %pad_maximum_fusion), channel_id=1, replica_groups=mesh['pair'=8,'tile'=16] {'pair'}, dimensions={0} | all-to-all | bytes 2176000 | tf_op jit(solution)/shard_map/all_to_all | solution.py:201
  27.3 0.4 copy.20
  27.7 0.5 reshape.17
  28.2 7.3 %fusion = f32[400,130]{1,0:T(8,128)S(1)} fusion(f32[2000]{0:T(1024)S(1)} %bitcast.98, f32[2000]{0:T(1024)S(1)} %bitcast.96, f32[2000,136]{0,1:T(8,128)S(1)} %reshape.17, f32[2000]{0:T(1024)S(1)} %bitcast.94), kind=kOutput, calls=%fused_computation | convolution fusion | flops 1252259968 | bytes 1320000 | tf_op jit(solution)/shard_map/kt,kc->tc/dot_general | solution.py:208
  35.5 0.1 slice.135.r_ref.p_ref
  35.6 1.4 %collective-permute-start.1 = (f32[400,128]{1,0:T(8,128)S(1)}, f32[400,128]{1,0:T(8,128)S(1)}, u32[]{:S(2)}, u32[]{:S(2)}) collective-permute-start(f32[400,128]{1,0:T(8,128)S(1)} %slice.135.r_ref.p_ref), channel_id=1, source_target_pairs={{1,0},{2,1},{3,2},{4,3},{5,4},{6,5},{7,6},{8,7},{9,8},{10,9},{11,1... | collective-permute-start | bytes 614408 | tf_op jit(solution)/shard_map/ppermute | solution.py:36
  37.1 4.2 %collective-permute-start = (f32[400,128]{1,0:T(8,128)S(1)}, f32[400,128]{1,0:T(8,128)S(1)}, u32[]{:S(2)}, u32[]{:S(2)}) collective-permute-start(f32[400,128]{1,0:T(8,128)S(1)} %slice.135.r_ref.p_ref), channel_id=1, source_target_pairs={{0,1},{1,2},{2,3},{3,4},{4,5},{5,6},{6,7},{7,8},{8,9},{9,10},{10,1... | collective-permute-start | bytes 614408 | tf_op jit(solution)/shard_map/ppermute | solution.py:31
  41.2 1.9 %fusion.4 = f32[400,8]{0,1:T(8,128)S(1)} fusion(f32[2000]{0:T(1024)S(1)} %bitcast.97, f32[2000]{0:T(1024)S(1)} %bitcast.95, f32[2000]{0:T(1024)S(1)} %bitcast.93), kind=kOutput, calls=%fused_computation.6 | convolution fusion | flops 77632000 | bytes 36800 | tf_op jit(solution)/shard_map/kt,kd->td/dot_general | solution.py:211
  43.1 0.6 fusion.28
  43.7 2.2 %add_add_fusion.k_ref = f32[400,400]{1,0:T(8,128)} fusion(f32[400,400]{1,0:T(8,128)S(1)} %copy-done.3, f32[400]{0:T(512)S(1)} %negate_add_fusion, f32[400]{0:T(512)S(1)} %bitcast.82, f32[400]{0:T(512)S(1)} %bitcast.84, f32[400]{0:T(512)S(1)} %bitcast.86, f32[400]{0:T(512)S(1)} %bitcast.88, f32[400]{0:T(512)S(1)} %bitcast.90, f32[400]{0:T(512)S(1)} %bitcast.92, ...), kind=kLoop, calls=%fused_computation.16 | loop fusion | flops 7520000 | bytes 1292800 | tf_op jit(solution)/shard_map/add | solution.py:75
  45.9 0.8 fusion.41
  46.8 0.7 copy-done.1
  47.4 0.1 copy-done.2
  47.5 3.1 %shard_map.59 = (f32[400,128]{1,0:T(8,128)}, f32[128,128]{1,0:T(8,128)}) custom-call(f32[400,400]{1,0:T(8,128)} %add_add_fusion.k_ref, f32[400,128]{1,0:T(8,128)} %copy-done, f32[400,128]{1,0:T(8,128)} %copy-done.2, f32[400,128]{1,0:T(8,128)} %copy-done.1, f32[400,1]{1,0:T(8,128)} %get-tuple-element.45.rl_ref, f32[400,1]{1,0:T(8,128)} %get-tuple-element.44.rr_ref), custom_call_target="tpu_custom_call" | custom-call | tf_op jit(solution)/shard_map/pallas_call | solution.py:175
  50.6 1.3 collective-permute-start.3
  51.9 4.0 %collective-permute-start.2 = (f32[400,128]{1,0:T(8,128)}, f32[400,128]{1,0:T(8,128)S(1)}, u32[]{:S(2)}, u32[]{:S(2)}) collective-permute-start(f32[400,128]{1,0:T(8,128)} %get-tuple-element.19.w_ref.q_ref), channel_id=1, source_target_pairs={{0,1},{1,2},{2,3},{3,4},{4,5},{5,6},{6,7},{7,8},{8,9},{9,10},{10,1... | collective-permute-start | bytes 614408 | tf_op jit(solution)/shard_map/ppermute | solution.py:31
  55.9 12.9 %all-to-all-start.1 = ((f32[128,1,128]{2,1,0:T(1,128)}), f32[128,1,128]{2,1,0:T(1,128)S(1)}, u32[]{:S(2)}, u32[]{:S(2)}) async-start(f32[128,1,128]{2,1,0:T(1,128)} %bitcast.77), calls=%async_computation.1 | async-start | bytes 131072 | tf_op jit(solution)/shard_map/all_to_all | solution.py:179
  68.8 1.1 fusion.43
  70.0 3.0 %collective-permute-start.5 = (f32[400,1]{1,0:T(8,128)S(1)}, f32[400,1]{1,0:T(8,128)S(1)}, u32[]{:S(2)}, u32[]{:S(2)}) collective-permute-start(f32[400,1]{1,0:T(8,128)S(1)} %get-tuple-element.48), channel_id=1, source_target_pairs={{16,0},{32,16},{48,32},{64,48},{80,64},{96,80},{112,96},{17,1},{33... | collective-permute-start | bytes 4808 | tf_op jit(solution)/shard_map/ppermute | solution.py:36
  73.0 2.6 %collective-permute-start.4 = (f32[400,1]{1,0:T(8,128)S(1)}, f32[400,1]{1,0:T(8,128)S(1)}, u32[]{:S(2)}, u32[]{:S(2)}) collective-permute-start(f32[400,1]{1,0:T(8,128)S(1)} %get-tuple-element.49), channel_id=1, source_target_pairs={{0,16},{16,32},{32,48},{48,64},{64,80},{80,96},{96,112},{1,17},{17... | collective-permute-start | bytes 4808 | tf_op jit(solution)/shard_map/ppermute | solution.py:31
  75.6 2.0 %collective-permute-done.5.wr_ref.qr_ref = f32[400,1]{1,0:T(8,128)S(1)} collective-permute-done((f32[400,1]{1,0:T(8,128)S(1)}, f32[400,1]{1,0:T(8,128)S(1)}, u32[]{:S(2)}, u32[]{:S(2)}) %collective-permute-start.5) | collective-permute-done | bytes 1632 | tf_op jit(solution)/shard_map/ppermute | solution.py:36
  77.6 0.7 collective-permute-done.4.wl_ref.ql_ref
  78.3 0.1 all-to-all-done.1
  78.4 0.5 copy-done.7
  78.9 0.1 copy-done.9
  79.0 0.1 copy-done.4
  79.1 0.1 copy-done.5
  79.2 3.5 %shard_map.60 = (f32[400,128]{1,0:T(8,128)}, f32[400,128]{1,0:T(8,128)}, f32[400,128]{1,0:T(8,128)}, f32[128,128]{1,0:T(8,128)}, f32[1,128]{1,0:T(1,128)}) custom-call(f32[128,128]{1,0:T(8,128)} %bitcast.74, f32[400,400]{1,0:T(8,128)} %add_add_fusion.k_ref, f32[400,128]{1,0:T(8,128)} %copy-done, f32[400,128]{1,0:T(8,128)} %copy-done.2, ...), custom_call_target="tpu_custom_call" | custom-call | tf_op jit(solution)/shard_map/pallas_call | solution.py:175
  82.7 1.3 collective-permute-start.7
  84.0 4.0 %collective-permute-start.6 = (f32[400,128]{1,0:T(8,128)}, f32[400,128]{1,0:T(8,128)S(1)}, u32[]{:S(2)}, u32[]{:S(2)}) collective-permute-start(f32[400,128]{1,0:T(8,128)} %get-tuple-element.24.w_ref), channel_id=1, source_target_pairs={{0,1},{1,2},{2,3},{3,4},{4,5},{5,6},{6,7},{7,8},{8,9},{9,10},{10,1... | collective-permute-start | bytes 614408 | tf_op jit(solution)/shard_map/ppermute | solution.py:31
  88.0 13.1 %all-to-all-start.2 = ((f32[128,1,128]{2,1,0:T(1,128)}), f32[128,1,128]{2,1,0:T(1,128)S(1)}, u32[]{:S(2)}, u32[]{:S(2)}) async-start(f32[128,1,128]{2,1,0:T(1,128)} %bitcast.76), calls=%async_computation.2 | async-start | bytes 131072 | tf_op jit(solution)/shard_map/all_to_all | solution.py:179
  101.1 1.1 fusion.42
  102.2 3.0 %collective-permute-start.9 = (f32[400,1]{1,0:T(8,128)S(1)}, f32[400,1]{1,0:T(8,128)S(1)}, u32[]{:S(2)}, u32[]{:S(2)}) collective-permute-start(f32[400,1]{1,0:T(8,128)S(1)} %get-tuple-element.46), channel_id=1, source_target_pairs={{16,0},{32,16},{48,32},{64,48},{80,64},{96,80},{112,96},{17,1},{33... | collective-permute-start | bytes 4808 | tf_op jit(solution)/shard_map/ppermute | solution.py:36
  105.2 2.6 %collective-permute-start.8 = (f32[400,1]{1,0:T(8,128)S(1)}, f32[400,1]{1,0:T(8,128)S(1)}, u32[]{:S(2)}, u32[]{:S(2)}) collective-permute-start(f32[400,1]{1,0:T(8,128)S(1)} %get-tuple-element.47), channel_id=1, source_target_pairs={{0,16},{16,32},{32,48},{48,64},{64,80},{80,96},{96,112},{1,17},{17... | collective-permute-start | bytes 4808 | tf_op jit(solution)/shard_map/ppermute | solution.py:31
  107.8 2.0 %collective-permute-done.9.wr_ref = f32[400,1]{1,0:T(8,128)S(1)} collective-permute-done((f32[400,1]{1,0:T(8,128)S(1)}, f32[400,1]{1,0:T(8,128)S(1)}, u32[]{:S(2)}, u32[]{:S(2)}) %collective-permute-start.9) | collective-permute-done | bytes 1632 | tf_op jit(solution)/shard_map/ppermute | solution.py:36
  109.9 0.7 collective-permute-done.8.wl_ref
  110.5 0.1 all-to-all-done.2
  110.7 0.5 copy-done.13
  111.2 0.1 copy-done.8
  111.3 0.1 copy-done.10
  111.4 0.1 copy-done.11
  111.5 4.1 %shard_map.61 = (f32[400,128]{1,0:T(8,128)}, f32[400,128]{1,0:T(8,128)}, f32[400,128]{1,0:T(8,128)}, f32[400,128]{1,0:T(8,128)}, f32[400,128]{1,0:T(8,128)}, /*index=5*/f32[128,128]{1,0:T(8,128)}, f32[1,128]{1,0:T(1,128)}) custom-call(f32[128,128]{1,0:T(8,128)} %bitcast.73, f32[1,128]{1,0:T(1,128)} %get-tuple-element.21.scal_ref, ...), custom_call_target="tpu_custom_call" | custom-call | tf_op jit(solution)/shard_map/pallas_call | solution.py:175
  115.6 20.8 %all_to_all.39 = f32[128,1,128]{2,1,0:T(1,128)} all-to-all(f32[128,1,128]{2,1,0:T(1,128)} %bitcast.78), channel_id=1, replica_groups=mesh['pair'=8,'tile'=16] {'pair','tile'}, dimensions={0} | all-to-all | bytes 131072 | tf_op jit(solution)/shard_map/all_to_all | solution.py:179
  136.4 2.2 %shard_map.62 = (f32[400,128]{1,0:T(8,128)}, f32[400,128]{1,0:T(8,128)}) custom-call(f32[128,128]{1,0:T(8,128)} %bitcast.75, f32[1,128]{1,0:T(1,128)} %get-tuple-element.26.scal_ref, f32[400,128]{1,0:T(8,128)} %get-tuple-element.27.r_ref, f32[400,128]{1,0:T(8,128)} %get-tuple-element.28.p_ref, f32[400,128]{1,0:T(8,128)} %get-tuple-element.29.q_ref, ...), custom_call_target="tpu_custom_call" | custom-call | tf_op jit(solution)/shard_map/pallas_call | solution.py:175
  (38 shorter events, 0.2 us)
Async XLA Ops:
  3.8 0.7 copy-start.14
  35.6 10.3 %copy-start = (f32[400,128]{1,0:T(8,128)}, f32[400,128]{1,0:T(8,128)S(1)}, u32[]{:S(2)}) copy-start(f32[400,128]{1,0:T(8,128)S(1)} %slice.135.r_ref.p_ref) | copy-start | bytes 614404
  35.6 8.1 %copy-start.3 = (f32[400,400]{1,0:T(8,128)S(1)}, f32[400,400]{1,0:T(8,128)}, u32[]{:S(2)}) copy-start(f32[400,400]{1,0:T(8,128)} %constant.25.clone) | copy-start | bytes 1920004
  35.6 11.1 %collective-permute-start.1 = (f32[400,128]{1,0:T(8,128)S(1)}, f32[400,128]{1,0:T(8,128)S(1)}, u32[]{:S(2)}, u32[]{:S(2)}) collective-permute-start(f32[400,128]{1,0:T(8,128)S(1)} %slice.135.r_ref.p_ref), channel_id=1, source_target_pairs={{1,0},{2,1},{3,2},{4,3},{5,4},{6,5},{7,6},{8,7},{9,8},{10,9},{11,1... | collective-permute-start | bytes 614408 | tf_op jit(solution)/shard_map/ppermute | solution.py:36
  37.1 9.7 %collective-permute-start = (f32[400,128]{1,0:T(8,128)S(1)}, f32[400,128]{1,0:T(8,128)S(1)}, u32[]{:S(2)}, u32[]{:S(2)}) collective-permute-start(f32[400,128]{1,0:T(8,128)S(1)} %slice.135.r_ref.p_ref), channel_id=1, source_target_pairs={{0,1},{1,2},{2,3},{3,4},{4,5},{5,6},{6,7},{7,8},{8,9},{9,10},{10,1... | collective-permute-start | bytes 614408 | tf_op jit(solution)/shard_map/ppermute | solution.py:31
  46.7 0.7 copy-start.1
  46.8 0.7 copy-start.2
  50.6 27.8 %collective-permute-start.3 = (f32[400,128]{1,0:T(8,128)}, f32[400,128]{1,0:T(8,128)S(1)}, u32[]{:S(2)}, u32[]{:S(2)}) collective-permute-start(f32[400,128]{1,0:T(8,128)} %get-tuple-element.19.w_ref.q_ref), channel_id=1, source_target_pairs={{1,0},{2,1},{3,2},{4,3},{5,4},{6,5},{7,6},{8,7},{9,8},{10,9},{11,1... | collective-permute-start | bytes 614408 | tf_op jit(solution)/shard_map/ppermute | solution.py:36
  51.9 26.5 %collective-permute-start.2 = (f32[400,128]{1,0:T(8,128)}, f32[400,128]{1,0:T(8,128)S(1)}, u32[]{:S(2)}, u32[]{:S(2)}) collective-permute-start(f32[400,128]{1,0:T(8,128)} %get-tuple-element.19.w_ref.q_ref), channel_id=1, source_target_pairs={{0,1},{1,2},{2,3},{3,4},{4,5},{5,6},{6,7},{7,8},{8,9},{9,10},{10,1... | collective-permute-start | bytes 614408 | tf_op jit(solution)/shard_map/ppermute | solution.py:31
  55.9 22.5 %all-to-all-start.1 = ((f32[128,1,128]{2,1,0:T(1,128)}), f32[128,1,128]{2,1,0:T(1,128)S(1)}, u32[]{:S(2)}, u32[]{:S(2)}) async-start(f32[128,1,128]{2,1,0:T(1,128)} %bitcast.77), calls=%async_computation.1 | async-start | bytes 131072 | tf_op jit(solution)/shard_map/all_to_all | solution.py:179
  70.0 7.6 %collective-permute-start.5 = (f32[400,1]{1,0:T(8,128)S(1)}, f32[400,1]{1,0:T(8,128)S(1)}, u32[]{:S(2)}, u32[]{:S(2)}) collective-permute-start(f32[400,1]{1,0:T(8,128)S(1)} %get-tuple-element.48), channel_id=1, source_target_pairs={{16,0},{32,16},{48,32},{64,48},{80,64},{96,80},{112,96},{17,1},{33... | collective-permute-start | bytes 4808 | tf_op jit(solution)/shard_map/ppermute | solution.py:36
  73.0 5.3 %collective-permute-start.4 = (f32[400,1]{1,0:T(8,128)S(1)}, f32[400,1]{1,0:T(8,128)S(1)}, u32[]{:S(2)}, u32[]{:S(2)}) collective-permute-start(f32[400,1]{1,0:T(8,128)S(1)} %get-tuple-element.49), channel_id=1, source_target_pairs={{0,16},{16,32},{32,48},{48,64},{64,80},{80,96},{96,112},{1,17},{17... | collective-permute-start | bytes 4808 | tf_op jit(solution)/shard_map/ppermute | solution.py:31
  77.6 0.8 copy-start.6
  78.3 0.7 copy-start.7
  78.4 0.6 copy-start.9
  78.4 0.7 copy-start.4
  78.4 0.8 copy-start.5
  82.7 28.0 %collective-permute-start.7 = (f32[400,128]{1,0:T(8,128)}, f32[400,128]{1,0:T(8,128)S(1)}, u32[]{:S(2)}, u32[]{:S(2)}) collective-permute-start(f32[400,128]{1,0:T(8,128)} %get-tuple-element.24.w_ref), channel_id=1, source_target_pairs={{1,0},{2,1},{3,2},{4,3},{5,4},{6,5},{7,6},{8,7},{9,8},{10,9},{11,1... | collective-permute-start | bytes 614408 | tf_op jit(solution)/shard_map/ppermute | solution.py:36
  84.0 26.7 %collective-permute-start.6 = (f32[400,128]{1,0:T(8,128)}, f32[400,128]{1,0:T(8,128)S(1)}, u32[]{:S(2)}, u32[]{:S(2)}) collective-permute-start(f32[400,128]{1,0:T(8,128)} %get-tuple-element.24.w_ref), channel_id=1, source_target_pairs={{0,1},{1,2},{2,3},{3,4},{4,5},{5,6},{6,7},{7,8},{8,9},{9,10},{10,1... | collective-permute-start | bytes 614408 | tf_op jit(solution)/shard_map/ppermute | solution.py:31
  88.0 22.7 %all-to-all-start.2 = ((f32[128,1,128]{2,1,0:T(1,128)}), f32[128,1,128]{2,1,0:T(1,128)S(1)}, u32[]{:S(2)}, u32[]{:S(2)}) async-start(f32[128,1,128]{2,1,0:T(1,128)} %bitcast.76), calls=%async_computation.2 | async-start | bytes 131072 | tf_op jit(solution)/shard_map/all_to_all | solution.py:179
  102.2 7.6 %collective-permute-start.9 = (f32[400,1]{1,0:T(8,128)S(1)}, f32[400,1]{1,0:T(8,128)S(1)}, u32[]{:S(2)}, u32[]{:S(2)}) collective-permute-start(f32[400,1]{1,0:T(8,128)S(1)} %get-tuple-element.46), channel_id=1, source_target_pairs={{16,0},{32,16},{48,32},{64,48},{80,64},{96,80},{112,96},{17,1},{33... | collective-permute-start | bytes 4808 | tf_op jit(solution)/shard_map/ppermute | solution.py:36
  105.2 5.3 %collective-permute-start.8 = (f32[400,1]{1,0:T(8,128)S(1)}, f32[400,1]{1,0:T(8,128)S(1)}, u32[]{:S(2)}, u32[]{:S(2)}) collective-permute-start(f32[400,1]{1,0:T(8,128)S(1)} %get-tuple-element.47), channel_id=1, source_target_pairs={{0,16},{16,32},{32,48},{48,64},{64,80},{80,96},{96,112},{1,17},{17... | collective-permute-start | bytes 4808 | tf_op jit(solution)/shard_map/ppermute | solution.py:31
  109.9 0.8 copy-start.12
  110.5 0.7 copy-start.13
  110.7 0.6 copy-start.8
  110.7 0.7 copy-start.10
  110.7 0.8 copy-start.11

commit v5 on v4

--- a/solution.py
+++ b/solution.py
@@ -204,8 +204,20 @@
     later = got[:, cols + 3 : cols + 4]
     weight = got[:, cols + 4 : cols + 5]
     dates = jnp.arange(DATES, dtype=jnp.float32)
-    network = (dates[None, :] == later).astype(jnp.float32) - (dates[None, :] == earlier).astype(jnp.float32)
-    right_wide = jnp.einsum("kt,kc->tc", network, weight * values, precision=HIGHEST)
+    network = ((dates[None, :] == later).astype(jnp.float32) - (dates[None, :] == earlier).astype(jnp.float32)).astype(
+        jnp.bfloat16
+    )
+    weighted = weight * values
+    high = lax.reduce_precision(weighted, exponent_bits=8, mantissa_bits=7)
+    rest = weighted - high
+    middle = lax.reduce_precision(rest, exponent_bits=8, mantissa_bits=7)
+    low = rest - middle
+    high, middle, low = (part.astype(jnp.bfloat16) for part in (high, middle, low))
+    width = values.shape[1]
+    pieces = jnp.einsum(
+        "kt,kc->tc", network, jnp.concatenate([high, middle, low], axis=1), preferred_element_type=jnp.float32
+    )
+    right_wide = pieces[:, :width] + pieces[:, width : 2 * width] + pieces[:, 2 * width :]
     span_hot = (jnp.arange(SPAN, dtype=jnp.float32)[None, :] == (later - earlier)).astype(jnp.float32)
     start_hot = (dates[None, :] == earlier).astype(jnp.float32)
     span_weights = jnp.einsum("kt,kd->td", start_hot, span_hot * weight, precision=HIGHEST)

time: 139 us -> 134 us (0.964)
  matrix products: 9.14 us -> 3.81 us
    dot_general x1, matrix products: 7.28 us -> 1.95 us  [body(): jnp.einsum('kt,kc->tc', network, jnp.concatenate([high, middle, low], axi...]
where the time goes in v5:
time: 134 us
  starting transfers between devices  53.2 us (40%)
  blocking collectives  43.3 us (32%)
  Pallas kernels  12.9 us (10%)
  local copies, waits for them, and re-layouts  9.41 us (7%)
  waiting for transfers between devices  5.67 us (4%)
  other arithmetic  4.26 us (3%)
  matrix products  3.81 us (3%)
    all_to_all x2, starting transfers between devices, reduce_all(): return lax.all_to_all(send, ('pair', 'tile'), 0, 0, tiled=True)  26 us
    all_to_all x1, blocking collectives, body(): lax.all_to_all(chunks, 'pair', 0, 0, tiled=True)  22.7 us
    all_to_all x1, blocking collectives, reduce_all(): return lax.all_to_all(send, ('pair', 'tile'), 0, 0, tiled=True)  20.6 us
    ppermute x5, starting transfers between devices, from_prev(): return lax.ppermute(cells, axis, [(i, i + 1) for i in range(count - 1)])  17.2 us
    pallas_call x4, Pallas kernels, call(): pl.pallas_call(kernel, out_shape=[jax.ShapeDtypeStruct(s, jnp.float32) fo...  12.9 us
    ppermute x5, starting transfers between devices, from_next(): return lax.ppermute(cells, axis, [(i + 1, i) for i in range(count - 1)])  9.94 us
    unnamed x38, local copies, waits for them, and re-layouts  5.31 us
    ppermute x5, waiting for transfers between devices, from_next(): return lax.ppermute(cells, axis, [(i + 1, i) for i in range(count - 1)])  4.03 us
  transfers between devices with their start and end apart: 12, of which 6 were waited for; matrix products, arithmetic and copies ran while one was open for 6% of the time, Pallas kernels for 0%

profile of v5, /device:TPU:1, one launch (start us, length us, event | category | flops | bytes accessed | tf_op | source)
XLA Modules:
  0.0 133.5 jit_solution(2598096302041385427)
XLA Ops:
  0.6 0.8 slice_convert_fusion.1
  1.4 2.4 %copy.19 = f32[250,1,1024]{0,2,1:T(8,128)S(1)} copy(f32[250,1,1024]{2,1,0:T(1,128)} %param.4) | data formatting | bytes 2048000 | tf_op args[0]
  3.9 0.6 copy-done.14
  4.5 0.1 pad_maximum_fusion
  4.6 22.7 %all_to_all.38 = f32[8,250,136]{1,2,0:T(8,128)S(1)} all-to-all(f32[8,250,136]{1,2,0:T(8,128)S(1)} %pad_maximum_fusion), channel_id=1, replica_groups=mesh['pair'=8,'tile'=16] {'pair'}, dimensions={0} | all-to-all | bytes 2176000 | tf_op jit(solution)/shard_map/all_to_all | solution.py:201
  27.3 0.4 copy.20
  27.7 0.5 reshape.17
  28.2 0.3 reduce-precision_convert_fusion.1
  28.5 2.0 %fusion.1 = f32[400,390]{1,0:T(8,128)S(1)} fusion(f32[2000]{0:T(1024)S(1)} %bitcast.98, f32[2000]{0:T(1024)S(1)} %bitcast.96, bf16[2000,130]{0,1:T(8,128)(2,1)S(1)} %get-tuple-element.41, bf16[2000,130]{0,1:T(8,128)(2,1)S(1)} %get-tuple-element.42, bf16[2000,130]{0,1:T(8,128)(2,1)S(1)} %get-tuple-element.40), kind=kOutput, calls=%fused_computation.4 | convolution fusion | flops 633480000 | bytes 2200000 | tf_op jit(solution)/shard_map/kt,kc->tc/dot_general | solution.py:217
  30.5 0.3 slice_add_fusion
  30.8 0.1 slice.150.r_ref.p_ref
  30.9 1.4 %collective-permute-start.1 = (f32[400,128]{1,0:T(8,128)S(1)}, f32[400,128]{1,0:T(8,128)S(1)}, u32[]{:S(2)}, u32[]{:S(2)}) collective-permute-start(f32[400,128]{1,0:T(8,128)S(1)} %slice.150.r_ref.p_ref), channel_id=1, source_target_pairs={{1,0},{2,1},{3,2},{4,3},{5,4},{6,5},{7,6},{8,7},{9,8},{10,9},{11,1... | collective-permute-start | bytes 614408 | tf_op jit(solution)/shard_map/ppermute | solution.py:36
  32.3 4.0 %collective-permute-start = (f32[400,128]{1,0:T(8,128)S(1)}, f32[400,128]{1,0:T(8,128)S(1)}, u32[]{:S(2)}, u32[]{:S(2)}) collective-permute-start(f32[400,128]{1,0:T(8,128)S(1)} %slice.150.r_ref.p_ref), channel_id=1, source_target_pairs={{0,1},{1,2},{2,3},{3,4},{4,5},{5,6},{6,7},{7,8},{8,9},{9,10},{10,1... | collective-permute-start | bytes 614408 | tf_op jit(solution)/shard_map/ppermute | solution.py:31
  36.3 1.9 %fusion = f32[400,8]{0,1:T(8,128)S(1)} fusion(f32[2000]{0:T(1024)S(1)} %bitcast.97, f32[2000]{0:T(1024)S(1)} %bitcast.94, f32[2000]{0:T(1024)S(1)} %bitcast.95), kind=kOutput, calls=%fused_computation.3 | convolution fusion | flops 77632000 | bytes 36800 | tf_op jit(solution)/shard_map/kt,kd->td/dot_general | solution.py:223
  38.2 0.6 fusion.30
  38.8 2.2 %add_add_fusion.k_ref = f32[400,400]{1,0:T(8,128)} fusion(f32[400,400]{1,0:T(8,128)S(1)} %copy-done.3, f32[400]{0:T(512)S(1)} %negate_add_fusion, f32[400]{0:T(512)S(1)} %bitcast.82, f32[400]{0:T(512)S(1)} %bitcast.84, f32[400]{0:T(512)S(1)} %bitcast.86, f32[400]{0:T(512)S(1)} %bitcast.88, f32[400]{0:T(512)S(1)} %bitcast.90, f32[400]{0:T(512)S(1)} %bitcast.92, ...), kind=kLoop, calls=%fused_computation.24 | loop fusion | flops 7520000 | bytes 1292800 | tf_op jit(solution)/shard_map/add | solution.py:75
  41.0 0.8 fusion.44
  41.9 0.7 copy-done.1
  42.6 3.1 %shard_map.59 = (f32[400,128]{1,0:T(8,128)}, f32[128,128]{1,0:T(8,128)}) custom-call(f32[400,400]{1,0:T(8,128)} %add_add_fusion.k_ref, f32[400,128]{1,0:T(8,128)} %copy-done, f32[400,128]{1,0:T(8,128)} %copy-done.2, f32[400,128]{1,0:T(8,128)} %copy-done.1, f32[400,1]{1,0:T(8,128)} %get-tuple-element.48.rl_ref, f32[400,1]{1,0:T(8,128)} %get-tuple-element.47.rr_ref), custom_call_target="tpu_custom_call" | custom-call | tf_op jit(solution)/shard_map/pallas_call | solution.py:175
  45.7 1.3 collective-permute-start.3
  47.0 4.0 %collective-permute-start.2 = (f32[400,128]{1,0:T(8,128)}, f32[400,128]{1,0:T(8,128)S(1)}, u32[]{:S(2)}, u32[]{:S(2)}) collective-permute-start(f32[400,128]{1,0:T(8,128)} %get-tuple-element.19.w_ref.q_ref), channel_id=1, source_target_pairs={{0,1},{1,2},{2,3},{3,4},{4,5},{5,6},{6,7},{7,8},{8,9},{9,10},{10,1... | collective-permute-start | bytes 614408 | tf_op jit(solution)/shard_map/ppermute | solution.py:31
  51.0 12.9 %all-to-all-start.1 = ((f32[128,1,128]{2,1,0:T(1,128)}), f32[128,1,128]{2,1,0:T(1,128)S(1)}, u32[]{:S(2)}, u32[]{:S(2)}) async-start(f32[128,1,128]{2,1,0:T(1,128)} %bitcast.77), calls=%async_computation.1 | async-start | bytes 131072 | tf_op jit(solution)/shard_map/all_to_all | solution.py:179
  63.9 1.1 fusion.46
  65.1 3.0 %collective-permute-start.5 = (f32[400,1]{1,0:T(8,128)S(1)}, f32[400,1]{1,0:T(8,128)S(1)}, u32[]{:S(2)}, u32[]{:S(2)}) collective-permute-start(f32[400,1]{1,0:T(8,128)S(1)} %get-tuple-element.51), channel_id=1, source_target_pairs={{16,0},{32,16},{48,32},{64,48},{80,64},{96,80},{112,96},{17,1},{33... | collective-permute-start | bytes 4808 | tf_op jit(solution)/shard_map/ppermute | solution.py:36
  68.1 2.6 %collective-permute-start.4 = (f32[400,1]{1,0:T(8,128)S(1)}, f32[400,1]{1,0:T(8,128)S(1)}, u32[]{:S(2)}, u32[]{:S(2)}) collective-permute-start(f32[400,1]{1,0:T(8,128)S(1)} %get-tuple-element.52), channel_id=1, source_target_pairs={{0,16},{16,32},{32,48},{48,64},{64,80},{80,96},{96,112},{1,17},{17... | collective-permute-start | bytes 4808 | tf_op jit(solution)/shard_map/ppermute | solution.py:31
  70.7 2.0 %collective-permute-done.5.wr_ref.qr_ref = f32[400,1]{1,0:T(8,128)S(1)} collective-permute-done((f32[400,1]{1,0:T(8,128)S(1)}, f32[400,1]{1,0:T(8,128)S(1)}, u32[]{:S(2)}, u32[]{:S(2)}) %collective-permute-start.5) | collective-permute-done | bytes 1632 | tf_op jit(solution)/shard_map/ppermute | solution.py:36
  72.7 0.7 collective-permute-done.4.wl_ref.ql_ref
  73.4 0.1 all-to-all-done.1
  73.5 0.5 copy-done.7
  74.0 0.1 copy-done.9
  74.1 0.1 copy-done.4
  74.3 3.5 %shard_map.60 = (f32[400,128]{1,0:T(8,128)}, f32[400,128]{1,0:T(8,128)}, f32[400,128]{1,0:T(8,128)}, f32[128,128]{1,0:T(8,128)}, f32[1,128]{1,0:T(1,128)}) custom-call(f32[128,128]{1,0:T(8,128)} %bitcast.74, f32[400,400]{1,0:T(8,128)} %add_add_fusion.k_ref, f32[400,128]{1,0:T(8,128)} %copy-done, f32[400,128]{1,0:T(8,128)} %copy-done.2, ...), custom_call_target="tpu_custom_call" | custom-call | tf_op jit(solution)/shard_map/pallas_call | solution.py:175
  77.8 1.3 collective-permute-start.7
  79.1 4.0 %collective-permute-start.6 = (f32[400,128]{1,0:T(8,128)}, f32[400,128]{1,0:T(8,128)S(1)}, u32[]{:S(2)}, u32[]{:S(2)}) collective-permute-start(f32[400,128]{1,0:T(8,128)} %get-tuple-element.24.w_ref), channel_id=1, source_target_pairs={{0,1},{1,2},{2,3},{3,4},{4,5},{5,6},{6,7},{7,8},{8,9},{9,10},{10,1... | collective-permute-start | bytes 614408 | tf_op jit(solution)/shard_map/ppermute | solution.py:31
  83.1 13.1 %all-to-all-start.2 = ((f32[128,1,128]{2,1,0:T(1,128)}), f32[128,1,128]{2,1,0:T(1,128)S(1)}, u32[]{:S(2)}, u32[]{:S(2)}) async-start(f32[128,1,128]{2,1,0:T(1,128)} %bitcast.76), calls=%async_computation.2 | async-start | bytes 131072 | tf_op jit(solution)/shard_map/all_to_all | solution.py:179
  96.2 1.1 fusion.45
  97.3 3.0 %collective-permute-start.9 = (f32[400,1]{1,0:T(8,128)S(1)}, f32[400,1]{1,0:T(8,128)S(1)}, u32[]{:S(2)}, u32[]{:S(2)}) collective-permute-start(f32[400,1]{1,0:T(8,128)S(1)} %get-tuple-element.49), channel_id=1, source_target_pairs={{16,0},{32,16},{48,32},{64,48},{80,64},{96,80},{112,96},{17,1},{33... | collective-permute-start | bytes 4808 | tf_op jit(solution)/shard_map/ppermute | solution.py:36
  100.3 2.6 %collective-permute-start.8 = (f32[400,1]{1,0:T(8,128)S(1)}, f32[400,1]{1,0:T(8,128)S(1)}, u32[]{:S(2)}, u32[]{:S(2)}) collective-permute-start(f32[400,1]{1,0:T(8,128)S(1)} %get-tuple-element.50), channel_id=1, source_target_pairs={{0,16},{16,32},{32,48},{48,64},{64,80},{80,96},{96,112},{1,17},{17... | collective-permute-start | bytes 4808 | tf_op jit(solution)/shard_map/ppermute | solution.py:31
  102.9 2.0 %collective-permute-done.9.wr_ref = f32[400,1]{1,0:T(8,128)S(1)} collective-permute-done((f32[400,1]{1,0:T(8,128)S(1)}, f32[400,1]{1,0:T(8,128)S(1)}, u32[]{:S(2)}, u32[]{:S(2)}) %collective-permute-start.9) | collective-permute-done | bytes 1632 | tf_op jit(solution)/shard_map/ppermute | solution.py:36
  105.0 0.7 collective-permute-done.8.wl_ref
  105.6 0.2 all-to-all-done.2
  105.8 0.5 copy-done.13
  106.3 0.1 copy-done.8
  106.4 0.1 copy-done.10
  106.5 0.1 copy-done.11
  106.6 4.1 %shard_map.61 = (f32[400,128]{1,0:T(8,128)}, f32[400,128]{1,0:T(8,128)}, f32[400,128]{1,0:T(8,128)}, f32[400,128]{1,0:T(8,128)}, f32[400,128]{1,0:T(8,128)}, /*index=5*/f32[128,128]{1,0:T(8,128)}, f32[1,128]{1,0:T(1,128)}) custom-call(f32[128,128]{1,0:T(8,128)} %bitcast.73, f32[1,128]{1,0:T(1,128)} %get-tuple-element.21.scal_ref, ...), custom_call_target="tpu_custom_call" | custom-call | tf_op jit(solution)/shard_map/pallas_call | solution.py:175
  110.7 20.6 %all_to_all.39 = f32[128,1,128]{2,1,0:T(1,128)} all-to-all(f32[128,1,128]{2,1,0:T(1,128)} %bitcast.78), channel_id=1, replica_groups=mesh['pair'=8,'tile'=16] {'pair','tile'}, dimensions={0} | all-to-all | bytes 131072 | tf_op jit(solution)/shard_map/all_to_all | solution.py:179
  131.3 2.2 %shard_map.62 = (f32[400,128]{1,0:T(8,128)}, f32[400,128]{1,0:T(8,128)}) custom-call(f32[128,128]{1,0:T(8,128)} %bitcast.75, f32[1,128]{1,0:T(1,128)} %get-tuple-element.26.scal_ref, f32[400,128]{1,0:T(8,128)} %get-tuple-element.27.r_ref, f32[400,128]{1,0:T(8,128)} %get-tuple-element.28.p_ref, f32[400,128]{1,0:T(8,128)} %get-tuple-element.29.q_ref, ...), custom_call_target="tpu_custom_call" | custom-call | tf_op jit(solution)/shard_map/pallas_call | solution.py:175
  (40 shorter events, 0.4 us)
Async XLA Ops:
  3.8 0.7 copy-start.14
  30.9 10.1 %copy-start = (f32[400,128]{1,0:T(8,128)}, f32[400,128]{1,0:T(8,128)S(1)}, u32[]{:S(2)}) copy-start(f32[400,128]{1,0:T(8,128)S(1)} %slice.150.r_ref.p_ref) | copy-start | bytes 614404
  30.9 7.9 %copy-start.3 = (f32[400,400]{1,0:T(8,128)S(1)}, f32[400,400]{1,0:T(8,128)}, u32[]{:S(2)}) copy-start(f32[400,400]{1,0:T(8,128)} %constant.25.clone) | copy-start | bytes 1920004
  30.9 10.9 %collective-permute-start.1 = (f32[400,128]{1,0:T(8,128)S(1)}, f32[400,128]{1,0:T(8,128)S(1)}, u32[]{:S(2)}, u32[]{:S(2)}) collective-permute-start(f32[400,128]{1,0:T(8,128)S(1)} %slice.150.r_ref.p_ref), channel_id=1, source_target_pairs={{1,0},{2,1},{3,2},{4,3},{5,4},{6,5},{7,6},{8,7},{9,8},{10,9},{11,1... | collective-permute-start | bytes 614408 | tf_op jit(solution)/shard_map/ppermute | solution.py:36
  32.3 9.5 %collective-permute-start = (f32[400,128]{1,0:T(8,128)S(1)}, f32[400,128]{1,0:T(8,128)S(1)}, u32[]{:S(2)}, u32[]{:S(2)}) collective-permute-start(f32[400,128]{1,0:T(8,128)S(1)} %slice.150.r_ref.p_ref), channel_id=1, source_target_pairs={{0,1},{1,2},{2,3},{3,4},{4,5},{5,6},{6,7},{7,8},{8,9},{9,10},{10,1... | collective-permute-start | bytes 614408 | tf_op jit(solution)/shard_map/ppermute | solution.py:31
  41.8 0.7 copy-start.1
  41.9 0.7 copy-start.2
  45.7 27.8 %collective-permute-start.3 = (f32[400,128]{1,0:T(8,128)}, f32[400,128]{1,0:T(8,128)S(1)}, u32[]{:S(2)}, u32[]{:S(2)}) collective-permute-start(f32[400,128]{1,0:T(8,128)} %get-tuple-element.19.w_ref.q_ref), channel_id=1, source_target_pairs={{1,0},{2,1},{3,2},{4,3},{5,4},{6,5},{7,6},{8,7},{9,8},{10,9},{11,1... | collective-permute-start | bytes 614408 | tf_op jit(solution)/shard_map/ppermute | solution.py:36
  47.0 26.5 %collective-permute-start.2 = (f32[400,128]{1,0:T(8,128)}, f32[400,128]{1,0:T(8,128)S(1)}, u32[]{:S(2)}, u32[]{:S(2)}) collective-permute-start(f32[400,128]{1,0:T(8,128)} %get-tuple-element.19.w_ref.q_ref), channel_id=1, source_target_pairs={{0,1},{1,2},{2,3},{3,4},{4,5},{5,6},{6,7},{7,8},{8,9},{9,10},{10,1... | collective-permute-start | bytes 614408 | tf_op jit(solution)/shard_map/ppermute | solution.py:31
  51.0 22.5 %all-to-all-start.1 = ((f32[128,1,128]{2,1,0:T(1,128)}), f32[128,1,128]{2,1,0:T(1,128)S(1)}, u32[]{:S(2)}, u32[]{:S(2)}) async-start(f32[128,1,128]{2,1,0:T(1,128)} %bitcast.77), calls=%async_computation.1 | async-start | bytes 131072 | tf_op jit(solution)/shard_map/all_to_all | solution.py:179
  65.1 7.6 %collective-permute-start.5 = (f32[400,1]{1,0:T(8,128)S(1)}, f32[400,1]{1,0:T(8,128)S(1)}, u32[]{:S(2)}, u32[]{:S(2)}) collective-permute-start(f32[400,1]{1,0:T(8,128)S(1)} %get-tuple-element.51), channel_id=1, source_target_pairs={{16,0},{32,16},{48,32},{64,48},{80,64},{96,80},{112,96},{17,1},{33... | collective-permute-start | bytes 4808 | tf_op jit(solution)/shard_map/ppermute | solution.py:36
  68.1 5.3 %collective-permute-start.4 = (f32[400,1]{1,0:T(8,128)S(1)}, f32[400,1]{1,0:T(8,128)S(1)}, u32[]{:S(2)}, u32[]{:S(2)}) collective-permute-start(f32[400,1]{1,0:T(8,128)S(1)} %get-tuple-element.52), channel_id=1, source_target_pairs={{0,16},{16,32},{32,48},{48,64},{64,80},{80,96},{96,112},{1,17},{17... | collective-permute-start | bytes 4808 | tf_op jit(solution)/shard_map/ppermute | solution.py:31
  72.7 0.8 copy-start.6
  73.3 0.7 copy-start.7
  73.5 0.6 copy-start.9
  73.5 0.8 copy-start.4
  73.5 0.8 copy-start.5
  77.8 28.0 %collective-permute-start.7 = (f32[400,128]{1,0:T(8,128)}, f32[400,128]{1,0:T(8,128)S(1)}, u32[]{:S(2)}, u32[]{:S(2)}) collective-permute-start(f32[400,128]{1,0:T(8,128)} %get-tuple-element.24.w_ref), channel_id=1, source_target_pairs={{1,0},{2,1},{3,2},{4,3},{5,4},{6,5},{7,6},{8,7},{9,8},{10,9},{11,1... | collective-permute-start | bytes 614408 | tf_op jit(solution)/shard_map/ppermute | solution.py:36
  79.1 26.7 %collective-permute-start.6 = (f32[400,128]{1,0:T(8,128)}, f32[400,128]{1,0:T(8,128)S(1)}, u32[]{:S(2)}, u32[]{:S(2)}) collective-permute-start(f32[400,128]{1,0:T(8,128)} %get-tuple-element.24.w_ref), channel_id=1, source_target_pairs={{0,1},{1,2},{2,3},{3,4},{4,5},{5,6},{6,7},{7,8},{8,9},{9,10},{10,1... | collective-permute-start | bytes 614408 | tf_op jit(solution)/shard_map/ppermute | solution.py:31
  83.1 22.7 %all-to-all-start.2 = ((f32[128,1,128]{2,1,0:T(1,128)}), f32[128,1,128]{2,1,0:T(1,128)S(1)}, u32[]{:S(2)}, u32[]{:S(2)}) async-start(f32[128,1,128]{2,1,0:T(1,128)} %bitcast.76), calls=%async_computation.2 | async-start | bytes 131072 | tf_op jit(solution)/shard_map/all_to_all | solution.py:179
  97.3 7.6 %collective-permute-start.9 = (f32[400,1]{1,0:T(8,128)S(1)}, f32[400,1]{1,0:T(8,128)S(1)}, u32[]{:S(2)}, u32[]{:S(2)}) collective-permute-start(f32[400,1]{1,0:T(8,128)S(1)} %get-tuple-element.49), channel_id=1, source_target_pairs={{16,0},{32,16},{48,32},{64,48},{80,64},{96,80},{112,96},{17,1},{33... | collective-permute-start | bytes 4808 | tf_op jit(solution)/shard_map/ppermute | solution.py:36
  100.3 5.3 %collective-permute-start.8 = (f32[400,1]{1,0:T(8,128)S(1)}, f32[400,1]{1,0:T(8,128)S(1)}, u32[]{:S(2)}, u32[]{:S(2)}) collective-permute-start(f32[400,1]{1,0:T(8,128)S(1)} %get-tuple-element.50), channel_id=1, source_target_pairs={{0,16},{16,32},{32,48},{48,64},{64,80},{80,96},{96,112},{1,17},{17... | collective-permute-start | bytes 4808 | tf_op jit(solution)/shard_map/ppermute | solution.py:31
  105.0 0.9 copy-start.12
  105.6 0.7 copy-start.13
  105.8 0.6 copy-start.8
  105.8 0.7 copy-start.10
  105.8 0.8 copy-start.11

commit v6 on v5

--- a/solution.py
+++ b/solution.py
@@ -172,7 +172,13 @@
 
 
 def call(kernel, shapes, *args):
-    return pl.pallas_call(kernel, out_shape=[jax.ShapeDtypeStruct(s, jnp.float32) for s in shapes])(*args)
+    resident = pl.BlockSpec(memory_space=pltpu.VMEM)
+    return pl.pallas_call(
+        kernel,
+        out_shape=[jax.ShapeDtypeStruct(s, jnp.float32) for s in shapes],
+        in_specs=[resident] * len(args),
+        out_specs=[resident] * len(shapes),
+    )(*args)
 
 
 def reduce_all(send):

time: 134 us -> 134 us (level)
  no operation moved by 1% of the time
where the time goes in v6:
time: 134 us
  starting transfers between devices  53.2 us (40%)
  blocking collectives  43.3 us (32%)
  Pallas kernels  12.9 us (10%)
  local copies, waits for them, and re-layouts  9.41 us (7%)
  waiting for transfers between devices  5.67 us (4%)
  other arithmetic  4.26 us (3%)
  matrix products  3.81 us (3%)
    all_to_all x2, starting transfers between devices, reduce_all(): return lax.all_to_all(send, ('pair', 'tile'), 0, 0, tiled=True)  26 us
    all_to_all x1, blocking collectives, body(): lax.all_to_all(chunks, 'pair', 0, 0, tiled=True)  22.7 us
    all_to_all x1, blocking collectives, reduce_all(): return lax.all_to_all(send, ('pair', 'tile'), 0, 0, tiled=True)  20.6 us
    ppermute x5, starting transfers between devices, from_prev(): return lax.ppermute(cells, axis, [(i, i + 1) for i in range(count - 1)])  17.2 us
    pallas_call x4, Pallas kernels, call(): pl.pallas_call(kernel, out_shape=[jax.ShapeDtypeStruct(s, jnp.float32) fo...  12.9 us
    ppermute x5, starting transfers between devices, from_next(): return lax.ppermute(cells, axis, [(i + 1, i) for i in range(count - 1)])  9.94 us
    unnamed x38, local copies, waits for them, and re-layouts  5.31 us
    ppermute x5, waiting for transfers between devices, from_next(): return lax.ppermute(cells, axis, [(i + 1, i) for i in range(count - 1)])  4.03 us
  transfers between devices with their start and end apart: 12, of which 6 were waited for; matrix products, arithmetic and copies ran while one was open for 6% of the time, Pallas kernels for 0%

profile of v6, /device:TPU:1, one launch (start us, length us, event | category | flops | bytes accessed | tf_op | source)
XLA Modules:
  0.0 133.5 jit_solution(2598096302041385427)
XLA Ops:
  0.6 0.8 slice_convert_fusion.1
  1.4 2.4 %copy.19 = f32[250,1,1024]{0,2,1:T(8,128)S(1)} copy(f32[250,1,1024]{2,1,0:T(1,128)} %param.4) | data formatting | bytes 2048000 | tf_op args[0]
  3.9 0.6 copy-done.14
  4.5 0.1 pad_maximum_fusion
  4.6 22.7 %all_to_all.38 = f32[8,250,136]{1,2,0:T(8,128)S(1)} all-to-all(f32[8,250,136]{1,2,0:T(8,128)S(1)} %pad_maximum_fusion), channel_id=1, replica_groups=mesh['pair'=8,'tile'=16] {'pair'}, dimensions={0} | all-to-all | bytes 2176000 | tf_op jit(solution)/shard_map/all_to_all | solution.py:207
  27.3 0.4 copy.20
  27.7 0.5 reshape.17
  28.2 0.3 reduce-precision_convert_fusion.1
  28.5 2.0 %fusion.1 = f32[400,390]{1,0:T(8,128)S(1)} fusion(f32[2000]{0:T(1024)S(1)} %bitcast.98, f32[2000]{0:T(1024)S(1)} %bitcast.96, bf16[2000,130]{0,1:T(8,128)(2,1)S(1)} %get-tuple-element.41, bf16[2000,130]{0,1:T(8,128)(2,1)S(1)} %get-tuple-element.42, bf16[2000,130]{0,1:T(8,128)(2,1)S(1)} %get-tuple-element.40), kind=kOutput, calls=%fused_computation.4 | convolution fusion | flops 633480000 | bytes 2200000 | tf_op jit(solution)/shard_map/kt,kc->tc/dot_general | solution.py:223
  30.5 0.3 slice_add_fusion
  30.8 0.1 slice.150.r_ref.p_ref
  30.9 1.4 %collective-permute-start.1 = (f32[400,128]{1,0:T(8,128)S(1)}, f32[400,128]{1,0:T(8,128)S(1)}, u32[]{:S(2)}, u32[]{:S(2)}) collective-permute-start(f32[400,128]{1,0:T(8,128)S(1)} %slice.150.r_ref.p_ref), channel_id=1, source_target_pairs={{1,0},{2,1},{3,2},{4,3},{5,4},{6,5},{7,6},{8,7},{9,8},{10,9},{11,1... | collective-permute-start | bytes 614408 | tf_op jit(solution)/shard_map/ppermute | solution.py:36
  32.3 4.0 %collective-permute-start = (f32[400,128]{1,0:T(8,128)S(1)}, f32[400,128]{1,0:T(8,128)S(1)}, u32[]{:S(2)}, u32[]{:S(2)}) collective-permute-start(f32[400,128]{1,0:T(8,128)S(1)} %slice.150.r_ref.p_ref), channel_id=1, source_target_pairs={{0,1},{1,2},{2,3},{3,4},{4,5},{5,6},{6,7},{7,8},{8,9},{9,10},{10,1... | collective-permute-start | bytes 614408 | tf_op jit(solution)/shard_map/ppermute | solution.py:31
  36.3 1.9 %fusion = f32[400,8]{0,1:T(8,128)S(1)} fusion(f32[2000]{0:T(1024)S(1)} %bitcast.97, f32[2000]{0:T(1024)S(1)} %bitcast.94, f32[2000]{0:T(1024)S(1)} %bitcast.95), kind=kOutput, calls=%fused_computation.3 | convolution fusion | flops 77632000 | bytes 36800 | tf_op jit(solution)/shard_map/kt,kd->td/dot_general | solution.py:229
  38.2 0.6 fusion.30
  38.8 2.2 %add_add_fusion.k_ref = f32[400,400]{1,0:T(8,128)} fusion(f32[400,400]{1,0:T(8,128)S(1)} %copy-done.3, f32[400]{0:T(512)S(1)} %negate_add_fusion, f32[400]{0:T(512)S(1)} %bitcast.82, f32[400]{0:T(512)S(1)} %bitcast.84, f32[400]{0:T(512)S(1)} %bitcast.86, f32[400]{0:T(512)S(1)} %bitcast.88, f32[400]{0:T(512)S(1)} %bitcast.90, f32[400]{0:T(512)S(1)} %bitcast.92, ...), kind=kLoop, calls=%fused_computation.24 | loop fusion | flops 7520000 | bytes 1292800 | tf_op jit(solution)/shard_map/add | solution.py:75
  41.0 0.8 fusion.44
  41.9 0.7 copy-done.1
  42.6 3.1 %shard_map.59 = (f32[400,128]{1,0:T(8,128)}, f32[128,128]{1,0:T(8,128)}) custom-call(f32[400,400]{1,0:T(8,128)} %add_add_fusion.k_ref, f32[400,128]{1,0:T(8,128)} %copy-done, f32[400,128]{1,0:T(8,128)} %copy-done.2, f32[400,128]{1,0:T(8,128)} %copy-done.1, f32[400,1]{1,0:T(8,128)} %get-tuple-element.48.rl_ref, f32[400,1]{1,0:T(8,128)} %get-tuple-element.47.rr_ref), custom_call_target="tpu_custom_call" | custom-call | tf_op jit(solution)/shard_map/pallas_call | solution.py:176
  45.7 1.3 collective-permute-start.3
  47.0 4.0 %collective-permute-start.2 = (f32[400,128]{1,0:T(8,128)}, f32[400,128]{1,0:T(8,128)S(1)}, u32[]{:S(2)}, u32[]{:S(2)}) collective-permute-start(f32[400,128]{1,0:T(8,128)} %get-tuple-element.19.w_ref.q_ref), channel_id=1, source_target_pairs={{0,1},{1,2},{2,3},{3,4},{4,5},{5,6},{6,7},{7,8},{8,9},{9,10},{10,1... | collective-permute-start | bytes 614408 | tf_op jit(solution)/shard_map/ppermute | solution.py:31
  51.0 12.9 %all-to-all-start.1 = ((f32[128,1,128]{2,1,0:T(1,128)}), f32[128,1,128]{2,1,0:T(1,128)S(1)}, u32[]{:S(2)}, u32[]{:S(2)}) async-start(f32[128,1,128]{2,1,0:T(1,128)} %bitcast.77), calls=%async_computation.1 | async-start | bytes 131072 | tf_op jit(solution)/shard_map/all_to_all | solution.py:185
  63.9 1.1 fusion.46
  65.1 3.0 %collective-permute-start.5 = (f32[400,1]{1,0:T(8,128)S(1)}, f32[400,1]{1,0:T(8,128)S(1)}, u32[]{:S(2)}, u32[]{:S(2)}) collective-permute-start(f32[400,1]{1,0:T(8,128)S(1)} %get-tuple-element.51), channel_id=1, source_target_pairs={{16,0},{32,16},{48,32},{64,48},{80,64},{96,80},{112,96},{17,1},{33... | collective-permute-start | bytes 4808 | tf_op jit(solution)/shard_map/ppermute | solution.py:36
  68.1 2.6 %collective-permute-start.4 = (f32[400,1]{1,0:T(8,128)S(1)}, f32[400,1]{1,0:T(8,128)S(1)}, u32[]{:S(2)}, u32[]{:S(2)}) collective-permute-start(f32[400,1]{1,0:T(8,128)S(1)} %get-tuple-element.52), channel_id=1, source_target_pairs={{0,16},{16,32},{32,48},{48,64},{64,80},{80,96},{96,112},{1,17},{17... | collective-permute-start | bytes 4808 | tf_op jit(solution)/shard_map/ppermute | solution.py:31
  70.7 2.0 %collective-permute-done.5.wr_ref.qr_ref = f32[400,1]{1,0:T(8,128)S(1)} collective-permute-done((f32[400,1]{1,0:T(8,128)S(1)}, f32[400,1]{1,0:T(8,128)S(1)}, u32[]{:S(2)}, u32[]{:S(2)}) %collective-permute-start.5) | collective-permute-done | bytes 1632 | tf_op jit(solution)/shard_map/ppermute | solution.py:36
  72.7 0.7 collective-permute-done.4.wl_ref.ql_ref
  73.4 0.1 all-to-all-done.1
  73.5 0.5 copy-done.7
  74.0 0.1 copy-done.9
  74.1 0.1 copy-done.4
  74.3 3.5 %shard_map.60 = (f32[400,128]{1,0:T(8,128)}, f32[400,128]{1,0:T(8,128)}, f32[400,128]{1,0:T(8,128)}, f32[128,128]{1,0:T(8,128)}, f32[1,128]{1,0:T(1,128)}) custom-call(f32[128,128]{1,0:T(8,128)} %bitcast.74, f32[400,400]{1,0:T(8,128)} %add_add_fusion.k_ref, f32[400,128]{1,0:T(8,128)} %copy-done, f32[400,128]{1,0:T(8,128)} %copy-done.2, ...), custom_call_target="tpu_custom_call" | custom-call | tf_op jit(solution)/shard_map/pallas_call | solution.py:176
  77.8 1.3 collective-permute-start.7
  79.1 4.0 %collective-permute-start.6 = (f32[400,128]{1,0:T(8,128)}, f32[400,128]{1,0:T(8,128)S(1)}, u32[]{:S(2)}, u32[]{:S(2)}) collective-permute-start(f32[400,128]{1,0:T(8,128)} %get-tuple-element.24.w_ref), channel_id=1, source_target_pairs={{0,1},{1,2},{2,3},{3,4},{4,5},{5,6},{6,7},{7,8},{8,9},{9,10},{10,1... | collective-permute-start | bytes 614408 | tf_op jit(solution)/shard_map/ppermute | solution.py:31
  83.1 13.1 %all-to-all-start.2 = ((f32[128,1,128]{2,1,0:T(1,128)}), f32[128,1,128]{2,1,0:T(1,128)S(1)}, u32[]{:S(2)}, u32[]{:S(2)}) async-start(f32[128,1,128]{2,1,0:T(1,128)} %bitcast.76), calls=%async_computation.2 | async-start | bytes 131072 | tf_op jit(solution)/shard_map/all_to_all | solution.py:185
  96.2 1.1 fusion.45
  97.3 3.0 %collective-permute-start.9 = (f32[400,1]{1,0:T(8,128)S(1)}, f32[400,1]{1,0:T(8,128)S(1)}, u32[]{:S(2)}, u32[]{:S(2)}) collective-permute-start(f32[400,1]{1,0:T(8,128)S(1)} %get-tuple-element.49), channel_id=1, source_target_pairs={{16,0},{32,16},{48,32},{64,48},{80,64},{96,80},{112,96},{17,1},{33... | collective-permute-start | bytes 4808 | tf_op jit(solution)/shard_map/ppermute | solution.py:36
  100.3 2.6 %collective-permute-start.8 = (f32[400,1]{1,0:T(8,128)S(1)}, f32[400,1]{1,0:T(8,128)S(1)}, u32[]{:S(2)}, u32[]{:S(2)}) collective-permute-start(f32[400,1]{1,0:T(8,128)S(1)} %get-tuple-element.50), channel_id=1, source_target_pairs={{0,16},{16,32},{32,48},{48,64},{64,80},{80,96},{96,112},{1,17},{17... | collective-permute-start | bytes 4808 | tf_op jit(solution)/shard_map/ppermute | solution.py:31
  102.9 2.0 %collective-permute-done.9.wr_ref = f32[400,1]{1,0:T(8,128)S(1)} collective-permute-done((f32[400,1]{1,0:T(8,128)S(1)}, f32[400,1]{1,0:T(8,128)S(1)}, u32[]{:S(2)}, u32[]{:S(2)}) %collective-permute-start.9) | collective-permute-done | bytes 1632 | tf_op jit(solution)/shard_map/ppermute | solution.py:36
  105.0 0.7 collective-permute-done.8.wl_ref
  105.6 0.2 all-to-all-done.2
  105.8 0.5 copy-done.13
  106.3 0.1 copy-done.8
  106.4 0.1 copy-done.10
  106.5 0.1 copy-done.11
  106.6 4.1 %shard_map.61 = (f32[400,128]{1,0:T(8,128)}, f32[400,128]{1,0:T(8,128)}, f32[400,128]{1,0:T(8,128)}, f32[400,128]{1,0:T(8,128)}, f32[400,128]{1,0:T(8,128)}, /*index=5*/f32[128,128]{1,0:T(8,128)}, f32[1,128]{1,0:T(1,128)}) custom-call(f32[128,128]{1,0:T(8,128)} %bitcast.73, f32[1,128]{1,0:T(1,128)} %get-tuple-element.21.scal_ref, ...), custom_call_target="tpu_custom_call" | custom-call | tf_op jit(solution)/shard_map/pallas_call | solution.py:176
  110.7 20.6 %all_to_all.39 = f32[128,1,128]{2,1,0:T(1,128)} all-to-all(f32[128,1,128]{2,1,0:T(1,128)} %bitcast.78), channel_id=1, replica_groups=mesh['pair'=8,'tile'=16] {'pair','tile'}, dimensions={0} | all-to-all | bytes 131072 | tf_op jit(solution)/shard_map/all_to_all | solution.py:185
  131.3 2.2 %shard_map.62 = (f32[400,128]{1,0:T(8,128)}, f32[400,128]{1,0:T(8,128)}) custom-call(f32[128,128]{1,0:T(8,128)} %bitcast.75, f32[1,128]{1,0:T(1,128)} %get-tuple-element.26.scal_ref, f32[400,128]{1,0:T(8,128)} %get-tuple-element.27.r_ref, f32[400,128]{1,0:T(8,128)} %get-tuple-element.28.p_ref, f32[400,128]{1,0:T(8,128)} %get-tuple-element.29.q_ref, ...), custom_call_target="tpu_custom_call" | custom-call | tf_op jit(solution)/shard_map/pallas_call | solution.py:176
  (40 shorter events, 0.4 us)
Async XLA Ops:
  3.8 0.7 copy-start.14
  30.9 10.1 %copy-start = (f32[400,128]{1,0:T(8,128)}, f32[400,128]{1,0:T(8,128)S(1)}, u32[]{:S(2)}) copy-start(f32[400,128]{1,0:T(8,128)S(1)} %slice.150.r_ref.p_ref) | copy-start | bytes 614404
  30.9 7.9 %copy-start.3 = (f32[400,400]{1,0:T(8,128)S(1)}, f32[400,400]{1,0:T(8,128)}, u32[]{:S(2)}) copy-start(f32[400,400]{1,0:T(8,128)} %constant.25.clone) | copy-start | bytes 1920004
  30.9 10.9 %collective-permute-start.1 = (f32[400,128]{1,0:T(8,128)S(1)}, f32[400,128]{1,0:T(8,128)S(1)}, u32[]{:S(2)}, u32[]{:S(2)}) collective-permute-start(f32[400,128]{1,0:T(8,128)S(1)} %slice.150.r_ref.p_ref), channel_id=1, source_target_pairs={{1,0},{2,1},{3,2},{4,3},{5,4},{6,5},{7,6},{8,7},{9,8},{10,9},{11,1... | collective-permute-start | bytes 614408 | tf_op jit(solution)/shard_map/ppermute | solution.py:36
  32.3 9.5 %collective-permute-start = (f32[400,128]{1,0:T(8,128)S(1)}, f32[400,128]{1,0:T(8,128)S(1)}, u32[]{:S(2)}, u32[]{:S(2)}) collective-permute-start(f32[400,128]{1,0:T(8,128)S(1)} %slice.150.r_ref.p_ref), channel_id=1, source_target_pairs={{0,1},{1,2},{2,3},{3,4},{4,5},{5,6},{6,7},{7,8},{8,9},{9,10},{10,1... | collective-permute-start | bytes 614408 | tf_op jit(solution)/shard_map/ppermute | solution.py:31
  41.8 0.7 copy-start.1
  41.9 0.7 copy-start.2
  45.7 27.8 %collective-permute-start.3 = (f32[400,128]{1,0:T(8,128)}, f32[400,128]{1,0:T(8,128)S(1)}, u32[]{:S(2)}, u32[]{:S(2)}) collective-permute-start(f32[400,128]{1,0:T(8,128)} %get-tuple-element.19.w_ref.q_ref), channel_id=1, source_target_pairs={{1,0},{2,1},{3,2},{4,3},{5,4},{6,5},{7,6},{8,7},{9,8},{10,9},{11,1... | collective-permute-start | bytes 614408 | tf_op jit(solution)/shard_map/ppermute | solution.py:36
  47.0 26.5 %collective-permute-start.2 = (f32[400,128]{1,0:T(8,128)}, f32[400,128]{1,0:T(8,128)S(1)}, u32[]{:S(2)}, u32[]{:S(2)}) collective-permute-start(f32[400,128]{1,0:T(8,128)} %get-tuple-element.19.w_ref.q_ref), channel_id=1, source_target_pairs={{0,1},{1,2},{2,3},{3,4},{4,5},{5,6},{6,7},{7,8},{8,9},{9,10},{10,1... | collective-permute-start | bytes 614408 | tf_op jit(solution)/shard_map/ppermute | solution.py:31
  51.0 22.5 %all-to-all-start.1 = ((f32[128,1,128]{2,1,0:T(1,128)}), f32[128,1,128]{2,1,0:T(1,128)S(1)}, u32[]{:S(2)}, u32[]{:S(2)}) async-start(f32[128,1,128]{2,1,0:T(1,128)} %bitcast.77), calls=%async_computation.1 | async-start | bytes 131072 | tf_op jit(solution)/shard_map/all_to_all | solution.py:185
  65.1 7.6 %collective-permute-start.5 = (f32[400,1]{1,0:T(8,128)S(1)}, f32[400,1]{1,0:T(8,128)S(1)}, u32[]{:S(2)}, u32[]{:S(2)}) collective-permute-start(f32[400,1]{1,0:T(8,128)S(1)} %get-tuple-element.51), channel_id=1, source_target_pairs={{16,0},{32,16},{48,32},{64,48},{80,64},{96,80},{112,96},{17,1},{33... | collective-permute-start | bytes 4808 | tf_op jit(solution)/shard_map/ppermute | solution.py:36
  68.1 5.3 %collective-permute-start.4 = (f32[400,1]{1,0:T(8,128)S(1)}, f32[400,1]{1,0:T(8,128)S(1)}, u32[]{:S(2)}, u32[]{:S(2)}) collective-permute-start(f32[400,1]{1,0:T(8,128)S(1)} %get-tuple-element.52), channel_id=1, source_target_pairs={{0,16},{16,32},{32,48},{48,64},{64,80},{80,96},{96,112},{1,17},{17... | collective-permute-start | bytes 4808 | tf_op jit(solution)/shard_map/ppermute | solution.py:31
  72.7 0.8 copy-start.6
  73.3 0.7 copy-start.7
  73.5 0.6 copy-start.9
  73.5 0.8 copy-start.4
  73.5 0.8 copy-start.5
  77.8 28.0 %collective-permute-start.7 = (f32[400,128]{1,0:T(8,128)}, f32[400,128]{1,0:T(8,128)S(1)}, u32[]{:S(2)}, u32[]{:S(2)}) collective-permute-start(f32[400,128]{1,0:T(8,128)} %get-tuple-element.24.w_ref), channel_id=1, source_target_pairs={{1,0},{2,1},{3,2},{4,3},{5,4},{6,5},{7,6},{8,7},{9,8},{10,9},{11,1... | collective-permute-start | bytes 614408 | tf_op jit(solution)/shard_map/ppermute | solution.py:36
  79.1 26.7 %collective-permute-start.6 = (f32[400,128]{1,0:T(8,128)}, f32[400,128]{1,0:T(8,128)S(1)}, u32[]{:S(2)}, u32[]{:S(2)}) collective-permute-start(f32[400,128]{1,0:T(8,128)} %get-tuple-element.24.w_ref), channel_id=1, source_target_pairs={{0,1},{1,2},{2,3},{3,4},{4,5},{5,6},{6,7},{7,8},{8,9},{9,10},{10,1... | collective-permute-start | bytes 614408 | tf_op jit(solution)/shard_map/ppermute | solution.py:31
  83.1 22.7 %all-to-all-start.2 = ((f32[128,1,128]{2,1,0:T(1,128)}), f32[128,1,128]{2,1,0:T(1,128)S(1)}, u32[]{:S(2)}, u32[]{:S(2)}) async-start(f32[128,1,128]{2,1,0:T(1,128)} %bitcast.76), calls=%async_computation.2 | async-start | bytes 131072 | tf_op jit(solution)/shard_map/all_to_all | solution.py:185
  97.3 7.6 %collective-permute-start.9 = (f32[400,1]{1,0:T(8,128)S(1)}, f32[400,1]{1,0:T(8,128)S(1)}, u32[]{:S(2)}, u32[]{:S(2)}) collective-permute-start(f32[400,1]{1,0:T(8,128)S(1)} %get-tuple-element.49), channel_id=1, source_target_pairs={{16,0},{32,16},{48,32},{64,48},{80,64},{96,80},{112,96},{17,1},{33... | collective-permute-start | bytes 4808 | tf_op jit(solution)/shard_map/ppermute | solution.py:36
  100.3 5.3 %collective-permute-start.8 = (f32[400,1]{1,0:T(8,128)S(1)}, f32[400,1]{1,0:T(8,128)S(1)}, u32[]{:S(2)}, u32[]{:S(2)}) collective-permute-start(f32[400,1]{1,0:T(8,128)S(1)} %get-tuple-element.50), channel_id=1, source_target_pairs={{0,16},{16,32},{32,48},{48,64},{64,80},{80,96},{96,112},{1,17},{17... | collective-permute-start | bytes 4808 | tf_op jit(solution)/shard_map/ppermute | solution.py:31
  105.0 0.9 copy-start.12
  105.6 0.7 copy-start.13
  105.8 0.6 copy-start.8
  105.8 0.7 copy-start.10
  105.8 0.8 copy-start.11

commit v7 on v6

--- a/solution.py
+++ b/solution.py
@@ -63,16 +63,8 @@
     return jnp.sum(got, axis=0)
 
 
-def normal_matrix(weights):
-    dates = jnp.arange(DATES, dtype=jnp.int32)
-    offset = dates[None, :] - dates[:, None]
-    upper = jnp.zeros((DATES, DATES), jnp.float32)
-    for d in range(1, SPAN):
-        upper = upper + jnp.where(offset == d, -weights[:, d : d + 1], 0.0)
-    coupling = upper + upper.T
-    degree = -jnp.sum(coupling, axis=1)
-    diagonal = degree + (4.0 * spatial_weight + ridge_weight)
-    return coupling + jnp.where(offset == 0, diagonal[:, None], 0.0) + temporal_weight * temporal_matrix()
+def regularizer_matrix():
+    return temporal_weight * temporal_matrix() + (4.0 * spatial_weight + ridge_weight) * np.eye(DATES, dtype=np.float32)
 
 
 def lane_value(vector, j):
@@ -213,21 +205,18 @@
     network = ((dates[None, :] == later).astype(jnp.float32) - (dates[None, :] == earlier).astype(jnp.float32)).astype(
         jnp.bfloat16
     )
-    weighted = weight * values
-    high = lax.reduce_precision(weighted, exponent_bits=8, mantissa_bits=7)
-    rest = weighted - high
+    width = values.shape[1]
+    operand = jnp.concatenate([weight * values, weight * network.astype(jnp.float32)], axis=1)
+    high = lax.reduce_precision(operand, exponent_bits=8, mantissa_bits=7)
+    rest = operand - high
     middle = lax.reduce_precision(rest, exponent_bits=8, mantissa_bits=7)
     low = rest - middle
-    high, middle, low = (part.astype(jnp.bfloat16) for part in (high, middle, low))
-    width = values.shape[1]
-    pieces = jnp.einsum(
-        "kt,kc->tc", network, jnp.concatenate([high, middle, low], axis=1), preferred_element_type=jnp.float32
-    )
-    right_wide = pieces[:, :width] + pieces[:, width : 2 * width] + pieces[:, 2 * width :]
-    span_hot = (jnp.arange(SPAN, dtype=jnp.float32)[None, :] == (later - earlier)).astype(jnp.float32)
-    start_hot = (dates[None, :] == earlier).astype(jnp.float32)
-    span_weights = jnp.einsum("kt,kd->td", start_hot, span_hot * weight, precision=HIGHEST)
-    matrix = normal_matrix(span_weights)
+    parts = jnp.concatenate([p.astype(jnp.bfloat16) for p in (high, middle, low)], axis=1)
+    pieces = jnp.einsum("kt,kc->tc", network, parts, preferred_element_type=jnp.float32)
+    span = width + DATES
+    summed = pieces[:, :span] + pieces[:, span : 2 * span] + pieces[:, 2 * span :]
+    right_wide = summed[:, :width]
+    matrix = summed[:, width:] + regularizer_matrix()
     residual = right_wide[:, 1:-1]
     residual_halo = (
         from_prev(residual, "tile"),

time: 134 us -> 157 us (1.17)
  local copies, waits for them, and re-layouts: 9.41 us -> 23.3 us
  other arithmetic: 4.26 us -> 7.53 us
  matrix products: 3.81 us -> 6.37 us
    concatenate x0 -> x1, local copies, waits for them, and re-layouts: none -> 11.5 us  [body(): jnp.concatenate([p.astype(jnp.bfloat16) for p in (high, middle, low)], ax...]
    convert_element_type x1, other arithmetic: 0.31 us -> 3.92 us  [body(): p.astype(jnp.bfloat16)]
    dot_general x2 -> x1, matrix products: 3.81 us -> 6.37 us  [body(): jnp.einsum('kt,kc->tc', network, parts, preferred_element_type=jnp.float32)]
    mul x0 -> x1, local copies, waits for them, and re-layouts: none -> 1.82 us  [body(): weight * values]
    unnamed x38 -> x40, local copies, waits for them, and re-layouts: 5.31 us -> 5.86 us
  transfers between devices with their start and end apart: 12 -> 12, of which waited for: 6 -> 8; matrix products, arithmetic and copies ran while one was open for 6% -> 3% of each run, Pallas kernels for 0% -> 0%
where the time goes in v7:
time: 157 us; the launch traced here: 156 us
  starting transfers between devices  54.4 us (35%)
  blocking collectives  43.4 us (28%)
  local copies, waits for them, and re-layouts  23.3 us (15%)
  Pallas kernels  12.9 us (8%)
  other arithmetic  7.53 us (5%)
  waiting for transfers between devices  6.76 us (4%)
  matrix products  6.37 us (4%)
    all_to_all x2, starting transfers between devices, reduce_all(): return lax.all_to_all(send, ('pair', 'tile'), 0, 0, tiled=True)  26.4 us
    all_to_all x1, blocking collectives, body(): lax.all_to_all(chunks, 'pair', 0, 0, tiled=True)  22.7 us
    all_to_all x1, blocking collectives, reduce_all(): return lax.all_to_all(send, ('pair', 'tile'), 0, 0, tiled=True)  20.8 us
    ppermute x5, starting transfers between devices, from_prev(): return lax.ppermute(cells, axis, [(i, i + 1) for i in range(count - 1)])  18.1 us
    pallas_call x4, Pallas kernels, call(): pl.pallas_call(kernel, out_shape=[jax.ShapeDtypeStruct(s, jnp.float32) fo...  12.9 us
    concatenate x1, local copies, waits for them, and re-layouts, body(): jnp.concatenate([p.astype(jnp.bfloat16) for p in (high, middle, low)], ax...  11.5 us
    ppermute x5, starting transfers between devices, from_next(): return lax.ppermute(cells, axis, [(i + 1, i) for i in range(count - 1)])  9.8 us
    dot_general x1, matrix products, body(): jnp.einsum('kt,kc->tc', network, parts, preferred_element_type=jnp.float32)  6.37 us
  transfers between devices with their start and end apart: 12, of which 8 were waited for; matrix products, arithmetic and copies ran while one was open for 3% of the time, Pallas kernels for 0%

profile of v7, /device:TPU:1, one launch (start us, length us, event | category | flops | bytes accessed | tf_op | source)
XLA Modules:
  0.0 155.7 jit_solution(17653699588378965241)
XLA Ops:
  0.6 0.8 slice_convert_fusion.1
  1.4 2.4 %copy.14 = f32[250,1,1024]{0,2,1:T(8,128)S(1)} copy(f32[250,1,1024]{2,1,0:T(1,128)} %param.4) | data formatting | bytes 2048000 | tf_op args[0]
  3.9 0.5 copy-done.15
  4.6 22.7 %all_to_all.38 = f32[8,250,136]{1,2,0:T(8,128)S(1)} all-to-all(f32[8,250,136]{1,2,0:T(8,128)S(1)} %pad_maximum_fusion.1), channel_id=1, replica_groups=mesh['pair'=8,'tile'=16] {'pair'}, dimensions={0} | all-to-all | bytes 2176000 | tf_op jit(solution)/shard_map/all_to_all | solution.py:199
  27.2 0.4 copy.15
  27.6 0.5 reshape.13
  28.1 0.1 slice_multiply_fusion
  28.3 1.8 %copy.16 = f32[2000,130]{1,0:T(8,128)} copy(f32[2000,130]{0,1:T(8,128)S(1)} %slice_multiply_fusion) | data formatting | bytes 2080000 | tf_op jit(solution)/shard_map/mul | solution.py:209
  30.1 0.9 convert_multiply_fusion
  30.9 0.7 copy-done
  31.6 3.9 %fusion = (bf16[2000,530]{1,0:T(8,128)(2,1)S(1)}, bf16[2000,530]{1,0:T(8,128)(2,1)}, bf16[2000,530]{1,0:T(8,128)(2,1)}) fusion(f32[2000,400]{1,0:T(8,128)S(1)} %convert_multiply_fusion, f32[2000,130]{1,0:T(8,128)S(1)} %copy-done), kind=kLoop, calls=%fused_computation.4 | loop fusion | flops 8480000 | bytes 10600000 | tf_op jit(solution)/shard_map/convert_element_type | solution.py:214
  35.6 11.5 %concatenate.11 = bf16[2000,1590]{1,0:T(8,128)(2,1)} concatenate(bf16[2000,530]{1,0:T(8,128)(2,1)} %get-tuple-element.42, bf16[2000,530]{1,0:T(8,128)(2,1)} %get-tuple-element.41, bf16[2000,530]{1,0:T(8,128)(2,1)S(1)} %get-tuple-element.40), dimensions={1} | concatenate | bytes 12720000 | tf_op jit(solution)/shard_map/concatenate | solution.py:214
  47.1 6.4 %fusion.1 = f32[400,1590]{1,0:T(8,128)S(1)} fusion(bf16[2000,1590]{1,0:T(8,128)(2,1)} %concatenate.11, f32[2000]{0:T(1024)S(1)} %bitcast.77, f32[2000]{0:T(1024)S(1)} %bitcast.75), kind=kOutput, calls=%fused_computation.10 | convolution fusion | flops 2548800000 | bytes 8920000 | tf_op jit(solution)/shard_map/kt,kc->tc/dot_general | solution.py:215
  53.5 0.6 slice_add_fusion
  54.1 0.1 slice.124.r_ref.p_ref
  54.2 1.3 collective-permute-start.1
  55.5 4.0 %collective-permute-start = (f32[400,128]{1,0:T(8,128)S(1)}, f32[400,128]{1,0:T(8,128)S(1)}, u32[]{:S(2)}, u32[]{:S(2)}) collective-permute-start(f32[400,128]{1,0:T(8,128)S(1)} %slice.124.r_ref.p_ref), channel_id=1, source_target_pairs={{0,1},{1,2},{2,3},{3,4},{4,5},{5,6},{6,7},{7,8},{8,9},{9,10},{10,1... | collective-permute-start | bytes 614408 | tf_op jit(solution)/shard_map/ppermute | solution.py:31
  59.5 1.2 slice_add_fusion.2.k_ref
  60.7 0.8 fusion.15
  61.5 0.4 collective-permute-done.1.rd_ref
  62.0 0.9 collective-permute-done.ru_ref
  62.8 0.7 copy-done.3
  63.5 3.1 %shard_map.59 = (f32[400,128]{1,0:T(8,128)}, f32[128,128]{1,0:T(8,128)}) custom-call(f32[400,400]{1,0:T(8,128)} %slice_add_fusion.2.k_ref, f32[400,128]{1,0:T(8,128)} %copy-done.1, f32[400,128]{1,0:T(8,128)} %copy-done.3, f32[400,128]{1,0:T(8,128)} %copy-done.2, f32[400,1]{1,0:T(8,128)} %get-tuple-element.47.rl_ref, f32[400,1]{1,0:T(8,128)} %get-tuple-element.46.rr_ref), custom_call_target="tpu_custom_call" | custom-call | tf_op jit(solution)/shard_map/pallas_call | solution.py:168
  66.6 1.3 collective-permute-start.3
  67.9 4.7 %collective-permute-start.2 = (f32[400,128]{1,0:T(8,128)}, f32[400,128]{1,0:T(8,128)S(1)}, u32[]{:S(2)}, u32[]{:S(2)}) collective-permute-start(f32[400,128]{1,0:T(8,128)} %get-tuple-element.19.w_ref.q_ref), channel_id=1, source_target_pairs={{0,1},{1,2},{2,3},{3,4},{4,5},{5,6},{6,7},{7,8},{8,9},{9,10},{10,1... | collective-permute-start | bytes 614408 | tf_op jit(solution)/shard_map/ppermute | solution.py:31
  72.6 13.3 %all-to-all-start.1 = ((f32[128,1,128]{2,1,0:T(1,128)}), f32[128,1,128]{2,1,0:T(1,128)S(1)}, u32[]{:S(2)}, u32[]{:S(2)}) async-start(f32[128,1,128]{2,1,0:T(1,128)} %bitcast.72), calls=%async_computation.1 | async-start | bytes 131072 | tf_op jit(solution)/shard_map/all_to_all | solution.py:177
  85.9 1.1 fusion.17
  87.1 3.0 %collective-permute-start.5 = (f32[400,1]{1,0:T(8,128)S(1)}, f32[400,1]{1,0:T(8,128)S(1)}, u32[]{:S(2)}, u32[]{:S(2)}) collective-permute-start(f32[400,1]{1,0:T(8,128)S(1)} %get-tuple-element.50), channel_id=1, source_target_pairs={{16,0},{32,16},{48,32},{64,48},{80,64},{96,80},{112,96},{17,1},{33... | collective-permute-start | bytes 4808 | tf_op jit(solution)/shard_map/ppermute | solution.py:36
  90.1 2.8 %collective-permute-start.4 = (f32[400,1]{1,0:T(8,128)S(1)}, f32[400,1]{1,0:T(8,128)S(1)}, u32[]{:S(2)}, u32[]{:S(2)}) collective-permute-start(f32[400,1]{1,0:T(8,128)S(1)} %get-tuple-element.51), channel_id=1, source_target_pairs={{0,16},{16,32},{32,48},{48,64},{64,80},{80,96},{96,112},{1,17},{17... | collective-permute-start | bytes 4808 | tf_op jit(solution)/shard_map/ppermute | solution.py:31
  92.9 1.8 %collective-permute-done.5.wr_ref.qr_ref = f32[400,1]{1,0:T(8,128)S(1)} collective-permute-done((f32[400,1]{1,0:T(8,128)S(1)}, f32[400,1]{1,0:T(8,128)S(1)}, u32[]{:S(2)}, u32[]{:S(2)}) %collective-permute-start.5) | collective-permute-done | bytes 1632 | tf_op jit(solution)/shard_map/ppermute | solution.py:36
  94.7 0.7 collective-permute-done.4.wl_ref.ql_ref
  95.4 0.1 all-to-all-done.1
  95.5 0.5 copy-done.8
  96.1 0.1 copy-done.5
  96.3 3.5 %shard_map.60 = (f32[400,128]{1,0:T(8,128)}, f32[400,128]{1,0:T(8,128)}, f32[400,128]{1,0:T(8,128)}, f32[128,128]{1,0:T(8,128)}, f32[1,128]{1,0:T(1,128)}) custom-call(f32[128,128]{1,0:T(8,128)} %bitcast.67, f32[400,400]{1,0:T(8,128)} %slice_add_fusion.2.k_ref, f32[400,128]{1,0:T(8,128)} %copy-done.1, f32[400,128]{1,0:T(8,128)} %copy-done.3, ...), custom_call_target="tpu_custom_call" | custom-call | tf_op jit(solution)/shard_map/pallas_call | solution.py:168
  99.8 1.3 collective-permute-start.7
  101.1 4.0 %collective-permute-start.6 = (f32[400,128]{1,0:T(8,128)}, f32[400,128]{1,0:T(8,128)S(1)}, u32[]{:S(2)}, u32[]{:S(2)}) collective-permute-start(f32[400,128]{1,0:T(8,128)} %get-tuple-element.24.w_ref), channel_id=1, source_target_pairs={{0,1},{1,2},{2,3},{3,4},{4,5},{5,6},{6,7},{7,8},{8,9},{9,10},{10,1... | collective-permute-start | bytes 614408 | tf_op jit(solution)/shard_map/ppermute | solution.py:31
  105.1 13.1 %all-to-all-start.2 = ((f32[128,1,128]{2,1,0:T(1,128)}), f32[128,1,128]{2,1,0:T(1,128)S(1)}, u32[]{:S(2)}, u32[]{:S(2)}) async-start(f32[128,1,128]{2,1,0:T(1,128)} %bitcast.71), calls=%async_computation.2 | async-start | bytes 131072 | tf_op jit(solution)/shard_map/all_to_all | solution.py:177
  118.2 1.1 fusion.16
  119.3 3.0 %collective-permute-start.9 = (f32[400,1]{1,0:T(8,128)S(1)}, f32[400,1]{1,0:T(8,128)S(1)}, u32[]{:S(2)}, u32[]{:S(2)}) collective-permute-start(f32[400,1]{1,0:T(8,128)S(1)} %get-tuple-element.48), channel_id=1, source_target_pairs={{16,0},{32,16},{48,32},{64,48},{80,64},{96,80},{112,96},{17,1},{33... | collective-permute-start | bytes 4808 | tf_op jit(solution)/shard_map/ppermute | solution.py:36
  122.3 2.6 %collective-permute-start.8 = (f32[400,1]{1,0:T(8,128)S(1)}, f32[400,1]{1,0:T(8,128)S(1)}, u32[]{:S(2)}, u32[]{:S(2)}) collective-permute-start(f32[400,1]{1,0:T(8,128)S(1)} %get-tuple-element.49), channel_id=1, source_target_pairs={{0,16},{16,32},{32,48},{48,64},{64,80},{80,96},{96,112},{1,17},{17... | collective-permute-start | bytes 4808 | tf_op jit(solution)/shard_map/ppermute | solution.py:31
  124.9 2.0 %collective-permute-done.9.wr_ref = f32[400,1]{1,0:T(8,128)S(1)} collective-permute-done((f32[400,1]{1,0:T(8,128)S(1)}, f32[400,1]{1,0:T(8,128)S(1)}, u32[]{:S(2)}, u32[]{:S(2)}) %collective-permute-start.9) | collective-permute-done | bytes 1632 | tf_op jit(solution)/shard_map/ppermute | solution.py:36
  127.0 0.7 collective-permute-done.8.wl_ref
  127.6 0.1 all-to-all-done.2
  127.8 0.5 copy-done.14
  128.5 4.1 %shard_map.61 = (f32[400,128]{1,0:T(8,128)}, f32[400,128]{1,0:T(8,128)}, f32[400,128]{1,0:T(8,128)}, f32[400,128]{1,0:T(8,128)}, f32[400,128]{1,0:T(8,128)}, /*index=5*/f32[128,128]{1,0:T(8,128)}, f32[1,128]{1,0:T(1,128)}) custom-call(f32[128,128]{1,0:T(8,128)} %bitcast.66, f32[1,128]{1,0:T(1,128)} %get-tuple-element.21.scal_ref, ...), custom_call_target="tpu_custom_call" | custom-call | tf_op jit(solution)/shard_map/pallas_call | solution.py:168
  132.7 20.8 %all_to_all.39 = f32[128,1,128]{2,1,0:T(1,128)} all-to-all(f32[128,1,128]{2,1,0:T(1,128)} %bitcast.73), channel_id=1, replica_groups=mesh['pair'=8,'tile'=16] {'pair','tile'}, dimensions={0} | all-to-all | bytes 131072 | tf_op jit(solution)/shard_map/all_to_all | solution.py:177
  153.4 2.2 %shard_map.62 = (f32[400,128]{1,0:T(8,128)}, f32[400,128]{1,0:T(8,128)}) custom-call(f32[128,128]{1,0:T(8,128)} %bitcast.68, f32[1,128]{1,0:T(1,128)} %get-tuple-element.26.scal_ref, f32[400,128]{1,0:T(8,128)} %get-tuple-element.27.r_ref, f32[400,128]{1,0:T(8,128)} %get-tuple-element.28.p_ref, f32[400,128]{1,0:T(8,128)} %get-tuple-element.29.q_ref, ...), custom_call_target="tpu_custom_call" | custom-call | tf_op jit(solution)/shard_map/pallas_call | solution.py:168
  (42 shorter events, 0.7 us)
Async XLA Ops:
  3.8 0.7 copy-start.15
  30.1 1.6 %copy-start = (f32[2000,130]{1,0:T(8,128)S(1)}, f32[2000,130]{1,0:T(8,128)}, u32[]{:S(2)}) copy-start(f32[2000,130]{1,0:T(8,128)} %copy.16) | copy-start | bytes 3120004
  53.5 6.0 %copy-start.4 = (f32[400,400]{1,0:T(8,128)S(1)}, f32[400,400]{1,0:T(8,128)}, u32[]{:S(2)}) copy-start(f32[400,400]{1,0:T(8,128)} %constant.5.clone) | copy-start | bytes 1920004
  54.2 8.6 %copy-start.1 = (f32[400,128]{1,0:T(8,128)}, f32[400,128]{1,0:T(8,128)S(1)}, u32[]{:S(2)}) copy-start(f32[400,128]{1,0:T(8,128)S(1)} %slice.124.r_ref.p_ref) | copy-start | bytes 614404
  54.2 7.8 %collective-permute-start.1 = (f32[400,128]{1,0:T(8,128)S(1)}, f32[400,128]{1,0:T(8,128)S(1)}, u32[]{:S(2)}, u32[]{:S(2)}) collective-permute-start(f32[400,128]{1,0:T(8,128)S(1)} %slice.124.r_ref.p_ref), channel_id=1, source_target_pairs={{1,0},{2,1},{3,2},{4,3},{5,4},{6,5},{7,6},{8,7},{9,8},{10,9},{11,1... | collective-permute-start | bytes 614408 | tf_op jit(solution)/shard_map/ppermute | solution.py:36
  55.5 7.3 %collective-permute-start = (f32[400,128]{1,0:T(8,128)S(1)}, f32[400,128]{1,0:T(8,128)S(1)}, u32[]{:S(2)}, u32[]{:S(2)}) collective-permute-start(f32[400,128]{1,0:T(8,128)S(1)} %slice.124.r_ref.p_ref), channel_id=1, source_target_pairs={{0,1},{1,2},{2,3},{3,4},{4,5},{5,6},{6,7},{7,8},{8,9},{9,10},{10,1... | collective-permute-start | bytes 614408 | tf_op jit(solution)/shard_map/ppermute | solution.py:31
  62.0 0.9 copy-start.2
  62.8 0.7 copy-start.3
  66.6 28.9 %collective-permute-start.3 = (f32[400,128]{1,0:T(8,128)}, f32[400,128]{1,0:T(8,128)S(1)}, u32[]{:S(2)}, u32[]{:S(2)}) collective-permute-start(f32[400,128]{1,0:T(8,128)} %get-tuple-element.19.w_ref.q_ref), channel_id=1, source_target_pairs={{1,0},{2,1},{3,2},{4,3},{5,4},{6,5},{7,6},{8,7},{9,8},{10,9},{11,1... | collective-permute-start | bytes 614408 | tf_op jit(solution)/shard_map/ppermute | solution.py:36
  67.9 27.6 %collective-permute-start.2 = (f32[400,128]{1,0:T(8,128)}, f32[400,128]{1,0:T(8,128)S(1)}, u32[]{:S(2)}, u32[]{:S(2)}) collective-permute-start(f32[400,128]{1,0:T(8,128)} %get-tuple-element.19.w_ref.q_ref), channel_id=1, source_target_pairs={{0,1},{1,2},{2,3},{3,4},{4,5},{5,6},{6,7},{7,8},{8,9},{9,10},{10,1... | collective-permute-start | bytes 614408 | tf_op jit(solution)/shard_map/ppermute | solution.py:31
  72.6 22.9 %all-to-all-start.1 = ((f32[128,1,128]{2,1,0:T(1,128)}), f32[128,1,128]{2,1,0:T(1,128)S(1)}, u32[]{:S(2)}, u32[]{:S(2)}) async-start(f32[128,1,128]{2,1,0:T(1,128)} %bitcast.72), calls=%async_computation.1 | async-start | bytes 131072 | tf_op jit(solution)/shard_map/all_to_all | solution.py:177
  87.1 7.6 %collective-permute-start.5 = (f32[400,1]{1,0:T(8,128)S(1)}, f32[400,1]{1,0:T(8,128)S(1)}, u32[]{:S(2)}, u32[]{:S(2)}) collective-permute-start(f32[400,1]{1,0:T(8,128)S(1)} %get-tuple-element.50), channel_id=1, source_target_pairs={{16,0},{32,16},{48,32},{64,48},{80,64},{96,80},{112,96},{17,1},{33... | collective-permute-start | bytes 4808 | tf_op jit(solution)/shard_map/ppermute | solution.py:36
  90.1 5.3 %collective-permute-start.4 = (f32[400,1]{1,0:T(8,128)S(1)}, f32[400,1]{1,0:T(8,128)S(1)}, u32[]{:S(2)}, u32[]{:S(2)}) collective-permute-start(f32[400,1]{1,0:T(8,128)S(1)} %get-tuple-element.51), channel_id=1, source_target_pairs={{0,16},{16,32},{32,48},{48,64},{64,80},{80,96},{96,112},{1,17},{17... | collective-permute-start | bytes 4808 | tf_op jit(solution)/shard_map/ppermute | solution.py:31
  94.7 0.8 copy-start.7
  95.4 0.7 copy-start.8
  95.5 0.6 copy-start.10
  95.5 0.7 copy-start.5
  95.5 0.8 copy-start.6
  99.8 28.0 %collective-permute-start.7 = (f32[400,128]{1,0:T(8,128)}, f32[400,128]{1,0:T(8,128)S(1)}, u32[]{:S(2)}, u32[]{:S(2)}) collective-permute-start(f32[400,128]{1,0:T(8,128)} %get-tuple-element.24.w_ref), channel_id=1, source_target_pairs={{1,0},{2,1},{3,2},{4,3},{5,4},{6,5},{7,6},{8,7},{9,8},{10,9},{11,1... | collective-permute-start | bytes 614408 | tf_op jit(solution)/shard_map/ppermute | solution.py:36
  101.1 26.7 %collective-permute-start.6 = (f32[400,128]{1,0:T(8,128)}, f32[400,128]{1,0:T(8,128)S(1)}, u32[]{:S(2)}, u32[]{:S(2)}) collective-permute-start(f32[400,128]{1,0:T(8,128)} %get-tuple-element.24.w_ref), channel_id=1, source_target_pairs={{0,1},{1,2},{2,3},{3,4},{4,5},{5,6},{6,7},{7,8},{8,9},{9,10},{10,1... | collective-permute-start | bytes 614408 | tf_op jit(solution)/shard_map/ppermute | solution.py:31
  105.1 22.7 %all-to-all-start.2 = ((f32[128,1,128]{2,1,0:T(1,128)}), f32[128,1,128]{2,1,0:T(1,128)S(1)}, u32[]{:S(2)}, u32[]{:S(2)}) async-start(f32[128,1,128]{2,1,0:T(1,128)} %bitcast.71), calls=%async_computation.2 | async-start | bytes 131072 | tf_op jit(solution)/shard_map/all_to_all | solution.py:177
  119.3 7.6 %collective-permute-start.9 = (f32[400,1]{1,0:T(8,128)S(1)}, f32[400,1]{1,0:T(8,128)S(1)}, u32[]{:S(2)}, u32[]{:S(2)}) collective-permute-start(f32[400,1]{1,0:T(8,128)S(1)} %get-tuple-element.48), channel_id=1, source_target_pairs={{16,0},{32,16},{48,32},{64,48},{80,64},{96,80},{112,96},{17,1},{33... | collective-permute-start | bytes 4808 | tf_op jit(solution)/shard_map/ppermute | solution.py:36
  122.3 5.3 %collective-permute-start.8 = (f32[400,1]{1,0:T(8,128)S(1)}, f32[400,1]{1,0:T(8,128)S(1)}, u32[]{:S(2)}, u32[]{:S(2)}) collective-permute-start(f32[400,1]{1,0:T(8,128)S(1)} %get-tuple-element.49), channel_id=1, source_target_pairs={{0,16},{16,32},{32,48},{48,64},{64,80},{80,96},{96,112},{1,17},{17... | collective-permute-start | bytes 4808 | tf_op jit(solution)/shard_map/ppermute | solution.py:31
  127.0 0.8 copy-start.13
  127.6 0.7 copy-start.14
  127.8 0.6 copy-start.9
  127.8 0.7 copy-start.11
  127.8 0.8 copy-start.12

commit v8 on v6

--- a/solution.py
+++ b/solution.py
@@ -107,29 +107,48 @@
     send_ref[...] = jnp.broadcast_to(row, send_ref.shape)
 
 
-def first_kernel(k_ref, r_ref, ru_ref, rd_ref, rl_ref, rr_ref, w_ref, send_ref):
+def image_kernel(k_ref, v_ref, vu_ref, vd_ref, vl_ref, vr_ref, w_out):
+    w_out[...] = operate(k_ref[...], v_ref[...], vu_ref[...], vd_ref[...], vl_ref[...], vr_ref[...])
+
+
+def gram_kernel(k_ref, r_ref, w_ref, wu_ref, wd_ref, wl_ref, wr_ref, z_out, send_ref):
     r = r_ref[...]
-    w = operate(k_ref[...], r, ru_ref[...], rd_ref[...], rl_ref[...], rr_ref[...])
-    w_ref[...] = w
-    send_buffer(send_ref, [r * r, r * w])
-
-
-def second_kernel(got_ref, k_ref, r_ref, ru_ref, rd_ref, rl_ref, rr_ref, w_ref, wu_ref, wd_ref, wl_ref, wr_ref,
-                  r_out, x_out, w_out, send_ref, scal_ref):
+    w = w_ref[...]
+    z = operate(k_ref[...], w, wu_ref[...], wd_ref[...], wl_ref[...], wr_ref[...])
+    z_out[...] = z
+    send_buffer(send_ref, [r * r, r * w, w * w, r * z, w * z])
+
+
+def block_kernel(got_ref, k_ref, r_ref, w_ref, z_ref, ru_ref, rd_ref, rl_ref, rr_ref, wu_ref, wd_ref, wl_ref, wr_ref,
+                 zu_ref, zd_ref, zl_ref, zr_ref, r_out, p_out, q_out, x_out, w_out, send_ref, scal_out):
     sums = jnp.sum(got_ref[...], axis=0, keepdims=True)
-    norm = lane_value(sums, 0)
-    alpha = norm / lane_value(sums, 1)
-    p = r_ref[...]
-    q = w_ref[...]
-    x_out[...] = alpha * p
-    r = p - alpha * q
+    norm_first = lane_value(sums, 0)
+    curvature_first = lane_value(sums, 1)
+    alpha_first = norm_first / curvature_first
+    norm = norm_first - 2.0 * alpha_first * curvature_first + alpha_first * alpha_first * lane_value(sums, 2)
+    beta = norm / norm_first
+    a = 1.0 + beta
+    b = -alpha_first
+    curvature = a * a * curvature_first + a * b * (lane_value(sums, 3) + lane_value(sums, 2)) + b * b * lane_value(sums, 4)
+    alpha = norm / curvature
+    r0 = r_ref[...]
+    w0 = w_ref[...]
+    z0 = z_ref[...]
+    p = a * r0 + b * w0
+    q = a * w0 + b * z0
+    p_out[...] = p
+    q_out[...] = q
+    x_out[...] = alpha_first * r0 + alpha * p
+    r = (r0 - alpha_first * w0) - alpha * q
     r_out[...] = r
-    halo = [h[...] - alpha * g[...] for h, g in zip((ru_ref, rd_ref, rl_ref, rr_ref), (wu_ref, wd_ref, wl_ref, wr_ref))]
+    halo = []
+    for hr, hw, hz in zip((ru_ref, rd_ref, rl_ref, rr_ref), (wu_ref, wd_ref, wl_ref, wr_ref), (zu_ref, zd_ref, zl_ref, zr_ref)):
+        halo.append((hr[...] - alpha_first * hw[...]) - alpha * (a * hw[...] + b * hz[...]))
     w = operate(k_ref[...], r, *halo)
     w_out[...] = w
     send_buffer(send_ref, [r * r, r * w, r * q, p * w, p * q])
-    lanes = lax.broadcasted_iota(jnp.int32, scal_ref.shape, 1)
-    scal_ref[...] = jnp.where(lanes == 0, norm, jnp.where(lanes == 1, alpha, 0.0))
+    lanes = lax.broadcasted_iota(jnp.int32, scal_out.shape, 1)
+    scal_out[...] = jnp.where(lanes == 0, norm, 0.0)
 
 
 def step_scalars(got_ref, scal_ref):
@@ -139,28 +158,6 @@
     beta = norm / lane_value(previous, 0)
     curvature = lane_value(sums, 1) + beta * (lane_value(sums, 2) + lane_value(sums, 3)) + beta * beta * lane_value(sums, 4)
     return norm, beta, norm / curvature
-
-
-def third_kernel(got_ref, scal_ref, k_ref, r_ref, p_ref, q_ref, x_ref, w_ref,
-                 ru_ref, rd_ref, rl_ref, rr_ref, qu_ref, qd_ref, ql_ref, qr_ref, wu_ref, wd_ref, wl_ref, wr_ref,
-                 r_out, p_out, q_out, x_out, w_out, send_ref, scal_out):
-    norm, beta, alpha = step_scalars(got_ref, scal_ref)
-    alpha_first = lane_value(scal_ref[...], 1)
-    p = r_ref[...] + beta * p_ref[...]
-    q = w_ref[...] + beta * q_ref[...]
-    p_out[...] = p
-    q_out[...] = q
-    x_out[...] = x_ref[...] + alpha * p
-    r = r_ref[...] - alpha * q
-    r_out[...] = r
-    halo = []
-    for h, k, g in zip((ru_ref, rd_ref, rl_ref, rr_ref), (qu_ref, qd_ref, ql_ref, qr_ref), (wu_ref, wd_ref, wl_ref, wr_ref)):
-        halo.append((h[...] - alpha_first * k[...]) - alpha * (g[...] + beta * k[...]))
-    w = operate(k_ref[...], r, *halo)
-    w_out[...] = w
-    send_buffer(send_ref, [r * r, r * w, r * q, p * w, p * q])
-    lanes = lax.broadcasted_iota(jnp.int32, scal_out.shape, 1)
-    scal_out[...] = jnp.where(lanes == 0, norm, jnp.where(lanes == 1, alpha, 0.0))
 
 
 def last_kernel(got_ref, scal_ref, r_ref, p_ref, q_ref, x_ref, w_ref, x_out, r_out):
@@ -239,18 +236,15 @@
     field = residual.shape
     lanes = 128
     send_shape = (count, lanes)
-    w0, send = call(first_kernel, [field, send_shape], matrix, residual, *residual_halo)
+    (w0,) = call(image_kernel, [field], matrix, residual, *residual_halo)
     w0_halo = exchange_rows_cols(w0)
+    z0, send = call(gram_kernel, [field, send_shape], matrix, residual, w0, *w0_halo)
     got = reduce_all(send)
-    r1, x1, w1, send, scal = call(
-        second_kernel, [field, field, field, send_shape, (1, lanes)], got, matrix, residual, *residual_halo, w0, *w0_halo
-    )
-    w1_halo = exchange_rows_cols(w1)
-    got = reduce_all(send)
+    z0_halo = exchange_rows_cols(z0)
     r2, p1, q1, x2, w2, send, scal = call(
-        third_kernel,
+        block_kernel,
         [field, field, field, field, field, send_shape, (1, lanes)],
-        got, scal, matrix, r1, residual, w0, x1, w1, *residual_halo, *w0_halo, *w1_halo,
+        got, matrix, residual, w0, z0, *residual_halo, *w0_halo, *z0_halo,
     )
     got = reduce_all(send)
     solution_field, residual = call(last_kernel, [field, field], got, scal, r2, p1, q1, x2, w2)

time: 134 us -> 125 us (0.933)
  starting transfers between devices: 53.2 us -> 43.5 us
    all_to_all x2 -> x1, starting transfers between devices: 26 us -> 16 us  [reduce_all(): return lax.all_to_all(send, ('pair', 'tile'), 0, 0, tiled=True)]
    unnamed x38 -> x36, local copies, waits for them, and re-layouts: 5.31 us -> 5.98 us
  transfers between devices with their start and end apart: 12 -> 11, of which waited for: 6 -> 5; matrix products, arithmetic and copies ran while one was open for 6% -> 6% of each run, Pallas kernels for 0% -> 0%
where the time goes in v8:
time: 125 us; the launch traced here: 124 us
  starting transfers between devices  43.5 us (35%)
  blocking collectives  43.4 us (35%)
  Pallas kernels  12.4 us (10%)
  local copies, waits for them, and re-layouts  10.1 us (8%)
  waiting for transfers between devices  5.51 us (4%)
  other arithmetic  4.27 us (3%)
  matrix products  3.77 us (3%)
    all_to_all x1, blocking collectives, body(): lax.all_to_all(chunks, 'pair', 0, 0, tiled=True)  22.7 us
    all_to_all x1, blocking collectives, reduce_all(): return lax.all_to_all(send, ('pair', 'tile'), 0, 0, tiled=True)  20.7 us
    ppermute x5, starting transfers between devices, from_prev(): return lax.ppermute(cells, axis, [(i, i + 1) for i in range(count - 1)])  16.7 us
    all_to_all x1, starting transfers between devices, reduce_all(): return lax.all_to_all(send, ('pair', 'tile'), 0, 0, tiled=True)  16 us
    pallas_call x4, Pallas kernels, call(): pl.pallas_call(kernel, out_shape=[jax.ShapeDtypeStruct(s, jnp.float32) fo...  12.4 us
    ppermute x5, starting transfers between devices, from_next(): return lax.ppermute(cells, axis, [(i + 1, i) for i in range(count - 1)])  10.7 us
    unnamed x36, local copies, waits for them, and re-layouts  5.98 us
    ppermute x5, waiting for transfers between devices, from_next(): return lax.ppermute(cells, axis, [(i + 1, i) for i in range(count - 1)])  3.51 us
  transfers between devices with their start and end apart: 11, of which 5 were waited for; matrix products, arithmetic and copies ran while one was open for 6% of the time, Pallas kernels for 0%

profile of v8, /device:TPU:1, one launch (start us, length us, event | category | flops | bytes accessed | tf_op | source)
XLA Modules:
  0.0 123.8 jit_solution(2959888715502215740)
XLA Ops:
  0.6 0.8 slice_convert_fusion.1
  1.4 2.4 %copy.19 = f32[250,1,1024]{0,2,1:T(8,128)S(1)} copy(f32[250,1,1024]{2,1,0:T(1,128)} %param.4) | data formatting | bytes 2048000 | tf_op args[0]
  3.9 0.6 copy-done.13
  4.5 0.1 pad_maximum_fusion
  4.6 22.7 %all_to_all.27 = f32[8,250,136]{1,2,0:T(8,128)S(1)} all-to-all(f32[8,250,136]{1,2,0:T(8,128)S(1)} %pad_maximum_fusion), channel_id=1, replica_groups=mesh['pair'=8,'tile'=16] {'pair'}, dimensions={0} | all-to-all | bytes 2176000 | tf_op jit(solution)/shard_map/all_to_all | solution.py:204
  27.3 0.4 copy.20
  27.7 0.5 reshape.15
  28.2 0.3 reduce-precision_convert_fusion.1
  28.5 1.9 %fusion.1 = f32[400,390]{1,0:T(8,128)S(1)} fusion(f32[2000]{0:T(1024)S(1)} %bitcast.92, f32[2000]{0:T(1024)S(1)} %bitcast.90, bf16[2000,130]{0,1:T(8,128)(2,1)S(1)} %get-tuple-element.31, bf16[2000,130]{0,1:T(8,128)(2,1)S(1)} %get-tuple-element.32, bf16[2000,130]{0,1:T(8,128)(2,1)S(1)} %get-tuple-element.30), kind=kOutput, calls=%fused_computation.4 | convolution fusion | flops 633480000 | bytes 2200000 | tf_op jit(solution)/shard_map/kt,kc->tc/dot_general | solution.py:220
  30.4 0.3 slice_add_fusion
  30.7 0.1 slice.150.v_ref.r_ref
  30.9 0.0 copy-start.1
  30.9 1.4 %collective-permute-start.1 = (f32[400,128]{1,0:T(8,128)S(1)}, f32[400,128]{1,0:T(8,128)S(1)}, u32[]{:S(2)}, u32[]{:S(2)}) collective-permute-start(f32[400,128]{1,0:T(8,128)S(1)} %slice.150.v_ref.r_ref), channel_id=1, source_target_pairs={{1,0},{2,1},{3,2},{4,3},{5,4},{6,5},{7,6},{8,7},{9,8},{10,9},{11,1... | collective-permute-start | bytes 614408 | tf_op jit(solution)/shard_map/ppermute | solution.py:36
  32.3 4.0 %collective-permute-start = (f32[400,128]{1,0:T(8,128)S(1)}, f32[400,128]{1,0:T(8,128)S(1)}, u32[]{:S(2)}, u32[]{:S(2)}) collective-permute-start(f32[400,128]{1,0:T(8,128)S(1)} %slice.150.v_ref.r_ref), channel_id=1, source_target_pairs={{0,1},{1,2},{2,3},{3,4},{4,5},{5,6},{6,7},{7,8},{8,9},{9,10},{10,1... | collective-permute-start | bytes 614408 | tf_op jit(solution)/shard_map/ppermute | solution.py:31
  36.3 1.9 %fusion = f32[400,8]{0,1:T(8,128)S(1)} fusion(f32[2000]{0:T(1024)S(1)} %bitcast.91, f32[2000]{0:T(1024)S(1)} %bitcast.88, f32[2000]{0:T(1024)S(1)} %bitcast.89), kind=kOutput, calls=%fused_computation.3 | convolution fusion | flops 77632000 | bytes 36800 | tf_op jit(solution)/shard_map/kt,kd->td/dot_general | solution.py:226
  38.2 0.6 fusion.30
  38.8 2.2 %add_add_fusion.k_ref = f32[400,400]{1,0:T(8,128)} fusion(f32[400,400]{1,0:T(8,128)S(1)} %copy-done.1, f32[400]{0:T(512)S(1)} %negate_add_fusion, f32[400]{0:T(512)S(1)} %bitcast.76, f32[400]{0:T(512)S(1)} %bitcast.78, f32[400]{0:T(512)S(1)} %bitcast.80, f32[400]{0:T(512)S(1)} %bitcast.82, f32[400]{0:T(512)S(1)} %bitcast.84, f32[400]{0:T(512)S(1)} %bitcast.86, ...), kind=kLoop, calls=%fused_computation.24 | loop fusion | flops 7520000 | bytes 1292800 | tf_op jit(solution)/shard_map/add | solution.py:75
  41.0 0.8 fusion.44
  41.8 0.7 copy-done.2
  42.5 0.1 copy-done.3
  42.5 3.0 %shard_map.59.w_ref = f32[400,128]{1,0:T(8,128)} custom-call(f32[400,400]{1,0:T(8,128)} %add_add_fusion.k_ref, f32[400,128]{1,0:T(8,128)} %copy-done, f32[400,128]{1,0:T(8,128)} %copy-done.3, f32[400,128]{1,0:T(8,128)} %copy-done.2, f32[400,1]{1,0:T(8,128)} %get-tuple-element.38.vl_ref.rl_ref, f32[400,1]{1,0:T(8,128)} %get-tuple-element.37.vr_ref.rr_ref), custom_call_target="tpu_custom_call" | custom-call | tf_op jit(solution)/shard_map/pallas_call | solution.py:173
  45.6 1.3 %collective-permute-start.3 = (f32[400,128]{1,0:T(8,128)}, f32[400,128]{1,0:T(8,128)S(1)}, u32[]{:S(2)}, u32[]{:S(2)}) collective-permute-start(f32[400,128]{1,0:T(8,128)} %shard_map.59.w_ref), channel_id=1, source_target_pairs={{1,0},{2,1},{3,2},{4,3},{5,4},{6,5},{7,6},{8,7},{9,8},{10,9},{11,1... | collective-permute-start | bytes 614408 | tf_op jit(solution)/shard_map/ppermute | solution.py:36
  46.9 4.0 %collective-permute-start.2 = (f32[400,128]{1,0:T(8,128)}, f32[400,128]{1,0:T(8,128)S(1)}, u32[]{:S(2)}, u32[]{:S(2)}) collective-permute-start(f32[400,128]{1,0:T(8,128)} %shard_map.59.w_ref), channel_id=1, source_target_pairs={{0,1},{1,2},{2,3},{3,4},{4,5},{5,6},{6,7},{7,8},{8,9},{9,10},{10,1... | collective-permute-start | bytes 614408 | tf_op jit(solution)/shard_map/ppermute | solution.py:31
  50.9 1.1 fusion.46
  52.0 3.8 %collective-permute-start.5 = (f32[400,1]{1,0:T(8,128)S(1)}, f32[400,1]{1,0:T(8,128)S(1)}, u32[]{:S(2)}, u32[]{:S(2)}) collective-permute-start(f32[400,1]{1,0:T(8,128)S(1)} %get-tuple-element.41), channel_id=1, source_target_pairs={{16,0},{32,16},{48,32},{64,48},{80,64},{96,80},{112,96},{17,1},{33... | collective-permute-start | bytes 4808 | tf_op jit(solution)/shard_map/ppermute | solution.py:36
  55.8 2.1 %collective-permute-start.4 = (f32[400,1]{1,0:T(8,128)S(1)}, f32[400,1]{1,0:T(8,128)S(1)}, u32[]{:S(2)}, u32[]{:S(2)}) collective-permute-start(f32[400,1]{1,0:T(8,128)S(1)} %get-tuple-element.42), channel_id=1, source_target_pairs={{0,16},{16,32},{32,48},{48,64},{64,80},{80,96},{96,112},{1,17},{17... | collective-permute-start | bytes 4808 | tf_op jit(solution)/shard_map/ppermute | solution.py:31
  57.9 1.5 %collective-permute-done.5.wr_ref = f32[400,1]{1,0:T(8,128)S(1)} collective-permute-done((f32[400,1]{1,0:T(8,128)S(1)}, f32[400,1]{1,0:T(8,128)S(1)}, u32[]{:S(2)}, u32[]{:S(2)}) %collective-permute-start.5) | collective-permute-done | bytes 1632 | tf_op jit(solution)/shard_map/ppermute | solution.py:36
  59.4 1.2 collective-permute-done.4.wl_ref
  60.6 0.7 copy-done.7
  61.3 0.1 copy-done.4
  61.3 0.7 copy-done.5
  62.0 3.2 %shard_map.60 = (f32[400,128]{1,0:T(8,128)}, f32[128,128]{1,0:T(8,128)}) custom-call(f32[400,400]{1,0:T(8,128)} %add_add_fusion.k_ref, f32[400,128]{1,0:T(8,128)} %copy-done, f32[400,128]{1,0:T(8,128)} %shard_map.59.w_ref, f32[400,128]{1,0:T(8,128)} %copy-done.5, f32[400,128]{1,0:T(8,128)} %copy-done.4, f32[400,1]{1,0:T(8,128)} %copy-done.7, f32[400,1]{1,0:T(8,128)} %copy-done.6), custom_call_target="tpu_custom_call" | custom-call | tf_op jit(solution)/shard_map/pallas_call | solution.py:173
  65.2 1.3 %collective-permute-start.7 = (f32[400,128]{1,0:T(8,128)}, f32[400,128]{1,0:T(8,128)S(1)}, u32[]{:S(2)}, u32[]{:S(2)}) collective-permute-start(f32[400,128]{1,0:T(8,128)} %get-tuple-element.14.z_ref), channel_id=1, source_target_pairs={{1,0},{2,1},{3,2},{4,3},{5,4},{6,5},{7,6},{8,7},{9,8},{10,9},{11,1... | collective-permute-start | bytes 614408 | tf_op jit(solution)/shard_map/ppermute | solution.py:36
  66.5 4.0 %collective-permute-start.6 = (f32[400,128]{1,0:T(8,128)}, f32[400,128]{1,0:T(8,128)S(1)}, u32[]{:S(2)}, u32[]{:S(2)}) collective-permute-start(f32[400,128]{1,0:T(8,128)} %get-tuple-element.14.z_ref), channel_id=1, source_target_pairs={{0,1},{1,2},{2,3},{3,4},{4,5},{5,6},{6,7},{7,8},{8,9},{9,10},{10,1... | collective-permute-start | bytes 614408 | tf_op jit(solution)/shard_map/ppermute | solution.py:31
  70.5 16.0 %all-to-all-start.1 = ((f32[128,1,128]{2,1,0:T(1,128)}), f32[128,1,128]{2,1,0:T(1,128)S(1)}, u32[]{:S(2)}, u32[]{:S(2)}) async-start(f32[128,1,128]{2,1,0:T(1,128)} %bitcast.71), calls=%async_computation.1 | async-start | bytes 131072 | tf_op jit(solution)/shard_map/all_to_all | solution.py:182
  86.6 1.1 fusion.45
  87.7 3.0 %collective-permute-start.9 = (f32[400,1]{1,0:T(8,128)S(1)}, f32[400,1]{1,0:T(8,128)S(1)}, u32[]{:S(2)}, u32[]{:S(2)}) collective-permute-start(f32[400,1]{1,0:T(8,128)S(1)} %get-tuple-element.39), channel_id=1, source_target_pairs={{16,0},{32,16},{48,32},{64,48},{80,64},{96,80},{112,96},{17,1},{33... | collective-permute-start | bytes 4808 | tf_op jit(solution)/shard_map/ppermute | solution.py:36
  90.7 2.6 %collective-permute-start.8 = (f32[400,1]{1,0:T(8,128)S(1)}, f32[400,1]{1,0:T(8,128)S(1)}, u32[]{:S(2)}, u32[]{:S(2)}) collective-permute-start(f32[400,1]{1,0:T(8,128)S(1)} %get-tuple-element.40), channel_id=1, source_target_pairs={{0,16},{16,32},{32,48},{48,64},{64,80},{80,96},{96,112},{1,17},{17... | collective-permute-start | bytes 4808 | tf_op jit(solution)/shard_map/ppermute | solution.py:31
  93.3 2.0 %collective-permute-done.9.zr_ref = f32[400,1]{1,0:T(8,128)S(1)} collective-permute-done((f32[400,1]{1,0:T(8,128)S(1)}, f32[400,1]{1,0:T(8,128)S(1)}, u32[]{:S(2)}, u32[]{:S(2)}) %collective-permute-start.9) | collective-permute-done | bytes 1632 | tf_op jit(solution)/shard_map/ppermute | solution.py:36
  95.3 0.7 collective-permute-done.8.zl_ref
  96.0 0.1 all-to-all-done.1
  96.2 0.5 copy-done.12
  96.7 0.1 copy-done.8
  96.7 0.1 copy-done.9
  96.8 0.1 copy-done.10
  96.9 3.9 %shard_map.61 = (f32[400,128]{1,0:T(8,128)}, f32[400,128]{1,0:T(8,128)}, f32[400,128]{1,0:T(8,128)}, f32[400,128]{1,0:T(8,128)}, f32[400,128]{1,0:T(8,128)}, /*index=5*/f32[128,128]{1,0:T(8,128)}, f32[1,128]{1,0:T(1,128)}) custom-call(f32[128,128]{1,0:T(8,128)} %bitcast.69, f32[400,400]{1,0:T(8,128)} %add_add_fusion.k_ref, f32[400,128]{1,0:T(8,128)} %copy-done, ...), custom_call_target="tpu_custom_call" | custom-call | tf_op jit(solution)/shard_map/pallas_call | solution.py:173
  100.9 20.7 %all_to_all.28 = f32[128,1,128]{2,1,0:T(1,128)} all-to-all(f32[128,1,128]{2,1,0:T(1,128)} %bitcast.72), channel_id=1, replica_groups=mesh['pair'=8,'tile'=16] {'pair','tile'}, dimensions={0} | all-to-all | bytes 131072 | tf_op jit(solution)/shard_map/all_to_all | solution.py:182
  121.6 2.2 %shard_map.62 = (f32[400,128]{1,0:T(8,128)}, f32[400,128]{1,0:T(8,128)}) custom-call(f32[128,128]{1,0:T(8,128)} %bitcast.70, f32[1,128]{1,0:T(1,128)} %get-tuple-element.16.scal_ref, f32[400,128]{1,0:T(8,128)} %get-tuple-element.17.r_ref, f32[400,128]{1,0:T(8,128)} %get-tuple-element.18.p_ref, f32[400,128]{1,0:T(8,128)} %get-tuple-element.19.q_ref, ...), custom_call_target="tpu_custom_call" | custom-call | tf_op jit(solution)/shard_map/pallas_call | solution.py:173
  (36 shorter events, 0.2 us)
Async XLA Ops:
  3.8 0.7 copy-start.13
  30.8 10.1 %copy-start = (f32[400,128]{1,0:T(8,128)}, f32[400,128]{1,0:T(8,128)S(1)}, u32[]{:S(2)}) copy-start(f32[400,128]{1,0:T(8,128)S(1)} %slice.150.v_ref.r_ref) | copy-start | bytes 614404
  30.9 7.9 %copy-start.1 = (f32[400,400]{1,0:T(8,128)S(1)}, f32[400,400]{1,0:T(8,128)}, u32[]{:S(2)}) copy-start(f32[400,400]{1,0:T(8,128)} %constant.25.clone) | copy-start | bytes 1920004
  30.9 10.9 %collective-permute-start.1 = (f32[400,128]{1,0:T(8,128)S(1)}, f32[400,128]{1,0:T(8,128)S(1)}, u32[]{:S(2)}, u32[]{:S(2)}) collective-permute-start(f32[400,128]{1,0:T(8,128)S(1)} %slice.150.v_ref.r_ref), channel_id=1, source_target_pairs={{1,0},{2,1},{3,2},{4,3},{5,4},{6,5},{7,6},{8,7},{9,8},{10,9},{11,1... | collective-permute-start | bytes 614408 | tf_op jit(solution)/shard_map/ppermute | solution.py:36
  32.3 9.5 %collective-permute-start = (f32[400,128]{1,0:T(8,128)S(1)}, f32[400,128]{1,0:T(8,128)S(1)}, u32[]{:S(2)}, u32[]{:S(2)}) collective-permute-start(f32[400,128]{1,0:T(8,128)S(1)} %slice.150.v_ref.r_ref), channel_id=1, source_target_pairs={{0,1},{1,2},{2,3},{3,4},{4,5},{5,6},{6,7},{7,8},{8,9},{9,10},{10,1... | collective-permute-start | bytes 614408 | tf_op jit(solution)/shard_map/ppermute | solution.py:31
  41.8 0.7 copy-start.2
  41.8 0.7 copy-start.3
  45.6 15.0 %collective-permute-start.3 = (f32[400,128]{1,0:T(8,128)}, f32[400,128]{1,0:T(8,128)S(1)}, u32[]{:S(2)}, u32[]{:S(2)}) collective-permute-start(f32[400,128]{1,0:T(8,128)} %shard_map.59.w_ref), channel_id=1, source_target_pairs={{1,0},{2,1},{3,2},{4,3},{5,4},{6,5},{7,6},{8,7},{9,8},{10,9},{11,1... | collective-permute-start | bytes 614408 | tf_op jit(solution)/shard_map/ppermute | solution.py:36
  46.9 13.7 %collective-permute-start.2 = (f32[400,128]{1,0:T(8,128)}, f32[400,128]{1,0:T(8,128)S(1)}, u32[]{:S(2)}, u32[]{:S(2)}) collective-permute-start(f32[400,128]{1,0:T(8,128)} %shard_map.59.w_ref), channel_id=1, source_target_pairs={{0,1},{1,2},{2,3},{3,4},{4,5},{5,6},{6,7},{7,8},{8,9},{9,10},{10,1... | collective-permute-start | bytes 614408 | tf_op jit(solution)/shard_map/ppermute | solution.py:31
  52.0 7.4 %collective-permute-start.5 = (f32[400,1]{1,0:T(8,128)S(1)}, f32[400,1]{1,0:T(8,128)S(1)}, u32[]{:S(2)}, u32[]{:S(2)}) collective-permute-start(f32[400,1]{1,0:T(8,128)S(1)} %get-tuple-element.41), channel_id=1, source_target_pairs={{16,0},{32,16},{48,32},{64,48},{80,64},{96,80},{112,96},{17,1},{33... | collective-permute-start | bytes 4808 | tf_op jit(solution)/shard_map/ppermute | solution.py:36
  55.8 4.8 %collective-permute-start.4 = (f32[400,1]{1,0:T(8,128)S(1)}, f32[400,1]{1,0:T(8,128)S(1)}, u32[]{:S(2)}, u32[]{:S(2)}) collective-permute-start(f32[400,1]{1,0:T(8,128)S(1)} %get-tuple-element.42), channel_id=1, source_target_pairs={{0,16},{16,32},{32,48},{48,64},{64,80},{80,96},{96,112},{1,17},{17... | collective-permute-start | bytes 4808 | tf_op jit(solution)/shard_map/ppermute | solution.py:31
  59.4 1.2 copy-start.6
  60.6 0.7 copy-start.7
  60.6 0.8 copy-start.4
  61.3 0.7 copy-start.5
  65.2 30.9 %collective-permute-start.7 = (f32[400,128]{1,0:T(8,128)}, f32[400,128]{1,0:T(8,128)S(1)}, u32[]{:S(2)}, u32[]{:S(2)}) collective-permute-start(f32[400,128]{1,0:T(8,128)} %get-tuple-element.14.z_ref), channel_id=1, source_target_pairs={{1,0},{2,1},{3,2},{4,3},{5,4},{6,5},{7,6},{8,7},{9,8},{10,9},{11,1... | collective-permute-start | bytes 614408 | tf_op jit(solution)/shard_map/ppermute | solution.py:36
  66.5 29.6 %collective-permute-start.6 = (f32[400,128]{1,0:T(8,128)}, f32[400,128]{1,0:T(8,128)S(1)}, u32[]{:S(2)}, u32[]{:S(2)}) collective-permute-start(f32[400,128]{1,0:T(8,128)} %get-tuple-element.14.z_ref), channel_id=1, source_target_pairs={{0,1},{1,2},{2,3},{3,4},{4,5},{5,6},{6,7},{7,8},{8,9},{9,10},{10,1... | collective-permute-start | bytes 614408 | tf_op jit(solution)/shard_map/ppermute | solution.py:31
  70.5 25.6 %all-to-all-start.1 = ((f32[128,1,128]{2,1,0:T(1,128)}), f32[128,1,128]{2,1,0:T(1,128)S(1)}, u32[]{:S(2)}, u32[]{:S(2)}) async-start(f32[128,1,128]{2,1,0:T(1,128)} %bitcast.71), calls=%async_computation.1 | async-start | bytes 131072 | tf_op jit(solution)/shard_map/all_to_all | solution.py:182
  87.7 7.6 %collective-permute-start.9 = (f32[400,1]{1,0:T(8,128)S(1)}, f32[400,1]{1,0:T(8,128)S(1)}, u32[]{:S(2)}, u32[]{:S(2)}) collective-permute-start(f32[400,1]{1,0:T(8,128)S(1)} %get-tuple-element.39), channel_id=1, source_target_pairs={{16,0},{32,16},{48,32},{64,48},{80,64},{96,80},{112,96},{17,1},{33... | collective-permute-start | bytes 4808 | tf_op jit(solution)/shard_map/ppermute | solution.py:36
  90.7 5.3 %collective-permute-start.8 = (f32[400,1]{1,0:T(8,128)S(1)}, f32[400,1]{1,0:T(8,128)S(1)}, u32[]{:S(2)}, u32[]{:S(2)}) collective-permute-start(f32[400,1]{1,0:T(8,128)S(1)} %get-tuple-element.40), channel_id=1, source_target_pairs={{0,16},{16,32},{32,48},{48,64},{64,80},{80,96},{96,112},{1,17},{17... | collective-permute-start | bytes 4808 | tf_op jit(solution)/shard_map/ppermute | solution.py:31
  95.3 0.8 copy-start.11
  96.0 0.7 copy-start.12
  96.1 0.6 copy-start.8
  96.1 0.7 copy-start.9
  96.1 0.8 copy-start.10

commit v9 on v8

--- a/solution.py
+++ b/solution.py
@@ -9,6 +9,7 @@
 DATES = 400
 ITERS = 3
 SPAN = 8
+GRAM_PAIRS = ((0, 0), (0, 1), (0, 2), (0, 3), (1, 1), (1, 2), (1, 3), (2, 2), (2, 3))
 
 temporal_weight = 2.0
 spatial_weight = 0.5
@@ -119,36 +120,49 @@
     send_buffer(send_ref, [r * r, r * w, w * w, r * z, w * z])
 
 
-def block_kernel(got_ref, k_ref, r_ref, w_ref, z_ref, ru_ref, rd_ref, rl_ref, rr_ref, wu_ref, wd_ref, wl_ref, wr_ref,
-                 zu_ref, zd_ref, zl_ref, zr_ref, r_out, p_out, q_out, x_out, w_out, send_ref, scal_out):
+def krylov_kernel(k_ref, r_ref, w_ref, z_ref, zu_ref, zd_ref, zl_ref, zr_ref, y_out, send_ref):
+    basis = [r_ref[...], w_ref[...], z_ref[...]]
+    y = operate(k_ref[...], basis[2], zu_ref[...], zd_ref[...], zl_ref[...], zr_ref[...])
+    y_out[...] = y
+    basis.append(y)
+    send_buffer(send_ref, [basis[i] * basis[j] for i, j in GRAM_PAIRS])
+
+
+def combine_kernel(got_ref, r_ref, w_ref, z_ref, y_ref, x_out, res_out):
     sums = jnp.sum(got_ref[...], axis=0, keepdims=True)
-    norm_first = lane_value(sums, 0)
-    curvature_first = lane_value(sums, 1)
-    alpha_first = norm_first / curvature_first
-    norm = norm_first - 2.0 * alpha_first * curvature_first + alpha_first * alpha_first * lane_value(sums, 2)
-    beta = norm / norm_first
-    a = 1.0 + beta
-    b = -alpha_first
-    curvature = a * a * curvature_first + a * b * (lane_value(sums, 3) + lane_value(sums, 2)) + b * b * lane_value(sums, 4)
-    alpha = norm / curvature
-    r0 = r_ref[...]
-    w0 = w_ref[...]
-    z0 = z_ref[...]
-    p = a * r0 + b * w0
-    q = a * w0 + b * z0
-    p_out[...] = p
-    q_out[...] = q
-    x_out[...] = alpha_first * r0 + alpha * p
-    r = (r0 - alpha_first * w0) - alpha * q
-    r_out[...] = r
-    halo = []
-    for hr, hw, hz in zip((ru_ref, rd_ref, rl_ref, rr_ref), (wu_ref, wd_ref, wl_ref, wr_ref), (zu_ref, zd_ref, zl_ref, zr_ref)):
-        halo.append((hr[...] - alpha_first * hw[...]) - alpha * (a * hw[...] + b * hz[...]))
-    w = operate(k_ref[...], r, *halo)
-    w_out[...] = w
-    send_buffer(send_ref, [r * r, r * w, r * q, p * w, p * q])
-    lanes = lax.broadcasted_iota(jnp.int32, scal_out.shape, 1)
-    scal_out[...] = jnp.where(lanes == 0, norm, 0.0)
+    zero = jnp.zeros((1, 1), jnp.float32)
+    gram = [[zero] * 4 for _ in range(4)]
+    for n, (i, j) in enumerate(GRAM_PAIRS):
+        gram[i][j] = gram[j][i] = lane_value(sums, n)
+
+    def dot(u, v):
+        total = zero
+        for i in range(4):
+            for j in range(4):
+                if u[i] is not None and v[j] is not None:
+                    total = total + u[i] * v[j] * gram[i][j]
+        return total
+
+    def mix(u, s, v):
+        return [a if b is None else (s * b if a is None else a + s * b) for a, b in zip(u, v)]
+
+    one = jnp.ones((1, 1), jnp.float32)
+    residual = [one, None, None, None]
+    direction = residual
+    solution_field = [None] * 4
+    norm_now = dot(residual, residual)
+    for iteration in range(ITERS):
+        image = [None] + direction[:3]
+        alpha = norm_now / dot(direction, image)
+        solution_field = mix(solution_field, alpha, direction)
+        residual = mix(residual, -alpha, image)
+        if iteration < ITERS - 1:
+            norm_next = dot(residual, residual)
+            direction = mix(residual, norm_next / norm_now, direction)
+            norm_now = norm_next
+    vectors = [r_ref, w_ref, z_ref, y_ref]
+    x_out[...] = sum(c * v[...] for c, v in zip(solution_field, vectors) if c is not None)
+    res_out[...] = sum(c * v[...] for c, v in zip(residual, vectors) if c is not None)
 
 
 def step_scalars(got_ref, scal_ref):
@@ -238,16 +252,11 @@
     send_shape = (count, lanes)
     (w0,) = call(image_kernel, [field], matrix, residual, *residual_halo)
     w0_halo = exchange_rows_cols(w0)
-    z0, send = call(gram_kernel, [field, send_shape], matrix, residual, w0, *w0_halo)
+    (z0,) = call(image_kernel, [field], matrix, w0, *w0_halo)
+    z0_halo = exchange_rows_cols(z0)
+    y0, send = call(krylov_kernel, [field, send_shape], matrix, residual, w0, z0, *z0_halo)
     got = reduce_all(send)
-    z0_halo = exchange_rows_cols(z0)
-    r2, p1, q1, x2, w2, send, scal = call(
-        block_kernel,
-        [field, field, field, field, field, send_shape, (1, lanes)],
-        got, matrix, residual, w0, z0, *residual_halo, *w0_halo, *z0_halo,
-    )
-    got = reduce_all(send)
-    solution_field, residual = call(last_kernel, [field, field], got, scal, r2, p1, q1, x2, w2)
+    solution_field, residual = call(combine_kernel, [field, field], got, residual, w0, z0, y0)
     return (solution_field[:, None, :], residual[:, None, :])
 
 

time: 125 us -> 112 us (0.90)
  starting transfers between devices: 43.5 us -> 25.1 us
  waiting for transfers between devices: 5.51 us -> 10.5 us
  blocking collectives: 43.4 us -> 45.5 us
    all_to_all x1 -> x0, starting transfers between devices: 16 us -> none  [reduce_all(): return lax.all_to_all(send, ('pair', 'tile'), 0, 0, tiled=True)]
    ppermute x5, waiting for transfers between devices: 3.51 us -> 9.42 us  [from_next(): return lax.ppermute(cells, axis, [(i + 1, i) for i in range(count - 1)])]
    ppermute x5, starting transfers between devices: 10.7 us -> 8.1 us  [from_next(): return lax.ppermute(cells, axis, [(i + 1, i) for i in range(count - 1)])]
    all_to_all x1, blocking collectives: 20.7 us -> 22.9 us  [reduce_all(): return lax.all_to_all(send, ('pair', 'tile'), 0, 0, tiled=True)]
  transfers between devices with their start and end apart: 11 -> 10, of which waited for: 5 -> 5; matrix products, arithmetic and copies ran while one was open for 6% -> 7% of each run, Pallas kernels for 0% -> 0%
where the time goes in v9:
time: 112 us
  blocking collectives  45.5 us (41%)
  starting transfers between devices  25.1 us (22%)
  Pallas kernels  11.6 us (10%)
  local copies, waits for them, and re-layouts  10.6 us (9%)
  waiting for transfers between devices  10.5 us (9%)
  matrix products  3.81 us (3%)
  other arithmetic  3.53 us (3%)
    all_to_all x1, blocking collectives, reduce_all(): return lax.all_to_all(send, ('pair', 'tile'), 0, 0, tiled=True)  22.9 us
    all_to_all x1, blocking collectives, body(): lax.all_to_all(chunks, 'pair', 0, 0, tiled=True)  22.7 us
    ppermute x5, starting transfers between devices, from_prev(): return lax.ppermute(cells, axis, [(i, i + 1) for i in range(count - 1)])  17 us
    pallas_call x4, Pallas kernels, call(): pl.pallas_call(kernel, out_shape=[jax.ShapeDtypeStruct(s, jnp.float32) fo...  11.6 us
    ppermute x5, waiting for transfers between devices, from_next(): return lax.ppermute(cells, axis, [(i + 1, i) for i in range(count - 1)])  9.42 us
    ppermute x5, starting transfers between devices, from_next(): return lax.ppermute(cells, axis, [(i + 1, i) for i in range(count - 1)])  8.1 us
    unnamed x36, local copies, waits for them, and re-layouts  6.54 us
    slice x2, local copies, waits for them, and re-layouts, exchange_rows_cols(): cells[:, :1]  2.28 us
  transfers between devices with their start and end apart: 10, of which 5 were waited for; matrix products, arithmetic and copies ran while one was open for 7% of the time, Pallas kernels for 0%

profile of v9, /device:TPU:1, one launch (start us, length us, event | category | flops | bytes accessed | tf_op | source)
XLA Modules:
  0.0 111.6 jit_solution(210883725942381740)
XLA Ops:
  0.6 2.4 %copy.19 = f32[250,1,1024]{0,2,1:T(8,128)S(1)} copy(f32[250,1,1024]{2,1,0:T(1,128)} %param.4) | data formatting | bytes 2048000 | tf_op args[0]
  3.1 0.0 copy-start.12
  3.1 0.0 copy-start.13
  3.2 0.5 copy-done.12
  3.8 0.0 copy-done.13
  3.8 0.1 pad_maximum_fusion
  3.9 22.7 %all_to_all.16 = f32[8,250,136]{1,2,0:T(8,128)S(1)} all-to-all(f32[8,250,136]{1,2,0:T(8,128)S(1)} %pad_maximum_fusion), channel_id=1, replica_groups=mesh['pair'=8,'tile'=16] {'pair'}, dimensions={0} | all-to-all | bytes 2176000 | tf_op jit(solution)/shard_map/all_to_all | solution.py:218
  26.6 0.4 copy.20
  26.9 0.5 reshape.13
  27.5 0.3 reduce-precision_convert_fusion.1
  27.8 2.0 %fusion.1 = f32[400,390]{1,0:T(8,128)S(1)} fusion(f32[2000]{0:T(1024)S(1)} %bitcast.86, f32[2000]{0:T(1024)S(1)} %bitcast.84, bf16[2000,130]{0,1:T(8,128)(2,1)S(1)} %get-tuple-element.17, bf16[2000,130]{0,1:T(8,128)(2,1)S(1)} %get-tuple-element.18, bf16[2000,130]{0,1:T(8,128)(2,1)S(1)} %get-tuple-element.16), kind=kOutput, calls=%fused_computation.4 | convolution fusion | flops 633480000 | bytes 2200000 | tf_op jit(solution)/shard_map/kt,kc->tc/dot_general | solution.py:234
  29.7 0.3 slice_add_fusion
  30.0 0.1 slice.150.v_ref.r_ref
  30.1 0.0 copy-start.1
  30.2 3.3 %collective-permute-start = (f32[400,128]{1,0:T(8,128)S(1)}, f32[400,128]{1,0:T(8,128)S(1)}, u32[]{:S(2)}, u32[]{:S(2)}) collective-permute-start(f32[400,128]{1,0:T(8,128)S(1)} %slice.150.v_ref.r_ref), channel_id=1, source_target_pairs={{0,1},{1,2},{2,3},{3,4},{4,5},{5,6},{6,7},{7,8},{8,9},{9,10},{10,1... | collective-permute-start | bytes 614408 | tf_op jit(solution)/shard_map/ppermute | solution.py:32
  33.4 1.3 %collective-permute-start.1 = (f32[400,128]{1,0:T(8,128)S(1)}, f32[400,128]{1,0:T(8,128)S(1)}, u32[]{:S(2)}, u32[]{:S(2)}) collective-permute-start(f32[400,128]{1,0:T(8,128)S(1)} %slice.150.v_ref.r_ref), channel_id=1, source_target_pairs={{1,0},{2,1},{3,2},{4,3},{5,4},{6,5},{7,6},{8,7},{9,8},{10,9},{11,1... | collective-permute-start | bytes 614408 | tf_op jit(solution)/shard_map/ppermute | solution.py:37
  34.7 1.9 %fusion = f32[400,8]{0,1:T(8,128)S(1)} fusion(f32[2000]{0:T(1024)S(1)} %bitcast.85, f32[2000]{0:T(1024)S(1)} %bitcast.82, f32[2000]{0:T(1024)S(1)} %bitcast.83), kind=kOutput, calls=%fused_computation.3 | convolution fusion | flops 77632000 | bytes 36800 | tf_op jit(solution)/shard_map/kt,kd->td/dot_general | solution.py:240
  36.6 0.6 fusion.30
  37.2 2.2 %add_add_fusion.k_ref = f32[400,400]{1,0:T(8,128)} fusion(f32[400,400]{1,0:T(8,128)S(1)} %copy-done.1, f32[400]{0:T(512)S(1)} %negate_add_fusion, f32[400]{0:T(512)S(1)} %bitcast.70, f32[400]{0:T(512)S(1)} %bitcast.72, f32[400]{0:T(512)S(1)} %bitcast.74, f32[400]{0:T(512)S(1)} %bitcast.76, f32[400]{0:T(512)S(1)} %bitcast.78, f32[400]{0:T(512)S(1)} %bitcast.80, ...), kind=kLoop, calls=%fused_computation.24 | loop fusion | flops 7520000 | bytes 1292800 | tf_op jit(solution)/shard_map/add | solution.py:76
  39.4 0.8 fusion.44
  40.2 0.6 collective-permute-done.1.vd_ref
  40.9 0.0 copy-done.6
  40.9 0.6 copy-done.7
  41.5 3.0 %shard_map.59.v_ref.w_ref = f32[400,128]{1,0:T(8,128)} custom-call(f32[400,400]{1,0:T(8,128)} %add_add_fusion.k_ref, f32[400,128]{1,0:T(8,128)} %copy-done, f32[400,128]{1,0:T(8,128)} %copy-done.6, f32[400,128]{1,0:T(8,128)} %copy-done.7, f32[400,1]{1,0:T(8,128)} %get-tuple-element.24.vl_ref, f32[400,1]{1,0:T(8,128)} %get-tuple-element.23.vr_ref), custom_call_target="tpu_custom_call" | custom-call | tf_op jit(solution)/shard_map/pallas_call | solution.py:187
  44.6 3.4 %collective-permute-start.2 = (f32[400,128]{1,0:T(8,128)}, f32[400,128]{1,0:T(8,128)S(1)}, u32[]{:S(2)}, u32[]{:S(2)}) collective-permute-start(f32[400,128]{1,0:T(8,128)} %shard_map.59.v_ref.w_ref), channel_id=1, source_target_pairs={{0,1},{1,2},{2,3},{3,4},{4,5},{5,6},{6,7},{7,8},{8,9},{9,10},{10,1... | collective-permute-start | bytes 614408 | tf_op jit(solution)/shard_map/ppermute | solution.py:32
  48.0 1.3 %collective-permute-start.3 = (f32[400,128]{1,0:T(8,128)}, f32[400,128]{1,0:T(8,128)S(1)}, u32[]{:S(2)}, u32[]{:S(2)}) collective-permute-start(f32[400,128]{1,0:T(8,128)} %shard_map.59.v_ref.w_ref), channel_id=1, source_target_pairs={{1,0},{2,1},{3,2},{4,3},{5,4},{6,5},{7,6},{8,7},{9,8},{10,9},{11,1... | collective-permute-start | bytes 614408 | tf_op jit(solution)/shard_map/ppermute | solution.py:37
  49.3 1.1 %fusion.46 = (f32[400,1]{1,0:T(8,128)S(1)}, f32[400,1]{1,0:T(8,128)S(1)}) fusion(f32[400,128]{1,0:T(8,128)} %shard_map.59.v_ref.w_ref), kind=kLoop, calls=%fused_computation.84 | loop fusion | bytes 6400 | tf_op jit(solution)/shard_map/slice | solution.py:204
  50.4 4.0 %collective-permute-start.4 = (f32[400,1]{1,0:T(8,128)S(1)}, f32[400,1]{1,0:T(8,128)S(1)}, u32[]{:S(2)}, u32[]{:S(2)}) collective-permute-start(f32[400,1]{1,0:T(8,128)S(1)} %get-tuple-element.28), channel_id=1, source_target_pairs={{0,16},{16,32},{32,48},{48,64},{64,80},{80,96},{96,112},{1,17},{17... | collective-permute-start | bytes 4808 | tf_op jit(solution)/shard_map/ppermute | solution.py:32
  54.5 1.9 %collective-permute-start.5 = (f32[400,1]{1,0:T(8,128)S(1)}, f32[400,1]{1,0:T(8,128)S(1)}, u32[]{:S(2)}, u32[]{:S(2)}) collective-permute-start(f32[400,1]{1,0:T(8,128)S(1)} %get-tuple-element.27), channel_id=1, source_target_pairs={{16,0},{32,16},{48,32},{64,48},{80,64},{96,80},{112,96},{17,1},{33... | collective-permute-start | bytes 4808 | tf_op jit(solution)/shard_map/ppermute | solution.py:37
  56.4 0.8 collective-permute-done.4.vl_ref
  57.1 4.4 %collective-permute-done.5.vr_ref = f32[400,1]{1,0:T(8,128)S(1)} collective-permute-done((f32[400,1]{1,0:T(8,128)S(1)}, f32[400,1]{1,0:T(8,128)S(1)}, u32[]{:S(2)}, u32[]{:S(2)}) %collective-permute-start.5) | collective-permute-done | bytes 1632 | tf_op jit(solution)/shard_map/ppermute | solution.py:37
  61.6 0.7 copy-done.11
  62.2 0.1 copy-done.8
  62.3 0.7 copy-done.9
  63.0 3.0 %shard_map.60.z_ref = f32[400,128]{1,0:T(8,128)} custom-call(f32[400,400]{1,0:T(8,128)} %add_add_fusion.k_ref, f32[400,128]{1,0:T(8,128)} %shard_map.59.v_ref.w_ref, f32[400,128]{1,0:T(8,128)} %copy-done.8, f32[400,128]{1,0:T(8,128)} %copy-done.9, f32[400,1]{1,0:T(8,128)} %copy-done.10, f32[400,1]{1,0:T(8,128)} %copy-done.11), custom_call_target="tpu_custom_call" | custom-call | tf_op jit(solution)/shard_map/pallas_call | solution.py:187
  66.0 4.3 %collective-permute-start.6 = (f32[400,128]{1,0:T(8,128)}, f32[400,128]{1,0:T(8,128)S(1)}, u32[]{:S(2)}, u32[]{:S(2)}) collective-permute-start(f32[400,128]{1,0:T(8,128)} %shard_map.60.z_ref), channel_id=1, source_target_pairs={{0,1},{1,2},{2,3},{3,4},{4,5},{5,6},{6,7},{7,8},{8,9},{9,10},{10,1... | collective-permute-start | bytes 614408 | tf_op jit(solution)/shard_map/ppermute | solution.py:32
  70.2 1.3 %collective-permute-start.7 = (f32[400,128]{1,0:T(8,128)}, f32[400,128]{1,0:T(8,128)S(1)}, u32[]{:S(2)}, u32[]{:S(2)}) collective-permute-start(f32[400,128]{1,0:T(8,128)} %shard_map.60.z_ref), channel_id=1, source_target_pairs={{1,0},{2,1},{3,2},{4,3},{5,4},{6,5},{7,6},{8,7},{9,8},{10,9},{11,1... | collective-permute-start | bytes 614408 | tf_op jit(solution)/shard_map/ppermute | solution.py:37
  71.5 1.1 %fusion.45 = (f32[400,1]{1,0:T(8,128)S(1)}, f32[400,1]{1,0:T(8,128)S(1)}) fusion(f32[400,128]{1,0:T(8,128)} %shard_map.60.z_ref), kind=kLoop, calls=%fused_computation.83 | loop fusion | bytes 6400 | tf_op jit(solution)/shard_map/slice | solution.py:204
  72.7 2.0 %collective-permute-start.8 = (f32[400,1]{1,0:T(8,128)S(1)}, f32[400,1]{1,0:T(8,128)S(1)}, u32[]{:S(2)}, u32[]{:S(2)}) collective-permute-start(f32[400,1]{1,0:T(8,128)S(1)} %get-tuple-element.26), channel_id=1, source_target_pairs={{0,16},{16,32},{32,48},{48,64},{64,80},{80,96},{96,112},{1,17},{17... | collective-permute-start | bytes 4808 | tf_op jit(solution)/shard_map/ppermute | solution.py:32
  74.7 2.3 %collective-permute-start.9 = (f32[400,1]{1,0:T(8,128)S(1)}, f32[400,1]{1,0:T(8,128)S(1)}, u32[]{:S(2)}, u32[]{:S(2)}) collective-permute-start(f32[400,1]{1,0:T(8,128)S(1)} %get-tuple-element.25), channel_id=1, source_target_pairs={{16,0},{32,16},{48,32},{64,48},{80,64},{96,80},{112,96},{17,1},{33... | collective-permute-start | bytes 4808 | tf_op jit(solution)/shard_map/ppermute | solution.py:37
  77.0 0.4 collective-permute-done.8.zl_ref
  77.4 4.4 %collective-permute-done.9.zr_ref = f32[400,1]{1,0:T(8,128)S(1)} collective-permute-done((f32[400,1]{1,0:T(8,128)S(1)}, f32[400,1]{1,0:T(8,128)S(1)}, u32[]{:S(2)}, u32[]{:S(2)}) %collective-permute-start.9) | collective-permute-done | bytes 1632 | tf_op jit(solution)/shard_map/ppermute | solution.py:37
  81.8 0.7 copy-done.5
  82.5 0.1 copy-done.2
  82.6 0.7 copy-done.3
  83.2 3.3 %shard_map.61 = (f32[400,128]{1,0:T(8,128)}, f32[128,128]{1,0:T(8,128)}) custom-call(f32[400,400]{1,0:T(8,128)} %add_add_fusion.k_ref, f32[400,128]{1,0:T(8,128)} %copy-done, f32[400,128]{1,0:T(8,128)} %shard_map.59.v_ref.w_ref, f32[400,128]{1,0:T(8,128)} %shard_map.60.z_ref, f32[400,128]{1,0:T(8,128)} %copy-done.2, f32[400,128]{1,0:T(8,128)} %copy-done.3, ...), custom_call_target="tpu_custom_call" | custom-call | tf_op jit(solution)/shard_map/pallas_call | solution.py:187
  86.5 22.9 %all_to_all.17 = f32[128,1,128]{2,1,0:T(1,128)} all-to-all(f32[128,1,128]{2,1,0:T(1,128)} %bitcast.66), channel_id=1, replica_groups=mesh['pair'=8,'tile'=16] {'pair','tile'}, dimensions={0} | all-to-all | bytes 131072 | tf_op jit(solution)/shard_map/all_to_all | solution.py:196
  109.4 2.2 %shard_map.62 = (f32[400,128]{1,0:T(8,128)}, f32[400,128]{1,0:T(8,128)}) custom-call(f32[128,128]{1,0:T(8,128)} %bitcast.65, f32[400,128]{1,0:T(8,128)} %copy-done, f32[400,128]{1,0:T(8,128)} %shard_map.59.v_ref.w_ref, f32[400,128]{1,0:T(8,128)} %shard_map.60.z_ref, f32[400,128]{1,0:T(8,128)} %get-tuple-element.7.y_ref), custom_call_target="tpu_custom_call" | custom-call | tf_op jit(solution)/shard_map/pallas_call | solution.py:187
  (34 shorter events, 0.2 us)
Async XLA Ops:
  3.1 0.7 copy-start.12
  3.1 0.7 copy-start.13
  30.1 9.3 %copy-start = (f32[400,128]{1,0:T(8,128)}, f32[400,128]{1,0:T(8,128)S(1)}, u32[]{:S(2)}) copy-start(f32[400,128]{1,0:T(8,128)S(1)} %slice.150.v_ref.r_ref) | copy-start | bytes 614404
  30.1 7.0 %copy-start.1 = (f32[400,400]{1,0:T(8,128)S(1)}, f32[400,400]{1,0:T(8,128)}, u32[]{:S(2)}) copy-start(f32[400,400]{1,0:T(8,128)} %constant.25.clone) | copy-start | bytes 1920004
  30.2 10.1 %collective-permute-start = (f32[400,128]{1,0:T(8,128)S(1)}, f32[400,128]{1,0:T(8,128)S(1)}, u32[]{:S(2)}, u32[]{:S(2)}) collective-permute-start(f32[400,128]{1,0:T(8,128)S(1)} %slice.150.v_ref.r_ref), channel_id=1, source_target_pairs={{0,1},{1,2},{2,3},{3,4},{4,5},{5,6},{6,7},{7,8},{8,9},{9,10},{10,1... | collective-permute-start | bytes 614408 | tf_op jit(solution)/shard_map/ppermute | solution.py:32
  33.4 7.4 %collective-permute-start.1 = (f32[400,128]{1,0:T(8,128)S(1)}, f32[400,128]{1,0:T(8,128)S(1)}, u32[]{:S(2)}, u32[]{:S(2)}) collective-permute-start(f32[400,128]{1,0:T(8,128)S(1)} %slice.150.v_ref.r_ref), channel_id=1, source_target_pairs={{1,0},{2,1},{3,2},{4,3},{5,4},{6,5},{7,6},{8,7},{9,8},{10,9},{11,1... | collective-permute-start | bytes 614408 | tf_op jit(solution)/shard_map/ppermute | solution.py:37
  40.2 0.7 copy-start.6
  40.9 0.7 copy-start.7
  44.6 17.0 %collective-permute-start.2 = (f32[400,128]{1,0:T(8,128)}, f32[400,128]{1,0:T(8,128)S(1)}, u32[]{:S(2)}, u32[]{:S(2)}) collective-permute-start(f32[400,128]{1,0:T(8,128)} %shard_map.59.v_ref.w_ref), channel_id=1, source_target_pairs={{0,1},{1,2},{2,3},{3,4},{4,5},{5,6},{6,7},{7,8},{8,9},{9,10},{10,1... | collective-permute-start | bytes 614408 | tf_op jit(solution)/shard_map/ppermute | solution.py:32
  48.0 13.5 %collective-permute-start.3 = (f32[400,128]{1,0:T(8,128)}, f32[400,128]{1,0:T(8,128)S(1)}, u32[]{:S(2)}, u32[]{:S(2)}) collective-permute-start(f32[400,128]{1,0:T(8,128)} %shard_map.59.v_ref.w_ref), channel_id=1, source_target_pairs={{1,0},{2,1},{3,2},{4,3},{5,4},{6,5},{7,6},{8,7},{9,8},{10,9},{11,1... | collective-permute-start | bytes 614408 | tf_op jit(solution)/shard_map/ppermute | solution.py:37
  50.4 6.7 %collective-permute-start.4 = (f32[400,1]{1,0:T(8,128)S(1)}, f32[400,1]{1,0:T(8,128)S(1)}, u32[]{:S(2)}, u32[]{:S(2)}) collective-permute-start(f32[400,1]{1,0:T(8,128)S(1)} %get-tuple-element.28), channel_id=1, source_target_pairs={{0,16},{16,32},{32,48},{48,64},{64,80},{80,96},{96,112},{1,17},{17... | collective-permute-start | bytes 4808 | tf_op jit(solution)/shard_map/ppermute | solution.py:32
  54.5 7.1 %collective-permute-start.5 = (f32[400,1]{1,0:T(8,128)S(1)}, f32[400,1]{1,0:T(8,128)S(1)}, u32[]{:S(2)}, u32[]{:S(2)}) collective-permute-start(f32[400,1]{1,0:T(8,128)S(1)} %get-tuple-element.27), channel_id=1, source_target_pairs={{16,0},{32,16},{48,32},{64,48},{80,64},{96,80},{112,96},{17,1},{33... | collective-permute-start | bytes 4808 | tf_op jit(solution)/shard_map/ppermute | solution.py:37
  57.1 4.4 %copy-start.10 = (f32[400,1]{1,0:T(8,128)}, f32[400,1]{1,0:T(8,128)S(1)}, u32[]{:S(2)}) copy-start(f32[400,1]{1,0:T(8,128)S(1)} %collective-permute-done.4.vl_ref) | copy-start | bytes 4804
  61.5 0.7 copy-start.11
  61.5 0.7 copy-start.8
  62.3 0.7 copy-start.9
  66.0 15.8 %collective-permute-start.6 = (f32[400,128]{1,0:T(8,128)}, f32[400,128]{1,0:T(8,128)S(1)}, u32[]{:S(2)}, u32[]{:S(2)}) collective-permute-start(f32[400,128]{1,0:T(8,128)} %shard_map.60.z_ref), channel_id=1, source_target_pairs={{0,1},{1,2},{2,3},{3,4},{4,5},{5,6},{6,7},{7,8},{8,9},{9,10},{10,1... | collective-permute-start | bytes 614408 | tf_op jit(solution)/shard_map/ppermute | solution.py:32
  70.2 11.6 %collective-permute-start.7 = (f32[400,128]{1,0:T(8,128)}, f32[400,128]{1,0:T(8,128)S(1)}, u32[]{:S(2)}, u32[]{:S(2)}) collective-permute-start(f32[400,128]{1,0:T(8,128)} %shard_map.60.z_ref), channel_id=1, source_target_pairs={{1,0},{2,1},{3,2},{4,3},{5,4},{6,5},{7,6},{8,7},{9,8},{10,9},{11,1... | collective-permute-start | bytes 614408 | tf_op jit(solution)/shard_map/ppermute | solution.py:37
  72.7 4.7 %collective-permute-start.8 = (f32[400,1]{1,0:T(8,128)S(1)}, f32[400,1]{1,0:T(8,128)S(1)}, u32[]{:S(2)}, u32[]{:S(2)}) collective-permute-start(f32[400,1]{1,0:T(8,128)S(1)} %get-tuple-element.26), channel_id=1, source_target_pairs={{0,16},{16,32},{32,48},{48,64},{64,80},{80,96},{96,112},{1,17},{17... | collective-permute-start | bytes 4808 | tf_op jit(solution)/shard_map/ppermute | solution.py:32
  74.7 7.1 %collective-permute-start.9 = (f32[400,1]{1,0:T(8,128)S(1)}, f32[400,1]{1,0:T(8,128)S(1)}, u32[]{:S(2)}, u32[]{:S(2)}) collective-permute-start(f32[400,1]{1,0:T(8,128)S(1)} %get-tuple-element.25), channel_id=1, source_target_pairs={{16,0},{32,16},{48,32},{64,48},{80,64},{96,80},{112,96},{17,1},{33... | collective-permute-start | bytes 4808 | tf_op jit(solution)/shard_map/ppermute | solution.py:37
  77.4 4.4 %copy-start.4 = (f32[400,1]{1,0:T(8,128)}, f32[400,1]{1,0:T(8,128)S(1)}, u32[]{:S(2)}) copy-start(f32[400,1]{1,0:T(8,128)S(1)} %collective-permute-done.8.zl_ref) | copy-start | bytes 4804
  81.8 0.7 copy-start.5
  81.8 0.7 copy-start.2
  82.6 0.7 copy-start.3

commit v10 on v9

--- a/solution.py
+++ b/solution.py
@@ -1,3 +1,5 @@
+import functools
+
 import numpy as np
 import jax
 import jax.numpy as jnp
@@ -108,8 +110,11 @@
     send_ref[...] = jnp.broadcast_to(row, send_ref.shape)
 
 
-def image_kernel(k_ref, v_ref, vu_ref, vd_ref, vl_ref, vr_ref, w_out):
-    w_out[...] = operate(k_ref[...], v_ref[...], vu_ref[...], vd_ref[...], vl_ref[...], vr_ref[...])
+def image_kernel(index, shift_ref, k_ref, v_ref, vu_ref, vd_ref, vl_ref, vr_ref, w_out):
+    v = v_ref[...]
+    w_out[...] = operate(k_ref[...], v, vu_ref[...], vd_ref[...], vl_ref[...], vr_ref[...]) - lane_value(
+        shift_ref[...], index
+    ) * v
 
 
 def gram_kernel(k_ref, r_ref, w_ref, wu_ref, wd_ref, wl_ref, wr_ref, z_out, send_ref):
@@ -120,16 +125,19 @@
     send_buffer(send_ref, [r * r, r * w, w * w, r * z, w * z])
 
 
-def krylov_kernel(k_ref, r_ref, w_ref, z_ref, zu_ref, zd_ref, zl_ref, zr_ref, y_out, send_ref):
+def krylov_kernel(shift_ref, k_ref, r_ref, w_ref, z_ref, zu_ref, zd_ref, zl_ref, zr_ref, y_out, send_ref):
     basis = [r_ref[...], w_ref[...], z_ref[...]]
-    y = operate(k_ref[...], basis[2], zu_ref[...], zd_ref[...], zl_ref[...], zr_ref[...])
+    y = operate(k_ref[...], basis[2], zu_ref[...], zd_ref[...], zl_ref[...], zr_ref[...]) - lane_value(
+        shift_ref[...], 2
+    ) * basis[2]
     y_out[...] = y
     basis.append(y)
     send_buffer(send_ref, [basis[i] * basis[j] for i, j in GRAM_PAIRS])
 
 
-def combine_kernel(got_ref, r_ref, w_ref, z_ref, y_ref, x_out, res_out):
+def combine_kernel(shift_ref, got_ref, r_ref, w_ref, z_ref, y_ref, x_out, res_out):
     sums = jnp.sum(got_ref[...], axis=0, keepdims=True)
+    shifts = [lane_value(shift_ref[...], k) for k in range(3)]
     zero = jnp.zeros((1, 1), jnp.float32)
     gram = [[zero] * 4 for _ in range(4)]
     for n, (i, j) in enumerate(GRAM_PAIRS):
@@ -152,7 +160,11 @@
     solution_field = [None] * 4
     norm_now = dot(residual, residual)
     for iteration in range(ITERS):
-        image = [None] + direction[:3]
+        image = [None] * 4
+        for k in range(3):
+            if direction[k] is not None:
+                image = mix(image, shifts[k], [None] * k + [direction[k]] + [None] * (3 - k))
+                image = mix(image, one, [None] * (k + 1) + [direction[k]] + [None] * (2 - k))
         alpha = norm_now / dot(direction, image)
         solution_field = mix(solution_field, alpha, direction)
         residual = mix(residual, -alpha, image)
@@ -250,13 +262,16 @@
     field = residual.shape
     lanes = 128
     send_shape = (count, lanes)
-    (w0,) = call(image_kernel, [field], matrix, residual, *residual_halo)
+    bound = jnp.max(jnp.sum(jnp.abs(matrix), axis=1)) + 4.0 * spatial_weight
+    nodes = np.cos(np.array([1.0, 5.0, 3.0]) * np.pi / 6.0).astype(np.float32)
+    shift = jnp.zeros((1, lanes), jnp.float32).at[0, :3].set(0.5 * bound * (1.0 + nodes))
+    (w0,) = call(functools.partial(image_kernel, 0), [field], shift, matrix, residual, *residual_halo)
     w0_halo = exchange_rows_cols(w0)
-    (z0,) = call(image_kernel, [field], matrix, w0, *w0_halo)
+    (z0,) = call(functools.partial(image_kernel, 1), [field], shift, matrix, w0, *w0_halo)
     z0_halo = exchange_rows_cols(z0)
-    y0, send = call(krylov_kernel, [field, send_shape], matrix, residual, w0, z0, *z0_halo)
+    y0, send = call(krylov_kernel, [field, send_shape], shift, matrix, residual, w0, z0, *z0_halo)
     got = reduce_all(send)
-    solution_field, residual = call(combine_kernel, [field, field], got, residual, w0, z0, y0)
+    solution_field, residual = call(combine_kernel, [field, field], shift, got, residual, w0, z0, y0)
     return (solution_field[:, None, :], residual[:, None, :])
 
 

time: 112 us -> 115 us (1.027)
  blocking collectives: 45.5 us -> 23.2 us
  waiting for transfers between devices: 10.5 us -> 25.1 us
  starting transfers between devices: 25.1 us -> 32.2 us
  other arithmetic: 3.53 us -> 5.61 us
    all_to_all x1 -> x0, blocking collectives: 22.7 us -> none  [body(): lax.all_to_all(chunks, 'pair', 0, 0, tiled=True)]
    all_to_all x0 -> x1, waiting for transfers between devices: none -> 15.2 us  [body(): lax.all_to_all(chunks, 'pair', 0, 0, tiled=True)]
    all_to_all x0 -> x1, starting transfers between devices: none -> 6.81 us  [body(): lax.all_to_all(chunks, 'pair', 0, 0, tiled=True)]
    add x1 -> x0, other arithmetic: 2.23 us -> none  [normal_matrix(): coupling + jnp.where(offset == 0, diagonal[:, None], 0.0)]
    reduce_sum x0 -> x1, other arithmetic: none -> 1.4 us  [body(): bound = jnp.max(jnp.sum(jnp.abs(matrix), axis=1)) + 4.0 * spatial_weight]
    another operation x0 -> x2, other arithmetic: none -> 1.29 us
    unnamed x36 -> x38, local copies, waits for them, and re-layouts: 6.54 us -> 6.59 us
  transfers between devices with their start and end apart: 10 -> 11, of which waited for: 5 -> 5; matrix products, arithmetic and copies ran while one was open for 7% -> 8% of each run, Pallas kernels for 0% -> 0%
where the time goes in v10:
time: 115 us; the launch traced here: 114 us
  starting transfers between devices  32.2 us (28%)
  waiting for transfers between devices  25.1 us (22%)
  blocking collectives  23.2 us (20%)
  Pallas kernels  11.4 us (10%)
  local copies, waits for them, and re-layouts  11.2 us (10%)
  other arithmetic  5.61 us (5%)
  matrix products  3.81 us (3%)
  between operations  1.63 us (1%)
    all_to_all x1, blocking collectives, reduce_all(): return lax.all_to_all(send, ('pair', 'tile'), 0, 0, tiled=True)  23.2 us
    ppermute x5, starting transfers between devices, from_prev(): return lax.ppermute(cells, axis, [(i, i + 1) for i in range(count - 1)])  17.3 us
    all_to_all x1, waiting for transfers between devices, body(): lax.all_to_all(chunks, 'pair', 0, 0, tiled=True)  15.2 us
    pallas_call x4, Pallas kernels, call(): pl.pallas_call(kernel, out_shape=[jax.ShapeDtypeStruct(s, jnp.float32) fo...  11.4 us
    ppermute x5, waiting for transfers between devices, from_next(): return lax.ppermute(cells, axis, [(i + 1, i) for i in range(count - 1)])  8.8 us
    ppermute x5, starting transfers between devices, from_next(): return lax.ppermute(cells, axis, [(i + 1, i) for i in range(count - 1)])  8.1 us
    all_to_all x1, starting transfers between devices, body(): lax.all_to_all(chunks, 'pair', 0, 0, tiled=True)  6.81 us
    unnamed x38, local copies, waits for them, and re-layouts  6.59 us
  transfers between devices with their start and end apart: 11, of which 5 were waited for; matrix products, arithmetic and copies ran while one was open for 8% of the time, Pallas kernels for 0%

profile of v10, /device:TPU:1, one launch (start us, length us, event | category | flops | bytes accessed | tf_op | source)
XLA Modules:
  0.0 114.1 jit_solution(11723330718359752343)
XLA Ops:
  0.6 2.4 %copy.20 = f32[250,1,1024]{0,2,1:T(8,128)S(1)} copy(f32[250,1,1024]{2,1,0:T(1,128)} %param.7) | data formatting | bytes 2048000 | tf_op args[0]
  3.2 0.5 copy-done.12
  3.8 1.1 pad_maximum_fusion
  4.9 6.8 %all-to-all-start = ((f32[8,250,136]{1,2,0:T(8,128)}), f32[8,250,136]{1,2,0:T(8,128)S(1)}, u32[]{:S(2)}, u32[]{:S(2)}) async-start(f32[8,250,136]{1,2,0:T(8,128)} %pad_maximum_fusion), calls=%async_computation | async-start | bytes 2228224 | tf_op jit(solution)/shard_map/all_to_all | solution.py:230
  11.7 0.6 compare_reduce_fusion
  12.4 15.2 %all-to-all-done = f32[8,250,136]{1,2,0:T(8,128)S(1)} async-done(((f32[8,250,136]{1,2,0:T(8,128)}), f32[8,250,136]{1,2,0:T(8,128)S(1)}, u32[]{:S(2)}, u32[]{:S(2)}) %all-to-all-start) | async-done | bytes 1088032 | tf_op jit(solution)/shard_map/all_to_all | solution.py:230
  27.5 0.4 copy.21
  27.9 0.5 reshape.43
  28.4 0.3 reduce-precision_convert_fusion.1
  28.7 2.0 %fusion.1 = f32[400,390]{1,0:T(8,128)S(1)} fusion(f32[2000]{0:T(1024)S(1)} %bitcast.88, f32[2000]{0:T(1024)S(1)} %bitcast.86, bf16[2000,130]{0,1:T(8,128)(2,1)S(1)} %get-tuple-element.31, bf16[2000,130]{0,1:T(8,128)(2,1)S(1)} %get-tuple-element.32, bf16[2000,130]{0,1:T(8,128)(2,1)S(1)} %get-tuple-element.30), kind=kOutput, calls=%fused_computation.4 | convolution fusion | flops 633480000 | bytes 2200000 | tf_op jit(solution)/shard_map/kt,kc->tc/dot_general | solution.py:246
  30.7 0.3 slice_add_fusion
  31.0 0.1 slice.166.v_ref.r_ref
  31.1 3.3 %collective-permute-start = (f32[400,128]{1,0:T(8,128)S(1)}, f32[400,128]{1,0:T(8,128)S(1)}, u32[]{:S(2)}, u32[]{:S(2)}) collective-permute-start(f32[400,128]{1,0:T(8,128)S(1)} %slice.166.v_ref.r_ref), channel_id=1, source_target_pairs={{0,1},{1,2},{2,3},{3,4},{4,5},{5,6},{6,7},{7,8},{8,9},{9,10},{10,1... | collective-permute-start | bytes 614408 | tf_op jit(solution)/shard_map/ppermute | solution.py:34
  34.4 1.3 %collective-permute-start.1 = (f32[400,128]{1,0:T(8,128)S(1)}, f32[400,128]{1,0:T(8,128)S(1)}, u32[]{:S(2)}, u32[]{:S(2)}) collective-permute-start(f32[400,128]{1,0:T(8,128)S(1)} %slice.166.v_ref.r_ref), channel_id=1, source_target_pairs={{1,0},{2,1},{3,2},{4,3},{5,4},{6,5},{7,6},{8,7},{9,8},{10,9},{11,1... | collective-permute-start | bytes 614408 | tf_op jit(solution)/shard_map/ppermute | solution.py:39
  35.7 1.9 %fusion = f32[400,8]{0,1:T(8,128)S(1)} fusion(f32[2000]{0:T(1024)S(1)} %bitcast.87, f32[2000]{0:T(1024)S(1)} %bitcast.84, f32[2000]{0:T(1024)S(1)} %bitcast.85), kind=kOutput, calls=%fused_computation.3 | convolution fusion | flops 77632000 | bytes 36800 | tf_op jit(solution)/shard_map/kt,kd->td/dot_general | solution.py:252
  37.6 0.6 fusion.30
  38.2 1.4 %abs_reduce_fusion = (f32[400]{0:T(512)S(1)}, f32[400,400]{1,0:T(8,128)}) fusion(f32[400,400]{1,0:T(8,128)S(1)} %copy-done.1, f32[400]{0:T(512)S(1)} %negate_add_fusion, f32[400]{0:T(512)S(1)} %bitcast.72, f32[400]{0:T(512)S(1)} %bitcast.74, f32[400]{0:T(512)S(1)} %bitcast.76, f32[400]{0:T(512)S(1)} %bitcast.78, f32[400]{0:T(512)S(1)} %bitcast.80, ...), kind=kLoop, calls=%fused_computation.24 | loop fusion | flops 7839600 | bytes 1294400 | tf_op jit(solution)/shard_map/reduce_sum | solution.py:265
  39.5 0.6 reduce_max.9
  40.8 0.7 fusion.41
  41.5 0.5 scatter.4.shift_ref
  42.0 0.8 fusion.45
  42.8 0.7 copy-done.2
  43.5 0.1 copy-done.3
  43.5 3.0 %shard_map.68.v_ref.w_ref = f32[400,128]{1,0:T(8,128)} custom-call(f32[1,128]{1,0:T(1,128)} %scatter.4.shift_ref, f32[400,400]{1,0:T(8,128)} %get-tuple-element.29.k_ref, f32[400,128]{1,0:T(8,128)} %copy-done, f32[400,128]{1,0:T(8,128)} %copy-done.2, f32[400,128]{1,0:T(8,128)} %copy-done.3, f32[400,1]{1,0:T(8,128)} %get-tuple-element.38.vl_ref, ...), custom_call_target="tpu_custom_call" | custom-call | tf_op jit(solution)/shard_map/pallas_call | solution.py:199
  46.5 4.0 %collective-permute-start.2 = (f32[400,128]{1,0:T(8,128)}, f32[400,128]{1,0:T(8,128)S(1)}, u32[]{:S(2)}, u32[]{:S(2)}) collective-permute-start(f32[400,128]{1,0:T(8,128)} %shard_map.68.v_ref.w_ref), channel_id=1, source_target_pairs={{0,1},{1,2},{2,3},{3,4},{4,5},{5,6},{6,7},{7,8},{8,9},{9,10},{10,1... | collective-permute-start | bytes 614408 | tf_op jit(solution)/shard_map/ppermute | solution.py:34
  50.5 1.3 %collective-permute-start.3 = (f32[400,128]{1,0:T(8,128)}, f32[400,128]{1,0:T(8,128)S(1)}, u32[]{:S(2)}, u32[]{:S(2)}) collective-permute-start(f32[400,128]{1,0:T(8,128)} %shard_map.68.v_ref.w_ref), channel_id=1, source_target_pairs={{1,0},{2,1},{3,2},{4,3},{5,4},{6,5},{7,6},{8,7},{9,8},{10,9},{11,1... | collective-permute-start | bytes 614408 | tf_op jit(solution)/shard_map/ppermute | solution.py:39
  51.8 1.1 fusion.47
  52.9 3.8 %collective-permute-start.4 = (f32[400,1]{1,0:T(8,128)S(1)}, f32[400,1]{1,0:T(8,128)S(1)}, u32[]{:S(2)}, u32[]{:S(2)}) collective-permute-start(f32[400,1]{1,0:T(8,128)S(1)} %get-tuple-element.42), channel_id=1, source_target_pairs={{0,16},{16,32},{32,48},{48,64},{64,80},{80,96},{96,112},{1,17},{17... | collective-permute-start | bytes 4808 | tf_op jit(solution)/shard_map/ppermute | solution.py:34
  56.7 1.9 %collective-permute-start.5 = (f32[400,1]{1,0:T(8,128)S(1)}, f32[400,1]{1,0:T(8,128)S(1)}, u32[]{:S(2)}, u32[]{:S(2)}) collective-permute-start(f32[400,1]{1,0:T(8,128)S(1)} %get-tuple-element.41), channel_id=1, source_target_pairs={{16,0},{32,16},{48,32},{64,48},{80,64},{96,80},{112,96},{17,1},{33... | collective-permute-start | bytes 4808 | tf_op jit(solution)/shard_map/ppermute | solution.py:39
  58.7 0.8 collective-permute-done.4.vl_ref
  59.4 4.4 %collective-permute-done.5.vr_ref = f32[400,1]{1,0:T(8,128)S(1)} collective-permute-done((f32[400,1]{1,0:T(8,128)S(1)}, f32[400,1]{1,0:T(8,128)S(1)}, u32[]{:S(2)}, u32[]{:S(2)}) %collective-permute-start.5) | collective-permute-done | bytes 1632 | tf_op jit(solution)/shard_map/ppermute | solution.py:39
  63.8 0.7 copy-done.11
  64.5 0.1 copy-done.5
  64.6 0.7 copy-done.7
  65.2 2.9 %shard_map.69.z_ref = f32[400,128]{1,0:T(8,128)} custom-call(f32[1,128]{1,0:T(1,128)} %scatter.4.shift_ref, f32[400,400]{1,0:T(8,128)} %get-tuple-element.29.k_ref, f32[400,128]{1,0:T(8,128)} %shard_map.68.v_ref.w_ref, f32[400,128]{1,0:T(8,128)} %copy-done.5, f32[400,128]{1,0:T(8,128)} %copy-done.7, f32[400,1]{1,0:T(8,128)} %copy-done.9, f32[400,1]{1,0:T(8,128)} %copy-done.11), custom_call_target="tpu_custom_call" | custom-call | tf_op jit(solution)/shard_map/pallas_call | solution.py:199
  68.2 4.3 %collective-permute-start.6 = (f32[400,128]{1,0:T(8,128)}, f32[400,128]{1,0:T(8,128)S(1)}, u32[]{:S(2)}, u32[]{:S(2)}) collective-permute-start(f32[400,128]{1,0:T(8,128)} %shard_map.69.z_ref), channel_id=1, source_target_pairs={{0,1},{1,2},{2,3},{3,4},{4,5},{5,6},{6,7},{7,8},{8,9},{9,10},{10,1... | collective-permute-start | bytes 614408 | tf_op jit(solution)/shard_map/ppermute | solution.py:34
  72.5 1.3 %collective-permute-start.7 = (f32[400,128]{1,0:T(8,128)}, f32[400,128]{1,0:T(8,128)S(1)}, u32[]{:S(2)}, u32[]{:S(2)}) collective-permute-start(f32[400,128]{1,0:T(8,128)} %shard_map.69.z_ref), channel_id=1, source_target_pairs={{1,0},{2,1},{3,2},{4,3},{5,4},{6,5},{7,6},{8,7},{9,8},{10,9},{11,1... | collective-permute-start | bytes 614408 | tf_op jit(solution)/shard_map/ppermute | solution.py:39
  73.8 1.1 fusion.46
  74.9 2.0 %collective-permute-start.8 = (f32[400,1]{1,0:T(8,128)S(1)}, f32[400,1]{1,0:T(8,128)S(1)}, u32[]{:S(2)}, u32[]{:S(2)}) collective-permute-start(f32[400,1]{1,0:T(8,128)S(1)} %get-tuple-element.40), channel_id=1, source_target_pairs={{0,16},{16,32},{32,48},{48,64},{64,80},{80,96},{96,112},{1,17},{17... | collective-permute-start | bytes 4808 | tf_op jit(solution)/shard_map/ppermute | solution.py:34
  77.0 2.3 %collective-permute-start.9 = (f32[400,1]{1,0:T(8,128)S(1)}, f32[400,1]{1,0:T(8,128)S(1)}, u32[]{:S(2)}, u32[]{:S(2)}) collective-permute-start(f32[400,1]{1,0:T(8,128)S(1)} %get-tuple-element.39), channel_id=1, source_target_pairs={{16,0},{32,16},{48,32},{64,48},{80,64},{96,80},{112,96},{17,1},{33... | collective-permute-start | bytes 4808 | tf_op jit(solution)/shard_map/ppermute | solution.py:39
  79.3 0.4 collective-permute-done.8.zl_ref
  79.6 4.4 %collective-permute-done.9.zr_ref = f32[400,1]{1,0:T(8,128)S(1)} collective-permute-done((f32[400,1]{1,0:T(8,128)S(1)}, f32[400,1]{1,0:T(8,128)S(1)}, u32[]{:S(2)}, u32[]{:S(2)}) %collective-permute-start.9) | collective-permute-done | bytes 1632 | tf_op jit(solution)/shard_map/ppermute | solution.py:39
  84.1 0.7 copy-done.10
  84.7 0.1 copy-done.4
  84.8 0.7 copy-done.6
  85.5 3.2 %shard_map.70 = (f32[400,128]{1,0:T(8,128)}, f32[128,128]{1,0:T(8,128)}) custom-call(f32[1,128]{1,0:T(1,128)} %scatter.4.shift_ref, f32[400,400]{1,0:T(8,128)} %get-tuple-element.29.k_ref, f32[400,128]{1,0:T(8,128)} %copy-done, f32[400,128]{1,0:T(8,128)} %shard_map.68.v_ref.w_ref, f32[400,128]{1,0:T(8,128)} %shard_map.69.z_ref, f32[400,128]{1,0:T(8,128)} %copy-done.4, ...), custom_call_target="tpu_custom_call" | custom-call | tf_op jit(solution)/shard_map/pallas_call | solution.py:199
  88.6 23.2 %all_to_all.16 = f32[128,1,128]{2,1,0:T(1,128)} all-to-all(f32[128,1,128]{2,1,0:T(1,128)} %bitcast.68), channel_id=1, replica_groups=mesh['pair'=8,'tile'=16] {'pair','tile'}, dimensions={0} | all-to-all | bytes 131072 | tf_op jit(solution)/shard_map/all_to_all | solution.py:208
  111.8 2.3 %shard_map.71 = (f32[400,128]{1,0:T(8,128)}, f32[400,128]{1,0:T(8,128)}) custom-call(f32[1,128]{1,0:T(1,128)} %scatter.4.shift_ref, f32[128,128]{1,0:T(8,128)} %bitcast.67, f32[400,128]{1,0:T(8,128)} %copy-done, f32[400,128]{1,0:T(8,128)} %shard_map.68.v_ref.w_ref, f32[400,128]{1,0:T(8,128)} %shard_map.69.z_ref, f32[400,128]{1,0:T(8,128)} %get-tuple-element.19.y_ref), custom_call_target="tpu_custom_call" | custom-call | tf_op jit(solution)/shard_map/pallas_call | solution.py:199
  (41 shorter events, 0.3 us)
Async XLA Ops:
  3.1 0.7 copy-start.12
  3.1 0.7 copy-start.13
  4.9 22.6 %all-to-all-start = ((f32[8,250,136]{1,2,0:T(8,128)}), f32[8,250,136]{1,2,0:T(8,128)S(1)}, u32[]{:S(2)}, u32[]{:S(2)}) async-start(f32[8,250,136]{1,2,0:T(8,128)} %pad_maximum_fusion), calls=%async_computation | async-start | bytes 2228224 | tf_op jit(solution)/shard_map/all_to_all | solution.py:230
  31.1 8.4 %copy-start = (f32[400,128]{1,0:T(8,128)}, f32[400,128]{1,0:T(8,128)S(1)}, u32[]{:S(2)}) copy-start(f32[400,128]{1,0:T(8,128)S(1)} %slice.166.v_ref.r_ref) | copy-start | bytes 614404
  31.1 7.0 %copy-start.1 = (f32[400,400]{1,0:T(8,128)S(1)}, f32[400,400]{1,0:T(8,128)}, u32[]{:S(2)}) copy-start(f32[400,400]{1,0:T(8,128)} %constant.62.clone) | copy-start | bytes 1920004
  31.1 11.7 %collective-permute-start = (f32[400,128]{1,0:T(8,128)S(1)}, f32[400,128]{1,0:T(8,128)S(1)}, u32[]{:S(2)}, u32[]{:S(2)}) collective-permute-start(f32[400,128]{1,0:T(8,128)S(1)} %slice.166.v_ref.r_ref), channel_id=1, source_target_pairs={{0,1},{1,2},{2,3},{3,4},{4,5},{5,6},{6,7},{7,8},{8,9},{9,10},{10,1... | collective-permute-start | bytes 614408 | tf_op jit(solution)/shard_map/ppermute | solution.py:34
  34.4 8.4 %collective-permute-start.1 = (f32[400,128]{1,0:T(8,128)S(1)}, f32[400,128]{1,0:T(8,128)S(1)}, u32[]{:S(2)}, u32[]{:S(2)}) collective-permute-start(f32[400,128]{1,0:T(8,128)S(1)} %slice.166.v_ref.r_ref), channel_id=1, source_target_pairs={{1,0},{2,1},{3,2},{4,3},{5,4},{6,5},{7,6},{8,7},{9,8},{10,9},{11,1... | collective-permute-start | bytes 614408 | tf_op jit(solution)/shard_map/ppermute | solution.py:39
  37.6 3.3 %copy-start.14 = (f32[3]{0:T(128)S(1)}, f32[3]{0:T(128)}, u32[]{:S(2)}) copy-start(f32[3]{0:T(128)} %constant.63.clone) | copy-start | bytes 40
  42.8 0.7 copy-start.2
  42.8 0.7 copy-start.3
  46.5 17.3 %collective-permute-start.2 = (f32[400,128]{1,0:T(8,128)}, f32[400,128]{1,0:T(8,128)S(1)}, u32[]{:S(2)}, u32[]{:S(2)}) collective-permute-start(f32[400,128]{1,0:T(8,128)} %shard_map.68.v_ref.w_ref), channel_id=1, source_target_pairs={{0,1},{1,2},{2,3},{3,4},{4,5},{5,6},{6,7},{7,8},{8,9},{9,10},{10,1... | collective-permute-start | bytes 614408 | tf_op jit(solution)/shard_map/ppermute | solution.py:34
  50.5 13.3 %collective-permute-start.3 = (f32[400,128]{1,0:T(8,128)}, f32[400,128]{1,0:T(8,128)S(1)}, u32[]{:S(2)}, u32[]{:S(2)}) collective-permute-start(f32[400,128]{1,0:T(8,128)} %shard_map.68.v_ref.w_ref), channel_id=1, source_target_pairs={{1,0},{2,1},{3,2},{4,3},{5,4},{6,5},{7,6},{8,7},{9,8},{10,9},{11,1... | collective-permute-start | bytes 614408 | tf_op jit(solution)/shard_map/ppermute | solution.py:39
  52.9 6.5 %collective-permute-start.4 = (f32[400,1]{1,0:T(8,128)S(1)}, f32[400,1]{1,0:T(8,128)S(1)}, u32[]{:S(2)}, u32[]{:S(2)}) collective-permute-start(f32[400,1]{1,0:T(8,128)S(1)} %get-tuple-element.42), channel_id=1, source_target_pairs={{0,16},{16,32},{32,48},{48,64},{64,80},{80,96},{96,112},{1,17},{17... | collective-permute-start | bytes 4808 | tf_op jit(solution)/shard_map/ppermute | solution.py:34
  56.7 7.1 %collective-permute-start.5 = (f32[400,1]{1,0:T(8,128)S(1)}, f32[400,1]{1,0:T(8,128)S(1)}, u32[]{:S(2)}, u32[]{:S(2)}) collective-permute-start(f32[400,1]{1,0:T(8,128)S(1)} %get-tuple-element.41), channel_id=1, source_target_pairs={{16,0},{32,16},{48,32},{64,48},{80,64},{96,80},{112,96},{17,1},{33... | collective-permute-start | bytes 4808 | tf_op jit(solution)/shard_map/ppermute | solution.py:39
  59.4 4.4 %copy-start.9 = (f32[400,1]{1,0:T(8,128)}, f32[400,1]{1,0:T(8,128)S(1)}, u32[]{:S(2)}) copy-start(f32[400,1]{1,0:T(8,128)S(1)} %collective-permute-done.4.vl_ref) | copy-start | bytes 4804
  63.8 0.7 copy-start.11
  63.8 0.7 copy-start.5
  64.6 0.7 copy-start.7
  68.2 15.8 %collective-permute-start.6 = (f32[400,128]{1,0:T(8,128)}, f32[400,128]{1,0:T(8,128)S(1)}, u32[]{:S(2)}, u32[]{:S(2)}) collective-permute-start(f32[400,128]{1,0:T(8,128)} %shard_map.69.z_ref), channel_id=1, source_target_pairs={{0,1},{1,2},{2,3},{3,4},{4,5},{5,6},{6,7},{7,8},{8,9},{9,10},{10,1... | collective-permute-start | bytes 614408 | tf_op jit(solution)/shard_map/ppermute | solution.py:34
  72.5 11.6 %collective-permute-start.7 = (f32[400,128]{1,0:T(8,128)}, f32[400,128]{1,0:T(8,128)S(1)}, u32[]{:S(2)}, u32[]{:S(2)}) collective-permute-start(f32[400,128]{1,0:T(8,128)} %shard_map.69.z_ref), channel_id=1, source_target_pairs={{1,0},{2,1},{3,2},{4,3},{5,4},{6,5},{7,6},{8,7},{9,8},{10,9},{11,1... | collective-permute-start | bytes 614408 | tf_op jit(solution)/shard_map/ppermute | solution.py:39
  74.9 4.7 %collective-permute-start.8 = (f32[400,1]{1,0:T(8,128)S(1)}, f32[400,1]{1,0:T(8,128)S(1)}, u32[]{:S(2)}, u32[]{:S(2)}) collective-permute-start(f32[400,1]{1,0:T(8,128)S(1)} %get-tuple-element.40), channel_id=1, source_target_pairs={{0,16},{16,32},{32,48},{48,64},{64,80},{80,96},{96,112},{1,17},{17... | collective-permute-start | bytes 4808 | tf_op jit(solution)/shard_map/ppermute | solution.py:34
  77.0 7.1 %collective-permute-start.9 = (f32[400,1]{1,0:T(8,128)S(1)}, f32[400,1]{1,0:T(8,128)S(1)}, u32[]{:S(2)}, u32[]{:S(2)}) collective-permute-start(f32[400,1]{1,0:T(8,128)S(1)} %get-tuple-element.39), channel_id=1, source_target_pairs={{16,0},{32,16},{48,32},{64,48},{80,64},{96,80},{112,96},{17,1},{33... | collective-permute-start | bytes 4808 | tf_op jit(solution)/shard_map/ppermute | solution.py:39
  79.6 4.4 %copy-start.8 = (f32[400,1]{1,0:T(8,128)}, f32[400,1]{1,0:T(8,128)S(1)}, u32[]{:S(2)}) copy-start(f32[400,1]{1,0:T(8,128)S(1)} %collective-permute-done.8.zl_ref) | copy-start | bytes 4804
  84.0 0.7 copy-start.10
  84.0 0.7 copy-start.4
  84.8 0.7 copy-start.6

commit v11 on v8

--- a/solution.py
+++ b/solution.py
@@ -194,18 +194,18 @@
 def body(phase, incidence, pair_weight):
     groups = lax.axis_size("pair")
     cols = phase.shape[2] // groups
-    padded = jnp.pad(phase[:, 0, :], ((0, 0), (1, 1)))
-    windows = jnp.stack([padded[:, j * cols : j * cols + cols + 2] for j in range(groups)])
+    padded = jnp.pad(phase[:, 0, :], ((0, 0), (2, 2)))
+    windows = jnp.stack([padded[:, j * cols : j * cols + cols + 4] for j in range(groups)])
     meta = jnp.stack(
         [incidence[:, 0].astype(jnp.float32), incidence[:, 1].astype(jnp.float32), pair_weight], axis=1
     )
-    meta = jnp.pad(meta, ((0, 0), (0, 3)))
+    meta = jnp.pad(meta, ((0, 0), (0, 1)))
     chunks = jnp.concatenate([windows, jnp.broadcast_to(meta, (groups,) + meta.shape)], axis=2)
     got = lax.all_to_all(chunks, "pair", 0, 0, tiled=True).reshape(-1, chunks.shape[2])
-    values = got[:, : cols + 2]
-    earlier = got[:, cols + 2 : cols + 3]
-    later = got[:, cols + 3 : cols + 4]
-    weight = got[:, cols + 4 : cols + 5]
+    values = got[:, : cols + 4]
+    earlier = got[:, cols + 4 : cols + 5]
+    later = got[:, cols + 5 : cols + 6]
+    weight = got[:, cols + 6 : cols + 7]
     dates = jnp.arange(DATES, dtype=jnp.float32)
     network = ((dates[None, :] == later).astype(jnp.float32) - (dates[None, :] == earlier).astype(jnp.float32)).astype(
         jnp.bfloat16
@@ -225,19 +225,27 @@
     start_hot = (dates[None, :] == earlier).astype(jnp.float32)
     span_weights = jnp.einsum("kt,kd->td", start_hot, span_hot * weight, precision=HIGHEST)
     matrix = normal_matrix(span_weights)
-    residual = right_wide[:, 1:-1]
-    residual_halo = (
-        from_prev(residual, "tile"),
-        from_next(residual, "tile"),
-        right_wide[:, :1],
-        right_wide[:, -1:],
-    )
+    residual = right_wide[:, 2:-2]
+    outer = jnp.concatenate([right_wide[:, 1], right_wide[:, -2], jnp.zeros((8 * 128 - 2 * DATES,), jnp.float32)])
+    payload = jnp.concatenate([residual, outer.reshape(8, 128)], axis=0)
+    above_wide = from_prev(payload, "tile")
+    below_wide = from_next(payload, "tile")
+    residual_halo = (above_wide[:DATES], below_wide[:DATES], right_wide[:, 1:2], right_wide[:, -2:-1])
+    above_outer = above_wide[DATES:].reshape(-1)
+    below_outer = below_wide[DATES:].reshape(-1)
+    edge = jnp.stack([right_wide[:, 1], right_wide[:, -2]], axis=1)
+    edge_rows = jnp.stack([above_outer[:DATES] + below_outer[:DATES], above_outer[DATES : 2 * DATES] + below_outer[DATES : 2 * DATES]], axis=1)
+    edge_cols = jnp.stack([right_wide[:, 0] + right_wide[:, 2], right_wide[:, -3] + right_wide[:, -1]], axis=1)
+    edge_image = jnp.dot(matrix, edge, precision=HIGHEST) - spatial_weight * (edge_rows + edge_cols)
+    place = lax.axis_index("pair")
+    inside = jnp.stack([place > 0, place < groups - 1]).astype(jnp.float32)
+    edge_image = edge_image * inside[None, :]
     count = lax.axis_size("pair") * lax.axis_size("tile")
     field = residual.shape
     lanes = 128
     send_shape = (count, lanes)
     (w0,) = call(image_kernel, [field], matrix, residual, *residual_halo)
-    w0_halo = exchange_rows_cols(w0)
+    w0_halo = (from_prev(w0, "tile"), from_next(w0, "tile"), edge_image[:, 0:1], edge_image[:, 1:2])
     z0, send = call(gram_kernel, [field, send_shape], matrix, residual, w0, *w0_halo)
     got = reduce_all(send)
     z0_halo = exchange_rows_cols(z0)

time: 125 us -> 120 us (0.960)
  blocking collectives: 43.4 us -> 20.8 us
  waiting for transfers between devices: 5.51 us -> 19.3 us
  starting transfers between devices: 43.5 us -> 45.1 us
  other arithmetic: 4.27 us -> 5.56 us
    all_to_all x1 -> x0, blocking collectives: 22.7 us -> none  [body(): lax.all_to_all(chunks, 'pair', 0, 0, tiled=True)]
    all_to_all x0 -> x1, waiting for transfers between devices: none -> 15.7 us  [body(): lax.all_to_all(chunks, 'pair', 0, 0, tiled=True)]
    all_to_all x0 -> x1, starting transfers between devices: none -> 6.81 us  [body(): lax.all_to_all(chunks, 'pair', 0, 0, tiled=True)]
    ppermute x5 -> x4, starting transfers between devices: 10.7 us -> 6.96 us  [from_next(): return lax.ppermute(cells, axis, [(i + 1, i) for i in range(count - 1)])]
    slice x2 -> x11, local copies, waits for them, and re-layouts: 0.92 us -> 3.54 us  [the longest x1 0.82 us: body(): edge_image[:, 1:2]]
    ppermute x5 -> x4, waiting for transfers between devices: 3.51 us -> 2.02 us  [from_next(): return lax.ppermute(cells, axis, [(i + 1, i) for i in range(count - 1)])]
    ppermute x5 -> x4, starting transfers between devices: 16.7 us -> 15.2 us  [from_prev(): return lax.ppermute(cells, axis, [(i, i + 1) for i in range(count - 1)])]
    unnamed x36 -> x32, local copies, waits for them, and re-layouts: 5.98 us -> 4.58 us
  transfers between devices with their start and end apart: 11 -> 10, of which waited for: 5 -> 5; matrix products, arithmetic and copies ran while one was open for 6% -> 8% of each run, Pallas kernels for 0% -> 0%
where the time goes in v11:
time: 120 us; the launch traced here: 119 us
  starting transfers between devices  45.1 us (38%)
  blocking collectives  20.8 us (17%)
  waiting for transfers between devices  19.3 us (16%)
  Pallas kernels  12.4 us (10%)
  local copies, waits for them, and re-layouts  10.3 us (9%)
  other arithmetic  5.56 us (5%)
  matrix products  4.96 us (4%)
    all_to_all x1, blocking collectives, reduce_all(): return lax.all_to_all(send, ('pair', 'tile'), 0, 0, tiled=True)  20.8 us
    all_to_all x1, starting transfers between devices, reduce_all(): return lax.all_to_all(send, ('pair', 'tile'), 0, 0, tiled=True)  16 us
    all_to_all x1, waiting for transfers between devices, body(): lax.all_to_all(chunks, 'pair', 0, 0, tiled=True)  15.7 us
    ppermute x4, starting transfers between devices, from_prev(): return lax.ppermute(cells, axis, [(i, i + 1) for i in range(count - 1)])  15.2 us
    pallas_call x4, Pallas kernels, call(): pl.pallas_call(kernel, out_shape=[jax.ShapeDtypeStruct(s, jnp.float32) fo...  12.4 us
    ppermute x4, starting transfers between devices, from_next(): return lax.ppermute(cells, axis, [(i + 1, i) for i in range(count - 1)])  6.96 us
    all_to_all x1, starting transfers between devices, body(): lax.all_to_all(chunks, 'pair', 0, 0, tiled=True)  6.81 us
    unnamed x32, local copies, waits for them, and re-layouts  4.58 us
  transfers between devices with their start and end apart: 10, of which 5 were waited for; matrix products, arithmetic and copies ran while one was open for 8% of the time, Pallas kernels for 0%

profile of v11, /device:TPU:1, one launch (start us, length us, event | category | flops | bytes accessed | tf_op | source)
XLA Modules:
  0.0 119.3 jit_solution(13983581549467277571)
XLA Ops:
  0.6 0.8 slice_convert_fusion.1
  1.4 2.4 %copy.41 = f32[250,1,1024]{0,2,1:T(8,128)S(1)} copy(f32[250,1,1024]{2,1,0:T(1,128)} %param.4) | data formatting | bytes 2048000 | tf_op args[0]
  3.9 0.6 copy-done.11
  4.5 1.1 pad_maximum_fusion
  5.6 6.8 %all-to-all-start = ((f32[8,250,136]{1,2,0:T(8,128)}), f32[8,250,136]{1,2,0:T(8,128)S(1)}, u32[]{:S(2)}, u32[]{:S(2)}) async-start(f32[8,250,136]{1,2,0:T(8,128)} %pad_maximum_fusion), calls=%async_computation | async-start | bytes 2228224 | tf_op jit(solution)/shard_map/all_to_all | solution.py:204
  12.5 15.7 %all-to-all-done = f32[8,250,136]{1,2,0:T(8,128)S(1)} async-done(((f32[8,250,136]{1,2,0:T(8,128)}), f32[8,250,136]{1,2,0:T(8,128)S(1)}, u32[]{:S(2)}, u32[]{:S(2)}) %all-to-all-start) | async-done | bytes 1088032 | tf_op jit(solution)/shard_map/all_to_all | solution.py:204
  28.3 0.4 copy.42
  28.6 0.5 reshape.41
  29.2 0.3 reduce-precision_convert_fusion.1
  29.5 2.0 %fusion.1 = f32[400,396]{1,0:T(8,128)S(1)} fusion(f32[2000]{0:T(1024)S(1)} %bitcast.109, f32[2000]{0:T(1024)S(1)} %bitcast.107, bf16[2000,132]{0,1:T(8,128)(2,1)S(1)} %get-tuple-element.35, bf16[2000,132]{0,1:T(8,128)(2,1)S(1)} %get-tuple-element.36, bf16[2000,132]{0,1:T(8,128)(2,1)S(1)} %get-tuple-element.34), kind=kOutput, calls=%fused_computation.4 | convolution fusion | flops 643152000 | bytes 2233600 | tf_op jit(solution)/shard_map/kt,kc->tc/dot_general | solution.py:220
  31.4 0.3 slice_add_fusion
  31.7 0.1 slice.202.v_ref.r_ref
  31.9 0.5 slice_reduce_fusion.1
  32.6 1.4 %collective-permute-start.1 = (f32[408,128]{1,0:T(8,128)S(1)}, f32[408,128]{1,0:T(8,128)S(1)}, u32[]{:S(2)}, u32[]{:S(2)}) collective-permute-start(f32[408,128]{1,0:T(8,128)S(1)} %pad_maximum_fusion.1), channel_id=1, source_target_pairs={{1,0},{2,1},{3,2},{4,3},{5,4},{6,5},{7,6},{8,7},{9,8},{10,9},{11,1... | collective-permute-start | bytes 626696 | tf_op jit(solution)/shard_map/ppermute | solution.py:36
  34.0 4.0 %collective-permute-start = (f32[408,128]{1,0:T(8,128)S(1)}, f32[408,128]{1,0:T(8,128)S(1)}, u32[]{:S(2)}, u32[]{:S(2)}) collective-permute-start(f32[408,128]{1,0:T(8,128)S(1)} %pad_maximum_fusion.1), channel_id=1, source_target_pairs={{0,1},{1,2},{2,3},{3,4},{4,5},{5,6},{6,7},{7,8},{8,9},{9,10},{10,1... | collective-permute-start | bytes 626696 | tf_op jit(solution)/shard_map/ppermute | solution.py:31
  38.0 1.9 %fusion = f32[400,8]{0,1:T(8,128)S(1)} fusion(f32[2000]{0:T(1024)S(1)} %bitcast.108, f32[2000]{0:T(1024)S(1)} %bitcast.105, f32[2000]{0:T(1024)S(1)} %bitcast.106), kind=kOutput, calls=%fused_computation.3 | convolution fusion | flops 77632000 | bytes 36800 | tf_op jit(solution)/shard_map/kt,kd->td/dot_general | solution.py:226
  39.9 0.6 fusion.31
  40.5 2.2 %add_add_fusion.k_ref = f32[400,400]{1,0:T(8,128)} fusion(f32[400,400]{1,0:T(8,128)S(1)} %copy-done.3, f32[400]{0:T(512)S(1)} %negate_add_fusion, f32[400]{0:T(512)S(1)} %bitcast.87, f32[400]{0:T(512)S(1)} %bitcast.90, f32[400]{0:T(512)S(1)} %bitcast.93, f32[400]{0:T(512)S(1)} %bitcast.96, f32[400]{0:T(512)S(1)} %bitcast.99, f32[400]{0:T(512)S(1)} %bitcast.102, ...), kind=kLoop, calls=%fused_computation.26 | loop fusion | flops 7520000 | bytes 1292800 | tf_op jit(solution)/shard_map/add | solution.py:75
  42.8 0.1 copy.48
  42.9 0.1 copy.51
  43.0 0.1 copy.50
  43.1 0.1 copy.47
  43.3 0.1 copy.46
  43.4 0.7 slice.206.vd_ref.rd_ref
  44.1 0.7 slice.205.vu_ref.ru_ref
  44.8 3.0 %shard_map.59.w_ref = f32[400,128]{1,0:T(8,128)} custom-call(f32[400,400]{1,0:T(8,128)} %add_add_fusion.k_ref, f32[400,128]{1,0:T(8,128)} %copy-done, f32[400,128]{1,0:T(8,128)} %slice.205.vu_ref.ru_ref, f32[400,128]{1,0:T(8,128)} %slice.206.vd_ref.rd_ref, f32[400,1]{1,0:T(8,128)} %copy-done.2, f32[400,1]{1,0:T(8,128)} %copy-done.1), custom_call_target="tpu_custom_call" | custom-call | tf_op jit(solution)/shard_map/pallas_call | solution.py:173
  47.8 1.3 %collective-permute-start.3 = (f32[400,128]{1,0:T(8,128)}, f32[400,128]{1,0:T(8,128)S(1)}, u32[]{:S(2)}, u32[]{:S(2)}) collective-permute-start(f32[400,128]{1,0:T(8,128)} %shard_map.59.w_ref), channel_id=1, source_target_pairs={{1,0},{2,1},{3,2},{4,3},{5,4},{6,5},{7,6},{8,7},{9,8},{10,9},{11,1... | collective-permute-start | bytes 614408 | tf_op jit(solution)/shard_map/ppermute | solution.py:36
  49.1 4.0 %collective-permute-start.2 = (f32[400,128]{1,0:T(8,128)}, f32[400,128]{1,0:T(8,128)S(1)}, u32[]{:S(2)}, u32[]{:S(2)}) collective-permute-start(f32[400,128]{1,0:T(8,128)} %shard_map.59.w_ref), channel_id=1, source_target_pairs={{0,1},{1,2},{2,3},{3,4},{4,5},{5,6},{6,7},{7,8},{8,9},{9,10},{10,1... | collective-permute-start | bytes 614408 | tf_op jit(solution)/shard_map/ppermute | solution.py:31
  53.3 0.1 copy.54
  53.4 1.1 fusion.10
  54.6 0.8 fusion.51
  55.4 0.8 collective-permute-done.2.wu_ref
  56.1 0.7 copy-done.5
  56.8 3.2 %shard_map.60 = (f32[400,128]{1,0:T(8,128)}, f32[128,128]{1,0:T(8,128)}) custom-call(f32[400,400]{1,0:T(8,128)} %add_add_fusion.k_ref, f32[400,128]{1,0:T(8,128)} %copy-done, f32[400,128]{1,0:T(8,128)} %shard_map.59.w_ref, f32[400,128]{1,0:T(8,128)} %copy-done.5, f32[400,128]{1,0:T(8,128)} %copy-done.4, f32[400,1]{1,0:T(8,128)} %get-tuple-element.50.wl_ref, ...), custom_call_target="tpu_custom_call" | custom-call | tf_op jit(solution)/shard_map/pallas_call | solution.py:173
  60.0 1.3 %collective-permute-start.5 = (f32[400,128]{1,0:T(8,128)}, f32[400,128]{1,0:T(8,128)S(1)}, u32[]{:S(2)}, u32[]{:S(2)}) collective-permute-start(f32[400,128]{1,0:T(8,128)} %get-tuple-element.14.z_ref), channel_id=1, source_target_pairs={{1,0},{2,1},{3,2},{4,3},{5,4},{6,5},{7,6},{8,7},{9,8},{10,9},{11,1... | collective-permute-start | bytes 614408 | tf_op jit(solution)/shard_map/ppermute | solution.py:36
  61.3 4.6 %collective-permute-start.4 = (f32[400,128]{1,0:T(8,128)}, f32[400,128]{1,0:T(8,128)S(1)}, u32[]{:S(2)}, u32[]{:S(2)}) collective-permute-start(f32[400,128]{1,0:T(8,128)} %get-tuple-element.14.z_ref), channel_id=1, source_target_pairs={{0,1},{1,2},{2,3},{3,4},{4,5},{5,6},{6,7},{7,8},{8,9},{9,10},{10,1... | collective-permute-start | bytes 614408 | tf_op jit(solution)/shard_map/ppermute | solution.py:31
  66.0 16.0 %all-to-all-start.1 = ((f32[128,1,128]{2,1,0:T(1,128)}), f32[128,1,128]{2,1,0:T(1,128)S(1)}, u32[]{:S(2)}, u32[]{:S(2)}) async-start(f32[128,1,128]{2,1,0:T(1,128)} %bitcast.81), calls=%async_computation.1 | async-start | bytes 131072 | tf_op jit(solution)/shard_map/all_to_all | solution.py:182
  82.0 1.1 fusion.50
  83.2 3.0 %collective-permute-start.7 = (f32[400,1]{1,0:T(8,128)S(1)}, f32[400,1]{1,0:T(8,128)S(1)}, u32[]{:S(2)}, u32[]{:S(2)}) collective-permute-start(f32[400,1]{1,0:T(8,128)S(1)} %get-tuple-element.47), channel_id=1, source_target_pairs={{16,0},{32,16},{48,32},{64,48},{80,64},{96,80},{112,96},{17,1},{33... | collective-permute-start | bytes 4808 | tf_op jit(solution)/shard_map/ppermute | solution.py:36
  86.1 2.6 %collective-permute-start.6 = (f32[400,1]{1,0:T(8,128)S(1)}, f32[400,1]{1,0:T(8,128)S(1)}, u32[]{:S(2)}, u32[]{:S(2)}) collective-permute-start(f32[400,1]{1,0:T(8,128)S(1)} %get-tuple-element.48), channel_id=1, source_target_pairs={{0,16},{16,32},{32,48},{48,64},{64,80},{80,96},{96,112},{1,17},{17... | collective-permute-start | bytes 4808 | tf_op jit(solution)/shard_map/ppermute | solution.py:31
  88.8 2.0 %collective-permute-done.7.zr_ref = f32[400,1]{1,0:T(8,128)S(1)} collective-permute-done((f32[400,1]{1,0:T(8,128)S(1)}, f32[400,1]{1,0:T(8,128)S(1)}, u32[]{:S(2)}, u32[]{:S(2)}) %collective-permute-start.7) | collective-permute-done | bytes 1632 | tf_op jit(solution)/shard_map/ppermute | solution.py:36
  90.8 0.7 collective-permute-done.6.zl_ref
  91.4 0.1 all-to-all-done.1
  91.6 0.5 copy-done.10
  92.2 0.1 copy-done.7
  92.4 4.0 %shard_map.61 = (f32[400,128]{1,0:T(8,128)}, f32[400,128]{1,0:T(8,128)}, f32[400,128]{1,0:T(8,128)}, f32[400,128]{1,0:T(8,128)}, f32[400,128]{1,0:T(8,128)}, /*index=5*/f32[128,128]{1,0:T(8,128)}, f32[1,128]{1,0:T(1,128)}) custom-call(f32[128,128]{1,0:T(8,128)} %bitcast.79, f32[400,400]{1,0:T(8,128)} %add_add_fusion.k_ref, f32[400,128]{1,0:T(8,128)} %copy-done, ...), custom_call_target="tpu_custom_call" | custom-call | tf_op jit(solution)/shard_map/pallas_call | solution.py:173
  96.3 20.8 %all_to_all.27 = f32[128,1,128]{2,1,0:T(1,128)} all-to-all(f32[128,1,128]{2,1,0:T(1,128)} %bitcast.82), channel_id=1, replica_groups=mesh['pair'=8,'tile'=16] {'pair','tile'}, dimensions={0} | all-to-all | bytes 131072 | tf_op jit(solution)/shard_map/all_to_all | solution.py:182
  117.1 2.2 %shard_map.62 = (f32[400,128]{1,0:T(8,128)}, f32[400,128]{1,0:T(8,128)}) custom-call(f32[128,128]{1,0:T(8,128)} %bitcast.80, f32[1,128]{1,0:T(1,128)} %get-tuple-element.16.scal_ref, f32[400,128]{1,0:T(8,128)} %get-tuple-element.17.r_ref, f32[400,128]{1,0:T(8,128)} %get-tuple-element.18.p_ref, f32[400,128]{1,0:T(8,128)} %get-tuple-element.19.q_ref, ...), custom_call_target="tpu_custom_call" | custom-call | tf_op jit(solution)/shard_map/pallas_call | solution.py:173
  (49 shorter events, 0.8 us)
Async XLA Ops:
  3.8 0.7 copy-start.11
  5.6 22.6 %all-to-all-start = ((f32[8,250,136]{1,2,0:T(8,128)}), f32[8,250,136]{1,2,0:T(8,128)S(1)}, u32[]{:S(2)}, u32[]{:S(2)}) async-start(f32[8,250,136]{1,2,0:T(8,128)} %pad_maximum_fusion), calls=%async_computation | async-start | bytes 2228224 | tf_op jit(solution)/shard_map/all_to_all | solution.py:204
  31.8 0.7 copy-start
  32.4 10.8 %copy-start.1 = (f32[400,1]{1,0:T(8,128)}, f32[400,1]{1,0:T(8,128)S(1)}, u32[]{:S(2)}) copy-start(f32[400,1]{1,0:T(8,128)S(1)} %get-tuple-element.45.vr_ref.rr_ref) | copy-start | bytes 4804
  32.4 10.9 %copy-start.2 = (f32[400,1]{1,0:T(8,128)}, f32[400,1]{1,0:T(8,128)S(1)}, u32[]{:S(2)}) copy-start(f32[400,1]{1,0:T(8,128)S(1)} %get-tuple-element.46.vl_ref.rl_ref) | copy-start | bytes 4804
  32.5 7.9 %copy-start.3 = (f32[400,400]{1,0:T(8,128)S(1)}, f32[400,400]{1,0:T(8,128)}, u32[]{:S(2)}) copy-start(f32[400,400]{1,0:T(8,128)} %constant.35.clone) | copy-start | bytes 1920004
  32.6 10.9 %collective-permute-start.1 = (f32[408,128]{1,0:T(8,128)S(1)}, f32[408,128]{1,0:T(8,128)S(1)}, u32[]{:S(2)}, u32[]{:S(2)}) collective-permute-start(f32[408,128]{1,0:T(8,128)S(1)} %pad_maximum_fusion.1), channel_id=1, source_target_pairs={{1,0},{2,1},{3,2},{4,3},{5,4},{6,5},{7,6},{8,7},{9,8},{10,9},{11,1... | collective-permute-start | bytes 626696 | tf_op jit(solution)/shard_map/ppermute | solution.py:36
  34.0 10.1 %collective-permute-start = (f32[408,128]{1,0:T(8,128)S(1)}, f32[408,128]{1,0:T(8,128)S(1)}, u32[]{:S(2)}, u32[]{:S(2)}) collective-permute-start(f32[408,128]{1,0:T(8,128)S(1)} %pad_maximum_fusion.1), channel_id=1, source_target_pairs={{0,1},{1,2},{2,3},{3,4},{4,5},{5,6},{6,7},{7,8},{8,9},{9,10},{10,1... | collective-permute-start | bytes 626696 | tf_op jit(solution)/shard_map/ppermute | solution.py:31
  47.8 7.5 %collective-permute-start.3 = (f32[400,128]{1,0:T(8,128)}, f32[400,128]{1,0:T(8,128)S(1)}, u32[]{:S(2)}, u32[]{:S(2)}) collective-permute-start(f32[400,128]{1,0:T(8,128)} %shard_map.59.w_ref), channel_id=1, source_target_pairs={{1,0},{2,1},{3,2},{4,3},{5,4},{6,5},{7,6},{8,7},{9,8},{10,9},{11,1... | collective-permute-start | bytes 614408 | tf_op jit(solution)/shard_map/ppermute | solution.py:36
  49.1 7.0 %collective-permute-start.2 = (f32[400,128]{1,0:T(8,128)}, f32[400,128]{1,0:T(8,128)S(1)}, u32[]{:S(2)}, u32[]{:S(2)}) collective-permute-start(f32[400,128]{1,0:T(8,128)} %shard_map.59.w_ref), channel_id=1, source_target_pairs={{0,1},{1,2},{2,3},{3,4},{4,5},{5,6},{6,7},{7,8},{8,9},{9,10},{10,1... | collective-permute-start | bytes 614408 | tf_op jit(solution)/shard_map/ppermute | solution.py:31
  55.4 0.8 copy-start.4
  56.1 0.7 copy-start.5
  60.0 31.6 %collective-permute-start.5 = (f32[400,128]{1,0:T(8,128)}, f32[400,128]{1,0:T(8,128)S(1)}, u32[]{:S(2)}, u32[]{:S(2)}) collective-permute-start(f32[400,128]{1,0:T(8,128)} %get-tuple-element.14.z_ref), channel_id=1, source_target_pairs={{1,0},{2,1},{3,2},{4,3},{5,4},{6,5},{7,6},{8,7},{9,8},{10,9},{11,1... | collective-permute-start | bytes 614408 | tf_op jit(solution)/shard_map/ppermute | solution.py:36
  61.3 30.3 %collective-permute-start.4 = (f32[400,128]{1,0:T(8,128)}, f32[400,128]{1,0:T(8,128)S(1)}, u32[]{:S(2)}, u32[]{:S(2)}) collective-permute-start(f32[400,128]{1,0:T(8,128)} %get-tuple-element.14.z_ref), channel_id=1, source_target_pairs={{0,1},{1,2},{2,3},{3,4},{4,5},{5,6},{6,7},{7,8},{8,9},{9,10},{10,1... | collective-permute-start | bytes 614408 | tf_op jit(solution)/shard_map/ppermute | solution.py:31
  66.0 25.6 %all-to-all-start.1 = ((f32[128,1,128]{2,1,0:T(1,128)}), f32[128,1,128]{2,1,0:T(1,128)S(1)}, u32[]{:S(2)}, u32[]{:S(2)}) async-start(f32[128,1,128]{2,1,0:T(1,128)} %bitcast.81), calls=%async_computation.1 | async-start | bytes 131072 | tf_op jit(solution)/shard_map/all_to_all | solution.py:182
  83.2 7.6 %collective-permute-start.7 = (f32[400,1]{1,0:T(8,128)S(1)}, f32[400,1]{1,0:T(8,128)S(1)}, u32[]{:S(2)}, u32[]{:S(2)}) collective-permute-start(f32[400,1]{1,0:T(8,128)S(1)} %get-tuple-element.47), channel_id=1, source_target_pairs={{16,0},{32,16},{48,32},{64,48},{80,64},{96,80},{112,96},{17,1},{33... | collective-permute-start | bytes 4808 | tf_op jit(solution)/shard_map/ppermute | solution.py:36
  86.1 5.3 %collective-permute-start.6 = (f32[400,1]{1,0:T(8,128)S(1)}, f32[400,1]{1,0:T(8,128)S(1)}, u32[]{:S(2)}, u32[]{:S(2)}) collective-permute-start(f32[400,1]{1,0:T(8,128)S(1)} %get-tuple-element.48), channel_id=1, source_target_pairs={{0,16},{16,32},{32,48},{48,64},{64,80},{80,96},{96,112},{1,17},{17... | collective-permute-start | bytes 4808 | tf_op jit(solution)/shard_map/ppermute | solution.py:31
  90.8 0.8 copy-start.9
  91.4 0.7 copy-start.10
  91.6 0.6 copy-start.6
  91.6 0.7 copy-start.7
  91.6 0.8 copy-start.8

commit v12 on v11

--- a/solution.py
+++ b/solution.py
@@ -107,8 +107,12 @@
     send_ref[...] = jnp.broadcast_to(row, send_ref.shape)
 
 
+def head(ref):
+    return ref[0:DATES]
+
+
 def image_kernel(k_ref, v_ref, vu_ref, vd_ref, vl_ref, vr_ref, w_out):
-    w_out[...] = operate(k_ref[...], v_ref[...], vu_ref[...], vd_ref[...], vl_ref[...], vr_ref[...])
+    w_out[...] = operate(k_ref[...], v_ref[...], head(vu_ref), head(vd_ref), vl_ref[...], vr_ref[...])
 
 
 def gram_kernel(k_ref, r_ref, w_ref, wu_ref, wd_ref, wl_ref, wr_ref, z_out, send_ref):
@@ -143,7 +147,7 @@
     r_out[...] = r
     halo = []
     for hr, hw, hz in zip((ru_ref, rd_ref, rl_ref, rr_ref), (wu_ref, wd_ref, wl_ref, wr_ref), (zu_ref, zd_ref, zl_ref, zr_ref)):
-        halo.append((hr[...] - alpha_first * hw[...]) - alpha * (a * hw[...] + b * hz[...]))
+        halo.append((head(hr) - alpha_first * hw[...]) - alpha * (a * hw[...] + b * hz[...]))
     w = operate(k_ref[...], r, *halo)
     w_out[...] = w
     send_buffer(send_ref, [r * r, r * w, r * q, p * w, p * q])
@@ -230,7 +234,7 @@
     payload = jnp.concatenate([residual, outer.reshape(8, 128)], axis=0)
     above_wide = from_prev(payload, "tile")
     below_wide = from_next(payload, "tile")
-    residual_halo = (above_wide[:DATES], below_wide[:DATES], right_wide[:, 1:2], right_wide[:, -2:-1])
+    residual_halo = (above_wide, below_wide, right_wide[:, 1:2], right_wide[:, -2:-1])
     above_outer = above_wide[DATES:].reshape(-1)
     below_outer = below_wide[DATES:].reshape(-1)
     edge = jnp.stack([right_wide[:, 1], right_wide[:, -2]], axis=1)

time: 120 us -> 120 us (level)
  local copies, waits for them, and re-layouts: 10.3 us -> 11.6 us
    slice x2 -> x0, local copies, waits for them, and re-layouts: 1.39 us -> none  [the longest x1 0.7 us: body(): below_wide[:DATES]]
    unnamed x32 -> x36, local copies, waits for them, and re-layouts: 4.58 us -> 5.93 us
  transfers between devices with their start and end apart: 10 -> 10, of which waited for: 5 -> 4; matrix products, arithmetic and copies ran while one was open for 8% -> 9% of each run, Pallas kernels for 0% -> 0%
where the time goes in v12:
time: 120 us; the launch traced here: 119 us
  starting transfers between devices  44.4 us (37%)
  blocking collectives  20.7 us (17%)
  waiting for transfers between devices  18.6 us (16%)
  Pallas kernels  12.4 us (10%)
  local copies, waits for them, and re-layouts  11.6 us (10%)
  other arithmetic  5.56 us (5%)
  matrix products  4.95 us (4%)
    all_to_all x1, blocking collectives, reduce_all(): return lax.all_to_all(send, ('pair', 'tile'), 0, 0, tiled=True)  20.7 us
    all_to_all x1, starting transfers between devices, reduce_all(): return lax.all_to_all(send, ('pair', 'tile'), 0, 0, tiled=True)  16 us
    all_to_all x1, waiting for transfers between devices, body(): lax.all_to_all(chunks, 'pair', 0, 0, tiled=True)  15.7 us
    ppermute x4, starting transfers between devices, from_prev(): return lax.ppermute(cells, axis, [(i, i + 1) for i in range(count - 1)])  14.6 us
    pallas_call x4, Pallas kernels, call(): pl.pallas_call(kernel, out_shape=[jax.ShapeDtypeStruct(s, jnp.float32) fo...  12.4 us
    ppermute x4, starting transfers between devices, from_next(): return lax.ppermute(cells, axis, [(i + 1, i) for i in range(count - 1)])  6.96 us
    all_to_all x1, starting transfers between devices, body(): lax.all_to_all(chunks, 'pair', 0, 0, tiled=True)  6.81 us
    unnamed x36, local copies, waits for them, and re-layouts  5.93 us
  transfers between devices with their start and end apart: 10, of which 4 were waited for; matrix products, arithmetic and copies ran while one was open for 9% of the time, Pallas kernels for 0%

profile of v12, /device:TPU:1, one launch (start us, length us, event | category | flops | bytes accessed | tf_op | source)
XLA Modules:
  0.0 119.2 jit_solution(8244912132005035860)
XLA Ops:
  0.6 0.8 slice_convert_fusion.1
  1.4 2.4 %copy.41 = f32[250,1,1024]{0,2,1:T(8,128)S(1)} copy(f32[250,1,1024]{2,1,0:T(1,128)} %param.4) | data formatting | bytes 2048000 | tf_op args[0]
  3.9 0.6 copy-done.13
  4.5 1.1 pad_maximum_fusion
  5.6 6.8 %all-to-all-start = ((f32[8,250,136]{1,2,0:T(8,128)}), f32[8,250,136]{1,2,0:T(8,128)S(1)}, u32[]{:S(2)}, u32[]{:S(2)}) async-start(f32[8,250,136]{1,2,0:T(8,128)} %pad_maximum_fusion), calls=%async_computation | async-start | bytes 2228224 | tf_op jit(solution)/shard_map/all_to_all | solution.py:208
  12.5 15.7 %all-to-all-done = f32[8,250,136]{1,2,0:T(8,128)S(1)} async-done(((f32[8,250,136]{1,2,0:T(8,128)}), f32[8,250,136]{1,2,0:T(8,128)S(1)}, u32[]{:S(2)}, u32[]{:S(2)}) %all-to-all-start) | async-done | bytes 1088032 | tf_op jit(solution)/shard_map/all_to_all | solution.py:208
  28.3 0.4 copy.42
  28.6 0.5 reshape.41
  29.2 0.3 reduce-precision_convert_fusion.1
  29.5 2.0 %fusion.1 = f32[400,396]{1,0:T(8,128)S(1)} fusion(f32[2000]{0:T(1024)S(1)} %bitcast.109, f32[2000]{0:T(1024)S(1)} %bitcast.107, bf16[2000,132]{0,1:T(8,128)(2,1)S(1)} %get-tuple-element.35, bf16[2000,132]{0,1:T(8,128)(2,1)S(1)} %get-tuple-element.36, bf16[2000,132]{0,1:T(8,128)(2,1)S(1)} %get-tuple-element.34), kind=kOutput, calls=%fused_computation.4 | convolution fusion | flops 643152000 | bytes 2233600 | tf_op jit(solution)/shard_map/kt,kc->tc/dot_general | solution.py:224
  31.4 0.3 slice_add_fusion
  31.7 0.1 slice.194.v_ref.r_ref
  31.8 0.5 slice_reduce_fusion.1
  32.5 1.4 %collective-permute-start.1 = (f32[408,128]{1,0:T(8,128)S(1)}, f32[408,128]{1,0:T(8,128)S(1)}, u32[]{:S(2)}, u32[]{:S(2)}) collective-permute-start(f32[408,128]{1,0:T(8,128)S(1)} %pad_maximum_fusion.1), channel_id=1, source_target_pairs={{1,0},{2,1},{3,2},{4,3},{5,4},{6,5},{7,6},{8,7},{9,8},{10,9},{11,1... | collective-permute-start | bytes 626696 | tf_op jit(solution)/shard_map/ppermute | solution.py:36
  34.0 4.0 %collective-permute-start = (f32[408,128]{1,0:T(8,128)S(1)}, f32[408,128]{1,0:T(8,128)S(1)}, u32[]{:S(2)}, u32[]{:S(2)}) collective-permute-start(f32[408,128]{1,0:T(8,128)S(1)} %pad_maximum_fusion.1), channel_id=1, source_target_pairs={{0,1},{1,2},{2,3},{3,4},{4,5},{5,6},{6,7},{7,8},{8,9},{9,10},{10,1... | collective-permute-start | bytes 626696 | tf_op jit(solution)/shard_map/ppermute | solution.py:31
  38.0 1.9 %fusion = f32[400,8]{0,1:T(8,128)S(1)} fusion(f32[2000]{0:T(1024)S(1)} %bitcast.108, f32[2000]{0:T(1024)S(1)} %bitcast.105, f32[2000]{0:T(1024)S(1)} %bitcast.106), kind=kOutput, calls=%fused_computation.3 | convolution fusion | flops 77632000 | bytes 36800 | tf_op jit(solution)/shard_map/kt,kd->td/dot_general | solution.py:230
  39.9 0.6 fusion.31
  40.4 2.2 %add_add_fusion.k_ref = f32[400,400]{1,0:T(8,128)} fusion(f32[400,400]{1,0:T(8,128)S(1)} %copy-done.5, f32[400]{0:T(512)S(1)} %negate_add_fusion, f32[400]{0:T(512)S(1)} %bitcast.87, f32[400]{0:T(512)S(1)} %bitcast.90, f32[400]{0:T(512)S(1)} %bitcast.93, f32[400]{0:T(512)S(1)} %bitcast.96, f32[400]{0:T(512)S(1)} %bitcast.99, f32[400]{0:T(512)S(1)} %bitcast.102, ...), kind=kLoop, calls=%fused_computation.26 | loop fusion | flops 7520000 | bytes 1292800 | tf_op jit(solution)/shard_map/add | solution.py:75
  42.8 0.1 copy.48
  42.9 0.1 copy.51
  43.0 0.1 copy.50
  43.1 0.1 copy.47
  43.3 0.1 copy.46
  43.4 0.7 copy-done.3
  44.1 0.7 copy-done.4
  44.8 3.0 %shard_map.59.w_ref = f32[400,128]{1,0:T(8,128)} custom-call(f32[400,400]{1,0:T(8,128)} %add_add_fusion.k_ref, f32[400,128]{1,0:T(8,128)} %copy-done, f32[408,128]{1,0:T(8,128)} %copy-done.4, f32[408,128]{1,0:T(8,128)} %copy-done.3, f32[400,1]{1,0:T(8,128)} %copy-done.2, f32[400,1]{1,0:T(8,128)} %copy-done.1), custom_call_target="tpu_custom_call" | custom-call | tf_op jit(solution)/shard_map/pallas_call | solution.py:177
  47.8 1.3 %collective-permute-start.3 = (f32[400,128]{1,0:T(8,128)}, f32[400,128]{1,0:T(8,128)S(1)}, u32[]{:S(2)}, u32[]{:S(2)}) collective-permute-start(f32[400,128]{1,0:T(8,128)} %shard_map.59.w_ref), channel_id=1, source_target_pairs={{1,0},{2,1},{3,2},{4,3},{5,4},{6,5},{7,6},{8,7},{9,8},{10,9},{11,1... | collective-permute-start | bytes 614408 | tf_op jit(solution)/shard_map/ppermute | solution.py:36
  49.1 4.0 %collective-permute-start.2 = (f32[400,128]{1,0:T(8,128)}, f32[400,128]{1,0:T(8,128)S(1)}, u32[]{:S(2)}, u32[]{:S(2)}) collective-permute-start(f32[400,128]{1,0:T(8,128)} %shard_map.59.w_ref), channel_id=1, source_target_pairs={{0,1},{1,2},{2,3},{3,4},{4,5},{5,6},{6,7},{7,8},{8,9},{9,10},{10,1... | collective-permute-start | bytes 614408 | tf_op jit(solution)/shard_map/ppermute | solution.py:31
  53.1 0.7 slice_bitcast_fusion.6
  53.8 0.7 slice_bitcast_fusion.7
  54.5 0.1 copy.54
  54.7 1.1 fusion.10
  55.8 0.8 fusion.51
  56.7 0.6 copy-done.6
  57.4 3.2 %shard_map.60 = (f32[400,128]{1,0:T(8,128)}, f32[128,128]{1,0:T(8,128)}) custom-call(f32[400,400]{1,0:T(8,128)} %add_add_fusion.k_ref, f32[400,128]{1,0:T(8,128)} %copy-done, f32[400,128]{1,0:T(8,128)} %shard_map.59.w_ref, f32[400,128]{1,0:T(8,128)} %copy-done.7, f32[400,128]{1,0:T(8,128)} %copy-done.6, f32[400,1]{1,0:T(8,128)} %get-tuple-element.50.wl_ref, ...), custom_call_target="tpu_custom_call" | custom-call | tf_op jit(solution)/shard_map/pallas_call | solution.py:177
  60.6 1.3 %collective-permute-start.5 = (f32[400,128]{1,0:T(8,128)}, f32[400,128]{1,0:T(8,128)S(1)}, u32[]{:S(2)}, u32[]{:S(2)}) collective-permute-start(f32[400,128]{1,0:T(8,128)} %get-tuple-element.14.z_ref), channel_id=1, source_target_pairs={{1,0},{2,1},{3,2},{4,3},{5,4},{6,5},{7,6},{8,7},{9,8},{10,9},{11,1... | collective-permute-start | bytes 614408 | tf_op jit(solution)/shard_map/ppermute | solution.py:36
  61.9 4.0 %collective-permute-start.4 = (f32[400,128]{1,0:T(8,128)}, f32[400,128]{1,0:T(8,128)S(1)}, u32[]{:S(2)}, u32[]{:S(2)}) collective-permute-start(f32[400,128]{1,0:T(8,128)} %get-tuple-element.14.z_ref), channel_id=1, source_target_pairs={{0,1},{1,2},{2,3},{3,4},{4,5},{5,6},{6,7},{7,8},{8,9},{9,10},{10,1... | collective-permute-start | bytes 614408 | tf_op jit(solution)/shard_map/ppermute | solution.py:31
  65.9 16.0 %all-to-all-start.1 = ((f32[128,1,128]{2,1,0:T(1,128)}), f32[128,1,128]{2,1,0:T(1,128)S(1)}, u32[]{:S(2)}, u32[]{:S(2)}) async-start(f32[128,1,128]{2,1,0:T(1,128)} %bitcast.81), calls=%async_computation.1 | async-start | bytes 131072 | tf_op jit(solution)/shard_map/all_to_all | solution.py:186
  81.9 1.1 fusion.50
  83.1 3.0 %collective-permute-start.7 = (f32[400,1]{1,0:T(8,128)S(1)}, f32[400,1]{1,0:T(8,128)S(1)}, u32[]{:S(2)}, u32[]{:S(2)}) collective-permute-start(f32[400,1]{1,0:T(8,128)S(1)} %get-tuple-element.47), channel_id=1, source_target_pairs={{16,0},{32,16},{48,32},{64,48},{80,64},{96,80},{112,96},{17,1},{33... | collective-permute-start | bytes 4808 | tf_op jit(solution)/shard_map/ppermute | solution.py:36
  86.1 2.6 %collective-permute-start.6 = (f32[400,1]{1,0:T(8,128)S(1)}, f32[400,1]{1,0:T(8,128)S(1)}, u32[]{:S(2)}, u32[]{:S(2)}) collective-permute-start(f32[400,1]{1,0:T(8,128)S(1)} %get-tuple-element.48), channel_id=1, source_target_pairs={{0,16},{16,32},{32,48},{48,64},{64,80},{80,96},{96,112},{1,17},{17... | collective-permute-start | bytes 4808 | tf_op jit(solution)/shard_map/ppermute | solution.py:31
  88.7 2.0 %collective-permute-done.7.zr_ref = f32[400,1]{1,0:T(8,128)S(1)} collective-permute-done((f32[400,1]{1,0:T(8,128)S(1)}, f32[400,1]{1,0:T(8,128)S(1)}, u32[]{:S(2)}, u32[]{:S(2)}) %collective-permute-start.7) | collective-permute-done | bytes 1632 | tf_op jit(solution)/shard_map/ppermute | solution.py:36
  90.7 0.7 collective-permute-done.6.zl_ref
  91.4 0.1 all-to-all-done.1
  91.5 0.5 copy-done.12
  92.3 4.0 %shard_map.61 = (f32[400,128]{1,0:T(8,128)}, f32[400,128]{1,0:T(8,128)}, f32[400,128]{1,0:T(8,128)}, f32[400,128]{1,0:T(8,128)}, f32[400,128]{1,0:T(8,128)}, /*index=5*/f32[128,128]{1,0:T(8,128)}, f32[1,128]{1,0:T(1,128)}) custom-call(f32[128,128]{1,0:T(8,128)} %bitcast.79, f32[400,400]{1,0:T(8,128)} %add_add_fusion.k_ref, f32[400,128]{1,0:T(8,128)} %copy-done, ...), custom_call_target="tpu_custom_call" | custom-call | tf_op jit(solution)/shard_map/pallas_call | solution.py:177
  96.3 20.7 %all_to_all.27 = f32[128,1,128]{2,1,0:T(1,128)} all-to-all(f32[128,1,128]{2,1,0:T(1,128)} %bitcast.82), channel_id=1, replica_groups=mesh['pair'=8,'tile'=16] {'pair','tile'}, dimensions={0} | all-to-all | bytes 131072 | tf_op jit(solution)/shard_map/all_to_all | solution.py:186
  117.0 2.2 %shard_map.62 = (f32[400,128]{1,0:T(8,128)}, f32[400,128]{1,0:T(8,128)}) custom-call(f32[128,128]{1,0:T(8,128)} %bitcast.80, f32[1,128]{1,0:T(1,128)} %get-tuple-element.16.scal_ref, f32[400,128]{1,0:T(8,128)} %get-tuple-element.17.r_ref, f32[400,128]{1,0:T(8,128)} %get-tuple-element.18.p_ref, f32[400,128]{1,0:T(8,128)} %get-tuple-element.19.q_ref, ...), custom_call_target="tpu_custom_call" | custom-call | tf_op jit(solution)/shard_map/pallas_call | solution.py:177
  (51 shorter events, 1.0 us)
Async XLA Ops:
  3.8 0.7 copy-start.13
  5.6 22.6 %all-to-all-start = ((f32[8,250,136]{1,2,0:T(8,128)}), f32[8,250,136]{1,2,0:T(8,128)S(1)}, u32[]{:S(2)}, u32[]{:S(2)}) async-start(f32[8,250,136]{1,2,0:T(8,128)} %pad_maximum_fusion), calls=%async_computation | async-start | bytes 2228224 | tf_op jit(solution)/shard_map/all_to_all | solution.py:208
  31.8 0.7 copy-start
  32.4 10.8 %copy-start.1 = (f32[400,1]{1,0:T(8,128)}, f32[400,1]{1,0:T(8,128)S(1)}, u32[]{:S(2)}) copy-start(f32[400,1]{1,0:T(8,128)S(1)} %get-tuple-element.45.vr_ref.rr_ref) | copy-start | bytes 4804
  32.4 10.9 %copy-start.2 = (f32[400,1]{1,0:T(8,128)}, f32[400,1]{1,0:T(8,128)S(1)}, u32[]{:S(2)}) copy-start(f32[400,1]{1,0:T(8,128)S(1)} %get-tuple-element.46.vl_ref.rl_ref) | copy-start | bytes 4804
  32.5 7.9 %copy-start.5 = (f32[400,400]{1,0:T(8,128)S(1)}, f32[400,400]{1,0:T(8,128)}, u32[]{:S(2)}) copy-start(f32[400,400]{1,0:T(8,128)} %constant.35.clone) | copy-start | bytes 1920004
  32.5 10.9 %collective-permute-start.1 = (f32[408,128]{1,0:T(8,128)S(1)}, f32[408,128]{1,0:T(8,128)S(1)}, u32[]{:S(2)}, u32[]{:S(2)}) collective-permute-start(f32[408,128]{1,0:T(8,128)S(1)} %pad_maximum_fusion.1), channel_id=1, source_target_pairs={{1,0},{2,1},{3,2},{4,3},{5,4},{6,5},{7,6},{8,7},{9,8},{10,9},{11,1... | collective-permute-start | bytes 626696 | tf_op jit(solution)/shard_map/ppermute | solution.py:36
  34.0 9.5 %collective-permute-start = (f32[408,128]{1,0:T(8,128)S(1)}, f32[408,128]{1,0:T(8,128)S(1)}, u32[]{:S(2)}, u32[]{:S(2)}) collective-permute-start(f32[408,128]{1,0:T(8,128)S(1)} %pad_maximum_fusion.1), channel_id=1, source_target_pairs={{0,1},{1,2},{2,3},{3,4},{4,5},{5,6},{6,7},{7,8},{8,9},{9,10},{10,1... | collective-permute-start | bytes 626696 | tf_op jit(solution)/shard_map/ppermute | solution.py:31
  43.4 0.7 copy-start.3
  44.1 0.7 copy-start.4
  47.8 8.8 %collective-permute-start.3 = (f32[400,128]{1,0:T(8,128)}, f32[400,128]{1,0:T(8,128)S(1)}, u32[]{:S(2)}, u32[]{:S(2)}) collective-permute-start(f32[400,128]{1,0:T(8,128)} %shard_map.59.w_ref), channel_id=1, source_target_pairs={{1,0},{2,1},{3,2},{4,3},{5,4},{6,5},{7,6},{8,7},{9,8},{10,9},{11,1... | collective-permute-start | bytes 614408 | tf_op jit(solution)/shard_map/ppermute | solution.py:36
  49.1 7.6 %collective-permute-start.2 = (f32[400,128]{1,0:T(8,128)}, f32[400,128]{1,0:T(8,128)S(1)}, u32[]{:S(2)}, u32[]{:S(2)}) collective-permute-start(f32[400,128]{1,0:T(8,128)} %shard_map.59.w_ref), channel_id=1, source_target_pairs={{0,1},{1,2},{2,3},{3,4},{4,5},{5,6},{6,7},{7,8},{8,9},{9,10},{10,1... | collective-permute-start | bytes 614408 | tf_op jit(solution)/shard_map/ppermute | solution.py:31
  56.6 0.7 copy-start.6
  56.7 0.7 copy-start.7
  60.6 30.9 %collective-permute-start.5 = (f32[400,128]{1,0:T(8,128)}, f32[400,128]{1,0:T(8,128)S(1)}, u32[]{:S(2)}, u32[]{:S(2)}) collective-permute-start(f32[400,128]{1,0:T(8,128)} %get-tuple-element.14.z_ref), channel_id=1, source_target_pairs={{1,0},{2,1},{3,2},{4,3},{5,4},{6,5},{7,6},{8,7},{9,8},{10,9},{11,1... | collective-permute-start | bytes 614408 | tf_op jit(solution)/shard_map/ppermute | solution.py:36
  61.9 29.6 %collective-permute-start.4 = (f32[400,128]{1,0:T(8,128)}, f32[400,128]{1,0:T(8,128)S(1)}, u32[]{:S(2)}, u32[]{:S(2)}) collective-permute-start(f32[400,128]{1,0:T(8,128)} %get-tuple-element.14.z_ref), channel_id=1, source_target_pairs={{0,1},{1,2},{2,3},{3,4},{4,5},{5,6},{6,7},{7,8},{8,9},{9,10},{10,1... | collective-permute-start | bytes 614408 | tf_op jit(solution)/shard_map/ppermute | solution.py:31
  65.9 25.6 %all-to-all-start.1 = ((f32[128,1,128]{2,1,0:T(1,128)}), f32[128,1,128]{2,1,0:T(1,128)S(1)}, u32[]{:S(2)}, u32[]{:S(2)}) async-start(f32[128,1,128]{2,1,0:T(1,128)} %bitcast.81), calls=%async_computation.1 | async-start | bytes 131072 | tf_op jit(solution)/shard_map/all_to_all | solution.py:186
  83.1 7.6 %collective-permute-start.7 = (f32[400,1]{1,0:T(8,128)S(1)}, f32[400,1]{1,0:T(8,128)S(1)}, u32[]{:S(2)}, u32[]{:S(2)}) collective-permute-start(f32[400,1]{1,0:T(8,128)S(1)} %get-tuple-element.47), channel_id=1, source_target_pairs={{16,0},{32,16},{48,32},{64,48},{80,64},{96,80},{112,96},{17,1},{33... | collective-permute-start | bytes 4808 | tf_op jit(solution)/shard_map/ppermute | solution.py:36
  86.1 5.3 %collective-permute-start.6 = (f32[400,1]{1,0:T(8,128)S(1)}, f32[400,1]{1,0:T(8,128)S(1)}, u32[]{:S(2)}, u32[]{:S(2)}) collective-permute-start(f32[400,1]{1,0:T(8,128)S(1)} %get-tuple-element.48), channel_id=1, source_target_pairs={{0,16},{16,32},{32,48},{48,64},{64,80},{80,96},{96,112},{1,17},{17... | collective-permute-start | bytes 4808 | tf_op jit(solution)/shard_map/ppermute | solution.py:31
  90.7 0.8 copy-start.11
  91.4 0.7 copy-start.12
  91.5 0.6 copy-start.8
  91.5 0.7 copy-start.9
  91.5 0.8 copy-start.10

commit v13 on v11

--- a/solution.py
+++ b/solution.py
@@ -223,7 +223,17 @@
     right_wide = pieces[:, :width] + pieces[:, width : 2 * width] + pieces[:, 2 * width :]
     span_hot = (jnp.arange(SPAN, dtype=jnp.float32)[None, :] == (later - earlier)).astype(jnp.float32)
     start_hot = (dates[None, :] == earlier).astype(jnp.float32)
-    span_weights = jnp.einsum("kt,kd->td", start_hot, span_hot * weight, precision=HIGHEST)
+    spread = span_hot * weight
+    spread_high = lax.reduce_precision(spread, exponent_bits=8, mantissa_bits=7)
+    spread_rest = spread - spread_high
+    spread_middle = lax.reduce_precision(spread_rest, exponent_bits=8, mantissa_bits=7)
+    spread_parts = jnp.concatenate(
+        [p.astype(jnp.bfloat16) for p in (spread_high, spread_middle, spread_rest - spread_middle)], axis=1
+    )
+    span_pieces = jnp.einsum(
+        "kt,kd->td", start_hot.astype(jnp.bfloat16), spread_parts, preferred_element_type=jnp.float32
+    )
+    span_weights = span_pieces[:, :SPAN] + span_pieces[:, SPAN : 2 * SPAN] + span_pieces[:, 2 * SPAN :]
     matrix = normal_matrix(span_weights)
     residual = right_wide[:, 2:-2]
     outer = jnp.concatenate([right_wide[:, 1], right_wide[:, -2], jnp.zeros((8 * 128 - 2 * DATES,), jnp.float32)])

time: 120 us -> 119 us (level)
  matrix products: 4.96 us -> 3.51 us
    dot_general x1, matrix products: 1.86 us -> 0.45 us  [body(): jnp.einsum('kt,kd->td', start_hot.astype(jnp.bfloat16), spread_parts, pre...]
  transfers between devices with their start and end apart: 10 -> 10, of which waited for: 5 -> 5; matrix products, arithmetic and copies ran while one was open for 8% -> 7% of each run, Pallas kernels for 0% -> 0%
where the time goes in v13:
time: 119 us; the launch traced here: 118 us
  starting transfers between devices  45.1 us (38%)
  blocking collectives  20.8 us (17%)
  waiting for transfers between devices  19.3 us (16%)
  Pallas kernels  12.4 us (10%)
  local copies, waits for them, and re-layouts  10.3 us (9%)
  other arithmetic  5.59 us (5%)
  matrix products  3.51 us (3%)
    all_to_all x1, blocking collectives, reduce_all(): return lax.all_to_all(send, ('pair', 'tile'), 0, 0, tiled=True)  20.8 us
    all_to_all x1, starting transfers between devices, reduce_all(): return lax.all_to_all(send, ('pair', 'tile'), 0, 0, tiled=True)  16 us
    all_to_all x1, waiting for transfers between devices, body(): lax.all_to_all(chunks, 'pair', 0, 0, tiled=True)  15.7 us
    ppermute x4, starting transfers between devices, from_prev(): return lax.ppermute(cells, axis, [(i, i + 1) for i in range(count - 1)])  15.2 us
    pallas_call x4, Pallas kernels, call(): pl.pallas_call(kernel, out_shape=[jax.ShapeDtypeStruct(s, jnp.float32) fo...  12.4 us
    ppermute x4, starting transfers between devices, from_next(): return lax.ppermute(cells, axis, [(i + 1, i) for i in range(count - 1)])  6.96 us
    all_to_all x1, starting transfers between devices, body(): lax.all_to_all(chunks, 'pair', 0, 0, tiled=True)  6.81 us
    unnamed x32, local copies, waits for them, and re-layouts  4.57 us
  transfers between devices with their start and end apart: 10, of which 5 were waited for; matrix products, arithmetic and copies ran while one was open for 7% of the time, Pallas kernels for 0%

profile of v13, /device:TPU:1, one launch (start us, length us, event | category | flops | bytes accessed | tf_op | source)
XLA Modules:
  0.0 118.0 jit_solution(10839818268886354632)
XLA Ops:
  0.6 0.8 slice_convert_fusion.1
  1.4 2.4 %copy.41 = f32[250,1,1024]{0,2,1:T(8,128)S(1)} copy(f32[250,1,1024]{2,1,0:T(1,128)} %param.4) | data formatting | bytes 2048000 | tf_op args[0]
  3.9 0.6 copy-done.11
  4.5 1.1 pad_maximum_fusion
  5.6 6.8 %all-to-all-start = ((f32[8,250,136]{1,2,0:T(8,128)}), f32[8,250,136]{1,2,0:T(8,128)S(1)}, u32[]{:S(2)}, u32[]{:S(2)}) async-start(f32[8,250,136]{1,2,0:T(8,128)} %pad_maximum_fusion), calls=%async_computation | async-start | bytes 2228224 | tf_op jit(solution)/shard_map/all_to_all | solution.py:204
  12.5 15.7 %all-to-all-done = f32[8,250,136]{1,2,0:T(8,128)S(1)} async-done(((f32[8,250,136]{1,2,0:T(8,128)}), f32[8,250,136]{1,2,0:T(8,128)S(1)}, u32[]{:S(2)}, u32[]{:S(2)}) %all-to-all-start) | async-done | bytes 1088032 | tf_op jit(solution)/shard_map/all_to_all | solution.py:204
  28.3 0.4 copy.42
  28.6 0.5 reshape.41
  29.2 0.3 reduce-precision_convert_fusion.1
  29.5 1.9 %fusion.1 = f32[400,396]{1,0:T(8,128)S(1)} fusion(f32[2000]{0:T(1024)S(1)} %bitcast.109, f32[2000]{0:T(1024)S(1)} %bitcast.107, bf16[2000,132]{0,1:T(8,128)(2,1)S(1)} %get-tuple-element.35, bf16[2000,132]{0,1:T(8,128)(2,1)S(1)} %get-tuple-element.36, bf16[2000,132]{0,1:T(8,128)(2,1)S(1)} %get-tuple-element.34), kind=kOutput, calls=%fused_computation.5 | convolution fusion | flops 643152000 | bytes 2233600 | tf_op jit(solution)/shard_map/kt,kc->tc/dot_general | solution.py:220
  31.4 0.3 slice_add_fusion
  31.7 0.1 slice.217.v_ref.r_ref
  31.8 0.5 slice_reduce_fusion.1
  32.5 1.4 %collective-permute-start.1 = (f32[408,128]{1,0:T(8,128)S(1)}, f32[408,128]{1,0:T(8,128)S(1)}, u32[]{:S(2)}, u32[]{:S(2)}) collective-permute-start(f32[408,128]{1,0:T(8,128)S(1)} %pad_maximum_fusion.1), channel_id=1, source_target_pairs={{1,0},{2,1},{3,2},{4,3},{5,4},{6,5},{7,6},{8,7},{9,8},{10,9},{11,1... | collective-permute-start | bytes 626696 | tf_op jit(solution)/shard_map/ppermute | solution.py:36
  33.9 4.0 %collective-permute-start = (f32[408,128]{1,0:T(8,128)S(1)}, f32[408,128]{1,0:T(8,128)S(1)}, u32[]{:S(2)}, u32[]{:S(2)}) collective-permute-start(f32[408,128]{1,0:T(8,128)S(1)} %pad_maximum_fusion.1), channel_id=1, source_target_pairs={{0,1},{1,2},{2,3},{3,4},{4,5},{5,6},{6,7},{7,8},{8,9},{9,10},{10,1... | collective-permute-start | bytes 626696 | tf_op jit(solution)/shard_map/ppermute | solution.py:31
  38.0 0.5 fusion.3
  38.5 0.6 fusion.29
  39.0 2.2 %add_add_fusion.k_ref = f32[400,400]{1,0:T(8,128)} fusion(f32[400,400]{1,0:T(8,128)S(1)} %copy-done.3, f32[400]{0:T(512)S(1)} %negate_add_fusion, f32[400]{0:T(512)S(1)} %bitcast.89, f32[400]{0:T(512)S(1)} %bitcast.92, f32[400]{0:T(512)S(1)} %bitcast.95, f32[400]{0:T(512)S(1)} %bitcast.98, f32[400]{0:T(512)S(1)} %bitcast.101, f32[400]{0:T(512)S(1)} %bitcast.104, ...), kind=kLoop, calls=%fused_computation.26 | loop fusion | flops 7520000 | bytes 1292800 | tf_op jit(solution)/shard_map/add | solution.py:75
  41.4 0.1 copy.48
  41.5 0.1 copy.51
  41.6 0.1 copy.50
  41.7 0.1 copy.47
  41.9 0.1 copy.46
  42.0 0.7 slice.221.vd_ref.rd_ref
  42.7 0.7 slice.220.vu_ref.ru_ref
  43.4 3.0 %shard_map.59.w_ref = f32[400,128]{1,0:T(8,128)} custom-call(f32[400,400]{1,0:T(8,128)} %add_add_fusion.k_ref, f32[400,128]{1,0:T(8,128)} %copy-done, f32[400,128]{1,0:T(8,128)} %slice.220.vu_ref.ru_ref, f32[400,128]{1,0:T(8,128)} %slice.221.vd_ref.rd_ref, f32[400,1]{1,0:T(8,128)} %copy-done.2, f32[400,1]{1,0:T(8,128)} %copy-done.1), custom_call_target="tpu_custom_call" | custom-call | tf_op jit(solution)/shard_map/pallas_call | solution.py:173
  46.4 1.3 %collective-permute-start.3 = (f32[400,128]{1,0:T(8,128)}, f32[400,128]{1,0:T(8,128)S(1)}, u32[]{:S(2)}, u32[]{:S(2)}) collective-permute-start(f32[400,128]{1,0:T(8,128)} %shard_map.59.w_ref), channel_id=1, source_target_pairs={{1,0},{2,1},{3,2},{4,3},{5,4},{6,5},{7,6},{8,7},{9,8},{10,9},{11,1... | collective-permute-start | bytes 614408 | tf_op jit(solution)/shard_map/ppermute | solution.py:36
  47.7 4.0 %collective-permute-start.2 = (f32[400,128]{1,0:T(8,128)}, f32[400,128]{1,0:T(8,128)S(1)}, u32[]{:S(2)}, u32[]{:S(2)}) collective-permute-start(f32[400,128]{1,0:T(8,128)} %shard_map.59.w_ref), channel_id=1, source_target_pairs={{0,1},{1,2},{2,3},{3,4},{4,5},{5,6},{6,7},{7,8},{8,9},{9,10},{10,1... | collective-permute-start | bytes 614408 | tf_op jit(solution)/shard_map/ppermute | solution.py:31
  51.8 0.1 copy.54
  52.0 1.1 fusion.12
  53.1 0.8 fusion.55
  54.0 0.8 collective-permute-done.2.wu_ref
  54.7 0.7 copy-done.5
  55.4 3.2 %shard_map.60 = (f32[400,128]{1,0:T(8,128)}, f32[128,128]{1,0:T(8,128)}) custom-call(f32[400,400]{1,0:T(8,128)} %add_add_fusion.k_ref, f32[400,128]{1,0:T(8,128)} %copy-done, f32[400,128]{1,0:T(8,128)} %shard_map.59.w_ref, f32[400,128]{1,0:T(8,128)} %copy-done.5, f32[400,128]{1,0:T(8,128)} %copy-done.4, f32[400,1]{1,0:T(8,128)} %get-tuple-element.50.wl_ref, ...), custom_call_target="tpu_custom_call" | custom-call | tf_op jit(solution)/shard_map/pallas_call | solution.py:173
  58.6 1.3 %collective-permute-start.5 = (f32[400,128]{1,0:T(8,128)}, f32[400,128]{1,0:T(8,128)S(1)}, u32[]{:S(2)}, u32[]{:S(2)}) collective-permute-start(f32[400,128]{1,0:T(8,128)} %get-tuple-element.14.z_ref), channel_id=1, source_target_pairs={{1,0},{2,1},{3,2},{4,3},{5,4},{6,5},{7,6},{8,7},{9,8},{10,9},{11,1... | collective-permute-start | bytes 614408 | tf_op jit(solution)/shard_map/ppermute | solution.py:36
  59.9 4.6 %collective-permute-start.4 = (f32[400,128]{1,0:T(8,128)}, f32[400,128]{1,0:T(8,128)S(1)}, u32[]{:S(2)}, u32[]{:S(2)}) collective-permute-start(f32[400,128]{1,0:T(8,128)} %get-tuple-element.14.z_ref), channel_id=1, source_target_pairs={{0,1},{1,2},{2,3},{3,4},{4,5},{5,6},{6,7},{7,8},{8,9},{9,10},{10,1... | collective-permute-start | bytes 614408 | tf_op jit(solution)/shard_map/ppermute | solution.py:31
  64.5 16.0 %all-to-all-start.1 = ((f32[128,1,128]{2,1,0:T(1,128)}), f32[128,1,128]{2,1,0:T(1,128)S(1)}, u32[]{:S(2)}, u32[]{:S(2)}) async-start(f32[128,1,128]{2,1,0:T(1,128)} %bitcast.83), calls=%async_computation.1 | async-start | bytes 131072 | tf_op jit(solution)/shard_map/all_to_all | solution.py:182
  80.6 1.1 fusion.54
  81.7 3.0 %collective-permute-start.7 = (f32[400,1]{1,0:T(8,128)S(1)}, f32[400,1]{1,0:T(8,128)S(1)}, u32[]{:S(2)}, u32[]{:S(2)}) collective-permute-start(f32[400,1]{1,0:T(8,128)S(1)} %get-tuple-element.47), channel_id=1, source_target_pairs={{16,0},{32,16},{48,32},{64,48},{80,64},{96,80},{112,96},{17,1},{33... | collective-permute-start | bytes 4808 | tf_op jit(solution)/shard_map/ppermute | solution.py:36
  84.7 2.6 %collective-permute-start.6 = (f32[400,1]{1,0:T(8,128)S(1)}, f32[400,1]{1,0:T(8,128)S(1)}, u32[]{:S(2)}, u32[]{:S(2)}) collective-permute-start(f32[400,1]{1,0:T(8,128)S(1)} %get-tuple-element.48), channel_id=1, source_target_pairs={{0,16},{16,32},{32,48},{48,64},{64,80},{80,96},{96,112},{1,17},{17... | collective-permute-start | bytes 4808 | tf_op jit(solution)/shard_map/ppermute | solution.py:31
  87.3 2.0 %collective-permute-done.7.zr_ref = f32[400,1]{1,0:T(8,128)S(1)} collective-permute-done((f32[400,1]{1,0:T(8,128)S(1)}, f32[400,1]{1,0:T(8,128)S(1)}, u32[]{:S(2)}, u32[]{:S(2)}) %collective-permute-start.7) | collective-permute-done | bytes 1632 | tf_op jit(solution)/shard_map/ppermute | solution.py:36
  89.3 0.7 collective-permute-done.6.zl_ref
  90.0 0.2 all-to-all-done.1
  90.2 0.5 copy-done.10
  90.8 0.1 copy-done.7
  91.0 3.9 %shard_map.61 = (f32[400,128]{1,0:T(8,128)}, f32[400,128]{1,0:T(8,128)}, f32[400,128]{1,0:T(8,128)}, f32[400,128]{1,0:T(8,128)}, f32[400,128]{1,0:T(8,128)}, /*index=5*/f32[128,128]{1,0:T(8,128)}, f32[1,128]{1,0:T(1,128)}) custom-call(f32[128,128]{1,0:T(8,128)} %bitcast.79, f32[400,400]{1,0:T(8,128)} %add_add_fusion.k_ref, f32[400,128]{1,0:T(8,128)} %copy-done, ...), custom_call_target="tpu_custom_call" | custom-call | tf_op jit(solution)/shard_map/pallas_call | solution.py:173
  94.9 20.8 %all_to_all.27 = f32[128,1,128]{2,1,0:T(1,128)} all-to-all(f32[128,1,128]{2,1,0:T(1,128)} %bitcast.84), channel_id=1, replica_groups=mesh['pair'=8,'tile'=16] {'pair','tile'}, dimensions={0} | all-to-all | bytes 131072 | tf_op jit(solution)/shard_map/all_to_all | solution.py:182
  115.7 2.2 %shard_map.62 = (f32[400,128]{1,0:T(8,128)}, f32[400,128]{1,0:T(8,128)}) custom-call(f32[128,128]{1,0:T(8,128)} %bitcast.80, f32[1,128]{1,0:T(1,128)} %get-tuple-element.16.scal_ref, f32[400,128]{1,0:T(8,128)} %get-tuple-element.17.r_ref, f32[400,128]{1,0:T(8,128)} %get-tuple-element.18.p_ref, f32[400,128]{1,0:T(8,128)} %get-tuple-element.19.q_ref, ...), custom_call_target="tpu_custom_call" | custom-call | tf_op jit(solution)/shard_map/pallas_call | solution.py:173
  (51 shorter events, 0.9 us)
Async XLA Ops:
  3.8 0.7 copy-start.11
  5.6 22.6 %all-to-all-start = ((f32[8,250,136]{1,2,0:T(8,128)}), f32[8,250,136]{1,2,0:T(8,128)S(1)}, u32[]{:S(2)}, u32[]{:S(2)}) async-start(f32[8,250,136]{1,2,0:T(8,128)} %pad_maximum_fusion), calls=%async_computation | async-start | bytes 2228224 | tf_op jit(solution)/shard_map/all_to_all | solution.py:204
  31.8 0.7 copy-start
  32.3 9.4 %copy-start.1 = (f32[400,1]{1,0:T(8,128)}, f32[400,1]{1,0:T(8,128)S(1)}, u32[]{:S(2)}) copy-start(f32[400,1]{1,0:T(8,128)S(1)} %get-tuple-element.45.vr_ref.rr_ref) | copy-start | bytes 4804
  32.3 9.5 %copy-start.2 = (f32[400,1]{1,0:T(8,128)}, f32[400,1]{1,0:T(8,128)S(1)}, u32[]{:S(2)}) copy-start(f32[400,1]{1,0:T(8,128)S(1)} %get-tuple-element.46.vl_ref.rl_ref) | copy-start | bytes 4804
  32.5 6.5 %copy-start.3 = (f32[400,400]{1,0:T(8,128)S(1)}, f32[400,400]{1,0:T(8,128)}, u32[]{:S(2)}) copy-start(f32[400,400]{1,0:T(8,128)} %constant.35.clone) | copy-start | bytes 1920004
  32.5 9.5 %collective-permute-start.1 = (f32[408,128]{1,0:T(8,128)S(1)}, f32[408,128]{1,0:T(8,128)S(1)}, u32[]{:S(2)}, u32[]{:S(2)}) collective-permute-start(f32[408,128]{1,0:T(8,128)S(1)} %pad_maximum_fusion.1), channel_id=1, source_target_pairs={{1,0},{2,1},{3,2},{4,3},{5,4},{6,5},{7,6},{8,7},{9,8},{10,9},{11,1... | collective-permute-start | bytes 626696 | tf_op jit(solution)/shard_map/ppermute | solution.py:36
  33.9 8.8 %collective-permute-start = (f32[408,128]{1,0:T(8,128)S(1)}, f32[408,128]{1,0:T(8,128)S(1)}, u32[]{:S(2)}, u32[]{:S(2)}) collective-permute-start(f32[408,128]{1,0:T(8,128)S(1)} %pad_maximum_fusion.1), channel_id=1, source_target_pairs={{0,1},{1,2},{2,3},{3,4},{4,5},{5,6},{6,7},{7,8},{8,9},{9,10},{10,1... | collective-permute-start | bytes 626696 | tf_op jit(solution)/shard_map/ppermute | solution.py:31
  46.4 7.5 %collective-permute-start.3 = (f32[400,128]{1,0:T(8,128)}, f32[400,128]{1,0:T(8,128)S(1)}, u32[]{:S(2)}, u32[]{:S(2)}) collective-permute-start(f32[400,128]{1,0:T(8,128)} %shard_map.59.w_ref), channel_id=1, source_target_pairs={{1,0},{2,1},{3,2},{4,3},{5,4},{6,5},{7,6},{8,7},{9,8},{10,9},{11,1... | collective-permute-start | bytes 614408 | tf_op jit(solution)/shard_map/ppermute | solution.py:36
  47.7 7.0 %collective-permute-start.2 = (f32[400,128]{1,0:T(8,128)}, f32[400,128]{1,0:T(8,128)S(1)}, u32[]{:S(2)}, u32[]{:S(2)}) collective-permute-start(f32[400,128]{1,0:T(8,128)} %shard_map.59.w_ref), channel_id=1, source_target_pairs={{0,1},{1,2},{2,3},{3,4},{4,5},{5,6},{6,7},{7,8},{8,9},{9,10},{10,1... | collective-permute-start | bytes 614408 | tf_op jit(solution)/shard_map/ppermute | solution.py:31
  54.0 0.8 copy-start.4
  54.7 0.7 copy-start.5
  58.6 31.6 %collective-permute-start.5 = (f32[400,128]{1,0:T(8,128)}, f32[400,128]{1,0:T(8,128)S(1)}, u32[]{:S(2)}, u32[]{:S(2)}) collective-permute-start(f32[400,128]{1,0:T(8,128)} %get-tuple-element.14.z_ref), channel_id=1, source_target_pairs={{1,0},{2,1},{3,2},{4,3},{5,4},{6,5},{7,6},{8,7},{9,8},{10,9},{11,1... | collective-permute-start | bytes 614408 | tf_op jit(solution)/shard_map/ppermute | solution.py:36
  59.9 30.3 %collective-permute-start.4 = (f32[400,128]{1,0:T(8,128)}, f32[400,128]{1,0:T(8,128)S(1)}, u32[]{:S(2)}, u32[]{:S(2)}) collective-permute-start(f32[400,128]{1,0:T(8,128)} %get-tuple-element.14.z_ref), channel_id=1, source_target_pairs={{0,1},{1,2},{2,3},{3,4},{4,5},{5,6},{6,7},{7,8},{8,9},{9,10},{10,1... | collective-permute-start | bytes 614408 | tf_op jit(solution)/shard_map/ppermute | solution.py:31
  64.5 25.6 %all-to-all-start.1 = ((f32[128,1,128]{2,1,0:T(1,128)}), f32[128,1,128]{2,1,0:T(1,128)S(1)}, u32[]{:S(2)}, u32[]{:S(2)}) async-start(f32[128,1,128]{2,1,0:T(1,128)} %bitcast.83), calls=%async_computation.1 | async-start | bytes 131072 | tf_op jit(solution)/shard_map/all_to_all | solution.py:182
  81.7 7.6 %collective-permute-start.7 = (f32[400,1]{1,0:T(8,128)S(1)}, f32[400,1]{1,0:T(8,128)S(1)}, u32[]{:S(2)}, u32[]{:S(2)}) collective-permute-start(f32[400,1]{1,0:T(8,128)S(1)} %get-tuple-element.47), channel_id=1, source_target_pairs={{16,0},{32,16},{48,32},{64,48},{80,64},{96,80},{112,96},{17,1},{33... | collective-permute-start | bytes 4808 | tf_op jit(solution)/shard_map/ppermute | solution.py:36
  84.7 5.3 %collective-permute-start.6 = (f32[400,1]{1,0:T(8,128)S(1)}, f32[400,1]{1,0:T(8,128)S(1)}, u32[]{:S(2)}, u32[]{:S(2)}) collective-permute-start(f32[400,1]{1,0:T(8,128)S(1)} %get-tuple-element.48), channel_id=1, source_target_pairs={{0,16},{16,32},{32,48},{48,64},{64,80},{80,96},{96,112},{1,17},{17... | collective-permute-start | bytes 4808 | tf_op jit(solution)/shard_map/ppermute | solution.py:31
  89.3 0.9 copy-start.9
  90.0 0.7 copy-start.10
  90.2 0.6 copy-start.6
  90.2 0.7 copy-start.7
  90.2 0.8 copy-start.8

commit v14 on v13

--- a/solution.py
+++ b/solution.py
@@ -66,11 +66,13 @@
 def normal_matrix(weights):
     dates = jnp.arange(DATES, dtype=jnp.int32)
     offset = dates[None, :] - dates[:, None]
-    upper = jnp.zeros((DATES, DATES), jnp.float32)
+    across = weights.T
+    coupling = jnp.zeros((DATES, DATES), jnp.float32)
+    degree = jnp.zeros((DATES,), jnp.float32)
     for d in range(1, SPAN):
-        upper = upper + jnp.where(offset == d, -weights[:, d : d + 1], 0.0)
-    coupling = upper + upper.T
-    degree = -jnp.sum(coupling, axis=1)
+        coupling = coupling + jnp.where(offset == d, -weights[:, d : d + 1], 0.0)
+        coupling = coupling + jnp.where(offset == -d, -across[d : d + 1, :], 0.0)
+        degree = degree + weights[:, d] + jnp.pad(weights[: DATES - d, d], (d, 0))
     diagonal = degree + (4.0 * spatial_weight + ridge_weight)
     return coupling + jnp.where(offset == 0, diagonal[:, None], 0.0) + temporal_weight * temporal_matrix()
 

time: 119 us -> 119 us (level)
    unnamed x32 -> x34, local copies, waits for them, and re-layouts: 4.57 us -> 4.55 us
  transfers between devices with their start and end apart: 10 -> 10, of which waited for: 5 -> 5; matrix products, arithmetic and copies ran while one was open for 7% -> 6% of each run, Pallas kernels for 0% -> 0%
where the time goes in v14:
time: 119 us; the launch traced here: 118 us
  starting transfers between devices  45.5 us (38%)
  blocking collectives  20.8 us (17%)
  waiting for transfers between devices  19.7 us (17%)
  Pallas kernels  12.5 us (11%)
  local copies, waits for them, and re-layouts  10.3 us (9%)
  other arithmetic  5.11 us (4%)
  matrix products  3.18 us (3%)
    all_to_all x1, blocking collectives, reduce_all(): return lax.all_to_all(send, ('pair', 'tile'), 0, 0, tiled=True)  20.8 us
    all_to_all x1, starting transfers between devices, reduce_all(): return lax.all_to_all(send, ('pair', 'tile'), 0, 0, tiled=True)  16.4 us
    all_to_all x1, waiting for transfers between devices, body(): lax.all_to_all(chunks, 'pair', 0, 0, tiled=True)  15.7 us
    ppermute x4, starting transfers between devices, from_prev(): return lax.ppermute(cells, axis, [(i, i + 1) for i in range(count - 1)])  15.5 us
    pallas_call x4, Pallas kernels, call(): pl.pallas_call(kernel, out_shape=[jax.ShapeDtypeStruct(s, jnp.float32) fo...  12.5 us
    ppermute x4, starting transfers between devices, from_next(): return lax.ppermute(cells, axis, [(i + 1, i) for i in range(count - 1)])  6.83 us
    all_to_all x1, starting transfers between devices, body(): lax.all_to_all(chunks, 'pair', 0, 0, tiled=True)  6.81 us
    unnamed x34, local copies, waits for them, and re-layouts  4.55 us
  transfers between devices with their start and end apart: 10, of which 5 were waited for; matrix products, arithmetic and copies ran while one was open for 6% of the time, Pallas kernels for 0%

profile of v14, /device:TPU:1, one launch (start us, length us, event | category | flops | bytes accessed | tf_op | source)
XLA Modules:
  0.0 118.1 jit_solution(17927814838084446178)
XLA Ops:
  0.6 0.8 slice_convert_fusion.1
  1.4 2.4 %copy.41 = f32[250,1,1024]{0,2,1:T(8,128)S(1)} copy(f32[250,1,1024]{2,1,0:T(1,128)} %param.4) | data formatting | bytes 2048000 | tf_op args[0]
  3.9 0.6 copy-done.12
  4.5 1.1 pad_maximum_fusion
  5.6 6.8 %all-to-all-start = ((f32[8,250,136]{1,2,0:T(8,128)}), f32[8,250,136]{1,2,0:T(8,128)S(1)}, u32[]{:S(2)}, u32[]{:S(2)}) async-start(f32[8,250,136]{1,2,0:T(8,128)} %pad_maximum_fusion), calls=%async_computation | async-start | bytes 2228224 | tf_op jit(solution)/shard_map/all_to_all | solution.py:206
  12.5 15.7 %all-to-all-done = f32[8,250,136]{1,2,0:T(8,128)S(1)} async-done(((f32[8,250,136]{1,2,0:T(8,128)}), f32[8,250,136]{1,2,0:T(8,128)S(1)}, u32[]{:S(2)}, u32[]{:S(2)}) %all-to-all-start) | async-done | bytes 1088032 | tf_op jit(solution)/shard_map/all_to_all | solution.py:206
  28.2 0.4 copy.42
  28.6 0.5 reshape.38
  29.2 0.5 fusion.3
  29.8 0.3 reduce-precision_convert_fusion.1
  30.1 2.0 %fusion.1 = f32[400,396]{1,0:T(8,128)S(1)} fusion(f32[2000]{0:T(1024)S(1)} %bitcast.124, f32[2000]{0:T(1024)S(1)} %bitcast.126, bf16[2000,132]{0,1:T(8,128)(2,1)S(1)} %get-tuple-element.35, bf16[2000,132]{0,1:T(8,128)(2,1)S(1)} %get-tuple-element.36, bf16[2000,132]{0,1:T(8,128)(2,1)S(1)} %get-tuple-element.34), kind=kOutput, calls=%fused_computation.5 | convolution fusion | flops 643152000 | bytes 2233600 | tf_op jit(solution)/shard_map/kt,kc->tc/dot_general | solution.py:222
  32.1 0.3 slice_add_fusion
  32.3 0.1 slice.294.v_ref.r_ref
  32.5 0.5 slice_reduce_fusion.1
  33.2 1.3 %collective-permute-start.1 = (f32[408,128]{1,0:T(8,128)S(1)}, f32[408,128]{1,0:T(8,128)S(1)}, u32[]{:S(2)}, u32[]{:S(2)}) collective-permute-start(f32[408,128]{1,0:T(8,128)S(1)} %pad_maximum_fusion.1), channel_id=1, source_target_pairs={{1,0},{2,1},{3,2},{4,3},{5,4},{6,5},{7,6},{8,7},{9,8},{10,9},{11,1... | collective-permute-start | bytes 626696 | tf_op jit(solution)/shard_map/ppermute | solution.py:36
  34.5 4.0 %collective-permute-start = (f32[408,128]{1,0:T(8,128)S(1)}, f32[408,128]{1,0:T(8,128)S(1)}, u32[]{:S(2)}, u32[]{:S(2)}) collective-permute-start(f32[408,128]{1,0:T(8,128)S(1)} %pad_maximum_fusion.1), channel_id=1, source_target_pairs={{0,1},{1,2},{2,3},{3,4},{4,5},{5,6},{6,7},{7,8},{8,9},{9,10},{10,1... | collective-permute-start | bytes 626696 | tf_op jit(solution)/shard_map/ppermute | solution.py:31
  38.6 2.2 %add_add_fusion.k_ref = f32[400,400]{1,0:T(8,128)} fusion(f32[400,400]{1,0:T(8,128)S(1)} %copy-done.4, f32[400]{0:T(512)S(1)} %add_add_fusion.1, f32[400]{0:T(512)S(1)} %bitcast.111, f32[400]{0:T(512)S(1)} %bitcast.123, f32[400]{0:T(512)S(1)} %bitcast.112, f32[400]{0:T(512)S(1)} %bitcast.122, f32[400]{0:T(512)S(1)} %bitcast.113, f32[400]{0:T(512)S(1)} %bitcast.121, ...), kind=kLoop, calls=%fused_computation.26 | loop fusion | flops 7360000 | bytes 1304000 | tf_op jit(solution)/shard_map/add | solution.py:77
  40.8 0.1 copy.49
  40.9 0.1 copy.48
  41.0 0.1 copy.51
  41.1 0.1 copy.50
  41.3 0.1 copy.47
  41.4 0.1 copy.46
  41.5 0.7 slice.298.vd_ref.rd_ref
  42.2 0.7 slice.297.vu_ref.ru_ref
  42.9 3.1 %shard_map.59.w_ref = f32[400,128]{1,0:T(8,128)} custom-call(f32[400,400]{1,0:T(8,128)} %add_add_fusion.k_ref, f32[400,128]{1,0:T(8,128)} %copy-done.1, f32[400,128]{1,0:T(8,128)} %slice.297.vu_ref.ru_ref, f32[400,128]{1,0:T(8,128)} %slice.298.vd_ref.rd_ref, f32[400,1]{1,0:T(8,128)} %copy-done.3, f32[400,1]{1,0:T(8,128)} %copy-done.2), custom_call_target="tpu_custom_call" | custom-call | tf_op jit(solution)/shard_map/pallas_call | solution.py:175
  46.0 1.3 %collective-permute-start.3 = (f32[400,128]{1,0:T(8,128)}, f32[400,128]{1,0:T(8,128)S(1)}, u32[]{:S(2)}, u32[]{:S(2)}) collective-permute-start(f32[400,128]{1,0:T(8,128)} %shard_map.59.w_ref), channel_id=1, source_target_pairs={{1,0},{2,1},{3,2},{4,3},{5,4},{6,5},{7,6},{8,7},{9,8},{10,9},{11,1... | collective-permute-start | bytes 614408 | tf_op jit(solution)/shard_map/ppermute | solution.py:36
  47.3 4.3 %collective-permute-start.2 = (f32[400,128]{1,0:T(8,128)}, f32[400,128]{1,0:T(8,128)S(1)}, u32[]{:S(2)}, u32[]{:S(2)}) collective-permute-start(f32[400,128]{1,0:T(8,128)} %shard_map.59.w_ref), channel_id=1, source_target_pairs={{0,1},{1,2},{2,3},{3,4},{4,5},{5,6},{6,7},{7,8},{8,9},{9,10},{10,1... | collective-permute-start | bytes 614408 | tf_op jit(solution)/shard_map/ppermute | solution.py:31
  51.7 0.1 copy.54
  51.8 0.8 fusion.12
  52.6 0.8 fusion.54
  53.5 1.1 collective-permute-done.2.wu_ref
  54.6 0.7 copy-done.6
  55.2 3.2 %shard_map.60 = (f32[400,128]{1,0:T(8,128)}, f32[128,128]{1,0:T(8,128)}) custom-call(f32[400,400]{1,0:T(8,128)} %add_add_fusion.k_ref, f32[400,128]{1,0:T(8,128)} %copy-done.1, f32[400,128]{1,0:T(8,128)} %shard_map.59.w_ref, f32[400,128]{1,0:T(8,128)} %copy-done.6, f32[400,128]{1,0:T(8,128)} %copy-done.5, f32[400,1]{1,0:T(8,128)} %get-tuple-element.50.wl_ref, ...), custom_call_target="tpu_custom_call" | custom-call | tf_op jit(solution)/shard_map/pallas_call | solution.py:175
  58.4 1.3 %collective-permute-start.5 = (f32[400,128]{1,0:T(8,128)}, f32[400,128]{1,0:T(8,128)S(1)}, u32[]{:S(2)}, u32[]{:S(2)}) collective-permute-start(f32[400,128]{1,0:T(8,128)} %get-tuple-element.14.z_ref), channel_id=1, source_target_pairs={{1,0},{2,1},{3,2},{4,3},{5,4},{6,5},{7,6},{8,7},{9,8},{10,9},{11,1... | collective-permute-start | bytes 614408 | tf_op jit(solution)/shard_map/ppermute | solution.py:36
  59.7 4.6 %collective-permute-start.4 = (f32[400,128]{1,0:T(8,128)}, f32[400,128]{1,0:T(8,128)S(1)}, u32[]{:S(2)}, u32[]{:S(2)}) collective-permute-start(f32[400,128]{1,0:T(8,128)} %get-tuple-element.14.z_ref), channel_id=1, source_target_pairs={{0,1},{1,2},{2,3},{3,4},{4,5},{5,6},{6,7},{7,8},{8,9},{9,10},{10,1... | collective-permute-start | bytes 614408 | tf_op jit(solution)/shard_map/ppermute | solution.py:31
  64.4 16.4 %all-to-all-start.1 = ((f32[128,1,128]{2,1,0:T(1,128)}), f32[128,1,128]{2,1,0:T(1,128)S(1)}, u32[]{:S(2)}, u32[]{:S(2)}) async-start(f32[128,1,128]{2,1,0:T(1,128)} %bitcast.107), calls=%async_computation.1 | async-start | bytes 131072 | tf_op jit(solution)/shard_map/all_to_all | solution.py:184
  80.8 1.1 fusion.53
  81.9 3.0 %collective-permute-start.7 = (f32[400,1]{1,0:T(8,128)S(1)}, f32[400,1]{1,0:T(8,128)S(1)}, u32[]{:S(2)}, u32[]{:S(2)}) collective-permute-start(f32[400,1]{1,0:T(8,128)S(1)} %get-tuple-element.47), channel_id=1, source_target_pairs={{16,0},{32,16},{48,32},{64,48},{80,64},{96,80},{112,96},{17,1},{33... | collective-permute-start | bytes 4808 | tf_op jit(solution)/shard_map/ppermute | solution.py:36
  84.9 2.6 %collective-permute-start.6 = (f32[400,1]{1,0:T(8,128)S(1)}, f32[400,1]{1,0:T(8,128)S(1)}, u32[]{:S(2)}, u32[]{:S(2)}) collective-permute-start(f32[400,1]{1,0:T(8,128)S(1)} %get-tuple-element.48), channel_id=1, source_target_pairs={{0,16},{16,32},{32,48},{48,64},{64,80},{80,96},{96,112},{1,17},{17... | collective-permute-start | bytes 4808 | tf_op jit(solution)/shard_map/ppermute | solution.py:31
  87.5 2.0 %collective-permute-done.7.zr_ref = f32[400,1]{1,0:T(8,128)S(1)} collective-permute-done((f32[400,1]{1,0:T(8,128)S(1)}, f32[400,1]{1,0:T(8,128)S(1)}, u32[]{:S(2)}, u32[]{:S(2)}) %collective-permute-start.7) | collective-permute-done | bytes 1632 | tf_op jit(solution)/shard_map/ppermute | solution.py:36
  89.5 0.7 collective-permute-done.6.zl_ref
  90.2 0.1 all-to-all-done.1
  90.3 0.5 copy-done.11
  90.9 0.1 copy-done.8
  91.1 4.0 %shard_map.61 = (f32[400,128]{1,0:T(8,128)}, f32[400,128]{1,0:T(8,128)}, f32[400,128]{1,0:T(8,128)}, f32[400,128]{1,0:T(8,128)}, f32[400,128]{1,0:T(8,128)}, /*index=5*/f32[128,128]{1,0:T(8,128)}, f32[1,128]{1,0:T(1,128)}) custom-call(f32[128,128]{1,0:T(8,128)} %bitcast.103, f32[400,400]{1,0:T(8,128)} %add_add_fusion.k_ref, f32[400,128]{1,0:T(8,128)} %copy-done.1, ...), custom_call_target="tpu_custom_call" | custom-call | tf_op jit(solution)/shard_map/pallas_call | solution.py:175
  95.1 20.8 %all_to_all.27 = f32[128,1,128]{2,1,0:T(1,128)} all-to-all(f32[128,1,128]{2,1,0:T(1,128)} %bitcast.108), channel_id=1, replica_groups=mesh['pair'=8,'tile'=16] {'pair','tile'}, dimensions={0} | all-to-all | bytes 131072 | tf_op jit(solution)/shard_map/all_to_all | solution.py:184
  115.9 2.2 %shard_map.62 = (f32[400,128]{1,0:T(8,128)}, f32[400,128]{1,0:T(8,128)}) custom-call(f32[128,128]{1,0:T(8,128)} %bitcast.104, f32[1,128]{1,0:T(1,128)} %get-tuple-element.16.scal_ref, f32[400,128]{1,0:T(8,128)} %get-tuple-element.17.r_ref, f32[400,128]{1,0:T(8,128)} %get-tuple-element.18.p_ref, f32[400,128]{1,0:T(8,128)} %get-tuple-element.19.q_ref, ...), custom_call_target="tpu_custom_call" | custom-call | tf_op jit(solution)/shard_map/pallas_call | solution.py:175
  (61 shorter events, 0.9 us)
Async XLA Ops:
  3.8 0.7 copy-start.12
  5.6 22.6 %all-to-all-start = ((f32[8,250,136]{1,2,0:T(8,128)}), f32[8,250,136]{1,2,0:T(8,128)S(1)}, u32[]{:S(2)}, u32[]{:S(2)}) async-start(f32[8,250,136]{1,2,0:T(8,128)} %pad_maximum_fusion), calls=%async_computation | async-start | bytes 2228224 | tf_op jit(solution)/shard_map/all_to_all | solution.py:206
  32.5 0.7 copy-start.1
  32.5 6.1 %copy-start.4 = (f32[400,400]{1,0:T(8,128)S(1)}, f32[400,400]{1,0:T(8,128)}, u32[]{:S(2)}) copy-start(f32[400,400]{1,0:T(8,128)} %constant.49.clone) | copy-start | bytes 1920004
  33.0 8.3 %copy-start.2 = (f32[400,1]{1,0:T(8,128)}, f32[400,1]{1,0:T(8,128)S(1)}, u32[]{:S(2)}) copy-start(f32[400,1]{1,0:T(8,128)S(1)} %get-tuple-element.45.vr_ref.rr_ref) | copy-start | bytes 4804
  33.0 8.4 %copy-start.3 = (f32[400,1]{1,0:T(8,128)}, f32[400,1]{1,0:T(8,128)S(1)}, u32[]{:S(2)}) copy-start(f32[400,1]{1,0:T(8,128)S(1)} %get-tuple-element.46.vl_ref.rl_ref) | copy-start | bytes 4804
  33.2 8.4 %collective-permute-start.1 = (f32[408,128]{1,0:T(8,128)S(1)}, f32[408,128]{1,0:T(8,128)S(1)}, u32[]{:S(2)}, u32[]{:S(2)}) collective-permute-start(f32[408,128]{1,0:T(8,128)S(1)} %pad_maximum_fusion.1), channel_id=1, source_target_pairs={{1,0},{2,1},{3,2},{4,3},{5,4},{6,5},{7,6},{8,7},{9,8},{10,9},{11,1... | collective-permute-start | bytes 626696 | tf_op jit(solution)/shard_map/ppermute | solution.py:36
  34.5 7.8 %collective-permute-start = (f32[408,128]{1,0:T(8,128)S(1)}, f32[408,128]{1,0:T(8,128)S(1)}, u32[]{:S(2)}, u32[]{:S(2)}) collective-permute-start(f32[408,128]{1,0:T(8,128)S(1)} %pad_maximum_fusion.1), channel_id=1, source_target_pairs={{0,1},{1,2},{2,3},{3,4},{4,5},{5,6},{6,7},{7,8},{8,9},{9,10},{10,1... | collective-permute-start | bytes 626696 | tf_op jit(solution)/shard_map/ppermute | solution.py:31
  42.9 8.9 %copy-start = (f32[400,400]{1,0:T(8,128)S(1)}, f32[400,400]{1,0:T(8,128)}, u32[]{:S(2)}) copy-start(f32[400,400]{1,0:T(8,128)} %add_add_fusion.k_ref) | copy-start | bytes 1920004
  46.0 7.4 %collective-permute-start.3 = (f32[400,128]{1,0:T(8,128)}, f32[400,128]{1,0:T(8,128)S(1)}, u32[]{:S(2)}, u32[]{:S(2)}) collective-permute-start(f32[400,128]{1,0:T(8,128)} %shard_map.59.w_ref), channel_id=1, source_target_pairs={{1,0},{2,1},{3,2},{4,3},{5,4},{6,5},{7,6},{8,7},{9,8},{10,9},{11,1... | collective-permute-start | bytes 614408 | tf_op jit(solution)/shard_map/ppermute | solution.py:36
  47.3 7.3 %collective-permute-start.2 = (f32[400,128]{1,0:T(8,128)}, f32[400,128]{1,0:T(8,128)S(1)}, u32[]{:S(2)}, u32[]{:S(2)}) collective-permute-start(f32[400,128]{1,0:T(8,128)} %shard_map.59.w_ref), channel_id=1, source_target_pairs={{0,1},{1,2},{2,3},{3,4},{4,5},{5,6},{6,7},{7,8},{8,9},{9,10},{10,1... | collective-permute-start | bytes 614408 | tf_op jit(solution)/shard_map/ppermute | solution.py:31
  53.4 1.1 copy-start.5
  54.6 0.7 copy-start.6
  58.4 31.9 %collective-permute-start.5 = (f32[400,128]{1,0:T(8,128)}, f32[400,128]{1,0:T(8,128)S(1)}, u32[]{:S(2)}, u32[]{:S(2)}) collective-permute-start(f32[400,128]{1,0:T(8,128)} %get-tuple-element.14.z_ref), channel_id=1, source_target_pairs={{1,0},{2,1},{3,2},{4,3},{5,4},{6,5},{7,6},{8,7},{9,8},{10,9},{11,1... | collective-permute-start | bytes 614408 | tf_op jit(solution)/shard_map/ppermute | solution.py:36
  59.7 30.6 %collective-permute-start.4 = (f32[400,128]{1,0:T(8,128)}, f32[400,128]{1,0:T(8,128)S(1)}, u32[]{:S(2)}, u32[]{:S(2)}) collective-permute-start(f32[400,128]{1,0:T(8,128)} %get-tuple-element.14.z_ref), channel_id=1, source_target_pairs={{0,1},{1,2},{2,3},{3,4},{4,5},{5,6},{6,7},{7,8},{8,9},{9,10},{10,1... | collective-permute-start | bytes 614408 | tf_op jit(solution)/shard_map/ppermute | solution.py:31
  64.4 26.0 %all-to-all-start.1 = ((f32[128,1,128]{2,1,0:T(1,128)}), f32[128,1,128]{2,1,0:T(1,128)S(1)}, u32[]{:S(2)}, u32[]{:S(2)}) async-start(f32[128,1,128]{2,1,0:T(1,128)} %bitcast.107), calls=%async_computation.1 | async-start | bytes 131072 | tf_op jit(solution)/shard_map/all_to_all | solution.py:184
  81.9 7.6 %collective-permute-start.7 = (f32[400,1]{1,0:T(8,128)S(1)}, f32[400,1]{1,0:T(8,128)S(1)}, u32[]{:S(2)}, u32[]{:S(2)}) collective-permute-start(f32[400,1]{1,0:T(8,128)S(1)} %get-tuple-element.47), channel_id=1, source_target_pairs={{16,0},{32,16},{48,32},{64,48},{80,64},{96,80},{112,96},{17,1},{33... | collective-permute-start | bytes 4808 | tf_op jit(solution)/shard_map/ppermute | solution.py:36
  84.9 5.3 %collective-permute-start.6 = (f32[400,1]{1,0:T(8,128)S(1)}, f32[400,1]{1,0:T(8,128)S(1)}, u32[]{:S(2)}, u32[]{:S(2)}) collective-permute-start(f32[400,1]{1,0:T(8,128)S(1)} %get-tuple-element.48), channel_id=1, source_target_pairs={{0,16},{16,32},{32,48},{48,64},{64,80},{80,96},{96,112},{1,17},{17... | collective-permute-start | bytes 4808 | tf_op jit(solution)/shard_map/ppermute | solution.py:31
  89.5 0.8 copy-start.10
  90.2 0.7 copy-start.11
  90.3 0.6 copy-start.7
  90.3 0.7 copy-start.8
  90.3 0.8 copy-start.9

commit v15 on v13

--- a/solution.py
+++ b/solution.py
@@ -195,13 +195,17 @@
     groups = lax.axis_size("pair")
     cols = phase.shape[2] // groups
     padded = jnp.pad(phase[:, 0, :], ((0, 0), (2, 2)))
-    windows = jnp.stack([padded[:, j * cols : j * cols + cols + 4] for j in range(groups)])
+    width = groups * cols
+    blocks = padded[:, 2 : width + 2].reshape(-1, groups, cols)
+    below_block = padded[:, :width].reshape(-1, groups, cols)[:, :, :2]
+    above_block = padded[:, 4 : width + 4].reshape(-1, groups, cols)[:, :, cols - 2 :]
+    windows = jnp.concatenate([below_block, blocks, above_block], axis=2)
     meta = jnp.stack(
         [incidence[:, 0].astype(jnp.float32), incidence[:, 1].astype(jnp.float32), pair_weight], axis=1
     )
     meta = jnp.pad(meta, ((0, 0), (0, 1)))
-    chunks = jnp.concatenate([windows, jnp.broadcast_to(meta, (groups,) + meta.shape)], axis=2)
-    got = lax.all_to_all(chunks, "pair", 0, 0, tiled=True).reshape(-1, chunks.shape[2])
+    chunks = jnp.concatenate([windows, jnp.broadcast_to(meta[:, None, :], (meta.shape[0], groups, meta.shape[1]))], axis=2)
+    got = lax.all_to_all(chunks, "pair", 1, 0, tiled=True).reshape(-1, chunks.shape[2])
     values = got[:, : cols + 4]
     earlier = got[:, cols + 4 : cols + 5]
     later = got[:, cols + 5 : cols + 6]

time: 119 us -> 121 us (1.017)
  local copies, waits for them, and re-layouts: 10.3 us -> 13.5 us
    slice x0 -> x5, local copies, waits for them, and re-layouts: none -> 3.13 us  [the longest x3 2.79 us: body(): below_block = padded[:, :width].reshape(-1, groups, cols)[:, :, :2]]
    unnamed x32 -> x30, local copies, waits for them, and re-layouts: 4.57 us -> 4.67 us
where the time goes in v15:
time: 121 us; the launch traced here: 120 us
  starting transfers between devices  45.1 us (37%)
  blocking collectives  20.8 us (17%)
  waiting for transfers between devices  19.3 us (16%)
  local copies, waits for them, and re-layouts  13.5 us (11%)
  Pallas kernels  12.4 us (10%)
  other arithmetic  4.9 us (4%)
  matrix products  3.5 us (3%)
    all_to_all x1, blocking collectives, reduce_all(): return lax.all_to_all(send, ('pair', 'tile'), 0, 0, tiled=True)  20.8 us
    all_to_all x1, starting transfers between devices, reduce_all(): return lax.all_to_all(send, ('pair', 'tile'), 0, 0, tiled=True)  16 us
    all_to_all x1, waiting for transfers between devices, body(): lax.all_to_all(chunks, 'pair', 1, 0, tiled=True)  15.7 us
    ppermute x4, starting transfers between devices, from_prev(): return lax.ppermute(cells, axis, [(i, i + 1) for i in range(count - 1)])  15.2 us
    pallas_call x4, Pallas kernels, call(): pl.pallas_call(kernel, out_shape=[jax.ShapeDtypeStruct(s, jnp.float32) fo...  12.4 us
    ppermute x4, starting transfers between devices, from_next(): return lax.ppermute(cells, axis, [(i + 1, i) for i in range(count - 1)])  6.96 us
    all_to_all x1, starting transfers between devices, body(): lax.all_to_all(chunks, 'pair', 1, 0, tiled=True)  6.81 us
    unnamed x30, local copies, waits for them, and re-layouts  4.67 us
  transfers between devices with their start and end apart: 10, of which 5 were waited for; matrix products, arithmetic and copies ran while one was open for 7% of the time, Pallas kernels for 0%

profile of v15, /device:TPU:1, one launch (start us, length us, event | category | flops | bytes accessed | tf_op | source)
XLA Modules:
  0.0 120.5 jit_solution(7414332402232013185)
XLA Ops:
  0.6 2.4 %copy.45 = f32[250,1,1024]{0,2,1:T(8,128)S(1)} copy(f32[250,1,1024]{2,1,0:T(1,128)} %param.4) | data formatting | bytes 2048000 | tf_op args[0]
  3.1 0.2 copy.68
  3.3 0.5 copy-done.12
  3.8 0.6 pad_slice_fusion.1
  4.4 1.3 %copy.44 = f32[250,1024]{0,1:T(8,128)} copy(f32[250,1024]{1,0:T(8,128)S(1)} %get-tuple-element.41) | data formatting | bytes 2048000 | tf_op jit(solution)/shard_map/slice | solution.py:200
  5.7 0.9 slice.173
  6.6 0.3 copy.46
  7.0 1.2 pad_maximum_fusion
  8.2 6.8 %all-to-all-start = ((f32[250,8,136]{0,2,1:T(8,128)}), f32[250,8,136]{0,2,1:T(8,128)S(1)}, u32[]{:S(2)}, u32[]{:S(2)}) async-start(f32[250,8,136]{0,2,1:T(8,128)} %pad_maximum_fusion), calls=%async_computation | async-start | bytes 2228224 | tf_op jit(solution)/shard_map/all_to_all | solution.py:208
  15.0 15.7 %all-to-all-done = f32[250,8,136]{0,2,1:T(8,128)S(1)} async-done(((f32[250,8,136]{0,2,1:T(8,128)}), f32[250,8,136]{0,2,1:T(8,128)S(1)}, u32[]{:S(2)}, u32[]{:S(2)}) %all-to-all-start) | async-done | bytes 1088032 | tf_op jit(solution)/shard_map/all_to_all | solution.py:208
  30.8 0.4 copy.47
  31.1 0.5 reshape.56
  31.7 0.3 reduce-precision_convert_fusion.1
  32.0 1.9 %fusion.1 = f32[400,396]{1,0:T(8,128)S(1)} fusion(f32[2000]{0:T(1024)S(1)} %bitcast.84, f32[2000]{0:T(1024)S(1)} %bitcast.82, bf16[2000,132]{0,1:T(8,128)(2,1)S(1)} %get-tuple-element.35, bf16[2000,132]{0,1:T(8,128)(2,1)S(1)} %get-tuple-element.36, bf16[2000,132]{0,1:T(8,128)(2,1)S(1)} %get-tuple-element.34), kind=kOutput, calls=%fused_computation.5 | convolution fusion | flops 643152000 | bytes 2233600 | tf_op jit(solution)/shard_map/kt,kc->tc/dot_general | solution.py:224
  33.9 0.3 slice_add_fusion
  34.3 0.5 slice_reduce_fusion.1
  35.0 1.4 %collective-permute-start.1 = (f32[408,128]{1,0:T(8,128)S(1)}, f32[408,128]{1,0:T(8,128)S(1)}, u32[]{:S(2)}, u32[]{:S(2)}) collective-permute-start(f32[408,128]{1,0:T(8,128)S(1)} %pad_maximum_fusion.1), channel_id=1, source_target_pairs={{1,0},{2,1},{3,2},{4,3},{5,4},{6,5},{7,6},{8,7},{9,8},{10,9},{11,1... | collective-permute-start | bytes 626696 | tf_op jit(solution)/shard_map/ppermute | solution.py:36
  36.5 4.0 %collective-permute-start = (f32[408,128]{1,0:T(8,128)S(1)}, f32[408,128]{1,0:T(8,128)S(1)}, u32[]{:S(2)}, u32[]{:S(2)}) collective-permute-start(f32[408,128]{1,0:T(8,128)S(1)} %pad_maximum_fusion.1), channel_id=1, source_target_pairs={{0,1},{1,2},{2,3},{3,4},{4,5},{5,6},{6,7},{7,8},{8,9},{9,10},{10,1... | collective-permute-start | bytes 626696 | tf_op jit(solution)/shard_map/ppermute | solution.py:31
  40.5 0.5 fusion.3
  41.0 0.6 fusion.29
  41.6 2.2 %add_add_fusion.k_ref = f32[400,400]{1,0:T(8,128)} fusion(f32[400,400]{1,0:T(8,128)S(1)} %copy-done.4, f32[400]{0:T(512)S(1)} %negate_add_fusion, f32[400]{0:T(512)S(1)} %bitcast.64, f32[400]{0:T(512)S(1)} %bitcast.67, f32[400]{0:T(512)S(1)} %bitcast.70, f32[400]{0:T(512)S(1)} %bitcast.73, f32[400]{0:T(512)S(1)} %bitcast.76, f32[400]{0:T(512)S(1)} %bitcast.79, ...), kind=kLoop, calls=%fused_computation.27 | loop fusion | flops 7520000 | bytes 1292800 | tf_op jit(solution)/shard_map/add | solution.py:75
  43.9 0.1 copy.53
  44.2 0.1 copy.52
  44.4 0.1 copy.51
  44.5 0.7 slice.196.vd_ref.rd_ref
  45.2 0.7 slice.195.vu_ref.ru_ref
  45.9 3.0 %shard_map.59.w_ref = f32[400,128]{1,0:T(8,128)} custom-call(f32[400,400]{1,0:T(8,128)} %add_add_fusion.k_ref, f32[400,128]{1,0:T(8,128)} %copy-done, f32[400,128]{1,0:T(8,128)} %slice.195.vu_ref.ru_ref, f32[400,128]{1,0:T(8,128)} %slice.196.vd_ref.rd_ref, f32[400,1]{1,0:T(8,128)} %copy-done.3, f32[400,1]{1,0:T(8,128)} %copy-done.2), custom_call_target="tpu_custom_call" | custom-call | tf_op jit(solution)/shard_map/pallas_call | solution.py:173
  49.0 1.3 %collective-permute-start.3 = (f32[400,128]{1,0:T(8,128)}, f32[400,128]{1,0:T(8,128)S(1)}, u32[]{:S(2)}, u32[]{:S(2)}) collective-permute-start(f32[400,128]{1,0:T(8,128)} %shard_map.59.w_ref), channel_id=1, source_target_pairs={{1,0},{2,1},{3,2},{4,3},{5,4},{6,5},{7,6},{8,7},{9,8},{10,9},{11,1... | collective-permute-start | bytes 614408 | tf_op jit(solution)/shard_map/ppermute | solution.py:36
  50.2 4.0 %collective-permute-start.2 = (f32[400,128]{1,0:T(8,128)}, f32[400,128]{1,0:T(8,128)S(1)}, u32[]{:S(2)}, u32[]{:S(2)}) collective-permute-start(f32[400,128]{1,0:T(8,128)} %shard_map.59.w_ref), channel_id=1, source_target_pairs={{0,1},{1,2},{2,3},{3,4},{4,5},{5,6},{6,7},{7,8},{8,9},{9,10},{10,1... | collective-permute-start | bytes 614408 | tf_op jit(solution)/shard_map/ppermute | solution.py:31
  54.4 0.1 copy.59
  54.5 1.1 fusion.12
  55.7 0.8 fusion.45
  56.5 0.7 collective-permute-done.2.wu_ref
  57.2 0.7 copy-done.6
  57.9 3.2 %shard_map.60 = (f32[400,128]{1,0:T(8,128)}, f32[128,128]{1,0:T(8,128)}) custom-call(f32[400,400]{1,0:T(8,128)} %add_add_fusion.k_ref, f32[400,128]{1,0:T(8,128)} %copy-done, f32[400,128]{1,0:T(8,128)} %shard_map.59.w_ref, f32[400,128]{1,0:T(8,128)} %copy-done.6, f32[400,128]{1,0:T(8,128)} %copy-done.5, f32[400,1]{1,0:T(8,128)} %get-tuple-element.52.wl_ref, ...), custom_call_target="tpu_custom_call" | custom-call | tf_op jit(solution)/shard_map/pallas_call | solution.py:173
  61.1 1.3 %collective-permute-start.5 = (f32[400,128]{1,0:T(8,128)}, f32[400,128]{1,0:T(8,128)S(1)}, u32[]{:S(2)}, u32[]{:S(2)}) collective-permute-start(f32[400,128]{1,0:T(8,128)} %get-tuple-element.14.z_ref), channel_id=1, source_target_pairs={{1,0},{2,1},{3,2},{4,3},{5,4},{6,5},{7,6},{8,7},{9,8},{10,9},{11,1... | collective-permute-start | bytes 614408 | tf_op jit(solution)/shard_map/ppermute | solution.py:36
  62.4 4.6 %collective-permute-start.4 = (f32[400,128]{1,0:T(8,128)}, f32[400,128]{1,0:T(8,128)S(1)}, u32[]{:S(2)}, u32[]{:S(2)}) collective-permute-start(f32[400,128]{1,0:T(8,128)} %get-tuple-element.14.z_ref), channel_id=1, source_target_pairs={{0,1},{1,2},{2,3},{3,4},{4,5},{5,6},{6,7},{7,8},{8,9},{9,10},{10,1... | collective-permute-start | bytes 614408 | tf_op jit(solution)/shard_map/ppermute | solution.py:31
  67.1 16.0 %all-to-all-start.1 = ((f32[128,1,128]{2,1,0:T(1,128)}), f32[128,1,128]{2,1,0:T(1,128)S(1)}, u32[]{:S(2)}, u32[]{:S(2)}) async-start(f32[128,1,128]{2,1,0:T(1,128)} %bitcast.58), calls=%async_computation.1 | async-start | bytes 131072 | tf_op jit(solution)/shard_map/all_to_all | solution.py:182
  83.1 1.1 fusion.44
  84.2 3.0 %collective-permute-start.7 = (f32[400,1]{1,0:T(8,128)S(1)}, f32[400,1]{1,0:T(8,128)S(1)}, u32[]{:S(2)}, u32[]{:S(2)}) collective-permute-start(f32[400,1]{1,0:T(8,128)S(1)} %get-tuple-element.49), channel_id=1, source_target_pairs={{16,0},{32,16},{48,32},{64,48},{80,64},{96,80},{112,96},{17,1},{33... | collective-permute-start | bytes 4808 | tf_op jit(solution)/shard_map/ppermute | solution.py:36
  87.2 2.6 %collective-permute-start.6 = (f32[400,1]{1,0:T(8,128)S(1)}, f32[400,1]{1,0:T(8,128)S(1)}, u32[]{:S(2)}, u32[]{:S(2)}) collective-permute-start(f32[400,1]{1,0:T(8,128)S(1)} %get-tuple-element.50), channel_id=1, source_target_pairs={{0,16},{16,32},{32,48},{48,64},{64,80},{80,96},{96,112},{1,17},{17... | collective-permute-start | bytes 4808 | tf_op jit(solution)/shard_map/ppermute | solution.py:31
  89.8 2.0 %collective-permute-done.7.zr_ref = f32[400,1]{1,0:T(8,128)S(1)} collective-permute-done((f32[400,1]{1,0:T(8,128)S(1)}, f32[400,1]{1,0:T(8,128)S(1)}, u32[]{:S(2)}, u32[]{:S(2)}) %collective-permute-start.7) | collective-permute-done | bytes 1632 | tf_op jit(solution)/shard_map/ppermute | solution.py:36
  91.9 0.7 collective-permute-done.6.zl_ref
  92.5 0.1 all-to-all-done.1
  92.7 0.5 copy-done.11
  93.5 4.0 %shard_map.61 = (f32[400,128]{1,0:T(8,128)}, f32[400,128]{1,0:T(8,128)}, f32[400,128]{1,0:T(8,128)}, f32[400,128]{1,0:T(8,128)}, f32[400,128]{1,0:T(8,128)}, /*index=5*/f32[128,128]{1,0:T(8,128)}, f32[1,128]{1,0:T(1,128)}) custom-call(f32[128,128]{1,0:T(8,128)} %bitcast.54, f32[400,400]{1,0:T(8,128)} %add_add_fusion.k_ref, f32[400,128]{1,0:T(8,128)} %copy-done, ...), custom_call_target="tpu_custom_call" | custom-call | tf_op jit(solution)/shard_map/pallas_call | solution.py:173
  97.4 20.8 %all_to_all.37 = f32[128,1,128]{2,1,0:T(1,128)} all-to-all(f32[128,1,128]{2,1,0:T(1,128)} %bitcast.59), channel_id=1, replica_groups=mesh['pair'=8,'tile'=16] {'pair','tile'}, dimensions={0} | all-to-all | bytes 131072 | tf_op jit(solution)/shard_map/all_to_all | solution.py:182
  118.2 2.2 %shard_map.62 = (f32[400,128]{1,0:T(8,128)}, f32[400,128]{1,0:T(8,128)}) custom-call(f32[128,128]{1,0:T(8,128)} %bitcast.55, f32[1,128]{1,0:T(1,128)} %get-tuple-element.16.scal_ref, f32[400,128]{1,0:T(8,128)} %get-tuple-element.17.r_ref, f32[400,128]{1,0:T(8,128)} %get-tuple-element.18.p_ref, f32[400,128]{1,0:T(8,128)} %get-tuple-element.19.q_ref, ...), custom_call_target="tpu_custom_call" | custom-call | tf_op jit(solution)/shard_map/pallas_call | solution.py:173
  (53 shorter events, 1.2 us)
Async XLA Ops:
  0.6 2.5 %copy-start.1 = (f32[250,1,1024]{2,1,0:T(1,128)S(1)}, f32[250,1,1024]{2,1,0:T(1,128)}, u32[]{:S(2)}) copy-start(f32[250,1,1024]{2,1,0:T(1,128)} %param.4) | copy-start | bytes 3072004
  3.1 0.7 copy-start.12
  5.7 1.2 %copy-start.13 = (f32[250]{0:T(256)S(1)}, f32[250]{0:T(256)}, u32[]{:S(2)}) copy-start(f32[250]{0:T(256)} %param.6) | copy-start | bytes 3004
  8.2 22.6 %all-to-all-start = ((f32[250,8,136]{0,2,1:T(8,128)}), f32[250,8,136]{0,2,1:T(8,128)S(1)}, u32[]{:S(2)}, u32[]{:S(2)}) async-start(f32[250,8,136]{0,2,1:T(8,128)} %pad_maximum_fusion), calls=%async_computation | async-start | bytes 2228224 | tf_op jit(solution)/shard_map/all_to_all | solution.py:208
  34.3 0.7 copy-start
  34.8 9.4 %copy-start.2 = (f32[400,1]{1,0:T(8,128)}, f32[400,1]{1,0:T(8,128)S(1)}, u32[]{:S(2)}) copy-start(f32[400,1]{1,0:T(8,128)S(1)} %get-tuple-element.47.vr_ref.rr_ref) | copy-start | bytes 4804
  34.8 9.5 %copy-start.3 = (f32[400,1]{1,0:T(8,128)}, f32[400,1]{1,0:T(8,128)S(1)}, u32[]{:S(2)}) copy-start(f32[400,1]{1,0:T(8,128)S(1)} %get-tuple-element.48.vl_ref.rl_ref) | copy-start | bytes 4804
  35.0 6.5 %copy-start.4 = (f32[400,400]{1,0:T(8,128)S(1)}, f32[400,400]{1,0:T(8,128)}, u32[]{:S(2)}) copy-start(f32[400,400]{1,0:T(8,128)} %constant.35.clone) | copy-start | bytes 1920004
  35.0 9.5 %collective-permute-start.1 = (f32[408,128]{1,0:T(8,128)S(1)}, f32[408,128]{1,0:T(8,128)S(1)}, u32[]{:S(2)}, u32[]{:S(2)}) collective-permute-start(f32[408,128]{1,0:T(8,128)S(1)} %pad_maximum_fusion.1), channel_id=1, source_target_pairs={{1,0},{2,1},{3,2},{4,3},{5,4},{6,5},{7,6},{8,7},{9,8},{10,9},{11,1... | collective-permute-start | bytes 626696 | tf_op jit(solution)/shard_map/ppermute | solution.py:36
  36.5 8.8 %collective-permute-start = (f32[408,128]{1,0:T(8,128)S(1)}, f32[408,128]{1,0:T(8,128)S(1)}, u32[]{:S(2)}, u32[]{:S(2)}) collective-permute-start(f32[408,128]{1,0:T(8,128)S(1)} %pad_maximum_fusion.1), channel_id=1, source_target_pairs={{0,1},{1,2},{2,3},{3,4},{4,5},{5,6},{6,7},{7,8},{8,9},{9,10},{10,1... | collective-permute-start | bytes 626696 | tf_op jit(solution)/shard_map/ppermute | solution.py:31
  49.0 7.5 %collective-permute-start.3 = (f32[400,128]{1,0:T(8,128)}, f32[400,128]{1,0:T(8,128)S(1)}, u32[]{:S(2)}, u32[]{:S(2)}) collective-permute-start(f32[400,128]{1,0:T(8,128)} %shard_map.59.w_ref), channel_id=1, source_target_pairs={{1,0},{2,1},{3,2},{4,3},{5,4},{6,5},{7,6},{8,7},{9,8},{10,9},{11,1... | collective-permute-start | bytes 614408 | tf_op jit(solution)/shard_map/ppermute | solution.py:36
  50.2 7.0 %collective-permute-start.2 = (f32[400,128]{1,0:T(8,128)}, f32[400,128]{1,0:T(8,128)S(1)}, u32[]{:S(2)}, u32[]{:S(2)}) collective-permute-start(f32[400,128]{1,0:T(8,128)} %shard_map.59.w_ref), channel_id=1, source_target_pairs={{0,1},{1,2},{2,3},{3,4},{4,5},{5,6},{6,7},{7,8},{8,9},{9,10},{10,1... | collective-permute-start | bytes 614408 | tf_op jit(solution)/shard_map/ppermute | solution.py:31
  56.5 0.7 copy-start.5
  57.2 0.7 copy-start.6
  61.1 31.6 %collective-permute-start.5 = (f32[400,128]{1,0:T(8,128)}, f32[400,128]{1,0:T(8,128)S(1)}, u32[]{:S(2)}, u32[]{:S(2)}) collective-permute-start(f32[400,128]{1,0:T(8,128)} %get-tuple-element.14.z_ref), channel_id=1, source_target_pairs={{1,0},{2,1},{3,2},{4,3},{5,4},{6,5},{7,6},{8,7},{9,8},{10,9},{11,1... | collective-permute-start | bytes 614408 | tf_op jit(solution)/shard_map/ppermute | solution.py:36
  62.4 30.3 %collective-permute-start.4 = (f32[400,128]{1,0:T(8,128)}, f32[400,128]{1,0:T(8,128)S(1)}, u32[]{:S(2)}, u32[]{:S(2)}) collective-permute-start(f32[400,128]{1,0:T(8,128)} %get-tuple-element.14.z_ref), channel_id=1, source_target_pairs={{0,1},{1,2},{2,3},{3,4},{4,5},{5,6},{6,7},{7,8},{8,9},{9,10},{10,1... | collective-permute-start | bytes 614408 | tf_op jit(solution)/shard_map/ppermute | solution.py:31
  67.1 25.6 %all-to-all-start.1 = ((f32[128,1,128]{2,1,0:T(1,128)}), f32[128,1,128]{2,1,0:T(1,128)S(1)}, u32[]{:S(2)}, u32[]{:S(2)}) async-start(f32[128,1,128]{2,1,0:T(1,128)} %bitcast.58), calls=%async_computation.1 | async-start | bytes 131072 | tf_op jit(solution)/shard_map/all_to_all | solution.py:182
  84.2 7.6 %collective-permute-start.7 = (f32[400,1]{1,0:T(8,128)S(1)}, f32[400,1]{1,0:T(8,128)S(1)}, u32[]{:S(2)}, u32[]{:S(2)}) collective-permute-start(f32[400,1]{1,0:T(8,128)S(1)} %get-tuple-element.49), channel_id=1, source_target_pairs={{16,0},{32,16},{48,32},{64,48},{80,64},{96,80},{112,96},{17,1},{33... | collective-permute-start | bytes 4808 | tf_op jit(solution)/shard_map/ppermute | solution.py:36
  87.2 5.3 %collective-permute-start.6 = (f32[400,1]{1,0:T(8,128)S(1)}, f32[400,1]{1,0:T(8,128)S(1)}, u32[]{:S(2)}, u32[]{:S(2)}) collective-permute-start(f32[400,1]{1,0:T(8,128)S(1)} %get-tuple-element.50), channel_id=1, source_target_pairs={{0,16},{16,32},{32,48},{48,64},{64,80},{80,96},{96,112},{1,17},{17... | collective-permute-start | bytes 4808 | tf_op jit(solution)/shard_map/ppermute | solution.py:31
  91.9 0.8 copy-start.10
  92.5 0.7 copy-start.11
  92.7 0.6 copy-start.7
  92.7 0.7 copy-start.8
  92.7 0.8 copy-start.9
